TPU v7x, 512 devices: a whole 4x8x8 slice. The times are simulated.
512 devices in a mesh: req: 4 (over x), exp: 8 (over z), shard: 16 (over y, core).
Axes of the slice: x: 4, y: 8, z: 8, core: 2. Of those that a mesh axis runs over, the one named last changes fastest.
Arguments:
- query_stretch: bfloat16 [8, 128, 2304], P('req', 'exp'), may hold values from -8 to 8
- resid_stretch: bfloat16 [8, 128, 2304], P('req', 'exp'), may hold values from -30 to 30
- route_ids: int32 [8, 128, 2], P('req', 'exp'), may hold values from 0 to 7, all different within a row; in each aligned block of 16 rows (0 to 15, 16 to 31, ..., all dimensions but the last counted through in order) at most 6 rows name the same one
- route_probs: bfloat16 [8, 128, 2], P('req', 'exp'), may hold values from 0.19921875 to 1
- request_order: int32 [8], replicated, may hold values from 0 to 7, each once
- prior_pages: int32 [4, 2], P('req'), may hold values from 63 to 189, as said below
- page_order: int32 [4, 256], P('req'), may hold values from 0 to 255, each once within a row
- key_pool: bfloat16 [4, 256, 64, 2304], P('req', ('exp', 'shard')), may hold values from -8 to 8
- value_pool: bfloat16 [4, 256, 64, 2304], P('req', ('exp', 'shard')), may hold values from -6 to 6
- norm_gain: float32 [2304], replicated, may hold values from 0.4 to 2.5
- out_proj: bfloat16 [2304, 2304], P('shard'), may hold values from -0.125 to 0.125
- gate_up: bfloat16 [8, 2, 2880, 2304], P('exp', None, 'shard'), may hold values from -0.125 to 0.125
- down_proj: bfloat16 [8, 2880, 2304], P('exp', 'shard'), may hold values from -0.109375 to 0.109375
Outputs:
- mixed_out: bfloat16 [8, 128, 2304], P('req', 'exp')
Inputs may be any that keep to these rules, and one draw needn't show every extreme that they name: `route_ids`: each row names 2 different experts. In each aligned block of 16 rows (one request's tokens b * 16 to (b + 1) * 16 - 1) no expert is named by more than 6 rows, a bound that some block reaches. `request_order`: A permutation of the requests. `prior_pages`: in each group the 2 counts sum to 252, so that the pool is full; one member of every group has exactly 189. `page_order`: each row is a permutation of the group's pool pages.
All inputs are finite; a program needn't handle non-finite values.
Results may differ from a plain program's by a relative error of at most 0.02.
Values may be sent and summed in bfloat16 or wider, within the bound.
No kernel may reach another device: no remote copies, remote signals or barrier semaphores. Data moves between devices by JAX's collectives and lax.ppermute only.
A program may use at most 64 MiB of HBM per device.

v0:
```python
import math

import jax
import jax.numpy as jnp
from jax import lax
from jax.sharding import PartitionSpec as P

H = 36


NEG_FILL = -1e30
EPSILON = 1e-06


def expert_rows(received, gate_up, down_proj):
    width = received.shape[-1]
    flat_rows = received.reshape(-1, width)
    both = lax.dot_general(
        flat_rows, gate_up[0], (((1,), (2,)), ((), ())), preferred_element_type=jnp.float32
    )
    active = (jax.nn.silu(both[:, 0]) * both[:, 1]).astype(jnp.bfloat16)
    partial_out = jnp.dot(active, down_proj[0], preferred_element_type=jnp.float32)
    return partial_out.reshape(received.shape)


def on_device(
    query_stretch,
    resid_stretch,
    route_ids,
    route_probs,
    request_order,
    prior_pages,
    page_order,
    key_pool,
    value_pool,
    norm_gain,
    out_proj,
    gate_up,
    down_proj,
):
    members = prior_pages.shape[1]
    tokens_here = query_stretch.shape[1]
    width = query_stretch.shape[2]
    head_size = width // H
    group_index = lax.axis_index("req")
    exp_index = lax.axis_index("exp")
    shard_index = lax.axis_index("shard")
    shard_count = lax.axis_size("shard")
    experts_count = lax.axis_size("exp")
    all_query, all_resid, all_ids, all_probs = (
        lax.all_gather(query_stretch, "req", axis=0, tiled=True),
        lax.all_gather(resid_stretch, "req", axis=0, tiled=True),
        lax.all_gather(route_ids, "req", axis=0, tiled=True),
        lax.all_gather(route_probs, "req", axis=0, tiled=True),
    )
    served = lax.dynamic_slice_in_dim(request_order, group_index * members, members)
    served_query = jnp.take(all_query, served, axis=0)
    served_resid = jnp.take(all_resid, served, axis=0)
    served_ids = jnp.take(all_ids, served, axis=0)
    served_probs = jnp.take(all_probs, served, axis=0)
    group_query = lax.all_gather(served_query, "exp", axis=1, tiled=True)
    stretch_len = group_query.shape[1]
    pages_here = key_pool.shape[1]
    page_size = key_pool.shape[2]
    device_index = exp_index * shard_count + shard_index
    physical = device_index * pages_here + jnp.arange(pages_here, dtype=jnp.int32)
    page_row = page_order[0]
    pool_size = page_row.shape[0]
    matched = page_row[None, :] == physical[:, None]
    located = jnp.sum(
        jnp.where(matched, jnp.arange(pool_size, dtype=jnp.int32)[None, :], 0), axis=1
    )
    prior_row = prior_pages[0]
    page_counts = prior_row + stretch_len // page_size
    page_ends = jnp.cumsum(page_counts)
    page_starts = page_ends - page_counts
    owner_slot = jnp.sum((located[:, None] >= page_ends[None, :]).astype(jnp.int32), axis=1)
    owner_hot = owner_slot[:, None] == jnp.arange(members, dtype=jnp.int32)[None, :]
    logical = located - jnp.sum(jnp.where(owner_hot, page_starts[None, :], 0), axis=1)
    prior_here = jnp.sum(jnp.where(owner_hot, prior_row[None, :], 0), axis=1)
    key_place = logical[:, None] * page_size + jnp.arange(page_size, dtype=jnp.int32)[None, :]
    query_place = (
        prior_here[:, None] * page_size + jnp.arange(stretch_len, dtype=jnp.int32)[None, :]
    )
    visible = key_place[:, None, :] <= query_place[:, :, None]
    page_query = jnp.take(group_query, owner_slot, axis=0).reshape(
        pages_here, stretch_len, H, head_size
    )
    key_rows = key_pool[0].reshape(pages_here, page_size, H, head_size)
    value_rows = value_pool[0].reshape(pages_here, page_size, H, head_size)
    scores = jnp.einsum(
        "pqhd,pkhd->phqk", page_query, key_rows, preferred_element_type=jnp.float32
    ) * (1.0 / math.sqrt(head_size))
    scores = jnp.where(visible[:, None, :, :], scores, NEG_FILL)
    page_peak = jnp.max(scores, axis=3)
    local_peak = jnp.max(
        jnp.where(owner_hot[:, :, None, None], page_peak[:, None], NEG_FILL), axis=0
    )
    row_peak = lax.pmax(local_peak, ("exp", "shard"))
    peak_here = jnp.take(row_peak, owner_slot, axis=0)
    weights_bf = jnp.where(
        visible[:, None, :, :], jnp.exp(scores - peak_here[..., None]), 0.0
    ).astype(jnp.bfloat16)
    page_totals = jnp.sum(weights_bf, axis=3, dtype=jnp.float32)
    page_context = jnp.einsum(
        "phqk,pkhd->pqhd", weights_bf, value_rows, preferred_element_type=jnp.float32
    )
    page_context = page_context.reshape(pages_here, stretch_len, width)
    context = jnp.sum(jnp.where(owner_hot[:, :, None, None], page_context[:, None], 0.0), axis=0)
    totals = jnp.sum(jnp.where(owner_hot[:, :, None, None], page_totals[:, None], 0.0), axis=0)
    context_all, totals_all = lax.psum((context, totals), ("exp", "shard"))
    context_mine = lax.dynamic_slice_in_dim(context_all, exp_index * tokens_here, tokens_here, 1)
    totals_mine = lax.dynamic_slice_in_dim(totals_all, exp_index * tokens_here, tokens_here, 2)
    per_head = context_mine.reshape(members, tokens_here, H, head_size)
    attended = (
        (per_head / jnp.transpose(totals_mine, (0, 2, 1))[..., None])
        .reshape(members, tokens_here, width)
        .astype(jnp.bfloat16)
    )
    projected_part = lax.dot_general(
        attended, out_proj, (((2,), (1,)), ((), ())), preferred_element_type=jnp.float32
    ).astype(jnp.bfloat16)
    projected = lax.all_gather(projected_part, "shard", axis=2, tiled=True)
    hidden_state = served_resid.astype(jnp.float32) + projected.astype(jnp.float32)
    mean_square = jnp.mean(hidden_state * hidden_state, axis=2, keepdims=True)
    normed = (hidden_state * lax.rsqrt(mean_square + EPSILON) * norm_gain).astype(jnp.bfloat16)
    top_count = served_ids.shape[2]
    capacity = min(tokens_here, max(2, 3 * tokens_here * top_count // (2 * experts_count)))
    flat_ids = served_ids.reshape(members, tokens_here * top_count)
    expert_hot = (
        flat_ids[:, :, None] == jnp.arange(experts_count, dtype=jnp.int32)[None, None, :]
    ).astype(jnp.int32)
    before = jnp.cumsum(expert_hot, axis=1) - expert_hot
    slot_place = jnp.sum(before * expert_hot, axis=2)
    slot_hot = (
        slot_place[:, :, None] == jnp.arange(capacity, dtype=jnp.int32)[None, None, :]
    ).astype(jnp.int32)
    place_table = (expert_hot[:, :, :, None] * slot_hot[:, :, None, :]).reshape(
        members, tokens_here, top_count, experts_count, capacity
    )
    pick_table = jnp.sum(place_table, axis=2).astype(jnp.bfloat16)
    sent_rows = jnp.einsum(
        "jtnc,jtd->njcd", pick_table, normed, preferred_element_type=jnp.float32
    ).astype(jnp.bfloat16)
    share_table = jnp.sum(
        place_table.astype(jnp.bfloat16) * served_probs[:, :, :, None, None], axis=2
    )
    partial_out = expert_rows(
        lax.all_to_all(sent_rows, "exp", split_axis=0, concat_axis=0, tiled=True),
        gate_up,
        down_proj,
    )
    expert_out = lax.psum(partial_out.astype(jnp.bfloat16), "shard")
    returned = lax.all_to_all(expert_out, "exp", split_axis=0, concat_axis=0, tiled=True)
    moe_term = jnp.einsum(
        "jtnc,njcd->jtd", share_table, returned, preferred_element_type=jnp.float32
    )
    mixed_out = (hidden_state + moe_term).astype(jnp.bfloat16)
    return mixed_out


def solution(mesh):
    return jax.shard_map(
        on_device,
        mesh=mesh,
        in_specs=(
            P("req", "exp", None),
            P("req", "exp", None),
            P("req", "exp", None),
            P("req", "exp", None),
            P(),
            P("req", None),
            P("req", None),
            P("req", ("exp", "shard"), None, None),
            P("req", ("exp", "shard"), None, None),
            P(),
            P("shard", None),
            P("exp", None, "shard", None),
            P("exp", "shard", None),
        ),
        out_specs=P("req", "exp", None),
        check_vma=False,
    )
```

profile of v0, /device:TPU:1, one launch (start us, length us, event | category | flops | bytes accessed | tf_op | source)
XLA Modules:
  0.0 1259.9 jit_solution(11993732823770950947)
XLA Ops:
  6.5 0.9 compare_and_fusion
  7.4 11.4 all_gather.19
  18.9 0.6 gather_fusion.5
  19.4 0.7 broadcast_select_fusion
  20.2 8.2 all_gather.22
  28.5 0.6 gather_fusion.2
  29.4 0.7 add_bitcast_fusion
  30.2 0.7 fusion.29
  30.9 0.9 fusion.26
  31.7 0.2 fusion.27
  31.9 0.6 reduce_window_sum.18
  32.6 2.8 reshape_squeeze.6
  35.4 1.4 copy.110
  36.8 0.2 select_reduce_fusion.5
  36.9 10.4 all_gather.18
  47.8 18.5 %all-gather.2.cloned.1.call-done = bf16[2,128,2304]{2,1,0:T(8,128)(2,1)} async-done(((bf16[2,16,2304]{2,1,0:T(8,128)(2,1)}), bf16[2,128,2304]{2,1,0:T(8,128)(2,1)}) %all-gather.2.cloned.1.call-update) | async-done | bytes 1179664 | tf_op jit(solution)/shard_map/all_gather | solution.py:61
  66.3 1.9 gather_fusion
  68.2 1.4 copy.90
  69.6 3.8 fusion.3
  73.6 490.0 %pmax.7 = f32[2,36,128]{2,1,0:T(8,128)S(1)} all-reduce(f32[2,36,128]{2,1,0:T(8,128)S(1)} %copy.92), channel_id=1, replica_groups=mesh['req'=4,'exp'=8,'shard'=16] {'exp','shard'}, use_global_device_ids=true, to_apply=%region_7.9 | all-reduce | flops 9216 | bytes 73728 | tf_op jit(solution)/shard_map/pmax | solution.py:99
  563.6 0.5 gather_fusion.1
  564.2 3.7 fusion.32
  567.9 3.1 copy.94
  571.0 3.7 select_reduce_fusion
  574.8 0.7 copy-done.5
  575.5 0.2 select_reduce_fusion.3
  575.8 0.6 gather_fusion.4
  576.4 2.4 convert_reduce_fusion
  578.9 491.2 %psum.22 = f32[2,36,128]{2,0,1:T(2,128)S(1)} all-reduce(f32[2,36,128]{2,0,1:T(2,128)S(1)} %select_reduce_fusion.1), channel_id=1, replica_groups=mesh['req'=4,'exp'=8,'shard'=16] {'exp','shard'}, use_global_device_ids=true, to_apply=%region_12.14 | all-reduce | flops 9216 | bytes 73728 | tf_op jit(solution)/shard_map/psum | solution.py:111
  1070.3 0.2 div.23
  1070.5 0.2 div.24
  1070.8 1.5 convolution_convert_fusion.2
  1072.4 23.8 %all_gather.21 = bf16[2,16,2304]{1,0,2:T(2,128)(2,1)S(1)} all-gather(bf16[2,16,144]{1,0,2:T(2,128)(2,1)S(1)} %copy.96), channel_id=1, replica_groups=mesh['req'=4,'exp'=8,'shard'=16] {'shard'}, dimensions={2}, use_global_device_ids=true | all-gather | bytes 156672 | tf_op jit(solution)/shard_map/all_gather | solution.py:123
  1096.3 1.4 copy.97
  1097.7 0.2 multiply_reduce_fusion
  1097.9 0.3 fusion
  1098.2 0.3 copy.100
  1098.6 20.1 %all_to_all.10 = bf16[8,2,6,2304]{3,1,2,0:T(2,128)(2,1)S(1)} all-to-all(bf16[8,2,6,2304]{3,1,2,0:T(2,128)(2,1)S(1)} %copy.100), channel_id=1, replica_groups=mesh['req'=4,'exp'=8,'shard'=16] {'exp'}, dimensions={0} | all-to-all | bytes 884736 | tf_op jit(solution)/shard_map/all_to_all | solution.py:149
  1118.7 0.9 reshape.247
  1119.6 1.6 fusion.4
  1121.5 1.0 convolution_convert_fusion.1
  1122.5 105.0 %all-reduce.5.cloned.1.call-done = bf16[8,2,6,2304]{3,0,2,1:T(8,128)(2,1)} async-done(((bf16[8,2,6,2304]{3,0,2,1:T(8,128)(2,1)}), bf16[8,2,6,2304]{3,0,2,1:T(8,128)(2,1)}) %all-reduce.5.cloned.1.call-update) | async-done | bytes 442384 | tf_op jit(solution)/shard_map/psum | solution.py:153
  1227.5 2.1 copy.105
  1229.6 6.7 all-to-all-start.1
  1236.3 7.9 all_gather.23
  1244.2 0.6 gather_fusion.3
  1244.9 7.6 all-to-all-done.1
  1252.5 0.9 fusion.2
  (59 shorter events, 2.3 us)
Async XLA Ops:
  6.5 1113.1 %copy-start = (bf16[1,2,180,2304]{3,1,2,0:T(2,128)(2,1)S(1)}, bf16[1,2,180,2304]{3,1,2,0:T(2,128)(2,1)}, u32[]{:S(2)}) copy-start(bf16[1,2,180,2304]{3,1,2,0:T(2,128)(2,1)} %param.26) | copy-start | bytes 4976644
  6.5 28.8 %copy-start.3 = (bf16[1,2,64,2304]{3,2,1,0:T(8,128)(2,1)S(1)}, bf16[1,2,64,2304]{3,2,1,0:T(8,128)(2,1)}, u32[]{:S(2)}) copy-start(bf16[1,2,64,2304]{3,2,1,0:T(8,128)(2,1)} %param.23) | copy-start | bytes 1769476
  6.5 59.7 %all-gather.2.cloned.1.call-start = ((), (), s32[]{:S(2)}) async-start(), calls=%async_computation.2 | async-start | bytes 1327104 | tf_op jit(solution)/shard_map/all_gather | solution.py:61
  18.9 17.9 %copy-start.8 = (s32[1,2]{1,0:T(1,128)S(1)}, s32[1,2]{1,0:T(1,128)}, u32[]{:S(2)}) copy-start(s32[1,2]{1,0:T(1,128)} %param.20) | copy-start | bytes 28
  19.4 17.5 %copy-start.4 = (bf16[2,16,2304]{2,1,0:T(8,128)(2,1)S(1)}, bf16[2,16,2304]{2,1,0:T(8,128)(2,1)}, u32[]{:S(2)}) copy-start(bf16[2,16,2304]{2,1,0:T(8,128)(2,1)} %param.16) | copy-start | bytes 442372
  20.2 1050.6 %all-reduce.3.cloned.1.call-start = ((), (), s32[]{:S(2)}) async-start(), calls=%async_computation.3 | async-start | bytes 4718592 | tf_op jit(solution)/shard_map/psum | solution.py:111
  69.6 494.6 %copy-start.1 = (bf16[1,2,64,2304]{2,3,1,0:T(8,128)(2,1)S(1)}, bf16[1,2,64,2304]{2,3,1,0:T(8,128)(2,1)}, u32[]{:S(2)}) copy-start(bf16[1,2,64,2304]{2,3,1,0:T(8,128)(2,1)} %copy.110) | copy-start | bytes 1769476
  574.7 0.8 copy-start.5
  574.7 652.8 %all-reduce.5.cloned.1.call-start = ((), (), s32[]{:S(2)}) async-start(), calls=%async_computation.4 | async-start | bytes 884736 | tf_op jit(solution)/shard_map/psum | solution.py:153
  1070.7 27.2 %copy-start.6 = (f32[2304]{0:T(1024)S(1)}, f32[2304]{0:T(1024)}, u32[]{:S(2)}) copy-start(f32[2304]{0:T(1024)} %param.24) | copy-start | bytes 27652
  1118.7 2.8 copy-start.2
  1121.3 115.0 %copy-start.7 = (bf16[2,16,2]{1,2,0:T(2,128)(2,1)S(1)}, bf16[2,16,2]{1,2,0:T(2,128)(2,1)}, u32[]{:S(2)}) copy-start(bf16[2,16,2]{1,2,0:T(2,128)(2,1)} %param.18) | copy-start | bytes 388
  1229.6 22.9 %all-to-all-start.1 = ((bf16[8,2,6,2304]{3,1,2,0:T(2,128)(2,1)}), bf16[8,2,6,2304]{3,1,2,0:T(2,128)(2,1)S(1)}, u32[]{:S(2)}, u32[]{:S(2)}) async-start(bf16[8,2,6,2304]{3,1,2,0:T(2,128)(2,1)} %copy.105), calls=%async_computation.1 | async-start | bytes 884736 | tf_op jit(solution)/shard_map/all_to_all | solution.py:154
Sparse Core Ops, SparseCore 0:
  20.3 45.9 all-gather.1
  574.8 197.8 all-reduce.2
  1122.6 104.7 all-reduce.4
where the time goes:
time: 1260 us
  blocking collectives  1060 us (84%)
  waiting for transfers between devices  131 us (10%)
  local copies, waits for them, and re-layouts  20.2 us (2%)
  between operations  13.4 us (1%)
  matrix products  12.9 us (1%)
    psum x1, blocking collectives, on_device(): context_all, totals_all = lax.psum((context, totals), ('exp', 'shard'))  491 us
    pmax x1, blocking collectives, on_device(): row_peak = lax.pmax(local_peak, ('exp', 'shard'))  490 us
    psum x1, waiting for transfers between devices, on_device(): expert_out = lax.psum(partial_out.astype(jnp.bfloat16), 'shard')  105 us
  transfers between devices with their start and end apart: 4, of which 3 were waited for; matrix products, arithmetic and copies ran while one was open for 1% of the time, Pallas kernels for 0%

commit v1 on v0

--- a/solution.py
+++ b/solution.py
@@ -96,8 +96,8 @@
     local_peak = jnp.max(
         jnp.where(owner_hot[:, :, None, None], page_peak[:, None], NEG_FILL), axis=0
     )
-    row_peak = lax.pmax(local_peak, ("exp", "shard"))
-    peak_here = jnp.take(row_peak, owner_slot, axis=0)
+    local_peak = local_peak.astype(jnp.bfloat16).astype(jnp.float32)
+    peak_here = jnp.take(local_peak, owner_slot, axis=0)
     weights_bf = jnp.where(
         visible[:, None, :, :], jnp.exp(scores - peak_here[..., None]), 0.0
     ).astype(jnp.bfloat16)
@@ -108,14 +108,33 @@
     page_context = page_context.reshape(pages_here, stretch_len, width)
     context = jnp.sum(jnp.where(owner_hot[:, :, None, None], page_context[:, None], 0.0), axis=0)
     totals = jnp.sum(jnp.where(owner_hot[:, :, None, None], page_totals[:, None], 0.0), axis=0)
-    context_all, totals_all = lax.psum((context, totals), ("exp", "shard"))
-    context_mine = lax.dynamic_slice_in_dim(context_all, exp_index * tokens_here, tokens_here, 1)
-    totals_mine = lax.dynamic_slice_in_dim(totals_all, exp_index * tokens_here, tokens_here, 2)
-    per_head = context_mine.reshape(members, tokens_here, H, head_size)
-    attended = (
-        (per_head / jnp.transpose(totals_mine, (0, 2, 1))[..., None])
-        .reshape(members, tokens_here, width)
-        .astype(jnp.bfloat16)
+    packed = jnp.concatenate(
+        [
+            context.astype(jnp.bfloat16),
+            jnp.transpose(local_peak, (0, 2, 1)).astype(jnp.bfloat16),
+            jnp.transpose(totals, (0, 2, 1)).astype(jnp.bfloat16),
+        ],
+        axis=2,
+    )
+    packed_width = packed.shape[2]
+    rows_each = members * tokens_here // shard_count
+    packed = packed.reshape(members, experts_count, tokens_here, packed_width)
+    packed = jnp.transpose(packed, (1, 0, 2, 3)).reshape(
+        experts_count * shard_count, rows_each, packed_width
+    )
+    arrived = lax.all_to_all(packed, ("exp", "shard"), 0, 0, tiled=True).astype(jnp.float32)
+    arrived_context = arrived[:, :, :width].reshape(-1, rows_each, H, head_size)
+    arrived_peak = arrived[:, :, width : width + H]
+    arrived_totals = arrived[:, :, width + H : width + 2 * H]
+    row_peak = jnp.max(arrived_peak, axis=0)
+    rescale = jnp.exp(arrived_peak - row_peak[None])
+    row_totals = jnp.sum(rescale * arrived_totals, axis=0)
+    row_context = jnp.sum(rescale[..., None] * arrived_context, axis=0)
+    row_attended = (
+        (row_context / row_totals[..., None]).reshape(rows_each, width).astype(jnp.bfloat16)
+    )
+    attended = lax.all_gather(row_attended, "shard", axis=0, tiled=True).reshape(
+        members, tokens_here, width
     )
     projected_part = lax.dot_general(
         attended, out_proj, (((2,), (1,)), ((), ())), preferred_element_type=jnp.float32

time: 1260 us -> 358 us (0.28)
  blocking collectives: 1060 us -> 94.4 us
  waiting for transfers between devices: 131 us -> 164 us
  starting transfers between devices: 6.75 us -> 22 us
  local copies, waits for them, and re-layouts: 20.2 us -> 35 us
    psum x1 -> x0, blocking collectives: 491 us -> none  [on_device(): context_all, totals_all = lax.psum((context, totals), ('exp', 'shard'))]
    pmax x1 -> x0, blocking collectives: 490 us -> none  [on_device(): row_peak = lax.pmax(local_peak, ('exp', 'shard'))]
    all_gather x1, waiting for transfers between devices: 18.5 us -> 39.5 us  [on_device(): group_query = lax.all_gather(served_query, 'exp', axis=1, tiled=True)]
    all_gather x0 -> x1, blocking collectives: none -> 17.3 us  [on_device(): lax.all_gather(row_attended, 'shard', axis=0, tiled=True)]
    all_to_all x0 -> x1, starting transfers between devices: none -> 15.3 us  [on_device(): lax.all_to_all(packed, ('exp', 'shard'), 0, 0, tiled=True)]
  transfers between devices with their start and end apart: 4 -> 4, of which waited for: 3 -> 4; matrix products, arithmetic and copies ran while one was open for 1% -> 3% of each run, Pallas kernels for 0% -> 0%
where the time goes in v1:
time: 358 us; the launch traced here: 357 us
  waiting for transfers between devices  164 us (46%)
  blocking collectives  94.4 us (26%)
  local copies, waits for them, and re-layouts  35 us (10%)
  starting transfers between devices  22 us (6%)
  other arithmetic  16 us (4%)
  between operations  13.7 us (4%)
  matrix products  11.8 us (3%)
    psum x1, waiting for transfers between devices, on_device(): expert_out = lax.psum(partial_out.astype(jnp.bfloat16), 'shard')  107 us
    all_gather x1, waiting for transfers between devices, on_device(): group_query = lax.all_gather(served_query, 'exp', axis=1, tiled=True)  39.5 us
    all_to_all x1, blocking collectives, on_device(): lax.all_to_all(sent_rows, 'exp', split_axis=0, concat_axis=0, tiled=True)  18.6 us
    all_gather x1, blocking collectives, on_device(): projected = lax.all_gather(projected_part, 'shard', axis=2, tiled=True)  18 us
    all_gather x1, blocking collectives, on_device(): lax.all_gather(row_attended, 'shard', axis=0, tiled=True)  17.3 us
    all_to_all x1, starting transfers between devices, on_device(): lax.all_to_all(packed, ('exp', 'shard'), 0, 0, tiled=True)  15.3 us
    all_gather x1, blocking collectives, on_device(): lax.all_gather(resid_stretch, 'req', axis=0, tiled=True)  12.2 us
    all_gather x1, blocking collectives, on_device(): lax.all_gather(query_stretch, 'req', axis=0, tiled=True)  11.4 us
  transfers between devices with their start and end apart: 4, of which 4 were waited for; matrix products, arithmetic and copies ran while one was open for 3% of the time, Pallas kernels for 0%

profile of v1, /device:TPU:1, one launch (start us, length us, event | category | flops | bytes accessed | tf_op | source)
XLA Modules:
  0.0 357.2 jit_solution(15122894932330850581)
XLA Ops:
  6.5 0.9 compare_and_fusion
  7.4 11.4 %all_gather.22 = bf16[8,16,2304]{2,1,0:T(8,128)(2,1)S(1)} all-gather(bf16[2,16,2304]{2,1,0:T(8,128)(2,1)} %param.15), channel_id=1, replica_groups=mesh['req'=4,'exp'=8,'shard'=16] {'req'}, dimensions={0}, use_global_device_ids=true | all-gather | bytes 737280 | tf_op jit(solution)/shard_map/all_gather | solution.py:51
  18.9 0.6 gather_fusion.5
  19.4 0.7 broadcast_select_fusion
  20.2 0.7 add_bitcast_fusion
  21.0 0.9 fusion.31
  22.1 2.8 reshape_squeeze.6
  24.9 1.4 copy.155
  26.8 39.5 %all-gather.3.cloned.1.call-done = bf16[2,128,2304]{2,1,0:T(8,128)(2,1)} async-done(((bf16[2,16,2304]{2,1,0:T(8,128)(2,1)}), bf16[2,128,2304]{2,1,0:T(8,128)(2,1)}) %all-gather.3.cloned.1.call-update) | async-done | bytes 1179664 | tf_op jit(solution)/shard_map/all_gather | solution.py:61
  66.3 1.9 gather_fusion
  68.2 1.4 copy.131
  69.6 3.8 %fusion.4 = (bf16[2,36,128]{2,1,0:T(8,128)(2,1)S(1)}, f32[2,36,128,64]{2,3,1,0:T(8,128)}) fusion(pred[2,128,64]{1,2,0:T(8,128)(4,1)S(1)} %broadcast_compare_fusion, bf16[2,128,36,64]{1,3,2,0:T(8,128)(2,1)} %bitcast.71, pred[2]{0:T(512)(128)(4,1)S(1)} %compare_and_fusion.1, bf16[2,64,36,64]{3,2,1,0:T(8,128)(2,1)} %reshape_squeeze.6), kind=kOutput, calls=%fused_computation.18 | convolution fusion | flops 77847552 | bytes 4163586 | tf_op jit(solution)/shard_map/pqhd,pkhd->phqk/dot_general | solution.py:91
  73.5 0.6 gather_fusion.1
  74.1 2.4 convert_reduce_fusion
  76.8 3.7 %fusion.36 = f32[2,36,128,64]{2,3,1,0:T(8,128)} fusion(bf16[2,64,36,64]{1,3,2,0:T(8,128)(2,1)S(1)} %bitcast.70, f32[2,36,128,64]{2,3,1,0:T(8,128)} %get-tuple-element.15, f32[2,36,128]{2,1,0:T(8,128)S(1)} %broadcast_select_fusion.2, pred[2,128,64]{1,2,0:T(8,128)(4,1)S(1)} %broadcast_compare_fusion), kind=kOutput, calls=%fused_computation.95 | convolution fusion | flops 78446592 | bytes 5361664 | tf_op jit(solution)/shard_map/phqk,pkhd->pqhd/dot_general | solution.py:105
  80.4 3.1 copy.135
  83.5 3.5 select_reduce_fusion
  87.1 2.4 concatenate.3
  89.5 1.1 copy.138
  90.6 3.8 %reshape.204 = bf16[128,2,2376]{2,1,0:T(2,128)(2,1)} reshape(bf16[8,2,16,2376]{3,2,1,0:T(8,128)(2,1)} %copy.138) | data formatting | bytes 2433024 | tf_op jit(solution)/shard_map/reshape | solution.py:122
  94.4 15.3 %all-to-all-start = ((bf16[128,2,2376]{2,1,0:T(2,128)(2,1)}), bf16[128,2,2376]{2,1,0:T(2,128)(2,1)S(1)}, u32[]{:S(2)}, u32[]{:S(2)}) async-start(bf16[128,2,2376]{2,1,0:T(2,128)(2,1)} %reshape.204), calls=%async_computation | async-start | bytes 2490368 | tf_op jit(solution)/shard_map/all_to_all | solution.py:125
  109.8 12.2 %all_gather.21 = bf16[8,16,2304]{2,1,0:T(8,128)(2,1)} all-gather(bf16[2,16,2304]{2,1,0:T(8,128)(2,1)S(1)} %copy-done.5), channel_id=1, replica_groups=mesh['req'=4,'exp'=8,'shard'=16] {'req'}, dimensions={0}, use_global_device_ids=true | all-gather | bytes 737280 | tf_op jit(solution)/shard_map/all_gather | solution.py:52
  122.0 1.6 gather_fusion.4
  123.6 9.0 %all_gather.26 = s32[8,16,2]{1,2,0:T(2,128)S(1)} all-gather(s32[2,16,2]{1,2,0:T(2,128)S(1)} %copy-done.7), channel_id=1, replica_groups=mesh['req'=4,'exp'=8,'shard'=16] {'req'}, dimensions={0}, use_global_device_ids=true | all-gather | bytes 1280 | tf_op jit(solution)/shard_map/all_gather | solution.py:53
  132.6 0.6 gather_fusion.2
  134.1 10.4 %all-to-all-done = bf16[128,2,2376]{2,1,0:T(2,128)(2,1)S(1)} async-done(((bf16[128,2,2376]{2,1,0:T(2,128)(2,1)}), bf16[128,2,2376]{2,1,0:T(2,128)(2,1)S(1)}, u32[]{:S(2)}, u32[]{:S(2)}) %all-to-all-start) | async-done | bytes 1216544 | tf_op jit(solution)/shard_map/all_to_all | solution.py:125
  144.4 0.9 convert_element_type.101
  145.5 1.3 copy-done.1
  146.8 0.2 fusion.19
  147.1 1.6 mul.107
  148.7 5.0 %copy.140 = f32[128,2,2304]{2,1,0:T(2,128)} copy(f32[128,2,2304]{0,2,1:T(8,128)} %bitcast.68) | data formatting | bytes 4718592 | tf_op jit(solution)/shard_map/mul | solution.py:132
  153.7 3.8 %fusion.3 = f32[2,2304]{1,0:T(2,128)S(1)} fusion(f32[128,2,2304]{2,1,0:T(2,128)} %copy.140, f32[128,2,2376]{2,1,0:T(2,128)} %copy-done.1), kind=kLoop, calls=%fused_computation.14 | loop fusion | flops 1175040 | bytes 4737024 | tf_op jit(solution)/shard_map/reduce_sum | solution.py:132
  157.7 17.3 %all-gather = bf16[16,2,2304]{2,1,0:T(2,128)(2,1)S(1)} all-gather(bf16[1,2,2304]{2,1,0:T(2,128)(2,1)S(1)} %fusion.30), channel_id=1, replica_groups=mesh['req'=4,'exp'=8,'shard'=16] {'shard'}, dimensions={0}, use_global_device_ids=true | all-gather | bytes 156672 | tf_op jit(solution)/shard_map/all_gather | solution.py:136
  175.0 0.3 convolution_convert_fusion.2
  175.5 18.0 %all_gather.25 = bf16[2,16,2304]{1,0,2:T(2,128)(2,1)S(1)} all-gather(bf16[2,16,144]{1,0,2:T(2,128)(2,1)S(1)} %copy.141), channel_id=1, replica_groups=mesh['req'=4,'exp'=8,'shard'=16] {'shard'}, dimensions={2}, use_global_device_ids=true | all-gather | bytes 156672 | tf_op jit(solution)/shard_map/all_gather | solution.py:142
  193.4 1.4 copy.142
  195.1 0.3 fusion
  195.4 0.3 copy.145
  195.8 18.6 %all_to_all.15 = bf16[8,2,6,2304]{3,1,2,0:T(2,128)(2,1)S(1)} all-to-all(bf16[8,2,6,2304]{3,1,2,0:T(2,128)(2,1)S(1)} %copy.145), channel_id=1, replica_groups=mesh['req'=4,'exp'=8,'shard'=16] {'exp'}, dimensions={0} | all-to-all | bytes 884736 | tf_op jit(solution)/shard_map/all_to_all | solution.py:168
  214.6 0.6 fusion.5
  215.4 2.2 convolution_convert_fusion.1
  217.6 106.8 %all-reduce.2.cloned.1.call-done = bf16[8,2,6,2304]{3,0,2,1:T(8,128)(2,1)} async-done(((bf16[8,2,6,2304]{3,0,2,1:T(8,128)(2,1)}), bf16[8,2,6,2304]{3,0,2,1:T(8,128)(2,1)}) %all-reduce.2.cloned.1.call-update) | async-done | bytes 442384 | tf_op jit(solution)/shard_map/psum | solution.py:172
  324.4 2.1 copy.150
  326.5 6.7 %all-to-all-start.2 = ((bf16[8,2,6,2304]{3,1,2,0:T(2,128)(2,1)}), bf16[8,2,6,2304]{3,1,2,0:T(2,128)(2,1)S(1)}, u32[]{:S(2)}, u32[]{:S(2)}) async-start(bf16[8,2,6,2304]{3,1,2,0:T(2,128)(2,1)} %copy.150), calls=%async_computation.2 | async-start | bytes 884736 | tf_op jit(solution)/shard_map/all_to_all | solution.py:173
  333.2 7.9 %all_gather.27 = bf16[8,16,2]{1,2,0:T(2,128)(2,1)S(1)} all-gather(bf16[2,16,2]{1,2,0:T(2,128)(2,1)S(1)} %copy-done.8), channel_id=1, replica_groups=mesh['req'=4,'exp'=8,'shard'=16] {'req'}, dimensions={0}, use_global_device_ids=true | all-gather | bytes 640 | tf_op jit(solution)/shard_map/all_gather | solution.py:54
  341.1 0.6 gather_fusion.3
  341.8 7.6 %all-to-all-done.2 = bf16[8,2,6,2304]{3,1,2,0:T(2,128)(2,1)S(1)} async-done(((bf16[8,2,6,2304]{3,1,2,0:T(2,128)(2,1)}), bf16[8,2,6,2304]{3,1,2,0:T(2,128)(2,1)S(1)}, u32[]{:S(2)}, u32[]{:S(2)}) %all-to-all-start.2) | async-done | bytes 442400 | tf_op jit(solution)/shard_map/all_to_all | solution.py:173
  349.4 0.9 fusion.2
  (71 shorter events, 3.7 us)
Async XLA Ops:
  6.5 208.0 %copy-start = (bf16[1,2,180,2304]{3,1,2,0:T(2,128)(2,1)S(1)}, bf16[1,2,180,2304]{3,1,2,0:T(2,128)(2,1)}, u32[]{:S(2)}) copy-start(bf16[1,2,180,2304]{3,1,2,0:T(2,128)(2,1)} %param.26) | copy-start | bytes 4976644
  6.5 18.4 %copy-start.4 = (bf16[1,2,64,2304]{3,2,1,0:T(8,128)(2,1)S(1)}, bf16[1,2,64,2304]{3,2,1,0:T(8,128)(2,1)}, u32[]{:S(2)}) copy-start(bf16[1,2,64,2304]{3,2,1,0:T(8,128)(2,1)} %param.23) | copy-start | bytes 1769476
  6.5 59.7 %all-gather.3.cloned.1.call-start = ((), (), s32[]{:S(2)}) async-start(), calls=%async_computation.3 | async-start | bytes 1327104 | tf_op jit(solution)/shard_map/all_gather | solution.py:61
  18.9 7.4 %copy-start.9 = (s32[1,2]{1,0:T(1,128)S(1)}, s32[1,2]{1,0:T(1,128)}, u32[]{:S(2)}) copy-start(s32[1,2]{1,0:T(1,128)} %param.20) | copy-start | bytes 28
  73.4 3.4 copy-start.2
  90.6 19.2 %copy-start.5 = (bf16[2,16,2304]{2,1,0:T(8,128)(2,1)S(1)}, bf16[2,16,2304]{2,1,0:T(8,128)(2,1)}, u32[]{:S(2)}) copy-start(bf16[2,16,2304]{2,1,0:T(8,128)(2,1)} %param.16) | copy-start | bytes 442372
  94.4 29.2 %copy-start.7 = (s32[2,16,2]{1,2,0:T(2,128)S(1)}, s32[2,16,2]{1,2,0:T(2,128)}, u32[]{:S(2)}) copy-start(s32[2,16,2]{1,2,0:T(2,128)} %param.17) | copy-start | bytes 772
  94.4 50.0 %all-to-all-start = ((bf16[128,2,2376]{2,1,0:T(2,128)(2,1)}), bf16[128,2,2376]{2,1,0:T(2,128)(2,1)S(1)}, u32[]{:S(2)}, u32[]{:S(2)}) async-start(bf16[128,2,2376]{2,1,0:T(2,128)(2,1)} %reshape.204), calls=%async_computation | async-start | bytes 2490368 | tf_op jit(solution)/shard_map/all_to_all | solution.py:125
  109.7 214.7 %all-reduce.2.cloned.1.call-start = ((), (), s32[]{:S(2)}) async-start(), calls=%async_computation.4 | async-start | bytes 884736 | tf_op jit(solution)/shard_map/psum | solution.py:172
  145.3 1.4 copy-start.1
  153.7 21.3 %copy-start.3 = (bf16[144,2304]{1,0:T(8,128)(2,1)S(1)}, bf16[144,2304]{1,0:T(8,128)(2,1)}, u32[]{:S(2)}) copy-start(bf16[144,2304]{1,0:T(8,128)(2,1)} %param.25) | copy-start | bytes 1990660
  157.5 37.6 %copy-start.6 = (f32[2304]{0:T(1024)S(1)}, f32[2304]{0:T(1024)}, u32[]{:S(2)}) copy-start(f32[2304]{0:T(1024)} %param.24) | copy-start | bytes 27652
  215.2 118.0 %copy-start.8 = (bf16[2,16,2]{1,2,0:T(2,128)(2,1)S(1)}, bf16[2,16,2]{1,2,0:T(2,128)(2,1)}, u32[]{:S(2)}) copy-start(bf16[2,16,2]{1,2,0:T(2,128)(2,1)} %param.18) | copy-start | bytes 388
  326.5 22.9 %all-to-all-start.2 = ((bf16[8,2,6,2304]{3,1,2,0:T(2,128)(2,1)}), bf16[8,2,6,2304]{3,1,2,0:T(2,128)(2,1)S(1)}, u32[]{:S(2)}, u32[]{:S(2)}) async-start(bf16[8,2,6,2304]{3,1,2,0:T(2,128)(2,1)} %copy.150), calls=%async_computation.2 | async-start | bytes 884736 | tf_op jit(solution)/shard_map/all_to_all | solution.py:173
Sparse Core Ops, SparseCore 0:
  20.3 45.9 all-gather.2
  217.7 106.6 all-reduce.1

commit v2 on v1

--- a/solution.py
+++ b/solution.py
@@ -168,13 +168,32 @@
         lax.all_to_all(sent_rows, "exp", split_axis=0, concat_axis=0, tiled=True),
         gate_up,
         down_proj,
-    )
-    expert_out = lax.psum(partial_out.astype(jnp.bfloat16), "shard")
-    returned = lax.all_to_all(expert_out, "exp", split_axis=0, concat_axis=0, tiled=True)
+    ).astype(jnp.bfloat16)
+    feature_block = width // shard_count
+    partial_out = partial_out.reshape(
+        experts_count, members, capacity, shard_count, feature_block
+    )
+    partial_out = jnp.transpose(partial_out, (0, 3, 1, 2, 4)).reshape(
+        experts_count * shard_count, members, capacity, feature_block
+    )
+    gathered_parts = lax.all_to_all(partial_out, ("exp", "shard"), 0, 0, tiled=True)
+    expert_out = (
+        jnp.sum(
+            gathered_parts.reshape(
+                experts_count, shard_count, members, capacity, feature_block
+            ).astype(jnp.float32),
+            axis=1,
+        )
+        .astype(jnp.bfloat16)
+    )
     moe_term = jnp.einsum(
-        "jtnc,njcd->jtd", share_table, returned, preferred_element_type=jnp.float32
-    )
-    mixed_out = (hidden_state + moe_term).astype(jnp.bfloat16)
+        "jtnc,njcd->jtd", share_table, expert_out, preferred_element_type=jnp.float32
+    )
+    hidden_block = lax.dynamic_slice_in_dim(
+        hidden_state, shard_index * feature_block, feature_block, 2
+    )
+    mixed_block = (hidden_block + moe_term).astype(jnp.bfloat16)
+    mixed_out = lax.all_gather(mixed_block, "shard", axis=2, tiled=True)
     return mixed_out
 
 

time: 358 us -> 283 us (0.79)
  waiting for transfers between devices: 164 us -> 67.4 us
  blocking collectives: 94.4 us -> 114 us
    psum x1 -> x0, waiting for transfers between devices: 107 us -> none  [on_device(): expert_out = lax.psum(partial_out.astype(jnp.bfloat16), 'shard')]
    all_gather x0 -> x1, blocking collectives: none -> 19.1 us  [on_device(): mixed_out = lax.all_gather(mixed_block, 'shard', axis=2, tiled=True)]
    all_to_all x1, waiting for transfers between devices: 7.59 us -> 17 us  [on_device(): lax.all_to_all(partial_out, ('exp', 'shard'), 0, 0, tiled=True)]
  transfers between devices with their start and end apart: 4 -> 3, of which waited for: 4 -> 3; matrix products, arithmetic and copies ran while one was open for 3% -> 4% of each run, Pallas kernels for 0% -> 0%
where the time goes in v2:
time: 283 us; the launch traced here: 282 us
  blocking collectives  114 us (40%)
  waiting for transfers between devices  67.4 us (24%)
  local copies, waits for them, and re-layouts  37.8 us (13%)
  starting transfers between devices  21.6 us (8%)
  other arithmetic  16.8 us (6%)
  between operations  13.8 us (5%)
  matrix products  10.9 us (4%)
    all_gather x1, waiting for transfers between devices, on_device(): group_query = lax.all_gather(served_query, 'exp', axis=1, tiled=True)  39.5 us
    all_gather x1, blocking collectives, on_device(): mixed_out = lax.all_gather(mixed_block, 'shard', axis=2, tiled=True)  19.1 us
    all_to_all x1, blocking collectives, on_device(): lax.all_to_all(sent_rows, 'exp', split_axis=0, concat_axis=0, tiled=True)  18.6 us
    all_gather x1, blocking collectives, on_device(): projected = lax.all_gather(projected_part, 'shard', axis=2, tiled=True)  18 us
    all_gather x1, blocking collectives, on_device(): lax.all_gather(row_attended, 'shard', axis=0, tiled=True)  17.3 us
    all_to_all x1, waiting for transfers between devices, on_device(): lax.all_to_all(partial_out, ('exp', 'shard'), 0, 0, tiled=True)  17 us
    all_to_all x1, starting transfers between devices, on_device(): lax.all_to_all(packed, ('exp', 'shard'), 0, 0, tiled=True)  15.3 us
    all_gather x1, blocking collectives, on_device(): lax.all_gather(resid_stretch, 'req', axis=0, tiled=True)  12.1 us
  transfers between devices with their start and end apart: 3, of which 3 were waited for; matrix products, arithmetic and copies ran while one was open for 4% of the time, Pallas kernels for 0%

profile of v2, /device:TPU:1, one launch (start us, length us, event | category | flops | bytes accessed | tf_op | source)
XLA Modules:
  0.0 282.0 jit_solution(8927762071287718742)
XLA Ops:
  6.5 0.9 compare_and_fusion
  7.4 11.4 %all_gather.25 = bf16[8,16,2304]{2,1,0:T(8,128)(2,1)S(1)} all-gather(bf16[2,16,2304]{2,1,0:T(8,128)(2,1)} %param.15), channel_id=1, replica_groups=mesh['req'=4,'exp'=8,'shard'=16] {'req'}, dimensions={0}, use_global_device_ids=true | all-gather | bytes 737280 | tf_op jit(solution)/shard_map/all_gather | solution.py:51
  18.9 0.6 gather_fusion.5
  19.4 0.7 broadcast_select_fusion
  20.2 0.7 add_bitcast_fusion
  21.0 0.9 fusion.31
  22.1 2.8 reshape_squeeze.6
  24.9 1.4 copy.170
  26.8 39.5 %all-gather.3.cloned.1.call-done = bf16[2,128,2304]{2,1,0:T(8,128)(2,1)} async-done(((bf16[2,16,2304]{2,1,0:T(8,128)(2,1)}), bf16[2,128,2304]{2,1,0:T(8,128)(2,1)}) %all-gather.3.cloned.1.call-update) | async-done | bytes 1179664 | tf_op jit(solution)/shard_map/all_gather | solution.py:61
  66.3 1.9 gather_fusion
  68.2 1.4 copy.143
  69.6 3.8 %fusion.2 = (bf16[2,36,128]{2,1,0:T(8,128)(2,1)S(1)}, f32[2,36,128,64]{2,3,1,0:T(8,128)}) fusion(pred[2,128,64]{1,2,0:T(8,128)(4,1)S(1)} %broadcast_compare_fusion, bf16[2,128,36,64]{1,3,2,0:T(8,128)(2,1)} %bitcast.80, pred[2]{0:T(512)(128)(4,1)S(1)} %compare_and_fusion.1, bf16[2,64,36,64]{3,2,1,0:T(8,128)(2,1)} %reshape_squeeze.6), kind=kOutput, calls=%fused_computation.15 | convolution fusion | flops 77847552 | bytes 4163586 | tf_op jit(solution)/shard_map/pqhd,pkhd->phqk/dot_general | solution.py:91
  73.5 0.6 gather_fusion.1
  74.1 2.4 convert_reduce_fusion
  76.8 3.7 %fusion.36 = f32[2,36,128,64]{2,3,1,0:T(8,128)} fusion(bf16[2,64,36,64]{1,3,2,0:T(8,128)(2,1)S(1)} %bitcast.78, f32[2,36,128,64]{2,3,1,0:T(8,128)} %get-tuple-element.17, f32[2,36,128]{2,1,0:T(8,128)S(1)} %broadcast_select_fusion.1, pred[2,128,64]{1,2,0:T(8,128)(4,1)S(1)} %broadcast_compare_fusion), kind=kOutput, calls=%fused_computation.95 | convolution fusion | flops 78446592 | bytes 5361664 | tf_op jit(solution)/shard_map/phqk,pkhd->pqhd/dot_general | solution.py:105
  80.4 3.1 %copy.147 = f32[2,128,2304]{2,1,0:T(8,128)} copy(f32[2,128,2304]{1,2,0:T(8,128)} %bitcast.75) | data formatting | bytes 4718592 | tf_op jit(solution)/shard_map/jit(_where)/broadcast_in_dim | solution.py:109
  83.5 3.5 %select_reduce_fusion = bf16[2,128,2304]{2,1,0:T(8,128)(2,1)} fusion(f32[2,128,2304]{2,1,0:T(8,128)} %copy.147, pred[2,2]{1,0:T(4,128)(4,1)S(1)} %iota_compare_fusion.3), kind=kLoop, calls=%fused_computation.6 | loop fusion | flops 1769472 | bytes 3538948 | tf_op jit(solution)/shard_map/reduce_sum | solution.py:109
  87.1 2.4 concatenate.3
  89.5 1.1 copy.150
  90.6 3.8 %reshape.213 = bf16[128,2,2376]{2,1,0:T(2,128)(2,1)} reshape(bf16[8,2,16,2376]{3,2,1,0:T(8,128)(2,1)} %copy.150) | data formatting | bytes 2433024 | tf_op jit(solution)/shard_map/reshape | solution.py:122
  94.4 15.3 %all-to-all-start = ((bf16[128,2,2376]{2,1,0:T(2,128)(2,1)}), bf16[128,2,2376]{2,1,0:T(2,128)(2,1)S(1)}, u32[]{:S(2)}, u32[]{:S(2)}) async-start(bf16[128,2,2376]{2,1,0:T(2,128)(2,1)} %reshape.213), calls=%async_computation | async-start | bytes 2490368 | tf_op jit(solution)/shard_map/all_to_all | solution.py:125
  109.7 12.1 %all_gather.24 = bf16[8,16,2304]{2,1,0:T(8,128)(2,1)S(1)} all-gather(bf16[2,16,2304]{2,1,0:T(8,128)(2,1)} %param.16), channel_id=1, replica_groups=mesh['req'=4,'exp'=8,'shard'=16] {'req'}, dimensions={0}, use_global_device_ids=true | all-gather | bytes 737280 | tf_op jit(solution)/shard_map/all_gather | solution.py:52
  121.8 1.2 gather_fusion.4
  123.0 9.0 %all_gather.29 = s32[8,16,2]{1,2,0:T(2,128)S(1)} all-gather(s32[2,16,2]{1,2,0:T(2,128)S(1)} %copy-done.8), channel_id=1, replica_groups=mesh['req'=4,'exp'=8,'shard'=16] {'req'}, dimensions={0}, use_global_device_ids=true | all-gather | bytes 1280 | tf_op jit(solution)/shard_map/all_gather | solution.py:53
  132.0 0.6 gather_fusion.2
  133.5 11.0 %all-to-all-done = bf16[128,2,2376]{2,1,0:T(2,128)(2,1)S(1)} async-done(((bf16[128,2,2376]{2,1,0:T(2,128)(2,1)}), bf16[128,2,2376]{2,1,0:T(2,128)(2,1)S(1)}, u32[]{:S(2)}, u32[]{:S(2)}) %all-to-all-start) | async-done | bytes 1216544 | tf_op jit(solution)/shard_map/all_to_all | solution.py:125
  144.4 0.9 convert_element_type.103
  145.4 1.3 copy-done.1
  147.0 1.6 mul.110
  148.6 5.0 %copy.152 = f32[128,2,2304]{2,1,0:T(2,128)} copy(f32[128,2,2304]{0,2,1:T(8,128)} %bitcast.76) | data formatting | bytes 4718592 | tf_op jit(solution)/shard_map/mul | solution.py:132
  153.6 3.8 %fusion.1 = f32[2,2304]{1,0:T(2,128)S(1)} fusion(f32[128,2,2304]{2,1,0:T(2,128)} %copy.152, f32[128,2,2376]{2,1,0:T(2,128)} %copy-done.1), kind=kLoop, calls=%fused_computation.11 | loop fusion | flops 1175040 | bytes 4737024 | tf_op jit(solution)/shard_map/reduce_sum | solution.py:132
  157.6 17.3 %all-gather = bf16[16,2,2304]{2,1,0:T(2,128)(2,1)S(1)} all-gather(bf16[1,2,2304]{2,1,0:T(2,128)(2,1)S(1)} %fusion.30), channel_id=1, replica_groups=mesh['req'=4,'exp'=8,'shard'=16] {'shard'}, dimensions={0}, use_global_device_ids=true | all-gather | bytes 156672 | tf_op jit(solution)/shard_map/all_gather | solution.py:136
  175.4 18.0 %all_gather.28 = bf16[2,16,2304]{1,0,2:T(2,128)(2,1)S(1)} all-gather(bf16[2,16,144]{1,0,2:T(2,128)(2,1)S(1)} %copy.153), channel_id=1, replica_groups=mesh['req'=4,'exp'=8,'shard'=16] {'shard'}, dimensions={2}, use_global_device_ids=true | all-gather | bytes 156672 | tf_op jit(solution)/shard_map/all_gather | solution.py:142
  193.4 1.4 copy.154
  195.0 1.1 fusion
  196.1 0.3 copy.157
  196.4 18.6 %all_to_all.15 = bf16[8,2,6,2304]{3,1,2,0:T(2,128)(2,1)S(1)} all-to-all(bf16[8,2,6,2304]{3,1,2,0:T(2,128)(2,1)S(1)} %copy.157), channel_id=1, replica_groups=mesh['req'=4,'exp'=8,'shard'=16] {'exp'}, dimensions={0} | all-to-all | bytes 884736 | tf_op jit(solution)/shard_map/all_to_all | solution.py:168
  215.2 0.6 fusion.3
  216.0 1.4 convolution_convert_fusion.1
  217.5 1.4 reshape.216
  218.8 1.7 copy.162
  220.5 6.3 %all-to-all-start.2 = ((bf16[128,2,6,144]{3,1,2,0:T(2,128)(2,1)}), bf16[128,2,6,144]{3,1,2,0:T(2,128)(2,1)S(1)}, u32[]{:S(2)}, u32[]{:S(2)}) async-start(bf16[128,2,6,144]{3,1,2,0:T(2,128)(2,1)} %bitcast.27), calls=%async_computation.2 | async-start | bytes 1572864 | tf_op jit(solution)/shard_map/all_to_all | solution.py:179
  226.9 8.2 %all_gather.30 = bf16[8,16,2]{1,2,0:T(2,128)(2,1)S(1)} all-gather(bf16[2,16,2]{1,2,0:T(2,128)(2,1)S(1)} %copy-done.9), channel_id=1, replica_groups=mesh['req'=4,'exp'=8,'shard'=16] {'req'}, dimensions={0}, use_global_device_ids=true | all-gather | bytes 640 | tf_op jit(solution)/shard_map/all_gather | solution.py:54
  235.1 0.6 gather_fusion.3
  235.8 17.0 %all-to-all-done.2 = bf16[128,2,6,144]{3,1,2,0:T(2,128)(2,1)S(1)} async-done(((bf16[128,2,6,144]{3,1,2,0:T(2,128)(2,1)}), bf16[128,2,6,144]{3,1,2,0:T(2,128)(2,1)S(1)}, u32[]{:S(2)}, u32[]{:S(2)}) %all-to-all-start.2) | async-done | bytes 442400 | tf_op jit(solution)/shard_map/all_to_all | solution.py:179
  252.8 0.8 bitcast_reduce_fusion
  253.9 19.1 %all_gather.31 = bf16[2,16,2304]{1,0,2:T(2,128)(2,1)S(1)} all-gather(bf16[2,16,144]{1,0,2:T(2,128)(2,1)S(1)} %copy.165), channel_id=1, replica_groups=mesh['req'=4,'exp'=8,'shard'=16] {'shard'}, dimensions={2}, use_global_device_ids=true | all-gather | bytes 156672 | tf_op jit(solution)/shard_map/all_gather | solution.py:196
  273.0 2.2 copy.166
  (75 shorter events, 4.5 us)
Async XLA Ops:
  6.5 208.7 %copy-start = (bf16[1,2,180,2304]{3,1,2,0:T(2,128)(2,1)S(1)}, bf16[1,2,180,2304]{3,1,2,0:T(2,128)(2,1)}, u32[]{:S(2)}) copy-start(bf16[1,2,180,2304]{3,1,2,0:T(2,128)(2,1)} %param.26) | copy-start | bytes 4976644
  6.5 18.4 %copy-start.4 = (bf16[1,2,64,2304]{3,2,1,0:T(8,128)(2,1)S(1)}, bf16[1,2,64,2304]{3,2,1,0:T(8,128)(2,1)}, u32[]{:S(2)}) copy-start(bf16[1,2,64,2304]{3,2,1,0:T(8,128)(2,1)} %param.23) | copy-start | bytes 1769476
  6.5 59.7 %all-gather.3.cloned.1.call-start = ((), (), s32[]{:S(2)}) async-start(), calls=%async_computation.3 | async-start | bytes 1327104 | tf_op jit(solution)/shard_map/all_gather | solution.py:61
  18.9 7.4 %copy-start.10 = (s32[1,2]{1,0:T(1,128)S(1)}, s32[1,2]{1,0:T(1,128)}, u32[]{:S(2)}) copy-start(s32[1,2]{1,0:T(1,128)} %param.20) | copy-start | bytes 28
  73.4 3.4 %copy-start.2 = (bf16[1,2,64,2304]{2,3,1,0:T(8,128)(2,1)S(1)}, bf16[1,2,64,2304]{2,3,1,0:T(8,128)(2,1)}, u32[]{:S(2)}) copy-start(bf16[1,2,64,2304]{2,3,1,0:T(8,128)(2,1)} %copy.170) | copy-start | bytes 1769476
  94.4 28.6 %copy-start.8 = (s32[2,16,2]{1,2,0:T(2,128)S(1)}, s32[2,16,2]{1,2,0:T(2,128)}, u32[]{:S(2)}) copy-start(s32[2,16,2]{1,2,0:T(2,128)} %param.17) | copy-start | bytes 772
  94.4 50.0 %all-to-all-start = ((bf16[128,2,2376]{2,1,0:T(2,128)(2,1)}), bf16[128,2,2376]{2,1,0:T(2,128)(2,1)S(1)}, u32[]{:S(2)}, u32[]{:S(2)}) async-start(bf16[128,2,2376]{2,1,0:T(2,128)(2,1)} %reshape.213), calls=%async_computation | async-start | bytes 2490368 | tf_op jit(solution)/shard_map/all_to_all | solution.py:125
  133.4 15.2 %copy-start.6 = (s32[2,16,2,8]{1,3,2,0:T(8,128)}, s32[2,16,2,8]{1,3,2,0:T(8,128)S(1)}, u32[]{:S(2)}) copy-start(s32[2,16,2,8]{1,3,2,0:T(8,128)S(1)} %fusion.26) | copy-start | bytes 6148
  145.3 1.4 copy-start.1
  153.6 21.3 %copy-start.3 = (bf16[144,2304]{1,0:T(8,128)(2,1)S(1)}, bf16[144,2304]{1,0:T(8,128)(2,1)}, u32[]{:S(2)}) copy-start(bf16[144,2304]{1,0:T(8,128)(2,1)} %param.25) | copy-start | bytes 1990660
  157.4 37.4 %copy-start.5 = (bf16[2,16,2304]{2,1,0:T(8,128)(2,1)S(1)}, bf16[2,16,2304]{2,1,0:T(8,128)(2,1)}, u32[]{:S(2)}) copy-start(bf16[2,16,2304]{2,1,0:T(8,128)(2,1)} %gather_fusion.4) | copy-start | bytes 442372
  217.4 9.4 %copy-start.9 = (bf16[2,16,2]{1,2,0:T(2,128)(2,1)S(1)}, bf16[2,16,2]{1,2,0:T(2,128)(2,1)}, u32[]{:S(2)}) copy-start(bf16[2,16,2]{1,2,0:T(2,128)(2,1)} %param.18) | copy-start | bytes 388
  217.5 18.3 %copy-start.7 = (s32[2,16,2,8]{1,3,2,0:T(8,128)S(1)}, s32[2,16,2,8]{1,3,2,0:T(8,128)}, u32[]{:S(2)}) copy-start(s32[2,16,2,8]{1,3,2,0:T(8,128)} %copy-done.6) | copy-start | bytes 6148
  220.5 32.3 %all-to-all-start.2 = ((bf16[128,2,6,144]{3,1,2,0:T(2,128)(2,1)}), bf16[128,2,6,144]{3,1,2,0:T(2,128)(2,1)S(1)}, u32[]{:S(2)}, u32[]{:S(2)}) async-start(bf16[128,2,6,144]{3,1,2,0:T(2,128)(2,1)} %bitcast.27), calls=%async_computation.2 | async-start | bytes 1572864 | tf_op jit(solution)/shard_map/all_to_all | solution.py:179
Sparse Core Ops, SparseCore 0:
  20.3 45.9 all-gather.2

commit v3 on v2

--- a/solution.py
+++ b/solution.py
@@ -47,18 +47,25 @@
     shard_index = lax.axis_index("shard")
     shard_count = lax.axis_size("shard")
     experts_count = lax.axis_size("exp")
-    all_query, all_resid, all_ids, all_probs = (
-        lax.all_gather(query_stretch, "req", axis=0, tiled=True),
-        lax.all_gather(resid_stretch, "req", axis=0, tiled=True),
-        lax.all_gather(route_ids, "req", axis=0, tiled=True),
-        lax.all_gather(route_probs, "req", axis=0, tiled=True),
-    )
+    extras = jnp.concatenate(
+        [resid_stretch, route_probs, route_ids.astype(jnp.bfloat16)], axis=2
+    )
+    all_query = lax.all_gather(query_stretch, "req", axis=0, tiled=True)
+    all_extras = lax.all_gather(extras, "req", axis=0, tiled=True)
     served = lax.dynamic_slice_in_dim(request_order, group_index * members, members)
     served_query = jnp.take(all_query, served, axis=0)
-    served_resid = jnp.take(all_resid, served, axis=0)
-    served_ids = jnp.take(all_ids, served, axis=0)
-    served_probs = jnp.take(all_probs, served, axis=0)
-    group_query = lax.all_gather(served_query, "exp", axis=1, tiled=True)
+    served_extras = jnp.take(all_extras, served, axis=0)
+    top_count = route_ids.shape[2]
+    served_resid = served_extras[:, :, :width]
+    served_probs = served_extras[:, :, width : width + top_count]
+    served_ids = served_extras[:, :, width + top_count :].astype(jnp.int32)
+    spread_query = jnp.broadcast_to(
+        served_query[None], (experts_count,) + served_query.shape
+    )
+    group_query = lax.all_to_all(spread_query, "exp", 0, 0, tiled=False)
+    group_query = jnp.transpose(group_query, (1, 0, 2, 3)).reshape(
+        members, experts_count * tokens_here, width
+    )
     stretch_len = group_query.shape[1]
     pages_here = key_pool.shape[1]
     page_size = key_pool.shape[2]
@@ -143,7 +150,6 @@
     hidden_state = served_resid.astype(jnp.float32) + projected.astype(jnp.float32)
     mean_square = jnp.mean(hidden_state * hidden_state, axis=2, keepdims=True)
     normed = (hidden_state * lax.rsqrt(mean_square + EPSILON) * norm_gain).astype(jnp.bfloat16)
-    top_count = served_ids.shape[2]
     capacity = min(tokens_here, max(2, 3 * tokens_here * top_count // (2 * experts_count)))
     flat_ids = served_ids.reshape(members, tokens_here * top_count)
     expert_hot = (

time: 283 us -> 263 us (0.929)
  blocking collectives: 114 us -> 95.8 us
  between operations: 13.8 us -> 0.43 us
  starting transfers between devices: 21.6 us -> 28.5 us
  waiting for transfers between devices: 67.4 us -> 70.7 us
    all_gather x1 -> x0, waiting for transfers between devices: 39.5 us -> none  [on_device(): group_query = lax.all_gather(served_query, 'exp', axis=1, tiled=True)]
    all_to_all x0 -> x1, waiting for transfers between devices: none -> 26.1 us  [on_device(): group_query = lax.all_to_all(spread_query, 'exp', 0, 0, tiled=False)]
    all_gather x4 -> x2, blocking collectives: 40.7 us -> 22.9 us  [the longest x1 11.6 us: on_device(): all_query = lax.all_gather(query_stretch, 'req', axis=0, tiled=True)]
    all_to_all x0 -> x1, starting transfers between devices: none -> 11.4 us  [on_device(): group_query = lax.all_to_all(spread_query, 'exp', 0, 0, tiled=False)]
    all_to_all x1, waiting for transfers between devices: 17 us -> 25.8 us  [on_device(): lax.all_to_all(partial_out, ('exp', 'shard'), 0, 0, tiled=True)]
    all_to_all x1, waiting for transfers between devices: 11 us -> 18.8 us  [on_device(): lax.all_to_all(packed, ('exp', 'shard'), 0, 0, tiled=True)]
    all_to_all x1, starting transfers between devices: 15.3 us -> 10.7 us  [on_device(): lax.all_to_all(packed, ('exp', 'shard'), 0, 0, tiled=True)]
  transfers between devices with their start and end apart: 3 -> 3, of which waited for: 3 -> 3; matrix products, arithmetic and copies ran while one was open for 4% -> 3% of each run, Pallas kernels for 0% -> 0%
where the time goes in v3:
time: 263 us; the launch traced here: 262 us
  blocking collectives  95.8 us (36%)
  waiting for transfers between devices  70.7 us (27%)
  local copies, waits for them, and re-layouts  40.4 us (15%)
  starting transfers between devices  28.5 us (11%)
  other arithmetic  16.1 us (6%)
  matrix products  9.84 us (4%)
    all_to_all x1, waiting for transfers between devices, on_device(): group_query = lax.all_to_all(spread_query, 'exp', 0, 0, tiled=False)  26.1 us
    all_to_all x1, waiting for transfers between devices, on_device(): lax.all_to_all(partial_out, ('exp', 'shard'), 0, 0, tiled=True)  25.8 us
    all_gather x1, blocking collectives, on_device(): mixed_out = lax.all_gather(mixed_block, 'shard', axis=2, tiled=True)  19.1 us
    all_to_all x1, waiting for transfers between devices, on_device(): lax.all_to_all(packed, ('exp', 'shard'), 0, 0, tiled=True)  18.8 us
    all_to_all x1, blocking collectives, on_device(): lax.all_to_all(sent_rows, 'exp', split_axis=0, concat_axis=0, tiled=True)  18.6 us
    all_gather x1, blocking collectives, on_device(): projected = lax.all_gather(projected_part, 'shard', axis=2, tiled=True)  18 us
    all_gather x1, blocking collectives, on_device(): lax.all_gather(row_attended, 'shard', axis=0, tiled=True)  17.3 us
    all_gather x1, blocking collectives, on_device(): all_query = lax.all_gather(query_stretch, 'req', axis=0, tiled=True)  11.6 us
  transfers between devices with their start and end apart: 3, of which 3 were waited for; matrix products, arithmetic and copies ran while one was open for 3% of the time, Pallas kernels for 0%

profile of v3, /device:TPU:1, one launch (start us, length us, event | category | flops | bytes accessed | tf_op | source)
XLA Modules:
  0.0 261.7 jit_solution(5101840935848856986)
XLA Ops:
  0.0 0.9 compare_and_fusion.1
  0.9 11.6 %all_gather.16 = bf16[8,16,2304]{2,1,0:T(8,128)(2,1)S(1)} all-gather(bf16[2,16,2304]{2,1,0:T(8,128)(2,1)} %param.13), channel_id=1, replica_groups=mesh['req'=4,'exp'=8,'shard'=16] {'req'}, dimensions={0}, use_global_device_ids=true | all-gather | bytes 737280 | tf_op jit(solution)/shard_map/all_gather | solution.py:53
  12.5 0.6 gather_fusion.1
  13.1 1.1 broadcast_in_dim.200
  14.3 11.4 %all-to-all-start = ((bf16[8,2,16,2304]{3,2,1,0:T(8,128)(2,1)}), bf16[8,2,16,2304]{3,2,1,0:T(8,128)(2,1)}, u32[]{:S(2)}, u32[]{:S(2)}) async-start(bf16[8,2,16,2304]{3,2,1,0:T(8,128)(2,1)} %broadcast_in_dim.200), calls=%async_computation | async-start | bytes 2359296 | tf_op jit(solution)/shard_map/all_to_all | solution.py:65
  26.3 2.0 reshape_squeeze.6
  28.3 1.4 copy.179
  30.2 26.1 %all-to-all-done = bf16[8,2,16,2304]{3,2,1,0:T(8,128)(2,1)} async-done(((bf16[8,2,16,2304]{3,2,1,0:T(8,128)(2,1)}), bf16[8,2,16,2304]{3,2,1,0:T(8,128)(2,1)}, u32[]{:S(2)}, u32[]{:S(2)}) %all-to-all-start) | async-done | bytes 1179680 | tf_op jit(solution)/shard_map/all_to_all | solution.py:65
  56.2 1.3 copy.150
  57.6 1.7 gather_fusion.2
  59.3 2.5 copy.151
  61.7 3.4 %fusion.2 = (bf16[2,36,128]{2,1,0:T(8,128)(2,1)S(1)}, f32[2,36,128,64]{2,3,1,0:T(8,128)}) fusion(pred[2,128,64]{1,2,0:T(8,128)(4,1)S(1)} %broadcast_compare_fusion, bf16[2,128,36,64]{1,3,2,0:T(8,128)(2,1)} %bitcast.84, pred[2]{0:T(512)(128)(4,1)S(1)} %compare_and_fusion, bf16[2,64,36,64]{3,2,1,0:T(8,128)(2,1)S(1)} %copy-done.3), kind=kOutput, calls=%fused_computation.13 | convolution fusion | flops 77847552 | bytes 4163586 | tf_op jit(solution)/shard_map/pqhd,pkhd->phqk/dot_general | solution.py:98
  65.2 0.6 gather_fusion.3
  65.9 2.4 convert_reduce_fusion
  68.5 3.7 %fusion.36 = f32[2,36,128,64]{2,3,1,0:T(8,128)} fusion(bf16[2,64,36,64]{1,3,2,0:T(8,128)(2,1)S(1)} %bitcast.82, f32[2,36,128,64]{2,3,1,0:T(8,128)} %get-tuple-element.18, f32[2,36,128]{2,1,0:T(8,128)S(1)} %broadcast_select_fusion.2, pred[2,128,64]{1,2,0:T(8,128)(4,1)S(1)} %broadcast_compare_fusion), kind=kOutput, calls=%fused_computation.92 | convolution fusion | flops 78446592 | bytes 5361664 | tf_op jit(solution)/shard_map/phqk,pkhd->pqhd/dot_general | solution.py:112
  72.2 3.1 %copy.155 = f32[2,128,2304]{2,1,0:T(8,128)} copy(f32[2,128,2304]{1,2,0:T(8,128)} %bitcast.78) | data formatting | bytes 4718592 | tf_op jit(solution)/shard_map/jit(_where)/broadcast_in_dim | solution.py:116
  75.2 3.5 %select_reduce_fusion = bf16[2,128,2304]{2,1,0:T(8,128)(2,1)} fusion(f32[2,128,2304]{2,1,0:T(8,128)} %copy.155, pred[2,2]{1,0:T(4,128)(4,1)S(1)} %iota_compare_fusion.3), kind=kLoop, calls=%fused_computation.4 | loop fusion | flops 1769472 | bytes 3538948 | tf_op jit(solution)/shard_map/reduce_sum | solution.py:116
  78.9 2.4 concatenate.7
  81.2 1.1 copy.158
  82.4 3.9 %reshape.198 = bf16[128,2,2376]{2,1,0:T(2,128)(2,1)} reshape(bf16[8,2,16,2376]{3,2,1,0:T(8,128)(2,1)} %copy.158) | data formatting | bytes 2433024 | tf_op jit(solution)/shard_map/reshape | solution.py:129
  86.2 10.7 %all-to-all-start.1 = ((bf16[128,2,2376]{2,1,0:T(2,128)(2,1)}), bf16[128,2,2376]{2,1,0:T(2,128)(2,1)S(1)}, u32[]{:S(2)}, u32[]{:S(2)}) async-start(bf16[128,2,2376]{2,1,0:T(2,128)(2,1)} %reshape.198), calls=%async_computation.1 | async-start | bytes 2490368 | tf_op jit(solution)/shard_map/all_to_all | solution.py:132
  97.2 0.7 concatenate.6
  97.9 11.4 %all_gather.15 = bf16[8,16,2308]{2,1,0:T(8,128)(2,1)S(1)} all-gather(bf16[2,16,2308]{2,1,0:T(8,128)(2,1)} %concatenate.6), channel_id=1, replica_groups=mesh['req'=4,'exp'=8,'shard'=16] {'req'}, dimensions={0}, use_global_device_ids=true | all-gather | bytes 738560 | tf_op jit(solution)/shard_map/all_gather | solution.py:54
  109.3 1.2 gather_fusion
  110.5 1.0 broadcast_select_fusion
  111.5 0.6 fusion.37
  112.8 18.8 %all-to-all-done.1 = bf16[128,2,2376]{2,1,0:T(2,128)(2,1)S(1)} async-done(((bf16[128,2,2376]{2,1,0:T(2,128)(2,1)}), bf16[128,2,2376]{2,1,0:T(2,128)(2,1)S(1)}, u32[]{:S(2)}, u32[]{:S(2)}) %all-to-all-start.1) | async-done | bytes 1216544 | tf_op jit(solution)/shard_map/all_to_all | solution.py:132
  131.7 0.9 convert_element_type.110
  132.7 1.3 copy-done.1
  134.3 1.6 mul.110
  135.9 5.0 %copy.160 = f32[128,2,2304]{2,1,0:T(2,128)} copy(f32[128,2,2304]{0,2,1:T(8,128)} %bitcast.79) | data formatting | bytes 4718592 | tf_op jit(solution)/shard_map/mul | solution.py:139
  140.9 3.8 %fusion.1 = f32[2,2304]{1,0:T(2,128)S(1)} fusion(f32[128,2,2304]{2,1,0:T(2,128)} %copy.160, f32[128,2,2376]{2,1,0:T(2,128)} %copy-done.1), kind=kLoop, calls=%fused_computation.9 | loop fusion | flops 1175040 | bytes 4737024 | tf_op jit(solution)/shard_map/reduce_sum | solution.py:139
  144.9 17.3 %all-gather = bf16[16,2,2304]{2,1,0:T(2,128)(2,1)S(1)} all-gather(bf16[1,2,2304]{2,1,0:T(2,128)(2,1)S(1)} %fusion.30), channel_id=1, replica_groups=mesh['req'=4,'exp'=8,'shard'=16] {'shard'}, dimensions={0}, use_global_device_ids=true | all-gather | bytes 156672 | tf_op jit(solution)/shard_map/all_gather | solution.py:143
  162.2 0.3 convolution_convert_fusion.2
  162.7 18.0 %all_gather.18 = bf16[2,16,2304]{1,0,2:T(2,128)(2,1)S(1)} all-gather(bf16[2,16,144]{1,0,2:T(2,128)(2,1)S(1)} %copy.161), channel_id=1, replica_groups=mesh['req'=4,'exp'=8,'shard'=16] {'shard'}, dimensions={2}, use_global_device_ids=true | all-gather | bytes 156672 | tf_op jit(solution)/shard_map/all_gather | solution.py:149
  180.7 1.4 copy.162
  182.2 0.3 fusion
  182.6 0.3 copy.166
  182.9 18.6 %all_to_all.20 = bf16[8,2,6,2304]{3,1,2,0:T(2,128)(2,1)S(1)} all-to-all(bf16[8,2,6,2304]{3,1,2,0:T(2,128)(2,1)S(1)} %copy.166), channel_id=1, replica_groups=mesh['req'=4,'exp'=8,'shard'=16] {'exp'}, dimensions={0} | all-to-all | bytes 884736 | tf_op jit(solution)/shard_map/all_to_all | solution.py:174
  201.7 0.6 fusion.3
  202.5 1.4 convolution_convert_fusion.1
  204.0 1.4 reshape.201
  205.3 1.7 copy.171
  207.0 6.3 %all-to-all-start.3 = ((bf16[128,2,6,144]{3,1,2,0:T(2,128)(2,1)}), bf16[128,2,6,144]{3,1,2,0:T(2,128)(2,1)S(1)}, u32[]{:S(2)}, u32[]{:S(2)}) async-start(bf16[128,2,6,144]{3,1,2,0:T(2,128)(2,1)} %bitcast.29), calls=%async_computation.3 | async-start | bytes 1572864 | tf_op jit(solution)/shard_map/all_to_all | solution.py:185
  213.5 25.8 %all-to-all-done.3 = bf16[128,2,6,144]{3,1,2,0:T(2,128)(2,1)S(1)} async-done(((bf16[128,2,6,144]{3,1,2,0:T(2,128)(2,1)}), bf16[128,2,6,144]{3,1,2,0:T(2,128)(2,1)S(1)}, u32[]{:S(2)}, u32[]{:S(2)}) %all-to-all-start.3) | async-done | bytes 442400 | tf_op jit(solution)/shard_map/all_to_all | solution.py:185
  239.3 0.8 bitcast_reduce_fusion
  240.4 19.1 %all_gather.19 = bf16[2,16,2304]{1,0,2:T(2,128)(2,1)S(1)} all-gather(bf16[2,16,144]{1,0,2:T(2,128)(2,1)S(1)} %copy.174), channel_id=1, replica_groups=mesh['req'=4,'exp'=8,'shard'=16] {'shard'}, dimensions={2}, use_global_device_ids=true | all-gather | bytes 156672 | tf_op jit(solution)/shard_map/all_gather | solution.py:202
  259.5 2.2 copy.175
  (90 shorter events, 4.5 us)
Async XLA Ops:
  0.0 201.7 %copy-start = (bf16[1,2,180,2304]{3,1,2,0:T(2,128)(2,1)S(1)}, bf16[1,2,180,2304]{3,1,2,0:T(2,128)(2,1)}, u32[]{:S(2)}) copy-start(bf16[1,2,180,2304]{3,1,2,0:T(2,128)(2,1)} %param.24) | copy-start | bytes 4976644
  0.9 24.8 %copy-start.17 = (s32[1,2]{1,0:T(1,128)S(1)}, s32[1,2]{1,0:T(1,128)}, u32[]{:S(2)}) copy-start(s32[1,2]{1,0:T(1,128)} %param.18) | copy-start | bytes 28
  0.9 25.0 %copy-start.16 = (s32[1,256]{1,0:T(1,128)S(1)}, s32[1,256]{1,0:T(1,128)}, u32[]{:S(2)}) copy-start(s32[1,256]{1,0:T(1,128)} %param.19) | copy-start | bytes 3076
  0.9 25.4 %copy-start.6 = (bf16[1,2,64,2304]{3,2,1,0:T(8,128)(2,1)S(1)}, bf16[1,2,64,2304]{3,2,1,0:T(8,128)(2,1)}, u32[]{:S(2)}) copy-start(bf16[1,2,64,2304]{3,2,1,0:T(8,128)(2,1)} %param.20) | copy-start | bytes 1769476
  14.3 14.0 %copy-start.5 = (bf16[1,2,64,2304]{3,2,1,0:T(8,128)(2,1)S(1)}, bf16[1,2,64,2304]{3,2,1,0:T(8,128)(2,1)}, u32[]{:S(2)}) copy-start(bf16[1,2,64,2304]{3,2,1,0:T(8,128)(2,1)} %param.21) | copy-start | bytes 1769476
  14.3 42.0 %all-to-all-start = ((bf16[8,2,16,2304]{3,2,1,0:T(8,128)(2,1)}), bf16[8,2,16,2304]{3,2,1,0:T(8,128)(2,1)}, u32[]{:S(2)}, u32[]{:S(2)}) async-start(bf16[8,2,16,2304]{3,2,1,0:T(8,128)(2,1)} %broadcast_in_dim.200), calls=%async_computation | async-start | bytes 2359296 | tf_op jit(solution)/shard_map/all_to_all | solution.py:65
  59.3 2.5 copy-start.3
  65.1 3.4 %copy-start.2 = (bf16[1,2,64,2304]{2,3,1,0:T(8,128)(2,1)S(1)}, bf16[1,2,64,2304]{2,3,1,0:T(8,128)(2,1)}, u32[]{:S(2)}) copy-start(bf16[1,2,64,2304]{2,3,1,0:T(8,128)(2,1)} %copy.179) | copy-start | bytes 1769476
  82.4 14.6 %copy-start.14 = (s32[2,16,2]{1,2,0:T(2,128)S(1)}, s32[2,16,2]{1,2,0:T(2,128)}, u32[]{:S(2)}) copy-start(s32[2,16,2]{1,2,0:T(2,128)} %param.15) | copy-start | bytes 772
  82.4 14.7 %copy-start.15 = (bf16[2,16,2]{1,2,0:T(2,128)(2,1)S(1)}, bf16[2,16,2]{1,2,0:T(2,128)(2,1)}, u32[]{:S(2)}) copy-start(bf16[2,16,2]{1,2,0:T(2,128)(2,1)} %param.16) | copy-start | bytes 388
  82.4 14.8 %copy-start.7 = (bf16[2,16,2304]{2,1,0:T(8,128)(2,1)S(1)}, bf16[2,16,2304]{2,1,0:T(8,128)(2,1)}, u32[]{:S(2)}) copy-start(bf16[2,16,2304]{2,1,0:T(8,128)(2,1)} %param.14) | copy-start | bytes 442372
  86.2 45.4 %all-to-all-start.1 = ((bf16[128,2,2376]{2,1,0:T(2,128)(2,1)}), bf16[128,2,2376]{2,1,0:T(2,128)(2,1)S(1)}, u32[]{:S(2)}, u32[]{:S(2)}) async-start(bf16[128,2,2376]{2,1,0:T(2,128)(2,1)} %reshape.198), calls=%async_computation.1 | async-start | bytes 2490368 | tf_op jit(solution)/shard_map/all_to_all | solution.py:132
  112.8 21.4 %copy-start.8 = (s32[2,16,2,6]{1,3,2,0:T(8,128)}, s32[2,16,2,6]{1,3,2,0:T(8,128)S(1)}, u32[]{:S(2)}) copy-start(s32[2,16,2,6]{1,3,2,0:T(8,128)S(1)} %fusion.27) | copy-start | bytes 4612
  112.8 21.4 %copy-start.10 = (s32[2,16,2,8]{1,3,2,0:T(8,128)}, s32[2,16,2,8]{1,3,2,0:T(8,128)S(1)}, u32[]{:S(2)}) copy-start(s32[2,16,2,8]{1,3,2,0:T(8,128)S(1)} %fusion.26) | copy-start | bytes 6148
  132.5 1.4 copy-start.1
  140.9 21.3 %copy-start.4 = (bf16[144,2304]{1,0:T(8,128)(2,1)S(1)}, bf16[144,2304]{1,0:T(8,128)(2,1)}, u32[]{:S(2)}) copy-start(bf16[144,2304]{1,0:T(8,128)(2,1)} %param.23) | copy-start | bytes 1990660
  144.7 37.5 %copy-start.13 = (f32[2304]{0:T(1024)S(1)}, f32[2304]{0:T(1024)}, u32[]{:S(2)}) copy-start(f32[2304]{0:T(1024)} %param.22) | copy-start | bytes 27652
  203.9 9.4 %copy-start.12 = (bf16[2,16,2]{2,1,0:T(8,128)(2,1)S(1)}, bf16[2,16,2]{2,1,0:T(8,128)(2,1)}, u32[]{:S(2)}) copy-start(bf16[2,16,2]{2,1,0:T(8,128)(2,1)} %get-tuple-element.13) | copy-start | bytes 388
  203.9 9.5 %copy-start.9 = (s32[2,16,2,6]{1,3,2,0:T(8,128)S(1)}, s32[2,16,2,6]{1,3,2,0:T(8,128)}, u32[]{:S(2)}) copy-start(s32[2,16,2,6]{1,3,2,0:T(8,128)} %copy-done.8) | copy-start | bytes 4612
  204.0 9.5 %copy-start.11 = (s32[2,16,2,8]{1,3,2,0:T(8,128)S(1)}, s32[2,16,2,8]{1,3,2,0:T(8,128)}, u32[]{:S(2)}) copy-start(s32[2,16,2,8]{1,3,2,0:T(8,128)} %copy-done.10) | copy-start | bytes 6148
  207.0 32.3 %all-to-all-start.3 = ((bf16[128,2,6,144]{3,1,2,0:T(2,128)(2,1)}), bf16[128,2,6,144]{3,1,2,0:T(2,128)(2,1)S(1)}, u32[]{:S(2)}, u32[]{:S(2)}) async-start(bf16[128,2,6,144]{3,1,2,0:T(2,128)(2,1)} %bitcast.29), calls=%async_computation.3 | async-start | bytes 1572864 | tf_op jit(solution)/shard_map/all_to_all | solution.py:185

commit v4 on v3

--- a/solution.py
+++ b/solution.py
@@ -63,12 +63,9 @@
         served_query[None], (experts_count,) + served_query.shape
     )
     group_query = lax.all_to_all(spread_query, "exp", 0, 0, tiled=False)
-    group_query = jnp.transpose(group_query, (1, 0, 2, 3)).reshape(
-        members, experts_count * tokens_here, width
-    )
-    stretch_len = group_query.shape[1]
     pages_here = key_pool.shape[1]
     page_size = key_pool.shape[2]
+    keys_here = pages_here * page_size
     device_index = exp_index * shard_count + shard_index
     physical = device_index * pages_here + jnp.arange(pages_here, dtype=jnp.int32)
     page_row = page_order[0]
@@ -78,57 +75,50 @@
         jnp.where(matched, jnp.arange(pool_size, dtype=jnp.int32)[None, :], 0), axis=1
     )
     prior_row = prior_pages[0]
-    page_counts = prior_row + stretch_len // page_size
+    page_counts = prior_row + experts_count * tokens_here // page_size
     page_ends = jnp.cumsum(page_counts)
     page_starts = page_ends - page_counts
     owner_slot = jnp.sum((located[:, None] >= page_ends[None, :]).astype(jnp.int32), axis=1)
     owner_hot = owner_slot[:, None] == jnp.arange(members, dtype=jnp.int32)[None, :]
     logical = located - jnp.sum(jnp.where(owner_hot, page_starts[None, :], 0), axis=1)
-    prior_here = jnp.sum(jnp.where(owner_hot, prior_row[None, :], 0), axis=1)
-    key_place = logical[:, None] * page_size + jnp.arange(page_size, dtype=jnp.int32)[None, :]
+    key_place = (
+        logical[:, None] * page_size + jnp.arange(page_size, dtype=jnp.int32)[None, :]
+    ).reshape(keys_here)
+    key_owner = jnp.repeat(owner_slot, page_size)
     query_place = (
-        prior_here[:, None] * page_size + jnp.arange(stretch_len, dtype=jnp.int32)[None, :]
-    )
-    visible = key_place[:, None, :] <= query_place[:, :, None]
-    page_query = jnp.take(group_query, owner_slot, axis=0).reshape(
-        pages_here, stretch_len, H, head_size
-    )
-    key_rows = key_pool[0].reshape(pages_here, page_size, H, head_size)
-    value_rows = value_pool[0].reshape(pages_here, page_size, H, head_size)
+        prior_row[None, :, None] * page_size
+        + jnp.arange(experts_count, dtype=jnp.int32)[:, None, None] * tokens_here
+        + jnp.arange(tokens_here, dtype=jnp.int32)[None, None, :]
+    )
+    visible = (key_owner[None, None, None, :] == jnp.arange(members, dtype=jnp.int32)[None, :, None, None]) & (
+        key_place[None, None, None, :] <= query_place[..., None]
+    )
+    query_rows = group_query.reshape(experts_count, members, tokens_here, H, head_size)
+    key_rows = key_pool[0].reshape(keys_here, H, head_size)
+    value_rows = value_pool[0].reshape(keys_here, H, head_size)
     scores = jnp.einsum(
-        "pqhd,pkhd->phqk", page_query, key_rows, preferred_element_type=jnp.float32
+        "ejthd,khd->ejhtk", query_rows, key_rows, preferred_element_type=jnp.float32
     ) * (1.0 / math.sqrt(head_size))
-    scores = jnp.where(visible[:, None, :, :], scores, NEG_FILL)
-    page_peak = jnp.max(scores, axis=3)
-    local_peak = jnp.max(
-        jnp.where(owner_hot[:, :, None, None], page_peak[:, None], NEG_FILL), axis=0
-    )
-    local_peak = local_peak.astype(jnp.bfloat16).astype(jnp.float32)
-    peak_here = jnp.take(local_peak, owner_slot, axis=0)
+    scores = jnp.where(visible[:, :, None], scores, NEG_FILL)
+    local_peak = jnp.max(scores, axis=4).astype(jnp.bfloat16).astype(jnp.float32)
     weights_bf = jnp.where(
-        visible[:, None, :, :], jnp.exp(scores - peak_here[..., None]), 0.0
-    ).astype(jnp.bfloat16)
-    page_totals = jnp.sum(weights_bf, axis=3, dtype=jnp.float32)
-    page_context = jnp.einsum(
-        "phqk,pkhd->pqhd", weights_bf, value_rows, preferred_element_type=jnp.float32
-    )
-    page_context = page_context.reshape(pages_here, stretch_len, width)
-    context = jnp.sum(jnp.where(owner_hot[:, :, None, None], page_context[:, None], 0.0), axis=0)
-    totals = jnp.sum(jnp.where(owner_hot[:, :, None, None], page_totals[:, None], 0.0), axis=0)
+        visible[:, :, None], jnp.exp(scores - local_peak[..., None]), 0.0
+    ).astype(jnp.bfloat16)
+    totals = jnp.sum(weights_bf, axis=4, dtype=jnp.float32)
+    context = jnp.einsum(
+        "ejhtk,khd->ejthd", weights_bf, value_rows, preferred_element_type=jnp.float32
+    ).reshape(experts_count, members, tokens_here, width)
     packed = jnp.concatenate(
         [
             context.astype(jnp.bfloat16),
-            jnp.transpose(local_peak, (0, 2, 1)).astype(jnp.bfloat16),
-            jnp.transpose(totals, (0, 2, 1)).astype(jnp.bfloat16),
+            jnp.transpose(local_peak, (0, 1, 3, 2)).astype(jnp.bfloat16),
+            jnp.transpose(totals, (0, 1, 3, 2)).astype(jnp.bfloat16),
         ],
-        axis=2,
-    )
-    packed_width = packed.shape[2]
+        axis=3,
+    )
+    packed_width = packed.shape[3]
     rows_each = members * tokens_here // shard_count
-    packed = packed.reshape(members, experts_count, tokens_here, packed_width)
-    packed = jnp.transpose(packed, (1, 0, 2, 3)).reshape(
-        experts_count * shard_count, rows_each, packed_width
-    )
+    packed = packed.reshape(experts_count * shard_count, rows_each, packed_width)
     arrived = lax.all_to_all(packed, ("exp", "shard"), 0, 0, tiled=True).astype(jnp.float32)
     arrived_context = arrived[:, :, :width].reshape(-1, rows_each, H, head_size)
     arrived_peak = arrived[:, :, width : width + H]

time: 263 us -> 257 us (0.977)
  other arithmetic: 16.1 us -> 13.1 us
    convert_element_type x2 -> x4, local copies, waits for them, and re-layouts: 0.28 us -> 7.83 us  [the longest x2 7.4 us: on_device(): context.astype(jnp.bfloat16)]
    gather x3 -> x0, local copies, waits for them, and re-layouts: 4.7 us -> none  [the longest x2 4.15 us: on_device(): jnp.take(group_query, owner_slot, axis=0)]
    broadcast_in_dim x1, local copies, waits for them, and re-layouts: 3.07 us -> 0.07 us  [on_device(): key_owner = jnp.repeat(owner_slot, page_size)]
    reduce_sum x3 -> x1, other arithmetic: 5.95 us -> 3.09 us  [on_device(): totals = jnp.sum(weights_bf, axis=4, dtype=jnp.float32)]
  transfers between devices with their start and end apart: 3 -> 3, of which waited for: 3 -> 3; matrix products, arithmetic and copies ran while one was open for 3% -> 4% of each run, Pallas kernels for 0% -> 0%
where the time goes in v4:
time: 257 us; the launch traced here: 256 us
  blocking collectives  95.6 us (37%)
  waiting for transfers between devices  70.5 us (27%)
  local copies, waits for them, and re-layouts  39.8 us (15%)
  starting transfers between devices  26.7 us (10%)
  other arithmetic  13.1 us (5%)
  matrix products  9.98 us (4%)
    all_to_all x1, waiting for transfers between devices, on_device(): lax.all_to_all(partial_out, ('exp', 'shard'), 0, 0, tiled=True)  25.8 us
    all_to_all x1, waiting for transfers between devices, on_device(): group_query = lax.all_to_all(spread_query, 'exp', 0, 0, tiled=False)  25.7 us
    all_gather x1, blocking collectives, on_device(): mixed_out = lax.all_gather(mixed_block, 'shard', axis=2, tiled=True)  19.1 us
    all_to_all x1, waiting for transfers between devices, on_device(): lax.all_to_all(packed, ('exp', 'shard'), 0, 0, tiled=True)  19 us
    all_to_all x1, blocking collectives, on_device(): lax.all_to_all(sent_rows, 'exp', split_axis=0, concat_axis=0, tiled=True)  18.6 us
    all_gather x1, blocking collectives, on_device(): projected = lax.all_gather(projected_part, 'shard', axis=2, tiled=True)  18 us
    all_gather x1, blocking collectives, on_device(): lax.all_gather(row_attended, 'shard', axis=0, tiled=True)  17.3 us
    all_gather x1, blocking collectives, on_device(): all_query = lax.all_gather(query_stretch, 'req', axis=0, tiled=True)  11.6 us
  transfers between devices with their start and end apart: 3, of which 3 were waited for; matrix products, arithmetic and copies ran while one was open for 4% of the time, Pallas kernels for 0%

profile of v4, /device:TPU:1, one launch (start us, length us, event | category | flops | bytes accessed | tf_op | source)
XLA Modules:
  0.0 256.2 jit_solution(16162100720119714300)
XLA Ops:
  0.0 0.9 compare_and_fusion.1
  0.9 11.6 %all_gather.16 = bf16[8,16,2304]{2,1,0:T(8,128)(2,1)S(1)} all-gather(bf16[2,16,2304]{2,1,0:T(8,128)(2,1)} %param.13), channel_id=1, replica_groups=mesh['req'=4,'exp'=8,'shard'=16] {'req'}, dimensions={0}, use_global_device_ids=true | all-gather | bytes 737280 | tf_op jit(solution)/shard_map/all_gather | solution.py:53
  12.5 0.6 gather_fusion.1
  13.1 1.1 broadcast_in_dim.117
  14.2 11.3 %all-to-all-start = ((bf16[8,2,16,2304]{3,2,1,0:T(8,128)(2,1)}), bf16[8,2,16,2304]{3,2,1,0:T(8,128)(2,1)S(1)}, u32[]{:S(2)}, u32[]{:S(2)}) async-start(bf16[8,2,16,2304]{3,2,1,0:T(8,128)(2,1)} %broadcast_in_dim.117), calls=%async_computation | async-start | bytes 2359296 | tf_op jit(solution)/shard_map/all_to_all | solution.py:65
  25.9 0.2 fusion.31
  26.6 2.0 reshape.238
  28.6 2.8 %reshape.239 = bf16[128,36,64]{2,1,0:T(8,128)(2,1)} reshape(bf16[1,2,64,2304]{3,2,1,0:T(8,128)(2,1)} %param.21) | data formatting | bytes 1179648 | tf_op jit(solution)/shard_map/reshape;squeeze | solution.py:98
  31.7 25.7 %all-to-all-done = bf16[8,2,16,2304]{3,2,1,0:T(8,128)(2,1)S(1)} async-done(((bf16[8,2,16,2304]{3,2,1,0:T(8,128)(2,1)}), bf16[8,2,16,2304]{3,2,1,0:T(8,128)(2,1)S(1)}, u32[]{:S(2)}, u32[]{:S(2)}) %all-to-all-start) | async-done | bytes 1179680 | tf_op jit(solution)/shard_map/all_to_all | solution.py:65
  57.5 3.0 %reshape.203 = bf16[8,2,16,36,64]{4,3,2,1,0:T(8,128)(2,1)} reshape(bf16[8,2,16,2304]{3,2,1,0:T(8,128)(2,1)S(1)} %all-to-all-done) | data formatting | bytes 2359296 | tf_op jit(solution)/shard_map/reshape | solution.py:96
  60.5 3.8 %bitcast_reduce_fusion = (bf16[8,2,36,16]{3,1,0,2:T(2,128)(2,1)S(1)}, f32[36,8,2,16,128]{4,3,2,1,0:T(8,128)S(1)}) fusion(pred[8,2,16,128]{3,2,1,0:T(8,128)(4,1)S(1)} %compare_and_fusion, bf16[128,36,64,1,1]{2,1,0,4,3:T(8,128)(2,1)} %bitcast.85, bf16[8,2,16,36,64]{4,3,2,1,0:T(8,128)(2,1)} %reshape.203), kind=kOutput, calls=%fused_computation.3 | convolution fusion | flops 154524672 | bytes 6539264 | tf_op jit(solution)/shard_map/ejthd,khd->ejhtk/dot_general | solution.py:99
  64.4 3.1 %fusion.34 = bf16[8,2,36,16]{3,1,0,2:T(2,128)(2,1)S(1)} fusion(f32[8,2,36,16]{3,1,0,2:T(2,128)S(1)} %convert_element_type.187, f32[36,8,2,16,128]{4,3,2,1,0:T(8,128)S(1)} %get-tuple-element.16, pred[8,2,16,128]{3,2,1,0:T(8,128)(4,1)S(1)} %compare_and_fusion), kind=kLoop, calls=%fused_computation.82 | loop fusion | flops 7068672 | bytes 4806656 | tf_op jit(solution)/shard_map/reduce_sum | solution.py:107
  67.5 0.2 copy.82
  67.7 3.4 %convert_bitcast_fusion = bf16[8,2,16,36,64]{4,2,1,0,3:T(8,128)(2,1)S(1)} fusion(bf16[128,36,64,1,1]{2,1,0,4,3:T(8,128)(2,1)S(1)} %bitcast.84, f32[36,8,2,16,128]{4,3,2,1,0:T(8,128)} %copy-done.2, f32[8,2,36,16]{3,1,0,2:T(2,128)S(1)} %convert_element_type.187, pred[8,2,16,128]{3,2,1,0:T(8,128)(4,1)S(1)} %compare_and_fusion), kind=kOutput, calls=%fused_computation.15 | convolution fusion | flops 157483008 | bytes 6557696 | tf_op jit(solution)/shard_map/ejhtk,khd->ejthd/dot_general | solution.py:108
  71.1 3.1 %copy.80 = bf16[8,2,16,36,64]{4,3,2,1,0:T(8,128)(2,1)} copy(bf16[8,2,16,36,64]{4,2,1,0,3:T(8,128)(2,1)S(1)} %convert_bitcast_fusion) | data formatting | bytes 2359296 | tf_op jit(solution)/shard_map/convert_element_type | solution.py:113
  74.2 4.3 %convert_element_type.117 = bf16[8,2,16,2304]{3,2,1,0:T(8,128)(2,1)} reshape(bf16[8,2,16,36,64]{4,3,2,1,0:T(8,128)(2,1)} %copy.80) | data formatting | bytes 2359296 | tf_op jit(solution)/shard_map/convert_element_type | solution.py:113
  78.5 0.2 copy.81
  78.7 2.4 concatenate.7
  81.1 1.3 reshape.204
  82.5 9.0 %all-to-all-start.1 = ((bf16[128,2,2376]{2,1,0:T(2,128)(2,1)}), bf16[128,2,2376]{2,1,0:T(2,128)(2,1)S(1)}, u32[]{:S(2)}, u32[]{:S(2)}) async-start(bf16[128,2,2376]{2,1,0:T(2,128)(2,1)} %reshape.204), calls=%async_computation.1 | async-start | bytes 2490368 | tf_op jit(solution)/shard_map/all_to_all | solution.py:122
  91.7 0.7 concatenate.6
  92.5 11.2 %all_gather.15 = bf16[8,16,2308]{2,1,0:T(8,128)(2,1)S(1)} all-gather(bf16[2,16,2308]{2,1,0:T(8,128)(2,1)} %concatenate.6), channel_id=1, replica_groups=mesh['req'=4,'exp'=8,'shard'=16] {'req'}, dimensions={0}, use_global_device_ids=true | all-gather | bytes 738560 | tf_op jit(solution)/shard_map/all_gather | solution.py:54
  103.7 1.2 gather_fusion
  104.9 1.0 broadcast_select_fusion
  105.9 0.6 fusion.36
  107.2 19.0 %all-to-all-done.1 = bf16[128,2,2376]{2,1,0:T(2,128)(2,1)S(1)} async-done(((bf16[128,2,2376]{2,1,0:T(2,128)(2,1)}), bf16[128,2,2376]{2,1,0:T(2,128)(2,1)S(1)}, u32[]{:S(2)}, u32[]{:S(2)}) %all-to-all-start.1) | async-done | bytes 1216544 | tf_op jit(solution)/shard_map/all_to_all | solution.py:122
  126.2 0.9 convert_element_type.120
  127.3 1.3 copy-done.1
  128.5 0.2 fusion.19
  128.9 1.6 mul.124
  130.5 5.0 %copy.84 = f32[128,2,2304]{2,1,0:T(2,128)} copy(f32[128,2,2304]{0,2,1:T(8,128)} %bitcast.82) | data formatting | bytes 4718592 | tf_op jit(solution)/shard_map/mul | solution.py:129
  135.5 3.8 %fusion.4 = f32[2,2304]{1,0:T(2,128)S(1)} fusion(f32[128,2,2304]{2,1,0:T(2,128)} %copy.84, f32[128,2,2376]{2,1,0:T(2,128)} %copy-done.1), kind=kLoop, calls=%fused_computation.12 | loop fusion | flops 1175040 | bytes 4737024 | tf_op jit(solution)/shard_map/reduce_sum | solution.py:129
  139.5 17.3 %all-gather = bf16[16,2,2304]{2,1,0:T(2,128)(2,1)S(1)} all-gather(bf16[1,2,2304]{2,1,0:T(2,128)(2,1)S(1)} %fusion.29), channel_id=1, replica_groups=mesh['req'=4,'exp'=8,'shard'=16] {'shard'}, dimensions={0}, use_global_device_ids=true | all-gather | bytes 156672 | tf_op jit(solution)/shard_map/all_gather | solution.py:133
  156.8 0.3 convolution_convert_fusion.2
  157.3 18.0 %all_gather.18 = bf16[2,16,2304]{1,0,2:T(2,128)(2,1)S(1)} all-gather(bf16[2,16,144]{1,0,2:T(2,128)(2,1)S(1)} %copy.85), channel_id=1, replica_groups=mesh['req'=4,'exp'=8,'shard'=16] {'shard'}, dimensions={2}, use_global_device_ids=true | all-gather | bytes 156672 | tf_op jit(solution)/shard_map/all_gather | solution.py:139
  175.3 1.4 copy.86
  176.8 0.3 fusion.3
  177.2 0.3 copy.90
  177.5 18.6 %all_to_all.20 = bf16[8,2,6,2304]{3,1,2,0:T(2,128)(2,1)S(1)} all-to-all(bf16[8,2,6,2304]{3,1,2,0:T(2,128)(2,1)S(1)} %copy.90), channel_id=1, replica_groups=mesh['req'=4,'exp'=8,'shard'=16] {'exp'}, dimensions={0} | all-to-all | bytes 884736 | tf_op jit(solution)/shard_map/all_to_all | solution.py:164
  196.3 0.6 fusion.7
  197.1 1.4 convolution_convert_fusion.1
  198.5 1.4 reshape.207
  199.9 1.7 copy.95
  201.6 6.3 %all-to-all-start.3 = ((bf16[128,2,6,144]{3,1,2,0:T(2,128)(2,1)}), bf16[128,2,6,144]{3,1,2,0:T(2,128)(2,1)S(1)}, u32[]{:S(2)}, u32[]{:S(2)}) async-start(bf16[128,2,6,144]{3,1,2,0:T(2,128)(2,1)} %bitcast.23), calls=%async_computation.3 | async-start | bytes 1572864 | tf_op jit(solution)/shard_map/all_to_all | solution.py:175
  208.1 25.8 %all-to-all-done.3 = bf16[128,2,6,144]{3,1,2,0:T(2,128)(2,1)S(1)} async-done(((bf16[128,2,6,144]{3,1,2,0:T(2,128)(2,1)}), bf16[128,2,6,144]{3,1,2,0:T(2,128)(2,1)S(1)}, u32[]{:S(2)}, u32[]{:S(2)}) %all-to-all-start.3) | async-done | bytes 442400 | tf_op jit(solution)/shard_map/all_to_all | solution.py:175
  233.9 0.8 bitcast_reduce_fusion.1
  234.9 19.1 %all_gather.19 = bf16[2,16,2304]{1,0,2:T(2,128)(2,1)S(1)} all-gather(bf16[2,16,144]{1,0,2:T(2,128)(2,1)S(1)} %copy.98), channel_id=1, replica_groups=mesh['req'=4,'exp'=8,'shard'=16] {'shard'}, dimensions={2}, use_global_device_ids=true | all-gather | bytes 156672 | tf_op jit(solution)/shard_map/all_gather | solution.py:192
  254.0 2.2 copy.99
  (87 shorter events, 3.9 us)
Async XLA Ops:
  0.0 196.3 %copy-start = (bf16[1,2,180,2304]{3,1,2,0:T(2,128)(2,1)S(1)}, bf16[1,2,180,2304]{3,1,2,0:T(2,128)(2,1)}, u32[]{:S(2)}) copy-start(bf16[1,2,180,2304]{3,1,2,0:T(2,128)(2,1)} %param.24) | copy-start | bytes 4976644
  0.9 24.7 %copy-start.18 = (s32[1,2]{1,0:T(1,128)S(1)}, s32[1,2]{1,0:T(1,128)}, u32[]{:S(2)}) copy-start(s32[1,2]{1,0:T(1,128)} %param.18) | copy-start | bytes 28
  0.9 24.9 %copy-start.17 = (s32[1,256]{1,0:T(1,128)S(1)}, s32[1,256]{1,0:T(1,128)}, u32[]{:S(2)}) copy-start(s32[1,256]{1,0:T(1,128)} %param.19) | copy-start | bytes 3076
  0.9 25.7 %copy-start.7 = (bf16[1,2,64,2304]{3,2,1,0:T(8,128)(2,1)S(1)}, bf16[1,2,64,2304]{3,2,1,0:T(8,128)(2,1)}, u32[]{:S(2)}) copy-start(bf16[1,2,64,2304]{3,2,1,0:T(8,128)(2,1)} %param.20) | copy-start | bytes 1769476
  14.2 43.3 %all-to-all-start = ((bf16[8,2,16,2304]{3,2,1,0:T(8,128)(2,1)}), bf16[8,2,16,2304]{3,2,1,0:T(8,128)(2,1)S(1)}, u32[]{:S(2)}, u32[]{:S(2)}) async-start(bf16[8,2,16,2304]{3,2,1,0:T(8,128)(2,1)} %broadcast_in_dim.117), calls=%async_computation | async-start | bytes 2359296 | tf_op jit(solution)/shard_map/all_to_all | solution.py:65
  64.2 3.2 %copy-start.2 = (f32[36,8,2,16,128]{4,3,2,1,0:T(8,128)}, f32[36,8,2,16,128]{4,3,2,1,0:T(8,128)S(1)}, u32[]{:S(2)}) copy-start(f32[36,8,2,16,128]{4,3,2,1,0:T(8,128)S(1)} %get-tuple-element.16) | copy-start | bytes 14155780
  64.2 3.2 %copy-start.5 = (bf16[8,2,36,16]{3,1,0,2:T(2,128)(2,1)}, bf16[8,2,36,16]{3,1,0,2:T(2,128)(2,1)S(1)}, u32[]{:S(2)}) copy-start(bf16[8,2,36,16]{3,1,0,2:T(2,128)(2,1)S(1)} %get-tuple-element.15) | copy-start | bytes 55300
  64.4 3.3 %copy-start.3 = (bf16[128,36,64]{2,1,0:T(8,128)(2,1)S(1)}, bf16[128,36,64]{2,1,0:T(8,128)(2,1)}, u32[]{:S(2)}) copy-start(bf16[128,36,64]{2,1,0:T(8,128)(2,1)} %reshape.239) | copy-start | bytes 1769476
  74.2 4.3 %copy-start.6 = (bf16[8,2,36,16]{3,1,0,2:T(2,128)(2,1)S(1)}, bf16[8,2,36,16]{3,1,0,2:T(2,128)(2,1)}, u32[]{:S(2)}) copy-start(bf16[8,2,36,16]{3,1,0,2:T(2,128)(2,1)} %copy-done.5) | copy-start | bytes 55300
  81.1 10.4 %copy-start.15 = (s32[2,16,2]{1,2,0:T(2,128)S(1)}, s32[2,16,2]{1,2,0:T(2,128)}, u32[]{:S(2)}) copy-start(s32[2,16,2]{1,2,0:T(2,128)} %param.15) | copy-start | bytes 772
  81.1 10.5 %copy-start.16 = (bf16[2,16,2]{1,2,0:T(2,128)(2,1)S(1)}, bf16[2,16,2]{1,2,0:T(2,128)(2,1)}, u32[]{:S(2)}) copy-start(bf16[2,16,2]{1,2,0:T(2,128)(2,1)} %param.16) | copy-start | bytes 388
  81.1 10.6 %copy-start.8 = (bf16[2,16,2304]{2,1,0:T(8,128)(2,1)S(1)}, bf16[2,16,2304]{2,1,0:T(8,128)(2,1)}, u32[]{:S(2)}) copy-start(bf16[2,16,2304]{2,1,0:T(8,128)(2,1)} %param.14) | copy-start | bytes 442372
  82.5 43.8 %all-to-all-start.1 = ((bf16[128,2,2376]{2,1,0:T(2,128)(2,1)}), bf16[128,2,2376]{2,1,0:T(2,128)(2,1)S(1)}, u32[]{:S(2)}, u32[]{:S(2)}) async-start(bf16[128,2,2376]{2,1,0:T(2,128)(2,1)} %reshape.204), calls=%async_computation.1 | async-start | bytes 2490368 | tf_op jit(solution)/shard_map/all_to_all | solution.py:122
  107.2 21.6 %copy-start.9 = (s32[2,16,2,6]{1,3,2,0:T(8,128)}, s32[2,16,2,6]{1,3,2,0:T(8,128)S(1)}, u32[]{:S(2)}) copy-start(s32[2,16,2,6]{1,3,2,0:T(8,128)S(1)} %fusion.28) | copy-start | bytes 4612
  107.2 21.6 %copy-start.11 = (s32[2,16,2,8]{1,3,2,0:T(8,128)}, s32[2,16,2,8]{1,3,2,0:T(8,128)S(1)}, u32[]{:S(2)}) copy-start(s32[2,16,2,8]{1,3,2,0:T(8,128)S(1)} %fusion.27) | copy-start | bytes 6148
  127.1 1.4 copy-start.1
  135.5 21.3 %copy-start.4 = (bf16[144,2304]{1,0:T(8,128)(2,1)S(1)}, bf16[144,2304]{1,0:T(8,128)(2,1)}, u32[]{:S(2)}) copy-start(bf16[144,2304]{1,0:T(8,128)(2,1)} %param.23) | copy-start | bytes 1990660
  139.3 37.5 %copy-start.14 = (f32[2304]{0:T(1024)S(1)}, f32[2304]{0:T(1024)}, u32[]{:S(2)}) copy-start(f32[2304]{0:T(1024)} %param.22) | copy-start | bytes 27652
  198.5 9.4 %copy-start.13 = (bf16[2,16,2]{2,1,0:T(8,128)(2,1)S(1)}, bf16[2,16,2]{2,1,0:T(8,128)(2,1)}, u32[]{:S(2)}) copy-start(bf16[2,16,2]{2,1,0:T(8,128)(2,1)} %get-tuple-element.11) | copy-start | bytes 388
  198.5 9.5 %copy-start.10 = (s32[2,16,2,6]{1,3,2,0:T(8,128)S(1)}, s32[2,16,2,6]{1,3,2,0:T(8,128)}, u32[]{:S(2)}) copy-start(s32[2,16,2,6]{1,3,2,0:T(8,128)} %copy-done.9) | copy-start | bytes 4612
  198.5 9.5 %copy-start.12 = (s32[2,16,2,8]{1,3,2,0:T(8,128)S(1)}, s32[2,16,2,8]{1,3,2,0:T(8,128)}, u32[]{:S(2)}) copy-start(s32[2,16,2,8]{1,3,2,0:T(8,128)} %copy-done.11) | copy-start | bytes 6148
  201.6 32.3 %all-to-all-start.3 = ((bf16[128,2,6,144]{3,1,2,0:T(2,128)(2,1)}), bf16[128,2,6,144]{3,1,2,0:T(2,128)(2,1)S(1)}, u32[]{:S(2)}, u32[]{:S(2)}) async-start(bf16[128,2,6,144]{3,1,2,0:T(2,128)(2,1)} %bitcast.23), calls=%async_computation.3 | async-start | bytes 1572864 | tf_op jit(solution)/shard_map/all_to_all | solution.py:175

commit v5 on v4

--- a/solution.py
+++ b/solution.py
@@ -55,14 +55,15 @@
     served = lax.dynamic_slice_in_dim(request_order, group_index * members, members)
     served_query = jnp.take(all_query, served, axis=0)
     served_extras = jnp.take(all_extras, served, axis=0)
+    spread_query = jnp.broadcast_to(
+        served_query[None], (experts_count,) + served_query.shape
+    )
+    group_query = lax.all_to_all(spread_query, "exp", 0, 0, tiled=False)
+    group_query, served_extras = lax.optimization_barrier((group_query, served_extras))
     top_count = route_ids.shape[2]
     served_resid = served_extras[:, :, :width]
     served_probs = served_extras[:, :, width : width + top_count]
     served_ids = served_extras[:, :, width + top_count :].astype(jnp.int32)
-    spread_query = jnp.broadcast_to(
-        served_query[None], (experts_count,) + served_query.shape
-    )
-    group_query = lax.all_to_all(spread_query, "exp", 0, 0, tiled=False)
     pages_here = key_pool.shape[1]
     page_size = key_pool.shape[2]
     keys_here = pages_here * page_size

time: 257 us -> 257 us (level)
    all_to_all x1, waiting for transfers between devices: 19 us -> 33.4 us  [on_device(): lax.all_to_all(packed, ('exp', 'shard'), 0, 0, tiled=True)]
    all_to_all x1, waiting for transfers between devices: 25.7 us -> 12.1 us  [on_device(): group_query = lax.all_to_all(spread_query, 'exp', 0, 0, tiled=False)]
where the time goes in v5:
time: 257 us
  blocking collectives  95 us (37%)
  waiting for transfers between devices  71.2 us (28%)
  local copies, waits for them, and re-layouts  40.6 us (16%)
  starting transfers between devices  26.7 us (10%)
  other arithmetic  12.2 us (5%)
  matrix products  10.3 us (4%)
    all_to_all x1, waiting for transfers between devices, on_device(): lax.all_to_all(packed, ('exp', 'shard'), 0, 0, tiled=True)  33.4 us
    all_to_all x1, waiting for transfers between devices, on_device(): lax.all_to_all(partial_out, ('exp', 'shard'), 0, 0, tiled=True)  25.8 us
    all_gather x1, blocking collectives, on_device(): mixed_out = lax.all_gather(mixed_block, 'shard', axis=2, tiled=True)  19.1 us
    all_to_all x1, blocking collectives, on_device(): lax.all_to_all(sent_rows, 'exp', split_axis=0, concat_axis=0, tiled=True)  18.6 us
    all_gather x1, blocking collectives, on_device(): projected = lax.all_gather(projected_part, 'shard', axis=2, tiled=True)  18 us
    all_gather x1, blocking collectives, on_device(): lax.all_gather(row_attended, 'shard', axis=0, tiled=True)  17.3 us
    all_to_all x1, waiting for transfers between devices, on_device(): group_query = lax.all_to_all(spread_query, 'exp', 0, 0, tiled=False)  12.1 us
    all_gather x1, blocking collectives, on_device(): all_query = lax.all_gather(query_stretch, 'req', axis=0, tiled=True)  11.6 us
  transfers between devices with their start and end apart: 3, of which 3 were waited for; matrix products, arithmetic and copies ran while one was open for 4% of the time, Pallas kernels for 0%

profile of v5, /device:TPU:1, one launch (start us, length us, event | category | flops | bytes accessed | tf_op | source)
XLA Modules:
  0.0 256.5 jit_solution(3802957944053696097)
XLA Ops:
  0.0 0.9 compare_and_fusion.1
  0.9 11.6 %all_gather.15 = bf16[8,16,2304]{2,1,0:T(8,128)(2,1)S(1)} all-gather(bf16[2,16,2304]{2,1,0:T(8,128)(2,1)} %param.13), channel_id=1, replica_groups=mesh['req'=4,'exp'=8,'shard'=16] {'req'}, dimensions={0}, use_global_device_ids=true | all-gather | bytes 737280 | tf_op jit(solution)/shard_map/all_gather | solution.py:53
  12.5 0.6 gather_fusion
  13.1 1.1 broadcast_in_dim.107
  14.2 11.3 %all-to-all-start = ((bf16[8,2,16,2304]{3,2,1,0:T(8,128)(2,1)}), bf16[8,2,16,2304]{3,2,1,0:T(8,128)(2,1)S(1)}, u32[]{:S(2)}, u32[]{:S(2)}) async-start(bf16[8,2,16,2304]{3,2,1,0:T(8,128)(2,1)} %broadcast_in_dim.107), calls=%async_computation | async-start | bytes 2359296 | tf_op jit(solution)/shard_map/all_to_all | solution.py:61
  25.8 0.8 concatenate.6
  26.5 10.6 %all_gather.16 = bf16[8,16,2308]{2,1,0:T(8,128)(2,1)S(1)} all-gather(bf16[2,16,2308]{2,1,0:T(8,128)(2,1)} %concatenate.6), channel_id=1, replica_groups=mesh['req'=4,'exp'=8,'shard'=16] {'req'}, dimensions={0}, use_global_device_ids=true | all-gather | bytes 738560 | tf_op jit(solution)/shard_map/all_gather | solution.py:54
  37.1 1.2 gather_fusion.1
  38.7 0.2 fusion.31
  38.9 0.2 fusion.32
  39.4 2.8 %reshape.238 = bf16[128,36,64]{2,1,0:T(8,128)(2,1)} reshape(bf16[1,2,64,2304]{3,2,1,0:T(8,128)(2,1)} %param.20) | data formatting | bytes 1179648 | tf_op jit(solution)/shard_map/reshape;squeeze | solution.py:98
  42.2 2.8 %reshape.239 = bf16[128,36,64]{2,1,0:T(8,128)(2,1)} reshape(bf16[1,2,64,2304]{3,2,1,0:T(8,128)(2,1)} %param.21) | data formatting | bytes 1179648 | tf_op jit(solution)/shard_map/reshape;squeeze | solution.py:99
  45.5 12.1 %all-to-all-done = bf16[8,2,16,2304]{3,2,1,0:T(8,128)(2,1)S(1)} async-done(((bf16[8,2,16,2304]{3,2,1,0:T(8,128)(2,1)}), bf16[8,2,16,2304]{3,2,1,0:T(8,128)(2,1)S(1)}, u32[]{:S(2)}, u32[]{:S(2)}) %all-to-all-start) | async-done | bytes 1179680 | tf_op jit(solution)/shard_map/all_to_all | solution.py:61
  57.5 3.0 %reshape.203 = bf16[8,2,16,36,64]{4,3,2,1,0:T(8,128)(2,1)} reshape(bf16[8,2,16,2304]{3,2,1,0:T(8,128)(2,1)S(1)} %all-to-all-done) | data formatting | bytes 2359296 | tf_op jit(solution)/shard_map/reshape | solution.py:97
  60.5 3.8 %bitcast_reduce_fusion = (bf16[8,2,36,16]{3,1,0,2:T(2,128)(2,1)S(1)}, f32[36,8,2,16,128]{4,3,2,1,0:T(8,128)S(1)}) fusion(pred[8,2,16,128]{3,2,1,0:T(8,128)(4,1)S(1)} %compare_and_fusion, bf16[128,36,64,1,1]{2,1,0,4,3:T(8,128)(2,1)} %bitcast.85, bf16[8,2,16,36,64]{4,3,2,1,0:T(8,128)(2,1)} %reshape.203), kind=kOutput, calls=%fused_computation.3 | convolution fusion | flops 154524672 | bytes 6539264 | tf_op jit(solution)/shard_map/ejthd,khd->ejhtk/dot_general | solution.py:100
  64.4 3.1 %fusion.34 = bf16[8,2,36,16]{3,1,0,2:T(2,128)(2,1)S(1)} fusion(f32[8,2,36,16]{3,1,0,2:T(2,128)S(1)} %convert_element_type.187, f32[36,8,2,16,128]{4,3,2,1,0:T(8,128)S(1)} %get-tuple-element.20, pred[8,2,16,128]{3,2,1,0:T(8,128)(4,1)S(1)} %compare_and_fusion), kind=kLoop, calls=%fused_computation.82 | loop fusion | flops 7068672 | bytes 4806656 | tf_op jit(solution)/shard_map/reduce_sum | solution.py:108
  67.5 0.2 copy.82
  67.7 3.8 %convert_bitcast_fusion = bf16[8,2,16,36,64]{4,2,1,0,3:T(8,128)(2,1)S(1)} fusion(bf16[128,36,64,1,1]{2,1,0,4,3:T(8,128)(2,1)} %bitcast.84, f32[36,8,2,16,128]{4,3,2,1,0:T(8,128)} %copy-done.2, f32[8,2,36,16]{3,1,0,2:T(2,128)S(1)} %convert_element_type.187, pred[8,2,16,128]{3,2,1,0:T(8,128)(4,1)S(1)} %compare_and_fusion), kind=kOutput, calls=%fused_computation.15 | convolution fusion | flops 157483008 | bytes 6557696 | tf_op jit(solution)/shard_map/ejhtk,khd->ejthd/dot_general | solution.py:109
  71.5 3.1 %copy.80 = bf16[8,2,16,36,64]{4,3,2,1,0:T(8,128)(2,1)} copy(bf16[8,2,16,36,64]{4,2,1,0,3:T(8,128)(2,1)S(1)} %convert_bitcast_fusion) | data formatting | bytes 2359296 | tf_op jit(solution)/shard_map/convert_element_type | solution.py:114
  74.5 4.3 %convert_element_type.117 = bf16[8,2,16,2304]{3,2,1,0:T(8,128)(2,1)} reshape(bf16[8,2,16,36,64]{4,3,2,1,0:T(8,128)(2,1)} %copy.80) | data formatting | bytes 2359296 | tf_op jit(solution)/shard_map/convert_element_type | solution.py:114
  78.8 0.2 copy.81
  79.1 2.4 concatenate.7
  81.4 1.3 reshape.204
  82.7 9.0 %all-to-all-start.1 = ((bf16[128,2,2376]{2,1,0:T(2,128)(2,1)}), bf16[128,2,2376]{2,1,0:T(2,128)(2,1)S(1)}, u32[]{:S(2)}, u32[]{:S(2)}) async-start(bf16[128,2,2376]{2,1,0:T(2,128)(2,1)} %reshape.204), calls=%async_computation.1 | async-start | bytes 2490368 | tf_op jit(solution)/shard_map/all_to_all | solution.py:123
  91.8 0.6 fusion.36
  93.1 33.4 %all-to-all-done.1 = bf16[128,2,2376]{2,1,0:T(2,128)(2,1)S(1)} async-done(((bf16[128,2,2376]{2,1,0:T(2,128)(2,1)}), bf16[128,2,2376]{2,1,0:T(2,128)(2,1)S(1)}, u32[]{:S(2)}, u32[]{:S(2)}) %all-to-all-start.1) | async-done | bytes 1216544 | tf_op jit(solution)/shard_map/all_to_all | solution.py:123
  126.5 0.9 convert_element_type.120
  127.5 1.3 copy-done.1
  128.8 0.2 fusion.19
  129.1 1.6 mul.124
  130.8 5.0 %copy.84 = f32[128,2,2304]{2,1,0:T(2,128)} copy(f32[128,2,2304]{0,2,1:T(8,128)} %bitcast.82) | data formatting | bytes 4718592 | tf_op jit(solution)/shard_map/mul | solution.py:130
  135.8 3.8 %fusion.4 = f32[2,2304]{1,0:T(2,128)S(1)} fusion(f32[128,2,2304]{2,1,0:T(2,128)} %copy.84, f32[128,2,2376]{2,1,0:T(2,128)} %copy-done.1), kind=kLoop, calls=%fused_computation.12 | loop fusion | flops 1175040 | bytes 4737024 | tf_op jit(solution)/shard_map/reduce_sum | solution.py:130
  139.8 17.3 %all-gather = bf16[16,2,2304]{2,1,0:T(2,128)(2,1)S(1)} all-gather(bf16[1,2,2304]{2,1,0:T(2,128)(2,1)S(1)} %fusion.29), channel_id=1, replica_groups=mesh['req'=4,'exp'=8,'shard'=16] {'shard'}, dimensions={0}, use_global_device_ids=true | all-gather | bytes 156672 | tf_op jit(solution)/shard_map/all_gather | solution.py:134
  157.1 0.3 convolution_convert_fusion.2
  157.6 18.0 %all_gather.18 = bf16[2,16,2304]{1,0,2:T(2,128)(2,1)S(1)} all-gather(bf16[2,16,144]{1,0,2:T(2,128)(2,1)S(1)} %copy.85), channel_id=1, replica_groups=mesh['req'=4,'exp'=8,'shard'=16] {'shard'}, dimensions={2}, use_global_device_ids=true | all-gather | bytes 156672 | tf_op jit(solution)/shard_map/all_gather | solution.py:140
  175.5 1.4 copy.86
  177.1 0.3 fusion.3
  177.4 0.3 copy.90
  177.8 18.6 %all_to_all.20 = bf16[8,2,6,2304]{3,1,2,0:T(2,128)(2,1)S(1)} all-to-all(bf16[8,2,6,2304]{3,1,2,0:T(2,128)(2,1)S(1)} %copy.90), channel_id=1, replica_groups=mesh['req'=4,'exp'=8,'shard'=16] {'exp'}, dimensions={0} | all-to-all | bytes 884736 | tf_op jit(solution)/shard_map/all_to_all | solution.py:165
  196.6 0.6 fusion.7
  197.4 1.4 convolution_convert_fusion.1
  198.8 1.4 reshape.207
  200.2 1.7 copy.95
  201.9 6.3 %all-to-all-start.3 = ((bf16[128,2,6,144]{3,1,2,0:T(2,128)(2,1)}), bf16[128,2,6,144]{3,1,2,0:T(2,128)(2,1)S(1)}, u32[]{:S(2)}, u32[]{:S(2)}) async-start(bf16[128,2,6,144]{3,1,2,0:T(2,128)(2,1)} %bitcast.23), calls=%async_computation.3 | async-start | bytes 1572864 | tf_op jit(solution)/shard_map/all_to_all | solution.py:176
  208.4 25.8 %all-to-all-done.3 = bf16[128,2,6,144]{3,1,2,0:T(2,128)(2,1)S(1)} async-done(((bf16[128,2,6,144]{3,1,2,0:T(2,128)(2,1)}), bf16[128,2,6,144]{3,1,2,0:T(2,128)(2,1)S(1)}, u32[]{:S(2)}, u32[]{:S(2)}) %all-to-all-start.3) | async-done | bytes 442400 | tf_op jit(solution)/shard_map/all_to_all | solution.py:176
  234.1 0.8 bitcast_reduce_fusion.1
  235.2 19.1 %all_gather.19 = bf16[2,16,2304]{1,0,2:T(2,128)(2,1)S(1)} all-gather(bf16[2,16,144]{1,0,2:T(2,128)(2,1)S(1)} %copy.98), channel_id=1, replica_groups=mesh['req'=4,'exp'=8,'shard'=16] {'shard'}, dimensions={2}, use_global_device_ids=true | all-gather | bytes 156672 | tf_op jit(solution)/shard_map/all_gather | solution.py:193
  254.3 2.2 copy.99
  (81 shorter events, 3.8 us)
Async XLA Ops:
  0.0 196.6 %copy-start = (bf16[1,2,180,2304]{3,1,2,0:T(2,128)(2,1)S(1)}, bf16[1,2,180,2304]{3,1,2,0:T(2,128)(2,1)}, u32[]{:S(2)}) copy-start(bf16[1,2,180,2304]{3,1,2,0:T(2,128)(2,1)} %param.24) | copy-start | bytes 4976644
  0.9 24.7 %copy-start.12 = (s32[2,16,2]{1,2,0:T(2,128)S(1)}, s32[2,16,2]{1,2,0:T(2,128)}, u32[]{:S(2)}) copy-start(s32[2,16,2]{1,2,0:T(2,128)} %param.15) | copy-start | bytes 772
  0.9 24.8 %copy-start.13 = (bf16[2,16,2]{1,2,0:T(2,128)(2,1)S(1)}, bf16[2,16,2]{1,2,0:T(2,128)(2,1)}, u32[]{:S(2)}) copy-start(bf16[2,16,2]{1,2,0:T(2,128)(2,1)} %param.16) | copy-start | bytes 388
  0.9 24.9 %copy-start.5 = (bf16[2,16,2304]{2,1,0:T(8,128)(2,1)S(1)}, bf16[2,16,2304]{2,1,0:T(8,128)(2,1)}, u32[]{:S(2)}) copy-start(bf16[2,16,2304]{2,1,0:T(8,128)(2,1)} %param.14) | copy-start | bytes 442372
  13.1 25.2 %copy-start.15 = (s32[1,2]{1,0:T(1,128)S(1)}, s32[1,2]{1,0:T(1,128)}, u32[]{:S(2)}) copy-start(s32[1,2]{1,0:T(1,128)} %param.18) | copy-start | bytes 28
  13.1 25.4 %copy-start.14 = (s32[1,256]{1,0:T(1,128)S(1)}, s32[1,256]{1,0:T(1,128)}, u32[]{:S(2)}) copy-start(s32[1,256]{1,0:T(1,128)} %param.19) | copy-start | bytes 3076
  14.2 43.3 %all-to-all-start = ((bf16[8,2,16,2304]{3,2,1,0:T(8,128)(2,1)}), bf16[8,2,16,2304]{3,2,1,0:T(8,128)(2,1)S(1)}, u32[]{:S(2)}, u32[]{:S(2)}) async-start(bf16[8,2,16,2304]{3,2,1,0:T(8,128)(2,1)} %broadcast_in_dim.107), calls=%async_computation | async-start | bytes 2359296 | tf_op jit(solution)/shard_map/all_to_all | solution.py:61
  38.3 7.0 %copy-start.4 = (bf16[2,16,2308]{2,1,0:T(8,128)(2,1)S(1)}, bf16[2,16,2308]{2,1,0:T(8,128)(2,1)}, u32[]{:S(2)}) copy-start(bf16[2,16,2308]{2,1,0:T(8,128)(2,1)} %gather_fusion.1) | copy-start | bytes 443140
  64.3 3.2 %copy-start.2 = (f32[36,8,2,16,128]{4,3,2,1,0:T(8,128)}, f32[36,8,2,16,128]{4,3,2,1,0:T(8,128)S(1)}, u32[]{:S(2)}) copy-start(f32[36,8,2,16,128]{4,3,2,1,0:T(8,128)S(1)} %get-tuple-element.20) | copy-start | bytes 14155780
  82.7 43.8 %all-to-all-start.1 = ((bf16[128,2,2376]{2,1,0:T(2,128)(2,1)}), bf16[128,2,2376]{2,1,0:T(2,128)(2,1)S(1)}, u32[]{:S(2)}, u32[]{:S(2)}) async-start(bf16[128,2,2376]{2,1,0:T(2,128)(2,1)} %reshape.204), calls=%async_computation.1 | async-start | bytes 2490368 | tf_op jit(solution)/shard_map/all_to_all | solution.py:123
  93.1 36.0 %copy-start.6 = (s32[2,16,2,6]{1,3,2,0:T(8,128)}, s32[2,16,2,6]{1,3,2,0:T(8,128)S(1)}, u32[]{:S(2)}) copy-start(s32[2,16,2,6]{1,3,2,0:T(8,128)S(1)} %fusion.28) | copy-start | bytes 4612
  93.1 36.0 %copy-start.8 = (s32[2,16,2,8]{1,3,2,0:T(8,128)}, s32[2,16,2,8]{1,3,2,0:T(8,128)S(1)}, u32[]{:S(2)}) copy-start(s32[2,16,2,8]{1,3,2,0:T(8,128)S(1)} %fusion.27) | copy-start | bytes 6148
  127.4 1.4 copy-start.1
  135.8 21.3 %copy-start.3 = (bf16[144,2304]{1,0:T(8,128)(2,1)S(1)}, bf16[144,2304]{1,0:T(8,128)(2,1)}, u32[]{:S(2)}) copy-start(bf16[144,2304]{1,0:T(8,128)(2,1)} %param.23) | copy-start | bytes 1990660
  139.6 37.5 %copy-start.11 = (f32[2304]{0:T(1024)S(1)}, f32[2304]{0:T(1024)}, u32[]{:S(2)}) copy-start(f32[2304]{0:T(1024)} %param.22) | copy-start | bytes 27652
  198.8 9.4 %copy-start.10 = (bf16[2,16,2]{2,1,0:T(8,128)(2,1)S(1)}, bf16[2,16,2]{2,1,0:T(8,128)(2,1)}, u32[]{:S(2)}) copy-start(bf16[2,16,2]{2,1,0:T(8,128)(2,1)} %get-tuple-element.15) | copy-start | bytes 388
  198.8 9.5 %copy-start.7 = (s32[2,16,2,6]{1,3,2,0:T(8,128)S(1)}, s32[2,16,2,6]{1,3,2,0:T(8,128)}, u32[]{:S(2)}) copy-start(s32[2,16,2,6]{1,3,2,0:T(8,128)} %copy-done.6) | copy-start | bytes 4612
  198.8 9.5 %copy-start.9 = (s32[2,16,2,8]{1,3,2,0:T(8,128)S(1)}, s32[2,16,2,8]{1,3,2,0:T(8,128)}, u32[]{:S(2)}) copy-start(s32[2,16,2,8]{1,3,2,0:T(8,128)} %copy-done.8) | copy-start | bytes 6148
  201.9 32.3 %all-to-all-start.3 = ((bf16[128,2,6,144]{3,1,2,0:T(2,128)(2,1)}), bf16[128,2,6,144]{3,1,2,0:T(2,128)(2,1)S(1)}, u32[]{:S(2)}, u32[]{:S(2)}) async-start(bf16[128,2,6,144]{3,1,2,0:T(2,128)(2,1)} %bitcast.23), calls=%async_computation.3 | async-start | bytes 1572864 | tf_op jit(solution)/shard_map/all_to_all | solution.py:176

commit v6 on v5

--- a/solution.py
+++ b/solution.py
@@ -21,6 +21,11 @@
     active = (jax.nn.silu(both[:, 0]) * both[:, 1]).astype(jnp.bfloat16)
     partial_out = jnp.dot(active, down_proj[0], preferred_element_type=jnp.float32)
     return partial_out.reshape(received.shape)
+
+
+def gather_blocks(block, axis_name, count):
+    spread = jnp.broadcast_to(block[None], (count,) + block.shape)
+    return lax.all_to_all(spread, axis_name, 0, 0, tiled=False)
 
 
 def on_device(
@@ -131,13 +136,15 @@
     row_attended = (
         (row_context / row_totals[..., None]).reshape(rows_each, width).astype(jnp.bfloat16)
     )
-    attended = lax.all_gather(row_attended, "shard", axis=0, tiled=True).reshape(
+    attended = gather_blocks(row_attended, "shard", shard_count).reshape(
         members, tokens_here, width
     )
     projected_part = lax.dot_general(
         attended, out_proj, (((2,), (1,)), ((), ())), preferred_element_type=jnp.float32
     ).astype(jnp.bfloat16)
-    projected = lax.all_gather(projected_part, "shard", axis=2, tiled=True)
+    projected = jnp.transpose(
+        gather_blocks(projected_part, "shard", shard_count), (1, 2, 0, 3)
+    ).reshape(members, tokens_here, width)
     hidden_state = served_resid.astype(jnp.float32) + projected.astype(jnp.float32)
     mean_square = jnp.mean(hidden_state * hidden_state, axis=2, keepdims=True)
     normed = (hidden_state * lax.rsqrt(mean_square + EPSILON) * norm_gain).astype(jnp.bfloat16)
@@ -190,7 +197,9 @@
         hidden_state, shard_index * feature_block, feature_block, 2
     )
     mixed_block = (hidden_block + moe_term).astype(jnp.bfloat16)
-    mixed_out = lax.all_gather(mixed_block, "shard", axis=2, tiled=True)
+    mixed_out = jnp.transpose(
+        gather_blocks(mixed_block, "shard", shard_count), (1, 2, 0, 3)
+    ).reshape(members, tokens_here, width)
     return mixed_out
 
 

time: 257 us -> 248 us (0.965)
  blocking collectives: 95 us -> 56.2 us
  waiting for transfers between devices: 71.2 us -> 92.6 us
  starting transfers between devices: 26.7 us -> 34.1 us
    all_gather x3 -> x0, blocking collectives: 54.3 us -> none  [the longest x1 19.1 us: on_device(): mixed_out = lax.all_gather(mixed_block, 'shard', axis=2, tiled=True)]
    all_to_all x0 -> x2, waiting for transfers between devices: none -> 20.3 us  [gather_blocks(): return lax.all_to_all(spread, axis_name, 0, 0, tiled=False)]
    all_to_all x0 -> x1, blocking collectives: none -> 15.4 us  [gather_blocks(): return lax.all_to_all(spread, axis_name, 0, 0, tiled=False)]
    all_to_all x0 -> x2, starting transfers between devices: none -> 8.19 us  [gather_blocks(): return lax.all_to_all(spread, axis_name, 0, 0, tiled=False)]
    all_gather x2 -> x0, local copies, waits for them, and re-layouts: 3.59 us -> none  [the longest x1 2.21 us: on_device(): mixed_out = lax.all_gather(mixed_block, 'shard', axis=2, tiled=True)]
  transfers between devices with their start and end apart: 3 -> 5, of which waited for: 3 -> 5; matrix products, arithmetic and copies ran while one was open for 4% -> 4% of each run, Pallas kernels for 0% -> 0%
where the time goes in v6:
time: 248 us; the launch traced here: 247 us
  waiting for transfers between devices  92.6 us (37%)
  blocking collectives  56.2 us (23%)
  local copies, waits for them, and re-layouts  40.9 us (16%)
  starting transfers between devices  34.1 us (14%)
  other arithmetic  12.4 us (5%)
  matrix products  9.97 us (4%)
    all_to_all x1, waiting for transfers between devices, on_device(): lax.all_to_all(packed, ('exp', 'shard'), 0, 0, tiled=True)  34.4 us
    all_to_all x1, waiting for transfers between devices, on_device(): lax.all_to_all(partial_out, ('exp', 'shard'), 0, 0, tiled=True)  25.9 us
    all_to_all x2, waiting for transfers between devices, gather_blocks(): return lax.all_to_all(spread, axis_name, 0, 0, tiled=False)  20.3 us
    all_to_all x1, blocking collectives, on_device(): lax.all_to_all(sent_rows, 'exp', split_axis=0, concat_axis=0, tiled=True)  18.6 us
    all_to_all x1, blocking collectives, gather_blocks(): return lax.all_to_all(spread, axis_name, 0, 0, tiled=False)  15.4 us
    all_to_all x1, waiting for transfers between devices, on_device(): group_query = lax.all_to_all(spread_query, 'exp', 0, 0, tiled=False)  12.1 us
    all_gather x1, blocking collectives, on_device(): all_query = lax.all_gather(query_stretch, 'req', axis=0, tiled=True)  11.6 us
    all_to_all x1, starting transfers between devices, on_device(): group_query = lax.all_to_all(spread_query, 'exp', 0, 0, tiled=False)  11.3 us
  transfers between devices with their start and end apart: 5, of which 5 were waited for; matrix products, arithmetic and copies ran while one was open for 4% of the time, Pallas kernels for 0%

profile of v6, /device:TPU:1, one launch (start us, length us, event | category | flops | bytes accessed | tf_op | source)
XLA Modules:
  0.0 246.6 jit_solution(1259864108926754285)
XLA Ops:
  0.0 0.9 compare_and_fusion.1
  0.9 11.6 %all_gather.6 = bf16[8,16,2304]{2,1,0:T(8,128)(2,1)S(1)} all-gather(bf16[2,16,2304]{2,1,0:T(8,128)(2,1)} %param.13), channel_id=1, replica_groups=mesh['req'=4,'exp'=8,'shard'=16] {'req'}, dimensions={0}, use_global_device_ids=true | all-gather | bytes 737280 | tf_op jit(solution)/shard_map/all_gather | solution.py:58
  12.5 0.6 gather_fusion
  13.1 1.1 broadcast_in_dim.125
  14.2 11.3 %all-to-all-start = ((bf16[8,2,16,2304]{3,2,1,0:T(8,128)(2,1)}), bf16[8,2,16,2304]{3,2,1,0:T(8,128)(2,1)S(1)}, u32[]{:S(2)}, u32[]{:S(2)}) async-start(bf16[8,2,16,2304]{3,2,1,0:T(8,128)(2,1)} %broadcast_in_dim.125), calls=%async_computation | async-start | bytes 2359296 | tf_op jit(solution)/shard_map/all_to_all | solution.py:66
  25.8 0.8 concatenate.6
  26.5 10.6 %all_gather.7 = bf16[8,16,2308]{2,1,0:T(8,128)(2,1)S(1)} all-gather(bf16[2,16,2308]{2,1,0:T(8,128)(2,1)} %concatenate.6), channel_id=1, replica_groups=mesh['req'=4,'exp'=8,'shard'=16] {'req'}, dimensions={0}, use_global_device_ids=true | all-gather | bytes 738560 | tf_op jit(solution)/shard_map/all_gather | solution.py:59
  37.1 1.2 gather_fusion.1
  39.4 2.8 %reshape.253 = bf16[128,36,64]{2,1,0:T(8,128)(2,1)} reshape(bf16[1,2,64,2304]{3,2,1,0:T(8,128)(2,1)} %param.20) | data formatting | bytes 1179648 | tf_op jit(solution)/shard_map/reshape;squeeze | solution.py:103
  42.2 2.8 %reshape.254 = bf16[128,36,64]{2,1,0:T(8,128)(2,1)} reshape(bf16[1,2,64,2304]{3,2,1,0:T(8,128)(2,1)} %param.21) | data formatting | bytes 1179648 | tf_op jit(solution)/shard_map/reshape;squeeze | solution.py:104
  45.5 12.1 %all-to-all-done = bf16[8,2,16,2304]{3,2,1,0:T(8,128)(2,1)S(1)} async-done(((bf16[8,2,16,2304]{3,2,1,0:T(8,128)(2,1)}), bf16[8,2,16,2304]{3,2,1,0:T(8,128)(2,1)S(1)}, u32[]{:S(2)}, u32[]{:S(2)}) %all-to-all-start) | async-done | bytes 1179680 | tf_op jit(solution)/shard_map/all_to_all | solution.py:66
  57.5 3.0 %reshape.219 = bf16[8,2,16,36,64]{4,3,2,1,0:T(8,128)(2,1)} reshape(bf16[8,2,16,2304]{3,2,1,0:T(8,128)(2,1)S(1)} %all-to-all-done) | data formatting | bytes 2359296 | tf_op jit(solution)/shard_map/reshape | solution.py:102
  60.5 3.8 %bitcast_reduce_fusion = (bf16[8,2,36,16]{3,1,0,2:T(2,128)(2,1)S(1)}, f32[36,8,2,16,128]{4,3,2,1,0:T(8,128)S(1)}) fusion(pred[8,2,16,128]{3,2,1,0:T(8,128)(4,1)S(1)} %compare_and_fusion, bf16[128,36,64,1,1]{2,1,0,4,3:T(8,128)(2,1)} %bitcast.90, bf16[8,2,16,36,64]{4,3,2,1,0:T(8,128)(2,1)} %reshape.219), kind=kOutput, calls=%fused_computation.3 | convolution fusion | flops 154524672 | bytes 6539264 | tf_op jit(solution)/shard_map/ejthd,khd->ejhtk/dot_general | solution.py:105
  64.4 3.7 %fusion.33 = bf16[8,2,36,16]{3,1,0,2:T(2,128)(2,1)} fusion(f32[8,2,36,16]{3,1,0,2:T(2,128)S(1)} %convert_element_type.189, f32[36,8,2,16,128]{4,3,2,1,0:T(8,128)S(1)} %get-tuple-element.20, pred[8,2,16,128]{3,2,1,0:T(8,128)(4,1)S(1)} %compare_and_fusion), kind=kLoop, calls=%fused_computation.82 | loop fusion | flops 7068672 | bytes 4806656 | tf_op jit(solution)/shard_map/reduce_sum | solution.py:113
  68.2 1.1 copy.94
  69.3 3.4 %convert_bitcast_fusion = bf16[8,2,16,36,64]{4,2,1,0,3:T(8,128)(2,1)S(1)} fusion(bf16[128,36,64,1,1]{2,1,0,4,3:T(8,128)(2,1)S(1)} %bitcast.89, f32[36,8,2,16,128]{4,3,2,1,0:T(8,128)} %copy-done.2, f32[8,2,36,16]{3,1,0,2:T(2,128)S(1)} %convert_element_type.189, pred[8,2,16,128]{3,2,1,0:T(8,128)(4,1)S(1)} %compare_and_fusion), kind=kOutput, calls=%fused_computation.15 | convolution fusion | flops 157483008 | bytes 6557696 | tf_op jit(solution)/shard_map/ejhtk,khd->ejthd/dot_general | solution.py:114
  72.7 3.1 %copy.92 = bf16[8,2,16,36,64]{4,3,2,1,0:T(8,128)(2,1)} copy(bf16[8,2,16,36,64]{4,2,1,0,3:T(8,128)(2,1)S(1)} %convert_bitcast_fusion) | data formatting | bytes 2359296 | tf_op jit(solution)/shard_map/convert_element_type | solution.py:119
  75.8 4.3 %convert_element_type.127 = bf16[8,2,16,2304]{3,2,1,0:T(8,128)(2,1)} reshape(bf16[8,2,16,36,64]{4,3,2,1,0:T(8,128)(2,1)} %copy.92) | data formatting | bytes 2359296 | tf_op jit(solution)/shard_map/convert_element_type | solution.py:119
  80.3 2.4 concatenate.7
  82.7 1.3 reshape.220
  84.0 9.0 %all-to-all-start.1 = ((bf16[128,2,2376]{2,1,0:T(2,128)(2,1)}), bf16[128,2,2376]{2,1,0:T(2,128)(2,1)S(1)}, u32[]{:S(2)}, u32[]{:S(2)}) async-start(bf16[128,2,2376]{2,1,0:T(2,128)(2,1)} %reshape.220), calls=%async_computation.1 | async-start | bytes 2490368 | tf_op jit(solution)/shard_map/all_to_all | solution.py:128
  93.4 34.4 %all-to-all-done.1 = bf16[128,2,2376]{2,1,0:T(2,128)(2,1)S(1)} async-done(((bf16[128,2,2376]{2,1,0:T(2,128)(2,1)}), bf16[128,2,2376]{2,1,0:T(2,128)(2,1)S(1)}, u32[]{:S(2)}, u32[]{:S(2)}) %all-to-all-start.1) | async-done | bytes 1216544 | tf_op jit(solution)/shard_map/all_to_all | solution.py:128
  127.8 0.9 convert_element_type.130
  128.8 1.3 copy-done.1
  130.4 1.6 mul.124
  132.0 5.0 %copy.96 = f32[128,2,2304]{2,1,0:T(2,128)} copy(f32[128,2,2304]{0,2,1:T(8,128)} %bitcast.87) | data formatting | bytes 4718592 | tf_op jit(solution)/shard_map/mul | solution.py:135
  137.0 3.8 %fusion.4 = f32[2,2304]{1,0:T(2,128)S(1)} fusion(f32[128,2,2304]{2,1,0:T(2,128)} %copy.96, f32[128,2,2376]{2,1,0:T(2,128)} %copy-done.1), kind=kLoop, calls=%fused_computation.12 | loop fusion | flops 1175040 | bytes 4737024 | tf_op jit(solution)/shard_map/reduce_sum | solution.py:135
  141.0 0.7 broadcast_in_dim.138
  141.7 4.8 %all-to-all-start.2 = ((bf16[16,2,2304]{2,1,0:T(2,128)(2,1)}), bf16[16,2,2304]{2,1,0:T(2,128)(2,1)S(1)}, u32[]{:S(2)}, u32[]{:S(2)}) async-start(bf16[16,2,2304]{2,1,0:T(2,128)(2,1)} %broadcast_in_dim.138), calls=%async_computation.2 | async-start | bytes 294912 | tf_op jit(solution)/shard_map/all_to_all | solution.py:28
  146.9 8.9 %all-to-all-done.2 = bf16[16,2,2304]{2,1,0:T(2,128)(2,1)S(1)} async-done(((bf16[16,2,2304]{2,1,0:T(2,128)(2,1)}), bf16[16,2,2304]{2,1,0:T(2,128)(2,1)S(1)}, u32[]{:S(2)}, u32[]{:S(2)}) %all-to-all-start.2) | async-done | bytes 147488 | tf_op jit(solution)/shard_map/all_to_all | solution.py:28
  155.9 0.3 convolution_convert_fusion.2
  156.2 0.8 broadcast_in_dim.139
  157.0 3.4 %all-to-all-start.3 = ((bf16[16,2,16,144]{3,2,1,0:T(8,128)(2,1)}), bf16[16,2,16,144]{3,2,1,0:T(8,128)(2,1)S(1)}, u32[]{:S(2)}, u32[]{:S(2)}) async-start(bf16[16,2,16,144]{3,2,1,0:T(8,128)(2,1)} %broadcast_in_dim.139), calls=%async_computation.3 | async-start | bytes 524288 | tf_op jit(solution)/shard_map/all_to_all | solution.py:28
  160.4 11.4 %all-to-all-done.3 = bf16[16,2,16,144]{3,2,1,0:T(8,128)(2,1)S(1)} async-done(((bf16[16,2,16,144]{3,2,1,0:T(8,128)(2,1)}), bf16[16,2,16,144]{3,2,1,0:T(8,128)(2,1)S(1)}, u32[]{:S(2)}, u32[]{:S(2)}) %all-to-all-start.3) | async-done | bytes 147488 | tf_op jit(solution)/shard_map/all_to_all | solution.py:28
  171.9 0.3 copy.97
  172.2 0.3 reshape.227
  172.6 0.3 fusion.3
  172.9 0.3 copy.101
  173.3 18.6 %all_to_all.35 = bf16[8,2,6,2304]{3,1,2,0:T(2,128)(2,1)S(1)} all-to-all(bf16[8,2,6,2304]{3,1,2,0:T(2,128)(2,1)S(1)} %copy.101), channel_id=1, replica_groups=mesh['req'=4,'exp'=8,'shard'=16] {'exp'}, dimensions={0} | all-to-all | bytes 884736 | tf_op jit(solution)/shard_map/all_to_all | solution.py:172
  192.2 0.6 fusion.7
  192.9 1.4 convolution_convert_fusion.1
  194.4 1.4 reshape.223
  195.8 1.7 copy.106
  197.4 5.6 %all-to-all-start.5 = ((bf16[128,2,6,144]{3,1,2,0:T(2,128)(2,1)}), bf16[128,2,6,144]{3,1,2,0:T(2,128)(2,1)S(1)}, u32[]{:S(2)}, u32[]{:S(2)}) async-start(bf16[128,2,6,144]{3,1,2,0:T(2,128)(2,1)} %bitcast.23), calls=%async_computation.5 | async-start | bytes 1572864 | tf_op jit(solution)/shard_map/all_to_all | solution.py:183
  203.2 25.9 %all-to-all-done.5 = bf16[128,2,6,144]{3,1,2,0:T(2,128)(2,1)S(1)} async-done(((bf16[128,2,6,144]{3,1,2,0:T(2,128)(2,1)}), bf16[128,2,6,144]{3,1,2,0:T(2,128)(2,1)S(1)}, u32[]{:S(2)}, u32[]{:S(2)}) %all-to-all-start.5) | async-done | bytes 442400 | tf_op jit(solution)/shard_map/all_to_all | solution.py:183
  229.1 0.8 bitcast_reduce_fusion.1
  230.1 15.4 %all_to_all.36 = bf16[16,2,16,144]{3,2,1,0:T(8,128)(2,1)S(1)} all-to-all(bf16[16,2,16,144]{3,2,1,0:T(8,128)(2,1)S(1)} %broadcast_in_dim.140), channel_id=1, replica_groups=mesh['req'=4,'exp'=8,'shard'=16] {'shard'}, dimensions={0} | all-to-all | bytes 294912 | tf_op jit(solution)/shard_map/all_to_all | solution.py:28
  245.6 1.0 reshape.226
  (83 shorter events, 4.6 us)
Async XLA Ops:
  0.0 192.2 %copy-start = (bf16[1,2,180,2304]{3,1,2,0:T(2,128)(2,1)S(1)}, bf16[1,2,180,2304]{3,1,2,0:T(2,128)(2,1)}, u32[]{:S(2)}) copy-start(bf16[1,2,180,2304]{3,1,2,0:T(2,128)(2,1)} %param.24) | copy-start | bytes 4976644
  0.9 24.7 %copy-start.10 = (s32[2,16,2]{1,2,0:T(2,128)S(1)}, s32[2,16,2]{1,2,0:T(2,128)}, u32[]{:S(2)}) copy-start(s32[2,16,2]{1,2,0:T(2,128)} %param.15) | copy-start | bytes 772
  0.9 24.8 %copy-start.11 = (bf16[2,16,2]{1,2,0:T(2,128)(2,1)S(1)}, bf16[2,16,2]{1,2,0:T(2,128)(2,1)}, u32[]{:S(2)}) copy-start(bf16[2,16,2]{1,2,0:T(2,128)(2,1)} %param.16) | copy-start | bytes 388
  0.9 24.9 %copy-start.8 = (bf16[2,16,2304]{2,1,0:T(8,128)(2,1)S(1)}, bf16[2,16,2304]{2,1,0:T(8,128)(2,1)}, u32[]{:S(2)}) copy-start(bf16[2,16,2304]{2,1,0:T(8,128)(2,1)} %param.14) | copy-start | bytes 442372
  13.1 25.2 %copy-start.13 = (s32[1,2]{1,0:T(1,128)S(1)}, s32[1,2]{1,0:T(1,128)}, u32[]{:S(2)}) copy-start(s32[1,2]{1,0:T(1,128)} %param.18) | copy-start | bytes 28
  13.1 25.4 %copy-start.12 = (s32[1,256]{1,0:T(1,128)S(1)}, s32[1,256]{1,0:T(1,128)}, u32[]{:S(2)}) copy-start(s32[1,256]{1,0:T(1,128)} %param.19) | copy-start | bytes 3076
  14.2 43.3 %all-to-all-start = ((bf16[8,2,16,2304]{3,2,1,0:T(8,128)(2,1)}), bf16[8,2,16,2304]{3,2,1,0:T(8,128)(2,1)S(1)}, u32[]{:S(2)}, u32[]{:S(2)}) async-start(bf16[8,2,16,2304]{3,2,1,0:T(8,128)(2,1)} %broadcast_in_dim.125), calls=%async_computation | async-start | bytes 2359296 | tf_op jit(solution)/shard_map/all_to_all | solution.py:66
  38.3 7.0 %copy-start.5 = (bf16[2,16,2308]{2,1,0:T(8,128)(2,1)S(1)}, bf16[2,16,2308]{2,1,0:T(8,128)(2,1)}, u32[]{:S(2)}) copy-start(bf16[2,16,2308]{2,1,0:T(8,128)(2,1)} %gather_fusion.1) | copy-start | bytes 443140
  64.3 3.9 %copy-start.2 = (f32[36,8,2,16,128]{4,3,2,1,0:T(8,128)}, f32[36,8,2,16,128]{4,3,2,1,0:T(8,128)S(1)}, u32[]{:S(2)}) copy-start(f32[36,8,2,16,128]{4,3,2,1,0:T(8,128)S(1)} %get-tuple-element.20) | copy-start | bytes 14155780
  64.3 3.9 %copy-start.6 = (bf16[8,2,36,16]{3,1,0,2:T(2,128)(2,1)}, bf16[8,2,36,16]{3,1,0,2:T(2,128)(2,1)S(1)}, u32[]{:S(2)}) copy-start(bf16[8,2,36,16]{3,1,0,2:T(2,128)(2,1)S(1)} %get-tuple-element.19) | copy-start | bytes 55300
  64.4 4.9 %copy-start.3 = (bf16[128,36,64]{2,1,0:T(8,128)(2,1)S(1)}, bf16[128,36,64]{2,1,0:T(8,128)(2,1)}, u32[]{:S(2)}) copy-start(bf16[128,36,64]{2,1,0:T(8,128)(2,1)} %reshape.254) | copy-start | bytes 1769476
  75.8 4.3 %copy-start.7 = (bf16[8,2,36,16]{3,1,0,2:T(2,128)(2,1)S(1)}, bf16[8,2,36,16]{3,1,0,2:T(2,128)(2,1)}, u32[]{:S(2)}) copy-start(bf16[8,2,36,16]{3,1,0,2:T(2,128)(2,1)} %copy-done.6) | copy-start | bytes 55300
  84.0 43.8 %all-to-all-start.1 = ((bf16[128,2,2376]{2,1,0:T(2,128)(2,1)}), bf16[128,2,2376]{2,1,0:T(2,128)(2,1)S(1)}, u32[]{:S(2)}, u32[]{:S(2)}) async-start(bf16[128,2,2376]{2,1,0:T(2,128)(2,1)} %reshape.220), calls=%async_computation.1 | async-start | bytes 2490368 | tf_op jit(solution)/shard_map/all_to_all | solution.py:128
  128.6 1.4 copy-start.1
  137.0 18.9 %copy-start.4 = (bf16[144,2304]{1,0:T(8,128)(2,1)S(1)}, bf16[144,2304]{1,0:T(8,128)(2,1)}, u32[]{:S(2)}) copy-start(bf16[144,2304]{1,0:T(8,128)(2,1)} %param.23) | copy-start | bytes 1990660
  141.7 14.1 %all-to-all-start.2 = ((bf16[16,2,2304]{2,1,0:T(2,128)(2,1)}), bf16[16,2,2304]{2,1,0:T(2,128)(2,1)S(1)}, u32[]{:S(2)}, u32[]{:S(2)}) async-start(bf16[16,2,2304]{2,1,0:T(2,128)(2,1)} %broadcast_in_dim.138), calls=%async_computation.2 | async-start | bytes 294912 | tf_op jit(solution)/shard_map/all_to_all | solution.py:28
  155.9 16.7 %copy-start.9 = (f32[2304]{0:T(1024)S(1)}, f32[2304]{0:T(1024)}, u32[]{:S(2)}) copy-start(f32[2304]{0:T(1024)} %param.22) | copy-start | bytes 27652
  157.0 14.9 %all-to-all-start.3 = ((bf16[16,2,16,144]{3,2,1,0:T(8,128)(2,1)}), bf16[16,2,16,144]{3,2,1,0:T(8,128)(2,1)S(1)}, u32[]{:S(2)}, u32[]{:S(2)}) async-start(bf16[16,2,16,144]{3,2,1,0:T(8,128)(2,1)} %broadcast_in_dim.139), calls=%async_computation.3 | async-start | bytes 524288 | tf_op jit(solution)/shard_map/all_to_all | solution.py:28
  197.4 31.7 %all-to-all-start.5 = ((bf16[128,2,6,144]{3,1,2,0:T(2,128)(2,1)}), bf16[128,2,6,144]{3,1,2,0:T(2,128)(2,1)S(1)}, u32[]{:S(2)}, u32[]{:S(2)}) async-start(bf16[128,2,6,144]{3,1,2,0:T(2,128)(2,1)} %bitcast.23), calls=%async_computation.5 | async-start | bytes 1572864 | tf_op jit(solution)/shard_map/all_to_all | solution.py:183

commit v7 on v6

--- a/solution.py
+++ b/solution.py
@@ -60,10 +60,17 @@
     served = lax.dynamic_slice_in_dim(request_order, group_index * members, members)
     served_query = jnp.take(all_query, served, axis=0)
     served_extras = jnp.take(all_extras, served, axis=0)
-    spread_query = jnp.broadcast_to(
-        served_query[None], (experts_count,) + served_query.shape
-    )
-    group_query = lax.all_to_all(spread_query, "exp", 0, 0, tiled=False)
+    core_index = shard_index % 2
+    own_member = lax.dynamic_slice_in_dim(served_query, core_index, 1, 0)
+    own_query = gather_blocks(own_member, "exp", experts_count)
+    partner_query = lax.ppermute(
+        own_query, "shard", [(i, i ^ 1) for i in range(shard_count)]
+    )
+    group_query = jnp.where(
+        core_index == 0,
+        jnp.concatenate([own_query, partner_query], axis=1),
+        jnp.concatenate([partner_query, own_query], axis=1),
+    )
     group_query, served_extras = lax.optimization_barrier((group_query, served_extras))
     top_count = route_ids.shape[2]
     served_resid = served_extras[:, :, :width]

time: 248 us -> 247 us (level)
  starting transfers between devices: 34.1 us -> 46.7 us
  waiting for transfers between devices: 92.6 us -> 81.4 us
    all_to_all x1 -> x0, waiting for transfers between devices: 12.1 us -> none  [on_device(): group_query = lax.all_to_all(spread_query, 'exp', 0, 0, tiled=False)]
    all_to_all x2 -> x3, starting transfers between devices: 8.19 us -> 19.5 us  [gather_blocks(): return lax.all_to_all(spread, axis_name, 0, 0, tiled=False)]
    all_to_all x1 -> x0, starting transfers between devices: 11.3 us -> none  [on_device(): group_query = lax.all_to_all(spread_query, 'exp', 0, 0, tiled=False)]
    ppermute x0 -> x1, starting transfers between devices: none -> 7.45 us  [on_device(): lax.ppermute(own_query, 'shard', [(i, i ^ 1) for i in range(shard_count)])]
    all_to_all x1, starting transfers between devices: 9.03 us -> 14.2 us  [on_device(): lax.all_to_all(packed, ('exp', 'shard'), 0, 0, tiled=True)]
    all_to_all x2 -> x3, waiting for transfers between devices: 20.3 us -> 20.3 us  [gather_blocks(): return lax.all_to_all(spread, axis_name, 0, 0, tiled=False)]
  transfers between devices with their start and end apart: 5 -> 6, of which waited for: 5 -> 5; matrix products, arithmetic and copies ran while one was open for 4% -> 4% of each run, Pallas kernels for 0% -> 0%
where the time goes in v7:
time: 247 us
  waiting for transfers between devices  81.4 us (33%)
  blocking collectives  55.8 us (23%)
  starting transfers between devices  46.7 us (19%)
  local copies, waits for them, and re-layouts  39 us (16%)
  other arithmetic  13.1 us (5%)
  matrix products  9.97 us (4%)
    all_to_all x1, waiting for transfers between devices, on_device(): lax.all_to_all(packed, ('exp', 'shard'), 0, 0, tiled=True)  34.4 us
    all_to_all x1, waiting for transfers between devices, on_device(): lax.all_to_all(partial_out, ('exp', 'shard'), 0, 0, tiled=True)  25.9 us
    all_to_all x3, waiting for transfers between devices, gather_blocks(): return lax.all_to_all(spread, axis_name, 0, 0, tiled=False)  20.3 us
    all_to_all x3, starting transfers between devices, gather_blocks(): return lax.all_to_all(spread, axis_name, 0, 0, tiled=False)  19.5 us
    all_to_all x1, blocking collectives, on_device(): lax.all_to_all(sent_rows, 'exp', split_axis=0, concat_axis=0, tiled=True)  18.6 us
    all_to_all x1, blocking collectives, gather_blocks(): return lax.all_to_all(spread, axis_name, 0, 0, tiled=False)  15.4 us
    all_to_all x1, starting transfers between devices, on_device(): lax.all_to_all(packed, ('exp', 'shard'), 0, 0, tiled=True)  14.2 us
    all_gather x1, blocking collectives, on_device(): all_query = lax.all_gather(query_stretch, 'req', axis=0, tiled=True)  11.4 us
  transfers between devices with their start and end apart: 6, of which 5 were waited for; matrix products, arithmetic and copies ran while one was open for 4% of the time, Pallas kernels for 0%

profile of v7, /device:TPU:1, one launch (start us, length us, event | category | flops | bytes accessed | tf_op | source)
XLA Modules:
  0.0 246.5 jit_solution(12159875392871849627)
XLA Ops:
  0.1 0.9 compare_and_fusion.1
  0.9 11.4 %all_gather.6 = bf16[8,16,2304]{2,1,0:T(8,128)(2,1)S(1)} all-gather(bf16[2,16,2304]{2,1,0:T(8,128)(2,1)} %param.13), channel_id=1, replica_groups=mesh['req'=4,'exp'=8,'shard'=16] {'req'}, dimensions={0}, use_global_device_ids=true | all-gather | bytes 737280 | tf_op jit(solution)/shard_map/all_gather | solution.py:58
  12.3 0.6 dynamic-slice
  12.9 0.6 gather_fusion
  13.5 0.7 fusion.21
  14.2 0.9 broadcast_in_dim.128
  15.0 11.3 %all-to-all-start = ((bf16[8,1,16,2304]{3,2,1,0:T(8,128)(2,1)}), bf16[8,1,16,2304]{3,2,1,0:T(8,128)(2,1)S(1)}, u32[]{:S(2)}, u32[]{:S(2)}) async-start(bf16[8,1,16,2304]{3,2,1,0:T(8,128)(2,1)} %broadcast_in_dim.128), calls=%async_computation | async-start | bytes 1179648 | tf_op jit(solution)/shard_map/all_to_all | solution.py:28
  27.5 10.4 %all_gather.7 = bf16[8,16,2308]{2,1,0:T(8,128)(2,1)S(1)} all-gather(bf16[2,16,2308]{2,1,0:T(8,128)(2,1)S(1)} %concatenate.14), channel_id=1, replica_groups=mesh['req'=4,'exp'=8,'shard'=16] {'req'}, dimensions={0}, use_global_device_ids=true | all-gather | bytes 738560 | tf_op jit(solution)/shard_map/all_gather | solution.py:59
  37.9 0.6 gather_fusion.1
  38.7 2.8 %reshape.253 = bf16[128,36,64]{2,1,0:T(8,128)(2,1)} reshape(bf16[1,2,64,2304]{3,2,1,0:T(8,128)(2,1)} %param.20) | data formatting | bytes 1179648 | tf_op jit(solution)/shard_map/reshape;squeeze | solution.py:110
  41.5 2.8 %reshape.254 = bf16[128,36,64]{2,1,0:T(8,128)(2,1)} reshape(bf16[1,2,64,2304]{3,2,1,0:T(8,128)(2,1)} %param.21) | data formatting | bytes 1179648 | tf_op jit(solution)/shard_map/reshape;squeeze | solution.py:111
  44.6 7.5 %collective-permute-start = (bf16[8,1,16,2304]{3,2,1,0:T(8,128)(2,1)S(1)}, bf16[8,1,16,2304]{3,2,1,0:T(8,128)(2,1)S(1)}, u32[]{:S(2)}, u32[]{:S(2)}) collective-permute-start(bf16[8,1,16,2304]{3,2,1,0:T(8,128)(2,1)S(1)} %all-to-all-done), channel_id=1, source_target_pairs={{0,1},{1,0},{2,3},{3,2},{4,5},{5,4},{6,7},{7,6},{8,9},{9,8},{10,11... | collective-permute-start | bytes 1769480 | tf_op jit(solution)/shard_map/ppermute | solution.py:66
  52.1 0.8 broadcast_select_fusion
  52.8 0.8 collective-permute-done
  53.8 3.0 %reshape.219 = bf16[8,2,16,36,64]{4,3,2,1,0:T(8,128)(2,1)} reshape(bf16[8,2,16,2304]{3,2,1,0:T(8,128)(2,1)S(1)} %maximum_select_fusion) | data formatting | bytes 2359296 | tf_op jit(solution)/shard_map/reshape | solution.py:109
  56.8 3.8 %bitcast_reduce_fusion = (bf16[8,2,36,16]{3,1,0,2:T(2,128)(2,1)S(1)}, f32[36,8,2,16,128]{4,3,2,1,0:T(8,128)S(1)}) fusion(pred[8,2,16,128]{3,2,1,0:T(8,128)(4,1)S(1)} %compare_and_fusion, bf16[128,36,64,1,1]{2,1,0,4,3:T(8,128)(2,1)} %bitcast.92, bf16[8,2,16,36,64]{4,3,2,1,0:T(8,128)(2,1)} %reshape.219), kind=kOutput, calls=%fused_computation.3 | convolution fusion | flops 154524672 | bytes 6539264 | tf_op jit(solution)/shard_map/ejthd,khd->ejhtk/dot_general | solution.py:112
  60.7 3.1 %fusion.34 = bf16[8,2,36,16]{3,1,0,2:T(2,128)(2,1)S(1)} fusion(f32[8,2,36,16]{3,1,0,2:T(2,128)S(1)} %convert_element_type.189, f32[36,8,2,16,128]{4,3,2,1,0:T(8,128)S(1)} %get-tuple-element.20, pred[8,2,16,128]{3,2,1,0:T(8,128)(4,1)S(1)} %compare_and_fusion), kind=kLoop, calls=%fused_computation.84 | loop fusion | flops 7068672 | bytes 4806656 | tf_op jit(solution)/shard_map/reduce_sum | solution.py:120
  64.0 3.4 %convert_bitcast_fusion = bf16[8,2,16,36,64]{4,2,1,0,3:T(8,128)(2,1)S(1)} fusion(bf16[128,36,64,1,1]{2,1,0,4,3:T(8,128)(2,1)S(1)} %bitcast.91, f32[36,8,2,16,128]{4,3,2,1,0:T(8,128)} %copy-done.2, f32[8,2,36,16]{3,1,0,2:T(2,128)S(1)} %convert_element_type.189, pred[8,2,16,128]{3,2,1,0:T(8,128)(4,1)S(1)} %compare_and_fusion), kind=kOutput, calls=%fused_computation.15 | convolution fusion | flops 157483008 | bytes 6557696 | tf_op jit(solution)/shard_map/ejhtk,khd->ejthd/dot_general | solution.py:121
  67.5 3.1 %copy.92 = bf16[8,2,16,36,64]{4,3,2,1,0:T(8,128)(2,1)} copy(bf16[8,2,16,36,64]{4,2,1,0,3:T(8,128)(2,1)S(1)} %convert_bitcast_fusion) | data formatting | bytes 2359296 | tf_op jit(solution)/shard_map/convert_element_type | solution.py:126
  70.5 4.3 %convert_element_type.127 = bf16[8,2,16,2304]{3,2,1,0:T(8,128)(2,1)} reshape(bf16[8,2,16,36,64]{4,3,2,1,0:T(8,128)(2,1)} %copy.92) | data formatting | bytes 2359296 | tf_op jit(solution)/shard_map/convert_element_type | solution.py:126
  75.1 2.4 concatenate.15
  77.4 1.3 reshape.220
  78.8 14.2 %all-to-all-start.1 = ((bf16[128,2,2376]{2,1,0:T(2,128)(2,1)}), bf16[128,2,2376]{2,1,0:T(2,128)(2,1)S(1)}, u32[]{:S(2)}, u32[]{:S(2)}) async-start(bf16[128,2,2376]{2,1,0:T(2,128)(2,1)} %reshape.220), calls=%async_computation.1 | async-start | bytes 2490368 | tf_op jit(solution)/shard_map/all_to_all | solution.py:135
  93.3 34.4 %all-to-all-done.1 = bf16[128,2,2376]{2,1,0:T(2,128)(2,1)S(1)} async-done(((bf16[128,2,2376]{2,1,0:T(2,128)(2,1)}), bf16[128,2,2376]{2,1,0:T(2,128)(2,1)S(1)}, u32[]{:S(2)}, u32[]{:S(2)}) %all-to-all-start.1) | async-done | bytes 1216544 | tf_op jit(solution)/shard_map/all_to_all | solution.py:135
  127.7 0.9 convert_element_type.130
  128.7 1.3 copy-done.1
  130.3 1.6 mul.124
  131.9 5.0 %copy.96 = f32[128,2,2304]{2,1,0:T(2,128)} copy(f32[128,2,2304]{0,2,1:T(8,128)} %bitcast.89) | data formatting | bytes 4718592 | tf_op jit(solution)/shard_map/mul | solution.py:142
  136.9 3.8 %fusion.4 = f32[2,2304]{1,0:T(2,128)S(1)} fusion(f32[128,2,2304]{2,1,0:T(2,128)} %copy.96, f32[128,2,2376]{2,1,0:T(2,128)} %copy-done.1), kind=kLoop, calls=%fused_computation.12 | loop fusion | flops 1175040 | bytes 4737024 | tf_op jit(solution)/shard_map/reduce_sum | solution.py:142
  140.9 0.7 broadcast_in_dim.141
  141.6 4.8 %all-to-all-start.2 = ((bf16[16,2,2304]{2,1,0:T(2,128)(2,1)}), bf16[16,2,2304]{2,1,0:T(2,128)(2,1)S(1)}, u32[]{:S(2)}, u32[]{:S(2)}) async-start(bf16[16,2,2304]{2,1,0:T(2,128)(2,1)} %broadcast_in_dim.141), calls=%async_computation.2 | async-start | bytes 294912 | tf_op jit(solution)/shard_map/all_to_all | solution.py:28
  146.8 8.9 %all-to-all-done.2 = bf16[16,2,2304]{2,1,0:T(2,128)(2,1)S(1)} async-done(((bf16[16,2,2304]{2,1,0:T(2,128)(2,1)}), bf16[16,2,2304]{2,1,0:T(2,128)(2,1)S(1)}, u32[]{:S(2)}, u32[]{:S(2)}) %all-to-all-start.2) | async-done | bytes 147488 | tf_op jit(solution)/shard_map/all_to_all | solution.py:28
  156.1 0.8 broadcast_in_dim.142
  156.9 3.4 %all-to-all-start.3 = ((bf16[16,2,16,144]{3,2,1,0:T(8,128)(2,1)}), bf16[16,2,16,144]{3,2,1,0:T(8,128)(2,1)S(1)}, u32[]{:S(2)}, u32[]{:S(2)}) async-start(bf16[16,2,16,144]{3,2,1,0:T(8,128)(2,1)} %broadcast_in_dim.142), calls=%async_computation.3 | async-start | bytes 524288 | tf_op jit(solution)/shard_map/all_to_all | solution.py:28
  160.3 11.4 %all-to-all-done.3 = bf16[16,2,16,144]{3,2,1,0:T(8,128)(2,1)S(1)} async-done(((bf16[16,2,16,144]{3,2,1,0:T(8,128)(2,1)}), bf16[16,2,16,144]{3,2,1,0:T(8,128)(2,1)S(1)}, u32[]{:S(2)}, u32[]{:S(2)}) %all-to-all-start.3) | async-done | bytes 147488 | tf_op jit(solution)/shard_map/all_to_all | solution.py:28
  171.8 0.3 copy.97
  172.5 0.3 fusion.3
  172.8 0.3 copy.101
  173.2 18.6 %all_to_all.35 = bf16[8,2,6,2304]{3,1,2,0:T(2,128)(2,1)S(1)} all-to-all(bf16[8,2,6,2304]{3,1,2,0:T(2,128)(2,1)S(1)} %copy.101), channel_id=1, replica_groups=mesh['req'=4,'exp'=8,'shard'=16] {'exp'}, dimensions={0} | all-to-all | bytes 884736 | tf_op jit(solution)/shard_map/all_to_all | solution.py:179
  192.1 0.6 fusion.7
  192.9 1.4 convolution_convert_fusion.1
  194.3 1.4 reshape.223
  195.7 1.7 copy.106
  197.3 5.6 %all-to-all-start.5 = ((bf16[128,2,6,144]{3,1,2,0:T(2,128)(2,1)}), bf16[128,2,6,144]{3,1,2,0:T(2,128)(2,1)S(1)}, u32[]{:S(2)}, u32[]{:S(2)}) async-start(bf16[128,2,6,144]{3,1,2,0:T(2,128)(2,1)} %bitcast.24), calls=%async_computation.5 | async-start | bytes 1572864 | tf_op jit(solution)/shard_map/all_to_all | solution.py:190
  203.1 25.9 %all-to-all-done.5 = bf16[128,2,6,144]{3,1,2,0:T(2,128)(2,1)S(1)} async-done(((bf16[128,2,6,144]{3,1,2,0:T(2,128)(2,1)}), bf16[128,2,6,144]{3,1,2,0:T(2,128)(2,1)S(1)}, u32[]{:S(2)}, u32[]{:S(2)}) %all-to-all-start.5) | async-done | bytes 442400 | tf_op jit(solution)/shard_map/all_to_all | solution.py:190
  229.0 0.8 bitcast_reduce_fusion.1
  230.0 15.4 %all_to_all.36 = bf16[16,2,16,144]{3,2,1,0:T(8,128)(2,1)S(1)} all-to-all(bf16[16,2,16,144]{3,2,1,0:T(8,128)(2,1)S(1)} %broadcast_in_dim.143), channel_id=1, replica_groups=mesh['req'=4,'exp'=8,'shard'=16] {'shard'}, dimensions={0} | all-to-all | bytes 294912 | tf_op jit(solution)/shard_map/all_to_all | solution.py:28
  245.5 1.0 reshape.226
  (87 shorter events, 5.4 us)
Async XLA Ops:
  0.0 192.1 %copy-start = (bf16[1,2,180,2304]{3,1,2,0:T(2,128)(2,1)S(1)}, bf16[1,2,180,2304]{3,1,2,0:T(2,128)(2,1)}, u32[]{:S(2)}) copy-start(bf16[1,2,180,2304]{3,1,2,0:T(2,128)(2,1)} %param.24) | copy-start | bytes 4976644
  0.0 26.3 %copy-start.10 = (s32[2,16,2]{1,2,0:T(2,128)S(1)}, s32[2,16,2]{1,2,0:T(2,128)}, u32[]{:S(2)}) copy-start(s32[2,16,2]{1,2,0:T(2,128)} %param.15) | copy-start | bytes 772
  0.0 26.4 %copy-start.11 = (bf16[2,16,2]{1,2,0:T(2,128)(2,1)S(1)}, bf16[2,16,2]{1,2,0:T(2,128)(2,1)}, u32[]{:S(2)}) copy-start(bf16[2,16,2]{1,2,0:T(2,128)(2,1)} %param.16) | copy-start | bytes 388
  0.0 26.6 %copy-start.13 = (s32[1,2]{1,0:T(1,128)S(1)}, s32[1,2]{1,0:T(1,128)}, u32[]{:S(2)}) copy-start(s32[1,2]{1,0:T(1,128)} %param.18) | copy-start | bytes 28
  0.0 26.7 %copy-start.12 = (s32[1,256]{1,0:T(1,128)S(1)}, s32[1,256]{1,0:T(1,128)}, u32[]{:S(2)}) copy-start(s32[1,256]{1,0:T(1,128)} %param.19) | copy-start | bytes 3076
  0.0 27.4 %copy-start.8 = (bf16[2,16,2304]{2,1,0:T(8,128)(2,1)S(1)}, bf16[2,16,2304]{2,1,0:T(8,128)(2,1)}, u32[]{:S(2)}) copy-start(bf16[2,16,2304]{2,1,0:T(8,128)(2,1)} %param.14) | copy-start | bytes 442372
  15.0 29.6 %all-to-all-start = ((bf16[8,1,16,2304]{3,2,1,0:T(8,128)(2,1)}), bf16[8,1,16,2304]{3,2,1,0:T(8,128)(2,1)S(1)}, u32[]{:S(2)}, u32[]{:S(2)}) async-start(bf16[8,1,16,2304]{3,2,1,0:T(8,128)(2,1)} %broadcast_in_dim.128), calls=%async_computation | async-start | bytes 1179648 | tf_op jit(solution)/shard_map/all_to_all | solution.py:28
  44.6 9.1 %collective-permute-start = (bf16[8,1,16,2304]{3,2,1,0:T(8,128)(2,1)S(1)}, bf16[8,1,16,2304]{3,2,1,0:T(8,128)(2,1)S(1)}, u32[]{:S(2)}, u32[]{:S(2)}) collective-permute-start(bf16[8,1,16,2304]{3,2,1,0:T(8,128)(2,1)S(1)} %all-to-all-done), channel_id=1, source_target_pairs={{0,1},{1,0},{2,3},{3,2},{4,5},{5,4},{6,7},{7,6},{8,9},{9,8},{10,11... | collective-permute-start | bytes 1769480 | tf_op jit(solution)/shard_map/ppermute | solution.py:66
  60.6 3.2 %copy-start.2 = (f32[36,8,2,16,128]{4,3,2,1,0:T(8,128)}, f32[36,8,2,16,128]{4,3,2,1,0:T(8,128)S(1)}, u32[]{:S(2)}) copy-start(f32[36,8,2,16,128]{4,3,2,1,0:T(8,128)S(1)} %get-tuple-element.20) | copy-start | bytes 14155780
  60.6 3.2 %copy-start.6 = (bf16[8,2,36,16]{3,1,0,2:T(2,128)(2,1)}, bf16[8,2,36,16]{3,1,0,2:T(2,128)(2,1)S(1)}, u32[]{:S(2)}) copy-start(bf16[8,2,36,16]{3,1,0,2:T(2,128)(2,1)S(1)} %get-tuple-element.19) | copy-start | bytes 55300
  60.7 3.3 %copy-start.3 = (bf16[128,36,64]{2,1,0:T(8,128)(2,1)S(1)}, bf16[128,36,64]{2,1,0:T(8,128)(2,1)}, u32[]{:S(2)}) copy-start(bf16[128,36,64]{2,1,0:T(8,128)(2,1)} %reshape.254) | copy-start | bytes 1769476
  70.5 4.3 %copy-start.7 = (bf16[8,2,36,16]{3,1,0,2:T(2,128)(2,1)S(1)}, bf16[8,2,36,16]{3,1,0,2:T(2,128)(2,1)}, u32[]{:S(2)}) copy-start(bf16[8,2,36,16]{3,1,0,2:T(2,128)(2,1)} %copy-done.6) | copy-start | bytes 55300
  77.4 15.5 %copy-start.5 = (bf16[2,16,2308]{2,1,0:T(8,128)(2,1)S(1)}, bf16[2,16,2308]{2,1,0:T(8,128)(2,1)}, u32[]{:S(2)}) copy-start(bf16[2,16,2308]{2,1,0:T(8,128)(2,1)} %broadcast_select_fusion) | copy-start | bytes 443140
  78.8 48.9 %all-to-all-start.1 = ((bf16[128,2,2376]{2,1,0:T(2,128)(2,1)}), bf16[128,2,2376]{2,1,0:T(2,128)(2,1)S(1)}, u32[]{:S(2)}, u32[]{:S(2)}) async-start(bf16[128,2,2376]{2,1,0:T(2,128)(2,1)} %reshape.220), calls=%async_computation.1 | async-start | bytes 2490368 | tf_op jit(solution)/shard_map/all_to_all | solution.py:135
  128.5 1.4 copy-start.1
  136.9 18.9 %copy-start.4 = (bf16[144,2304]{1,0:T(8,128)(2,1)S(1)}, bf16[144,2304]{1,0:T(8,128)(2,1)}, u32[]{:S(2)}) copy-start(bf16[144,2304]{1,0:T(8,128)(2,1)} %param.23) | copy-start | bytes 1990660
  141.6 14.1 %all-to-all-start.2 = ((bf16[16,2,2304]{2,1,0:T(2,128)(2,1)}), bf16[16,2,2304]{2,1,0:T(2,128)(2,1)S(1)}, u32[]{:S(2)}, u32[]{:S(2)}) async-start(bf16[16,2,2304]{2,1,0:T(2,128)(2,1)} %broadcast_in_dim.141), calls=%async_computation.2 | async-start | bytes 294912 | tf_op jit(solution)/shard_map/all_to_all | solution.py:28
  155.8 16.7 %copy-start.9 = (f32[2304]{0:T(1024)S(1)}, f32[2304]{0:T(1024)}, u32[]{:S(2)}) copy-start(f32[2304]{0:T(1024)} %param.22) | copy-start | bytes 27652
  156.9 14.9 %all-to-all-start.3 = ((bf16[16,2,16,144]{3,2,1,0:T(8,128)(2,1)}), bf16[16,2,16,144]{3,2,1,0:T(8,128)(2,1)S(1)}, u32[]{:S(2)}, u32[]{:S(2)}) async-start(bf16[16,2,16,144]{3,2,1,0:T(8,128)(2,1)} %broadcast_in_dim.142), calls=%async_computation.3 | async-start | bytes 524288 | tf_op jit(solution)/shard_map/all_to_all | solution.py:28
  197.3 31.7 %all-to-all-start.5 = ((bf16[128,2,6,144]{3,1,2,0:T(2,128)(2,1)}), bf16[128,2,6,144]{3,1,2,0:T(2,128)(2,1)S(1)}, u32[]{:S(2)}, u32[]{:S(2)}) async-start(bf16[128,2,6,144]{3,1,2,0:T(2,128)(2,1)} %bitcast.24), calls=%async_computation.5 | async-start | bytes 1572864 | tf_op jit(solution)/shard_map/all_to_all | solution.py:190

commit v8 on v7

--- a/solution.py
+++ b/solution.py
@@ -121,27 +121,67 @@
     context = jnp.einsum(
         "ejhtk,khd->ejthd", weights_bf, value_rows, preferred_element_type=jnp.float32
     ).reshape(experts_count, members, tokens_here, width)
+    half_width = width // 2
+    half_heads = H // 2
+    own_peak = jnp.transpose(local_peak, (0, 1, 3, 2))
+    own_totals = jnp.transpose(totals, (0, 1, 3, 2)).astype(jnp.bfloat16).astype(jnp.float32)
+    low_context = context[..., :half_width]
+    high_context = context[..., half_width:]
+    keep_context = jnp.where(core_index == 0, low_context, high_context)
+    give_context = jnp.where(core_index == 0, high_context, low_context)
+    message = jnp.concatenate(
+        [
+            give_context.astype(jnp.bfloat16),
+            own_peak.astype(jnp.bfloat16),
+            own_totals.astype(jnp.bfloat16),
+        ],
+        axis=3,
+    )
+    message = lax.ppermute(message, "shard", [(i, i ^ 1) for i in range(shard_count)])
+    other_context = message[..., :half_width].astype(jnp.float32)
+    other_peak = message[..., half_width : half_width + H].astype(jnp.float32)
+    other_totals = message[..., half_width + H :].astype(jnp.float32)
+    pair_peak = jnp.maximum(own_peak, other_peak)
+    own_scale = jnp.exp(own_peak - pair_peak)
+    other_scale = jnp.exp(other_peak - pair_peak)
+    pair_totals = own_scale * own_totals + other_scale * other_totals
+
+    def half_scale(scale):
+        kept = jnp.where(core_index == 0, scale[..., :half_heads], scale[..., half_heads:])
+        return jnp.repeat(kept, head_size, axis=3)
+
+    pair_context = half_scale(own_scale) * keep_context + half_scale(other_scale) * other_context
     packed = jnp.concatenate(
         [
-            context.astype(jnp.bfloat16),
-            jnp.transpose(local_peak, (0, 1, 3, 2)).astype(jnp.bfloat16),
-            jnp.transpose(totals, (0, 1, 3, 2)).astype(jnp.bfloat16),
+            pair_context.astype(jnp.bfloat16),
+            pair_peak.astype(jnp.bfloat16),
+            pair_totals.astype(jnp.bfloat16),
         ],
         axis=3,
     )
     packed_width = packed.shape[3]
     rows_each = members * tokens_here // shard_count
     packed = packed.reshape(experts_count * shard_count, rows_each, packed_width)
-    arrived = lax.all_to_all(packed, ("exp", "shard"), 0, 0, tiled=True).astype(jnp.float32)
-    arrived_context = arrived[:, :, :width].reshape(-1, rows_each, H, head_size)
-    arrived_peak = arrived[:, :, width : width + H]
-    arrived_totals = arrived[:, :, width + H : width + 2 * H]
+    arrived = lax.all_to_all(packed, ("exp", "shard"), 0, 0, tiled=True)
+    arrived = arrived.reshape(-1, 2, rows_each, packed_width)
+    arrived_peak = arrived[:, 0, :, half_width : half_width + H].astype(jnp.float32)
+    arrived_totals = arrived[:, 0, :, half_width + H :].astype(jnp.float32)
     row_peak = jnp.max(arrived_peak, axis=0)
     rescale = jnp.exp(arrived_peak - row_peak[None])
     row_totals = jnp.sum(rescale * arrived_totals, axis=0)
-    row_context = jnp.sum(rescale[..., None] * arrived_context, axis=0)
-    row_attended = (
-        (row_context / row_totals[..., None]).reshape(rows_each, width).astype(jnp.bfloat16)
+    row_halves = []
+    for half in range(2):
+        half_rescale = jnp.repeat(
+            rescale[:, :, half * half_heads : (half + 1) * half_heads], head_size, axis=2
+        )
+        row_halves.append(
+            jnp.sum(
+                half_rescale * arrived[:, half, :, :half_width].astype(jnp.float32), axis=0
+            )
+        )
+    row_context = jnp.concatenate(row_halves, axis=1)
+    row_attended = (row_context / jnp.repeat(row_totals, head_size, axis=1)).astype(
+        jnp.bfloat16
     )
     attended = gather_blocks(row_attended, "shard", shard_count).reshape(
         members, tokens_here, width

time: 247 us -> 259 us (1.049)
  waiting for transfers between devices: 81.4 us -> 69.4 us
  local copies, waits for them, and re-layouts: 39 us -> 50.8 us
  other arithmetic: 13.1 us -> 20.6 us
    all_to_all x1, waiting for transfers between devices: 34.4 us -> 21.6 us  [on_device(): arrived = lax.all_to_all(packed, ('exp', 'shard'), 0, 0, tiled=True)]
    reshape x0 -> x4, local copies, waits for them, and re-layouts: none -> 10.8 us  [the longest x2 5.16 us: half_scale(): return jnp.repeat(kept, head_size, axis=3)]
    broadcast_in_dim x0 -> x7, local copies, waits for them, and re-layouts: none -> 8.37 us  [the longest x2 4.32 us: half_scale(): return jnp.repeat(kept, head_size, axis=3)]
    convert_element_type x3 -> x0, local copies, waits for them, and re-layouts: 7.61 us -> none  [the longest x2 7.4 us: on_device(): context.astype(jnp.bfloat16)]
    transpose x0 -> x1, local copies, waits for them, and re-layouts: none -> 7.33 us  [on_device(): jnp.einsum('ejhtk,khd->ejthd', weights_bf, value_rows, preferred_element_...]
    mul x2 -> x0, local copies, waits for them, and re-layouts: 6.63 us -> none  [on_device(): row_context = jnp.sum(rescale[..., None] * arrived_context, axis=0)]
    convert_element_type x3 -> x4, other arithmetic: 0.98 us -> 5.8 us  [the longest x1 2.55 us: on_device(): pair_context.astype(jnp.bfloat16)]
  transfers between devices with their start and end apart: 6 -> 7, of which waited for: 5 -> 6; matrix products, arithmetic and copies ran while one was open for 4% -> 5% of each run, Pallas kernels for 0% -> 0%
where the time goes in v8:
time: 259 us; the launch traced here: 257 us
  waiting for transfers between devices  69.4 us (27%)
  blocking collectives  55.4 us (21%)
  local copies, waits for them, and re-layouts  50.8 us (20%)
  starting transfers between devices  48.4 us (19%)
  other arithmetic  20.6 us (8%)
  matrix products  12.4 us (5%)
    all_to_all x1, waiting for transfers between devices, on_device(): lax.all_to_all(partial_out, ('exp', 'shard'), 0, 0, tiled=True)  25.9 us
    all_to_all x1, waiting for transfers between devices, on_device(): arrived = lax.all_to_all(packed, ('exp', 'shard'), 0, 0, tiled=True)  21.6 us
    all_to_all x3, waiting for transfers between devices, gather_blocks(): return lax.all_to_all(spread, axis_name, 0, 0, tiled=False)  19.5 us
    all_to_all x3, starting transfers between devices, gather_blocks(): return lax.all_to_all(spread, axis_name, 0, 0, tiled=False)  18.5 us
    all_to_all x1, blocking collectives, on_device(): lax.all_to_all(sent_rows, 'exp', split_axis=0, concat_axis=0, tiled=True)  18.3 us
    all_to_all x1, blocking collectives, gather_blocks(): return lax.all_to_all(spread, axis_name, 0, 0, tiled=False)  15.4 us
    all_to_all x1, starting transfers between devices, on_device(): arrived = lax.all_to_all(packed, ('exp', 'shard'), 0, 0, tiled=True)  14.2 us
    all_gather x1, blocking collectives, on_device(): all_query = lax.all_gather(query_stretch, 'req', axis=0, tiled=True)  11.4 us
  transfers between devices with their start and end apart: 7, of which 6 were waited for; matrix products, arithmetic and copies ran while one was open for 5% of the time, Pallas kernels for 0%

profile of v8, /device:TPU:1, one launch (start us, length us, event | category | flops | bytes accessed | tf_op | source)
XLA Modules:
  0.0 257.5 jit_solution(8427370833501823602)
XLA Ops:
  0.1 0.9 compare_and_fusion.1
  0.9 11.4 %all_gather.6 = bf16[8,16,2304]{2,1,0:T(8,128)(2,1)S(1)} all-gather(bf16[2,16,2304]{2,1,0:T(8,128)(2,1)} %param.13), channel_id=1, replica_groups=mesh['req'=4,'exp'=8,'shard'=16] {'req'}, dimensions={0}, use_global_device_ids=true | all-gather | bytes 737280 | tf_op jit(solution)/shard_map/all_gather | solution.py:58
  14.2 0.8 broadcast_in_dim.145
  15.0 11.3 %all-to-all-start = ((bf16[8,1,16,2304]{3,2,1,0:T(8,128)(2,1)}), bf16[8,1,16,2304]{3,2,1,0:T(8,128)(2,1)S(1)}, u32[]{:S(2)}, u32[]{:S(2)}) async-start(bf16[8,1,16,2304]{3,2,1,0:T(8,128)(2,1)} %broadcast_in_dim.145), calls=%async_computation | async-start | bytes 1179648 | tf_op jit(solution)/shard_map/all_to_all | solution.py:28
  27.5 10.4 %all_gather.7 = bf16[8,16,2308]{2,1,0:T(8,128)(2,1)S(1)} all-gather(bf16[2,16,2308]{2,1,0:T(8,128)(2,1)S(1)} %concatenate.24), channel_id=1, replica_groups=mesh['req'=4,'exp'=8,'shard'=16] {'req'}, dimensions={0}, use_global_device_ids=true | all-gather | bytes 738560 | tf_op jit(solution)/shard_map/all_gather | solution.py:59
  38.7 2.8 %reshape.300 = bf16[128,36,64]{2,1,0:T(8,128)(2,1)} reshape(bf16[1,2,64,2304]{3,2,1,0:T(8,128)(2,1)} %param.20) | data formatting | bytes 1179648 | tf_op jit(solution)/shard_map/reshape;squeeze | solution.py:110
  41.5 2.9 %reshape.301 = bf16[128,36,64]{2,1,0:T(8,128)(2,1)} reshape(bf16[1,2,64,2304]{3,2,1,0:T(8,128)(2,1)} %param.21) | data formatting | bytes 1179648 | tf_op jit(solution)/shard_map/reshape;squeeze | solution.py:111
  44.6 7.5 %collective-permute-start = (bf16[8,1,16,2304]{3,2,1,0:T(8,128)(2,1)S(1)}, bf16[8,1,16,2304]{3,2,1,0:T(8,128)(2,1)S(1)}, u32[]{:S(2)}, u32[]{:S(2)}) collective-permute-start(bf16[8,1,16,2304]{3,2,1,0:T(8,128)(2,1)S(1)} %all-to-all-done), channel_id=1, source_target_pairs={{0,1},{1,0},{2,3},{3,2},{4,5},{5,4},{6,7},{7,6},{8,9},{9,8},{10,11... | collective-permute-start | bytes 1769480 | tf_op jit(solution)/shard_map/ppermute | solution.py:66
  52.8 0.9 collective-permute-done
  53.8 3.0 %reshape.259 = bf16[8,2,16,36,64]{4,3,2,1,0:T(8,128)(2,1)} reshape(bf16[8,2,16,2304]{3,2,1,0:T(8,128)(2,1)S(1)} %maximum_select_fusion) | data formatting | bytes 2359296 | tf_op jit(solution)/shard_map/reshape | solution.py:109
  56.9 5.8 %bitcast_reduce_fusion = (bf16[8,2,36,16]{3,1,0,2:T(2,128)(2,1)S(1)}, f32[36,8,2,16,128]{4,3,2,1,0:T(8,128)}) fusion(pred[8,2,16,128]{3,2,1,0:T(8,128)(4,1)S(1)} %compare_and_fusion, bf16[128,36,64,1,1]{2,1,0,4,3:T(8,128)(2,1)} %bitcast.113, bf16[8,2,16,36,64]{4,3,2,1,0:T(8,128)(2,1)} %reshape.259), kind=kOutput, calls=%fused_computation.3 | convolution fusion | flops 154524672 | bytes 6539264 | tf_op jit(solution)/shard_map/ejthd,khd->ejhtk/dot_general | solution.py:112
  63.2 5.0 %fusion.38 = bf16[8,2,36,16]{3,1,0,2:T(2,128)(2,1)S(1)} fusion(f32[8,2,36,16]{3,1,0,2:T(2,128)S(1)} %copy.164, f32[36,8,2,16,128]{4,3,2,1,0:T(8,128)} %get-tuple-element.28, pred[8,2,16,128]{3,2,1,0:T(8,128)(4,1)S(1)} %compare_and_fusion), kind=kLoop, calls=%fused_computation.98 | loop fusion | flops 7068672 | bytes 4806656 | tf_op jit(solution)/shard_map/reduce_sum | solution.py:120
  68.2 3.7 %convolution_bitcast_fusion = f32[8,2,16,36,64]{4,2,1,0,3:T(8,128)} fusion(bf16[128,36,64,1,1]{2,1,0,4,3:T(8,128)(2,1)S(1)} %bitcast.112, f32[36,8,2,16,128]{4,3,2,1,0:T(8,128)S(1)} %copy-done.1, f32[8,2,36,16]{3,1,0,2:T(2,128)S(1)} %copy.164, pred[8,2,16,128]{3,2,1,0:T(8,128)(4,1)S(1)} %compare_and_fusion), kind=kOutput, calls=%fused_computation.13 | convolution fusion | flops 156893184 | bytes 7737344 | tf_op jit(solution)/shard_map/ejhtk,khd->ejthd/dot_general | solution.py:121
  72.2 7.3 %copy.166 = f32[8,2,16,36,64]{4,3,2,1,0:T(8,128)} copy(f32[8,2,16,36,64]{4,2,1,0,3:T(8,128)} %convolution_bitcast_fusion) | data formatting | bytes 4718592 | tf_op jit(solution)/shard_map/ejhtk,khd->ejthd/transpose | solution.py:121
  79.5 4.9 %reshape.260 = f32[8,2,16,2304]{3,2,1,0:T(8,128)} reshape(f32[8,2,16,36,64]{4,3,2,1,0:T(8,128)} %copy.166) | data formatting | bytes 4718592 | tf_op jit(solution)/shard_map/reshape | solution.py:123
  84.4 1.7 select_convert_fusion
  86.4 2.5 collective-permute-start.1
  88.9 1.5 collective-permute-done.1
  91.3 2.2 broadcast_in_dim.159
  93.5 2.2 reshape.262
  95.7 2.2 broadcast_in_dim.158
  97.9 3.0 %reshape.261 = f32[8,2,16,1152]{3,2,1,0:T(8,128)} reshape(f32[8,2,16,18,64]{4,3,2,1,0:T(8,128)} %broadcast_in_dim.158) | data formatting | bytes 2359296 | tf_op jit(solution)/shard_map/reshape | solution.py:151
  100.8 2.6 add_convert_fusion
  103.4 1.0 concatenate.26
  104.4 1.1 reshape.263
  105.5 14.2 %all-to-all-start.1 = ((bf16[128,2,1224]{2,1,0:T(2,128)(2,1)}), bf16[128,2,1224]{2,1,0:T(2,128)(2,1)S(1)}, u32[]{:S(2)}, u32[]{:S(2)}) async-start(bf16[128,2,1224]{2,1,0:T(2,128)(2,1)} %reshape.263), calls=%async_computation.1 | async-start | bytes 1310720 | tf_op jit(solution)/shard_map/all_to_all | solution.py:165
  119.6 0.9 fusion.41
  121.3 21.6 %all-to-all-done.1 = bf16[128,2,1224]{2,1,0:T(2,128)(2,1)S(1)} async-done(((bf16[128,2,1224]{2,1,0:T(2,128)(2,1)}), bf16[128,2,1224]{2,1,0:T(2,128)(2,1)S(1)}, u32[]{:S(2)}, u32[]{:S(2)}) %all-to-all-start.1) | async-done | bytes 626720 | tf_op jit(solution)/shard_map/all_to_all | solution.py:165
  143.0 1.1 fusion.40
  146.3 1.1 broadcast_in_dim.163
  147.4 1.3 broadcast_in_dim.160
  148.7 1.1 broadcast_in_dim.161
  149.8 1.3 multiply_reduce_fusion
  151.1 1.2 multiply_reduce_fusion.1
  153.8 3.8 %all-to-all-start.2 = ((bf16[16,2,2304]{2,1,0:T(2,128)(2,1)}), bf16[16,2,2304]{2,1,0:T(2,128)(2,1)S(1)}, u32[]{:S(2)}, u32[]{:S(2)}) async-start(bf16[16,2,2304]{2,1,0:T(2,128)(2,1)} %broadcast_in_dim.165), calls=%async_computation.2 | async-start | bytes 294912 | tf_op jit(solution)/shard_map/all_to_all | solution.py:28
  157.6 0.9 select_reduce_fusion
  158.8 8.1 %all-to-all-done.2 = bf16[16,2,2304]{2,1,0:T(2,128)(2,1)S(1)} async-done(((bf16[16,2,2304]{2,1,0:T(2,128)(2,1)}), bf16[16,2,2304]{2,1,0:T(2,128)(2,1)S(1)}, u32[]{:S(2)}, u32[]{:S(2)}) %all-to-all-start.2) | async-done | bytes 147488 | tf_op jit(solution)/shard_map/all_to_all | solution.py:28
  167.3 0.8 broadcast_in_dim.166
  168.0 3.4 %all-to-all-start.3 = ((bf16[16,2,16,144]{3,2,1,0:T(8,128)(2,1)}), bf16[16,2,16,144]{3,2,1,0:T(8,128)(2,1)S(1)}, u32[]{:S(2)}, u32[]{:S(2)}) async-start(bf16[16,2,16,144]{3,2,1,0:T(8,128)(2,1)} %broadcast_in_dim.166), calls=%async_computation.3 | async-start | bytes 524288 | tf_op jit(solution)/shard_map/all_to_all | solution.py:28
  171.5 11.4 %all-to-all-done.3 = bf16[16,2,16,144]{3,2,1,0:T(8,128)(2,1)S(1)} async-done(((bf16[16,2,16,144]{3,2,1,0:T(8,128)(2,1)}), bf16[16,2,16,144]{3,2,1,0:T(8,128)(2,1)S(1)}, u32[]{:S(2)}, u32[]{:S(2)}) %all-to-all-start.3) | async-done | bytes 147488 | tf_op jit(solution)/shard_map/all_to_all | solution.py:28
  184.4 18.3 %all_to_all.35 = bf16[8,2,6,2304]{3,1,2,0:T(2,128)(2,1)S(1)} all-to-all(bf16[8,2,6,2304]{3,1,2,0:T(2,128)(2,1)S(1)} %copy.177), channel_id=1, replica_groups=mesh['req'=4,'exp'=8,'shard'=16] {'exp'}, dimensions={0} | all-to-all | bytes 884736 | tf_op jit(solution)/shard_map/all_to_all | solution.py:219
  203.6 1.4 convolution_convert_fusion.1
  205.1 1.4 reshape.268
  206.4 1.7 copy.182
  208.1 5.8 %all-to-all-start.5 = ((bf16[128,2,6,144]{3,1,2,0:T(2,128)(2,1)}), bf16[128,2,6,144]{3,1,2,0:T(2,128)(2,1)S(1)}, u32[]{:S(2)}, u32[]{:S(2)}) async-start(bf16[128,2,6,144]{3,1,2,0:T(2,128)(2,1)} %bitcast.26), calls=%async_computation.5 | async-start | bytes 1572864 | tf_op jit(solution)/shard_map/all_to_all | solution.py:230
  214.1 25.9 %all-to-all-done.5 = bf16[128,2,6,144]{3,1,2,0:T(2,128)(2,1)S(1)} async-done(((bf16[128,2,6,144]{3,1,2,0:T(2,128)(2,1)}), bf16[128,2,6,144]{3,1,2,0:T(2,128)(2,1)S(1)}, u32[]{:S(2)}, u32[]{:S(2)}) %all-to-all-start.5) | async-done | bytes 442400 | tf_op jit(solution)/shard_map/all_to_all | solution.py:230
  240.9 15.4 %all_to_all.36 = bf16[16,2,16,144]{3,2,1,0:T(8,128)(2,1)S(1)} all-to-all(bf16[16,2,16,144]{3,2,1,0:T(8,128)(2,1)S(1)} %broadcast_in_dim.167), channel_id=1, replica_groups=mesh['req'=4,'exp'=8,'shard'=16] {'shard'}, dimensions={0} | all-to-all | bytes 294912 | tf_op jit(solution)/shard_map/all_to_all | solution.py:28
  256.5 1.0 reshape.271
  (100 shorter events, 15.6 us)
Async XLA Ops:
  0.0 202.8 %copy-start = (bf16[1,2,180,2304]{3,1,2,0:T(2,128)(2,1)S(1)}, bf16[1,2,180,2304]{3,1,2,0:T(2,128)(2,1)}, u32[]{:S(2)}) copy-start(bf16[1,2,180,2304]{3,1,2,0:T(2,128)(2,1)} %param.24) | copy-start | bytes 4976644
  0.0 26.3 %copy-start.11 = (s32[1,2]{1,0:T(1,128)S(1)}, s32[1,2]{1,0:T(1,128)}, u32[]{:S(2)}) copy-start(s32[1,2]{1,0:T(1,128)} %param.18) | copy-start | bytes 28
  0.0 26.5 %copy-start.8 = (s32[2,16,2]{1,2,0:T(2,128)S(1)}, s32[2,16,2]{1,2,0:T(2,128)}, u32[]{:S(2)}) copy-start(s32[2,16,2]{1,2,0:T(2,128)} %param.15) | copy-start | bytes 772
  0.0 26.5 %copy-start.10 = (s32[1,256]{1,0:T(1,128)S(1)}, s32[1,256]{1,0:T(1,128)}, u32[]{:S(2)}) copy-start(s32[1,256]{1,0:T(1,128)} %param.19) | copy-start | bytes 3076
  0.0 27.3 %copy-start.9 = (bf16[2,16,2]{1,2,0:T(2,128)(2,1)S(1)}, bf16[2,16,2]{1,2,0:T(2,128)(2,1)}, u32[]{:S(2)}) copy-start(bf16[2,16,2]{1,2,0:T(2,128)(2,1)} %param.16) | copy-start | bytes 388
  0.0 27.4 %copy-start.6 = (bf16[2,16,2304]{2,1,0:T(8,128)(2,1)S(1)}, bf16[2,16,2304]{2,1,0:T(8,128)(2,1)}, u32[]{:S(2)}) copy-start(bf16[2,16,2304]{2,1,0:T(8,128)(2,1)} %param.14) | copy-start | bytes 442372
  15.0 29.6 %all-to-all-start = ((bf16[8,1,16,2304]{3,2,1,0:T(8,128)(2,1)}), bf16[8,1,16,2304]{3,2,1,0:T(8,128)(2,1)S(1)}, u32[]{:S(2)}, u32[]{:S(2)}) async-start(bf16[8,1,16,2304]{3,2,1,0:T(8,128)(2,1)} %broadcast_in_dim.145), calls=%async_computation | async-start | bytes 1179648 | tf_op jit(solution)/shard_map/all_to_all | solution.py:28
  44.6 9.1 %collective-permute-start = (bf16[8,1,16,2304]{3,2,1,0:T(8,128)(2,1)S(1)}, bf16[8,1,16,2304]{3,2,1,0:T(8,128)(2,1)S(1)}, u32[]{:S(2)}, u32[]{:S(2)}) collective-permute-start(bf16[8,1,16,2304]{3,2,1,0:T(8,128)(2,1)S(1)} %all-to-all-done), channel_id=1, source_target_pairs={{0,1},{1,0},{2,3},{3,2},{4,5},{5,4},{6,7},{7,6},{8,9},{9,8},{10,11... | collective-permute-start | bytes 1769480 | tf_op jit(solution)/shard_map/ppermute | solution.py:66
  56.8 11.3 %copy-start.2 = (bf16[128,36,64]{2,1,0:T(8,128)(2,1)S(1)}, bf16[128,36,64]{2,1,0:T(8,128)(2,1)}, u32[]{:S(2)}) copy-start(bf16[128,36,64]{2,1,0:T(8,128)(2,1)} %reshape.301) | copy-start | bytes 1769476
  63.2 5.0 %copy-start.1 = (f32[36,8,2,16,128]{4,3,2,1,0:T(8,128)S(1)}, f32[36,8,2,16,128]{4,3,2,1,0:T(8,128)}, u32[]{:S(2)}) copy-start(f32[36,8,2,16,128]{4,3,2,1,0:T(8,128)} %get-tuple-element.28) | copy-start | bytes 14155780
  86.4 4.0 %collective-permute-start.1 = (bf16[8,2,16,1224]{3,2,1,0:T(8,128)(2,1)S(1)}, bf16[8,2,16,1224]{3,2,1,0:T(8,128)(2,1)S(1)}, u32[]{:S(2)}, u32[]{:S(2)}) collective-permute-start(bf16[8,2,16,1224]{3,2,1,0:T(8,128)(2,1)S(1)} %concatenate.25), channel_id=1, source_target_pairs={{0,1},{1,0},{2,3},{3,2},{4,5},{5,4},{6,7},{7,6},{8,9},{9,8},{10,11... | collective-permute-start | bytes 1880072 | tf_op jit(solution)/shard_map/ppermute | solution.py:140
  90.4 0.9 copy-start.3
  105.5 37.5 %all-to-all-start.1 = ((bf16[128,2,1224]{2,1,0:T(2,128)(2,1)}), bf16[128,2,1224]{2,1,0:T(2,128)(2,1)S(1)}, u32[]{:S(2)}, u32[]{:S(2)}) async-start(bf16[128,2,1224]{2,1,0:T(2,128)(2,1)} %reshape.263), calls=%async_computation.1 | async-start | bytes 1310720 | tf_op jit(solution)/shard_map/all_to_all | solution.py:165
  149.8 17.1 %copy-start.4 = (bf16[144,2304]{1,0:T(8,128)(2,1)S(1)}, bf16[144,2304]{1,0:T(8,128)(2,1)}, u32[]{:S(2)}) copy-start(bf16[144,2304]{1,0:T(8,128)(2,1)} %param.23) | copy-start | bytes 1990660
  153.8 13.1 %all-to-all-start.2 = ((bf16[16,2,2304]{2,1,0:T(2,128)(2,1)}), bf16[16,2,2304]{2,1,0:T(2,128)(2,1)S(1)}, u32[]{:S(2)}, u32[]{:S(2)}) async-start(bf16[16,2,2304]{2,1,0:T(2,128)(2,1)} %broadcast_in_dim.165), calls=%async_computation.2 | async-start | bytes 294912 | tf_op jit(solution)/shard_map/all_to_all | solution.py:28
  158.7 24.9 %copy-start.5 = (bf16[2,16,2308]{2,1,0:T(8,128)(2,1)S(1)}, bf16[2,16,2308]{2,1,0:T(8,128)(2,1)}, u32[]{:S(2)}) copy-start(bf16[2,16,2308]{2,1,0:T(8,128)(2,1)} %broadcast_select_fusion) | copy-start | bytes 443140
  167.0 16.7 %copy-start.7 = (f32[2304]{0:T(1024)S(1)}, f32[2304]{0:T(1024)}, u32[]{:S(2)}) copy-start(f32[2304]{0:T(1024)} %param.22) | copy-start | bytes 27652
  168.0 14.9 %all-to-all-start.3 = ((bf16[16,2,16,144]{3,2,1,0:T(8,128)(2,1)}), bf16[16,2,16,144]{3,2,1,0:T(8,128)(2,1)S(1)}, u32[]{:S(2)}, u32[]{:S(2)}) async-start(bf16[16,2,16,144]{3,2,1,0:T(8,128)(2,1)} %broadcast_in_dim.166), calls=%async_computation.3 | async-start | bytes 524288 | tf_op jit(solution)/shard_map/all_to_all | solution.py:28
  208.1 31.8 %all-to-all-start.5 = ((bf16[128,2,6,144]{3,1,2,0:T(2,128)(2,1)}), bf16[128,2,6,144]{3,1,2,0:T(2,128)(2,1)S(1)}, u32[]{:S(2)}, u32[]{:S(2)}) async-start(bf16[128,2,6,144]{3,1,2,0:T(2,128)(2,1)} %bitcast.26), calls=%async_computation.5 | async-start | bytes 1572864 | tf_op jit(solution)/shard_map/all_to_all | solution.py:230

commit v9 on v8

--- a/solution.py
+++ b/solution.py
@@ -125,10 +125,20 @@
     half_heads = H // 2
     own_peak = jnp.transpose(local_peak, (0, 1, 3, 2))
     own_totals = jnp.transpose(totals, (0, 1, 3, 2)).astype(jnp.bfloat16).astype(jnp.float32)
-    low_context = context[..., :half_width]
-    high_context = context[..., half_width:]
-    keep_context = jnp.where(core_index == 0, low_context, high_context)
-    give_context = jnp.where(core_index == 0, high_context, low_context)
+    head_of_column = jnp.arange(half_width, dtype=jnp.int32) // head_size
+    widen_table = (
+        jnp.arange(half_heads, dtype=jnp.int32)[:, None] == head_of_column[None, :]
+    ).astype(jnp.float32)
+
+    def widen(scale):
+        return jnp.einsum(
+            "...h,hc->...c", scale, widen_table, precision=lax.Precision.HIGHEST
+        )
+
+    keep_context = lax.dynamic_slice_in_dim(context, core_index * half_width, half_width, 3)
+    give_context = lax.dynamic_slice_in_dim(
+        context, (1 - core_index) * half_width, half_width, 3
+    )
     message = jnp.concatenate(
         [
             give_context.astype(jnp.bfloat16),
@@ -147,8 +157,7 @@
     pair_totals = own_scale * own_totals + other_scale * other_totals
 
     def half_scale(scale):
-        kept = jnp.where(core_index == 0, scale[..., :half_heads], scale[..., half_heads:])
-        return jnp.repeat(kept, head_size, axis=3)
+        return widen(lax.dynamic_slice_in_dim(scale, core_index * half_heads, half_heads, 3))
 
     pair_context = half_scale(own_scale) * keep_context + half_scale(other_scale) * other_context
     packed = jnp.concatenate(
@@ -171,18 +180,13 @@
     row_totals = jnp.sum(rescale * arrived_totals, axis=0)
     row_halves = []
     for half in range(2):
-        half_rescale = jnp.repeat(
-            rescale[:, :, half * half_heads : (half + 1) * half_heads], head_size, axis=2
+        half_rescale = widen(rescale[:, :, half * half_heads : (half + 1) * half_heads])
+        half_context = jnp.sum(
+            half_rescale * arrived[:, half, :, :half_width].astype(jnp.float32), axis=0
         )
-        row_halves.append(
-            jnp.sum(
-                half_rescale * arrived[:, half, :, :half_width].astype(jnp.float32), axis=0
-            )
-        )
-    row_context = jnp.concatenate(row_halves, axis=1)
-    row_attended = (row_context / jnp.repeat(row_totals, head_size, axis=1)).astype(
-        jnp.bfloat16
-    )
+        half_totals = widen(row_totals[:, half * half_heads : (half + 1) * half_heads])
+        row_halves.append(half_context / half_totals)
+    row_attended = jnp.concatenate(row_halves, axis=1).astype(jnp.bfloat16)
     attended = gather_blocks(row_attended, "shard", shard_count).reshape(
         members, tokens_here, width
     )

time: 259 us -> 243 us (0.938)
  local copies, waits for them, and re-layouts: 50.8 us -> 36.7 us
  other arithmetic: 20.6 us -> 10.3 us
  matrix products: 12.4 us -> 18.4 us
    broadcast_in_dim x7 -> x0, local copies, waits for them, and re-layouts: 8.37 us -> none  [the longest x2 4.32 us: half_scale(): return jnp.repeat(kept, head_size, axis=3)]
    dot_general x0 -> x6, matrix products: none -> 6.04 us  [widen(): jnp.einsum('...h,hc->...c', scale, widen_table, precision=lax.Precision.H...]
    reshape x3 -> x0, local copies, waits for them, and re-layouts: 5.85 us -> none  [the longest x2 5.16 us: half_scale(): return jnp.repeat(kept, head_size, axis=3)]
    convert_element_type x3 -> x0, other arithmetic: 5.04 us -> none  [the longest x1 2.55 us: on_device(): pair_context.astype(jnp.bfloat16)]
  transfers between devices with their start and end apart: 7 -> 7, of which waited for: 6 -> 6; matrix products, arithmetic and copies ran while one was open for 5% -> 4% of each run, Pallas kernels for 0% -> 0%
where the time goes in v9:
time: 243 us; the launch traced here: 242 us
  waiting for transfers between devices  71.5 us (29%)
  blocking collectives  55.9 us (23%)
  starting transfers between devices  48.6 us (20%)
  local copies, waits for them, and re-layouts  36.7 us (15%)
  matrix products  18.4 us (8%)
  other arithmetic  10.3 us (4%)
    all_to_all x1, waiting for transfers between devices, on_device(): lax.all_to_all(partial_out, ('exp', 'shard'), 0, 0, tiled=True)  25.9 us
    all_to_all x1, waiting for transfers between devices, on_device(): arrived = lax.all_to_all(packed, ('exp', 'shard'), 0, 0, tiled=True)  23 us
    all_to_all x3, waiting for transfers between devices, gather_blocks(): return lax.all_to_all(spread, axis_name, 0, 0, tiled=False)  20.3 us
    all_to_all x1, blocking collectives, on_device(): lax.all_to_all(sent_rows, 'exp', split_axis=0, concat_axis=0, tiled=True)  18.7 us
    all_to_all x3, starting transfers between devices, gather_blocks(): return lax.all_to_all(spread, axis_name, 0, 0, tiled=False)  18.5 us
    all_to_all x1, blocking collectives, gather_blocks(): return lax.all_to_all(spread, axis_name, 0, 0, tiled=False)  15.4 us
    all_to_all x1, starting transfers between devices, on_device(): arrived = lax.all_to_all(packed, ('exp', 'shard'), 0, 0, tiled=True)  14.3 us
    all_gather x1, blocking collectives, on_device(): all_query = lax.all_gather(query_stretch, 'req', axis=0, tiled=True)  11.4 us
  transfers between devices with their start and end apart: 7, of which 6 were waited for; matrix products, arithmetic and copies ran while one was open for 4% of the time, Pallas kernels for 0%

profile of v9, /device:TPU:1, one launch (start us, length us, event | category | flops | bytes accessed | tf_op | source)
XLA Modules:
  0.0 241.8 jit_solution(10985939588001576395)
XLA Ops:
  0.1 0.9 compare_and_fusion.1
  0.9 11.4 %all_gather.6 = bf16[8,16,2304]{2,1,0:T(8,128)(2,1)S(1)} all-gather(bf16[2,16,2304]{2,1,0:T(8,128)(2,1)} %param.13), channel_id=1, replica_groups=mesh['req'=4,'exp'=8,'shard'=16] {'req'}, dimensions={0}, use_global_device_ids=true | all-gather | bytes 737280 | tf_op jit(solution)/shard_map/all_gather | solution.py:58
  12.3 0.6 dynamic-slice
  12.9 0.6 gather_fusion
  13.5 0.7 fusion.37
  14.2 0.8 broadcast_in_dim.128
  15.0 11.3 %all-to-all-start = ((bf16[8,1,16,2304]{3,2,1,0:T(8,128)(2,1)}), bf16[8,1,16,2304]{3,2,1,0:T(8,128)(2,1)S(1)}, u32[]{:S(2)}, u32[]{:S(2)}) async-start(bf16[8,1,16,2304]{3,2,1,0:T(8,128)(2,1)} %broadcast_in_dim.128), calls=%async_computation | async-start | bytes 1179648 | tf_op jit(solution)/shard_map/all_to_all | solution.py:28
  27.5 10.4 %all_gather.7 = bf16[8,16,2308]{2,1,0:T(8,128)(2,1)S(1)} all-gather(bf16[2,16,2308]{2,1,0:T(8,128)(2,1)S(1)} %concatenate.25), channel_id=1, replica_groups=mesh['req'=4,'exp'=8,'shard'=16] {'req'}, dimensions={0}, use_global_device_ids=true | all-gather | bytes 738560 | tf_op jit(solution)/shard_map/all_gather | solution.py:59
  38.1 0.6 gather_fusion.1
  38.7 2.8 %reshape.286 = bf16[128,36,64]{2,1,0:T(8,128)(2,1)} reshape(bf16[1,2,64,2304]{3,2,1,0:T(8,128)(2,1)} %param.20) | data formatting | bytes 1179648 | tf_op jit(solution)/shard_map/reshape;squeeze | solution.py:110
  41.5 2.9 %reshape.287 = bf16[128,36,64]{2,1,0:T(8,128)(2,1)} reshape(bf16[1,2,64,2304]{3,2,1,0:T(8,128)(2,1)} %param.21) | data formatting | bytes 1179648 | tf_op jit(solution)/shard_map/reshape;squeeze | solution.py:111
  44.6 7.5 %collective-permute-start = (bf16[8,1,16,2304]{3,2,1,0:T(8,128)(2,1)S(1)}, bf16[8,1,16,2304]{3,2,1,0:T(8,128)(2,1)S(1)}, u32[]{:S(2)}, u32[]{:S(2)}) collective-permute-start(bf16[8,1,16,2304]{3,2,1,0:T(8,128)(2,1)S(1)} %all-to-all-done), channel_id=1, source_target_pairs={{0,1},{1,0},{2,3},{3,2},{4,5},{5,4},{6,7},{7,6},{8,9},{9,8},{10,11... | collective-permute-start | bytes 1769480 | tf_op jit(solution)/shard_map/ppermute | solution.py:66
  52.1 0.7 broadcast_select_fusion
  52.8 0.9 collective-permute-done
  53.8 3.0 %reshape.244 = bf16[8,2,16,36,64]{4,3,2,1,0:T(8,128)(2,1)} reshape(bf16[8,2,16,2304]{3,2,1,0:T(8,128)(2,1)S(1)} %maximum_select_fusion) | data formatting | bytes 2359296 | tf_op jit(solution)/shard_map/reshape | solution.py:109
  56.9 5.8 %bitcast_reduce_fusion = (bf16[8,2,36,16]{3,1,0,2:T(2,128)(2,1)S(1)}, f32[36,8,2,16,128]{4,3,2,1,0:T(8,128)}) fusion(pred[8,2,16,128]{3,2,1,0:T(8,128)(4,1)S(1)} %compare_and_fusion, bf16[128,36,64,1,1]{2,1,0,4,3:T(8,128)(2,1)} %bitcast.123, bf16[8,2,16,36,64]{4,3,2,1,0:T(8,128)(2,1)} %reshape.244), kind=kOutput, calls=%fused_computation.3 | convolution fusion | flops 154524672 | bytes 6539264 | tf_op jit(solution)/shard_map/ejthd,khd->ejhtk/dot_general | solution.py:112
  63.2 5.0 %fusion.67 = bf16[8,2,36,16]{3,1,0,2:T(2,128)(2,1)S(1)} fusion(f32[8,2,36,16]{3,1,0,2:T(2,128)S(1)} %copy.105, f32[36,8,2,16,128]{4,3,2,1,0:T(8,128)} %get-tuple-element.29, pred[8,2,16,128]{3,2,1,0:T(8,128)(4,1)S(1)} %compare_and_fusion), kind=kLoop, calls=%fused_computation.128 | loop fusion | flops 7068672 | bytes 4806656 | tf_op jit(solution)/shard_map/reduce_sum | solution.py:120
  68.2 3.7 %convolution_bitcast_fusion = f32[8,2,16,36,64]{4,2,1,0,3:T(8,128)} fusion(bf16[128,36,64,1,1]{2,1,0,4,3:T(8,128)(2,1)S(1)} %bitcast.122, f32[36,8,2,16,128]{4,3,2,1,0:T(8,128)S(1)} %copy-done.1, f32[8,2,36,16]{3,1,0,2:T(2,128)S(1)} %copy.105, pred[8,2,16,128]{3,2,1,0:T(8,128)(4,1)S(1)} %compare_and_fusion), kind=kOutput, calls=%fused_computation.16 | convolution fusion | flops 156893184 | bytes 7737344 | tf_op jit(solution)/shard_map/ejhtk,khd->ejthd/dot_general | solution.py:121
  72.2 7.3 %copy.107 = f32[8,2,16,36,64]{4,3,2,1,0:T(8,128)} copy(f32[8,2,16,36,64]{4,2,1,0,3:T(8,128)} %convolution_bitcast_fusion) | data formatting | bytes 4718592 | tf_op jit(solution)/shard_map/ejhtk,khd->ejthd/transpose | solution.py:121
  79.5 4.9 %reshape.245 = f32[8,2,16,2304]{3,2,1,0:T(8,128)} reshape(f32[8,2,16,36,64]{4,3,2,1,0:T(8,128)} %copy.107) | data formatting | bytes 4718592 | tf_op jit(solution)/shard_map/reshape | solution.py:123
  84.4 1.3 dynamic-slice_convert_fusion
  86.0 2.5 %collective-permute-start.1 = (bf16[8,2,16,1224]{3,2,1,0:T(8,128)(2,1)S(1)}, bf16[8,2,16,1224]{3,2,1,0:T(8,128)(2,1)S(1)}, u32[]{:S(2)}, u32[]{:S(2)}) collective-permute-start(bf16[8,2,16,1224]{3,2,1,0:T(8,128)(2,1)S(1)} %concatenate.26), channel_id=1, source_target_pairs={{0,1},{1,0},{2,3},{3,2},{4,5},{5,4},{6,7},{7,6},{8,9},{9,8},{10,11... | collective-permute-start | bytes 1880072 | tf_op jit(solution)/shard_map/ppermute | solution.py:150
  88.5 1.5 collective-permute-done.1
  90.1 0.7 fusion.25
  90.8 2.1 add_convert_fusion
  93.2 1.1 reshape.246
  94.3 14.3 %all-to-all-start.1 = ((bf16[128,2,1224]{2,1,0:T(2,128)(2,1)}), bf16[128,2,1224]{2,1,0:T(2,128)(2,1)S(1)}, u32[]{:S(2)}, u32[]{:S(2)}) async-start(bf16[128,2,1224]{2,1,0:T(2,128)(2,1)} %reshape.246), calls=%async_computation.1 | async-start | bytes 1310720 | tf_op jit(solution)/shard_map/all_to_all | solution.py:174
  108.9 23.0 %all-to-all-done.1 = bf16[128,2,1224]{2,1,0:T(2,128)(2,1)S(1)} async-done(((bf16[128,2,1224]{2,1,0:T(2,128)(2,1)}), bf16[128,2,1224]{2,1,0:T(2,128)(2,1)S(1)}, u32[]{:S(2)}, u32[]{:S(2)}) %all-to-all-start.1) | async-done | bytes 626720 | tf_op jit(solution)/shard_map/all_to_all | solution.py:174
  132.0 1.2 fusion.69
  133.6 1.4 fusion.11
  135.1 1.4 fusion.10
  136.9 0.7 broadcast_in_dim.141
  137.7 3.8 %all-to-all-start.2 = ((bf16[16,2,2304]{2,1,0:T(2,128)(2,1)}), bf16[16,2,2304]{2,1,0:T(2,128)(2,1)S(1)}, u32[]{:S(2)}, u32[]{:S(2)}) async-start(bf16[16,2,2304]{2,1,0:T(2,128)(2,1)} %broadcast_in_dim.141), calls=%async_computation.2 | async-start | bytes 294912 | tf_op jit(solution)/shard_map/all_to_all | solution.py:28
  141.9 8.9 %all-to-all-done.2 = bf16[16,2,2304]{2,1,0:T(2,128)(2,1)S(1)} async-done(((bf16[16,2,2304]{2,1,0:T(2,128)(2,1)}), bf16[16,2,2304]{2,1,0:T(2,128)(2,1)S(1)}, u32[]{:S(2)}, u32[]{:S(2)}) %all-to-all-start.2) | async-done | bytes 147488 | tf_op jit(solution)/shard_map/all_to_all | solution.py:28
  151.2 0.8 broadcast_in_dim.142
  151.9 3.4 %all-to-all-start.3 = ((bf16[16,2,16,144]{3,2,1,0:T(8,128)(2,1)}), bf16[16,2,16,144]{3,2,1,0:T(8,128)(2,1)S(1)}, u32[]{:S(2)}, u32[]{:S(2)}) async-start(bf16[16,2,16,144]{3,2,1,0:T(8,128)(2,1)} %broadcast_in_dim.142), calls=%async_computation.3 | async-start | bytes 524288 | tf_op jit(solution)/shard_map/all_to_all | solution.py:28
  155.4 11.4 %all-to-all-done.3 = bf16[16,2,16,144]{3,2,1,0:T(8,128)(2,1)S(1)} async-done(((bf16[16,2,16,144]{3,2,1,0:T(8,128)(2,1)}), bf16[16,2,16,144]{3,2,1,0:T(8,128)(2,1)S(1)}, u32[]{:S(2)}, u32[]{:S(2)}) %all-to-all-start.3) | async-done | bytes 147488 | tf_op jit(solution)/shard_map/all_to_all | solution.py:28
  167.9 0.3 copy.117
  168.3 18.7 %all_to_all.35 = bf16[8,2,6,2304]{3,1,2,0:T(2,128)(2,1)S(1)} all-to-all(bf16[8,2,6,2304]{3,1,2,0:T(2,128)(2,1)S(1)} %copy.117), channel_id=1, replica_groups=mesh['req'=4,'exp'=8,'shard'=16] {'exp'}, dimensions={0} | all-to-all | bytes 884736 | tf_op jit(solution)/shard_map/all_to_all | solution.py:223
  187.2 0.6 fusion.8
  187.9 1.4 convolution_convert_fusion.1
  189.4 1.4 reshape.250
  190.8 1.7 copy.122
  192.4 5.8 %all-to-all-start.5 = ((bf16[128,2,6,144]{3,1,2,0:T(2,128)(2,1)}), bf16[128,2,6,144]{3,1,2,0:T(2,128)(2,1)S(1)}, u32[]{:S(2)}, u32[]{:S(2)}) async-start(bf16[128,2,6,144]{3,1,2,0:T(2,128)(2,1)} %bitcast.32), calls=%async_computation.5 | async-start | bytes 1572864 | tf_op jit(solution)/shard_map/all_to_all | solution.py:234
  198.4 25.9 %all-to-all-done.5 = bf16[128,2,6,144]{3,1,2,0:T(2,128)(2,1)S(1)} async-done(((bf16[128,2,6,144]{3,1,2,0:T(2,128)(2,1)}), bf16[128,2,6,144]{3,1,2,0:T(2,128)(2,1)S(1)}, u32[]{:S(2)}, u32[]{:S(2)}) %all-to-all-start.5) | async-done | bytes 442400 | tf_op jit(solution)/shard_map/all_to_all | solution.py:234
  224.3 0.8 bitcast_reduce_fusion.1
  225.3 15.4 %all_to_all.36 = bf16[16,2,16,144]{3,2,1,0:T(8,128)(2,1)S(1)} all-to-all(bf16[16,2,16,144]{3,2,1,0:T(8,128)(2,1)S(1)} %broadcast_in_dim.143), channel_id=1, replica_groups=mesh['req'=4,'exp'=8,'shard'=16] {'shard'}, dimensions={0} | all-to-all | bytes 294912 | tf_op jit(solution)/shard_map/all_to_all | solution.py:28
  240.8 1.0 reshape.253
  (90 shorter events, 7.1 us)
Async XLA Ops:
  0.0 187.2 %copy-start = (bf16[1,2,180,2304]{3,1,2,0:T(2,128)(2,1)S(1)}, bf16[1,2,180,2304]{3,1,2,0:T(2,128)(2,1)}, u32[]{:S(2)}) copy-start(bf16[1,2,180,2304]{3,1,2,0:T(2,128)(2,1)} %param.24) | copy-start | bytes 4976644
  0.0 26.3 %copy-start.10 = (s32[1,2]{1,0:T(1,128)S(1)}, s32[1,2]{1,0:T(1,128)}, u32[]{:S(2)}) copy-start(s32[1,2]{1,0:T(1,128)} %param.18) | copy-start | bytes 28
  0.0 26.5 %copy-start.7 = (s32[2,16,2]{1,2,0:T(2,128)S(1)}, s32[2,16,2]{1,2,0:T(2,128)}, u32[]{:S(2)}) copy-start(s32[2,16,2]{1,2,0:T(2,128)} %param.15) | copy-start | bytes 772
  0.0 26.5 %copy-start.9 = (s32[1,256]{1,0:T(1,128)S(1)}, s32[1,256]{1,0:T(1,128)}, u32[]{:S(2)}) copy-start(s32[1,256]{1,0:T(1,128)} %param.19) | copy-start | bytes 3076
  0.0 27.3 %copy-start.8 = (bf16[2,16,2]{1,2,0:T(2,128)(2,1)S(1)}, bf16[2,16,2]{1,2,0:T(2,128)(2,1)}, u32[]{:S(2)}) copy-start(bf16[2,16,2]{1,2,0:T(2,128)(2,1)} %param.16) | copy-start | bytes 388
  0.0 27.4 %copy-start.5 = (bf16[2,16,2304]{2,1,0:T(8,128)(2,1)S(1)}, bf16[2,16,2304]{2,1,0:T(8,128)(2,1)}, u32[]{:S(2)}) copy-start(bf16[2,16,2304]{2,1,0:T(8,128)(2,1)} %param.14) | copy-start | bytes 442372
  15.0 29.6 %all-to-all-start = ((bf16[8,1,16,2304]{3,2,1,0:T(8,128)(2,1)}), bf16[8,1,16,2304]{3,2,1,0:T(8,128)(2,1)S(1)}, u32[]{:S(2)}, u32[]{:S(2)}) async-start(bf16[8,1,16,2304]{3,2,1,0:T(8,128)(2,1)} %broadcast_in_dim.128), calls=%async_computation | async-start | bytes 1179648 | tf_op jit(solution)/shard_map/all_to_all | solution.py:28
  44.6 9.1 %collective-permute-start = (bf16[8,1,16,2304]{3,2,1,0:T(8,128)(2,1)S(1)}, bf16[8,1,16,2304]{3,2,1,0:T(8,128)(2,1)S(1)}, u32[]{:S(2)}, u32[]{:S(2)}) collective-permute-start(bf16[8,1,16,2304]{3,2,1,0:T(8,128)(2,1)S(1)} %all-to-all-done), channel_id=1, source_target_pairs={{0,1},{1,0},{2,3},{3,2},{4,5},{5,4},{6,7},{7,6},{8,9},{9,8},{10,11... | collective-permute-start | bytes 1769480 | tf_op jit(solution)/shard_map/ppermute | solution.py:66
  56.8 11.3 %copy-start.2 = (bf16[128,36,64]{2,1,0:T(8,128)(2,1)S(1)}, bf16[128,36,64]{2,1,0:T(8,128)(2,1)}, u32[]{:S(2)}) copy-start(bf16[128,36,64]{2,1,0:T(8,128)(2,1)} %reshape.287) | copy-start | bytes 1769476
  63.2 5.0 %copy-start.1 = (f32[36,8,2,16,128]{4,3,2,1,0:T(8,128)S(1)}, f32[36,8,2,16,128]{4,3,2,1,0:T(8,128)}, u32[]{:S(2)}) copy-start(f32[36,8,2,16,128]{4,3,2,1,0:T(8,128)} %get-tuple-element.29) | copy-start | bytes 14155780
  86.0 4.0 %collective-permute-start.1 = (bf16[8,2,16,1224]{3,2,1,0:T(8,128)(2,1)S(1)}, bf16[8,2,16,1224]{3,2,1,0:T(8,128)(2,1)S(1)}, u32[]{:S(2)}, u32[]{:S(2)}) collective-permute-start(bf16[8,2,16,1224]{3,2,1,0:T(8,128)(2,1)S(1)} %concatenate.26), channel_id=1, source_target_pairs={{0,1},{1,0},{2,3},{3,2},{4,5},{5,4},{6,7},{7,6},{8,9},{9,8},{10,11... | collective-permute-start | bytes 1880072 | tf_op jit(solution)/shard_map/ppermute | solution.py:150
  92.9 15.7 %copy-start.4 = (bf16[2,16,2308]{2,1,0:T(8,128)(2,1)S(1)}, bf16[2,16,2308]{2,1,0:T(8,128)(2,1)}, u32[]{:S(2)}) copy-start(bf16[2,16,2308]{2,1,0:T(8,128)(2,1)} %broadcast_select_fusion) | copy-start | bytes 443140
  94.3 56.6 %copy-start.3 = (bf16[144,2304]{1,0:T(8,128)(2,1)S(1)}, bf16[144,2304]{1,0:T(8,128)(2,1)}, u32[]{:S(2)}) copy-start(bf16[144,2304]{1,0:T(8,128)(2,1)} %param.23) | copy-start | bytes 1990660
  94.3 37.6 %all-to-all-start.1 = ((bf16[128,2,1224]{2,1,0:T(2,128)(2,1)}), bf16[128,2,1224]{2,1,0:T(2,128)(2,1)S(1)}, u32[]{:S(2)}, u32[]{:S(2)}) async-start(bf16[128,2,1224]{2,1,0:T(2,128)(2,1)} %reshape.246), calls=%async_computation.1 | async-start | bytes 1310720 | tf_op jit(solution)/shard_map/all_to_all | solution.py:174
  137.7 13.1 %all-to-all-start.2 = ((bf16[16,2,2304]{2,1,0:T(2,128)(2,1)}), bf16[16,2,2304]{2,1,0:T(2,128)(2,1)S(1)}, u32[]{:S(2)}, u32[]{:S(2)}) async-start(bf16[16,2,2304]{2,1,0:T(2,128)(2,1)} %broadcast_in_dim.141), calls=%async_computation.2 | async-start | bytes 294912 | tf_op jit(solution)/shard_map/all_to_all | solution.py:28
  150.9 16.7 %copy-start.6 = (f32[2304]{0:T(1024)S(1)}, f32[2304]{0:T(1024)}, u32[]{:S(2)}) copy-start(f32[2304]{0:T(1024)} %param.22) | copy-start | bytes 27652
  151.9 14.9 %all-to-all-start.3 = ((bf16[16,2,16,144]{3,2,1,0:T(8,128)(2,1)}), bf16[16,2,16,144]{3,2,1,0:T(8,128)(2,1)S(1)}, u32[]{:S(2)}, u32[]{:S(2)}) async-start(bf16[16,2,16,144]{3,2,1,0:T(8,128)(2,1)} %broadcast_in_dim.142), calls=%async_computation.3 | async-start | bytes 524288 | tf_op jit(solution)/shard_map/all_to_all | solution.py:28
  192.4 31.9 %all-to-all-start.5 = ((bf16[128,2,6,144]{3,1,2,0:T(2,128)(2,1)}), bf16[128,2,6,144]{3,1,2,0:T(2,128)(2,1)S(1)}, u32[]{:S(2)}, u32[]{:S(2)}) async-start(bf16[128,2,6,144]{3,1,2,0:T(2,128)(2,1)} %bitcast.32), calls=%async_computation.5 | async-start | bytes 1572864 | tf_op jit(solution)/shard_map/all_to_all | solution.py:234

commit v10 on v9

--- a/solution.py
+++ b/solution.py
@@ -113,7 +113,7 @@
         "ejthd,khd->ejhtk", query_rows, key_rows, preferred_element_type=jnp.float32
     ) * (1.0 / math.sqrt(head_size))
     scores = jnp.where(visible[:, :, None], scores, NEG_FILL)
-    local_peak = jnp.max(scores, axis=4).astype(jnp.bfloat16).astype(jnp.float32)
+    local_peak = lax.reduce_precision(jnp.max(scores, axis=4), 8, 7)
     weights_bf = jnp.where(
         visible[:, :, None], jnp.exp(scores - local_peak[..., None]), 0.0
     ).astype(jnp.bfloat16)
@@ -124,7 +124,7 @@
     half_width = width // 2
     half_heads = H // 2
     own_peak = jnp.transpose(local_peak, (0, 1, 3, 2))
-    own_totals = jnp.transpose(totals, (0, 1, 3, 2)).astype(jnp.bfloat16).astype(jnp.float32)
+    own_totals = lax.reduce_precision(jnp.transpose(totals, (0, 1, 3, 2)), 8, 7)
     head_of_column = jnp.arange(half_width, dtype=jnp.int32) // head_size
     widen_table = (
         jnp.arange(half_heads, dtype=jnp.int32)[:, None] == head_of_column[None, :]

time: 243 us -> 244 us (level)
  no operation moved by 1% of the time
where the time goes in v10:
time: 244 us; the launch traced here: 243 us
  waiting for transfers between devices  71.7 us (29%)
  blocking collectives  56 us (23%)
  starting transfers between devices  48.6 us (20%)
  local copies, waits for them, and re-layouts  35.4 us (15%)
  matrix products  18.9 us (8%)
  other arithmetic  11.7 us (5%)
    all_to_all x1, waiting for transfers between devices, on_device(): lax.all_to_all(partial_out, ('exp', 'shard'), 0, 0, tiled=True)  25.9 us
    all_to_all x1, waiting for transfers between devices, on_device(): arrived = lax.all_to_all(packed, ('exp', 'shard'), 0, 0, tiled=True)  23 us
    all_to_all x3, waiting for transfers between devices, gather_blocks(): return lax.all_to_all(spread, axis_name, 0, 0, tiled=False)  20.3 us
    all_to_all x1, blocking collectives, on_device(): lax.all_to_all(sent_rows, 'exp', split_axis=0, concat_axis=0, tiled=True)  18.7 us
    all_to_all x3, starting transfers between devices, gather_blocks(): return lax.all_to_all(spread, axis_name, 0, 0, tiled=False)  18.5 us
    all_to_all x1, blocking collectives, gather_blocks(): return lax.all_to_all(spread, axis_name, 0, 0, tiled=False)  15.4 us
    all_to_all x1, starting transfers between devices, on_device(): arrived = lax.all_to_all(packed, ('exp', 'shard'), 0, 0, tiled=True)  14.3 us
    all_gather x1, blocking collectives, on_device(): all_query = lax.all_gather(query_stretch, 'req', axis=0, tiled=True)  11.6 us
  transfers between devices with their start and end apart: 7, of which 6 were waited for; matrix products, arithmetic and copies ran while one was open for 4% of the time, Pallas kernels for 0%

profile of v10, /device:TPU:1, one launch (start us, length us, event | category | flops | bytes accessed | tf_op | source)
XLA Modules:
  0.0 242.8 jit_solution(6153255153202173879)
XLA Ops:
  0.1 11.6 %all_gather.6 = bf16[8,16,2304]{2,1,0:T(8,128)(2,1)S(1)} all-gather(bf16[2,16,2304]{2,1,0:T(8,128)(2,1)} %param.13), channel_id=1, replica_groups=mesh['req'=4,'exp'=8,'shard'=16] {'req'}, dimensions={0}, use_global_device_ids=true | all-gather | bytes 737280 | tf_op jit(solution)/shard_map/all_gather | solution.py:58
  11.6 0.7 compare_and_fusion.1
  12.9 0.6 dynamic-slice
  13.5 0.7 fusion.40
  14.2 0.8 broadcast_in_dim.128
  15.0 11.3 %all-to-all-start = ((bf16[8,1,16,2304]{3,2,1,0:T(8,128)(2,1)}), bf16[8,1,16,2304]{3,2,1,0:T(8,128)(2,1)S(1)}, u32[]{:S(2)}, u32[]{:S(2)}) async-start(bf16[8,1,16,2304]{3,2,1,0:T(8,128)(2,1)} %broadcast_in_dim.128), calls=%async_computation | async-start | bytes 1179648 | tf_op jit(solution)/shard_map/all_to_all | solution.py:28
  27.5 10.4 %all_gather.7 = bf16[8,16,2308]{2,1,0:T(8,128)(2,1)S(1)} all-gather(bf16[2,16,2308]{2,1,0:T(8,128)(2,1)S(1)} %concatenate.25), channel_id=1, replica_groups=mesh['req'=4,'exp'=8,'shard'=16] {'req'}, dimensions={0}, use_global_device_ids=true | all-gather | bytes 738560 | tf_op jit(solution)/shard_map/all_gather | solution.py:59
  37.9 0.6 gather_fusion.1
  38.7 2.8 %reshape.285 = bf16[128,36,64]{2,1,0:T(8,128)(2,1)} reshape(bf16[1,2,64,2304]{3,2,1,0:T(8,128)(2,1)} %param.20) | data formatting | bytes 1179648 | tf_op jit(solution)/shard_map/reshape;squeeze | solution.py:110
  41.5 2.9 %reshape.286 = bf16[128,36,64]{2,1,0:T(8,128)(2,1)} reshape(bf16[1,2,64,2304]{3,2,1,0:T(8,128)(2,1)} %param.21) | data formatting | bytes 1179648 | tf_op jit(solution)/shard_map/reshape;squeeze | solution.py:111
  44.6 7.5 %collective-permute-start = (bf16[8,1,16,2304]{3,2,1,0:T(8,128)(2,1)S(1)}, bf16[8,1,16,2304]{3,2,1,0:T(8,128)(2,1)S(1)}, u32[]{:S(2)}, u32[]{:S(2)}) collective-permute-start(bf16[8,1,16,2304]{3,2,1,0:T(8,128)(2,1)S(1)} %all-to-all-done), channel_id=1, source_target_pairs={{0,1},{1,0},{2,3},{3,2},{4,5},{5,4},{6,7},{7,6},{8,9},{9,8},{10,11... | collective-permute-start | bytes 1769480 | tf_op jit(solution)/shard_map/ppermute | solution.py:66
  52.1 0.7 broadcast_select_fusion
  52.8 0.9 collective-permute-done
  53.8 3.0 %reshape.243 = bf16[8,2,16,36,64]{4,3,2,1,0:T(8,128)(2,1)} reshape(bf16[8,2,16,2304]{3,2,1,0:T(8,128)(2,1)S(1)} %maximum_select_fusion) | data formatting | bytes 2359296 | tf_op jit(solution)/shard_map/reshape | solution.py:109
  56.9 5.7 %bitcast_reduce_fusion = (f32[8,2,36,16]{3,1,0,2:T(2,128)S(1)}, f32[36,8,2,16,128]{4,3,2,1,0:T(8,128)}) fusion(pred[8,2,16,128]{3,2,1,0:T(8,128)(4,1)S(1)} %compare_and_fusion, bf16[128,36,64,1,1]{2,1,0,4,3:T(8,128)(2,1)} %bitcast.131, bf16[8,2,16,36,64]{4,3,2,1,0:T(8,128)(2,1)} %reshape.243), kind=kOutput, calls=%fused_computation.3 | convolution fusion | flops 154524672 | bytes 6557696 | tf_op jit(solution)/shard_map/ejthd,khd->ejhtk/dot_general | solution.py:112
  62.8 0.7 bitcast_convert_fusion.1
  63.8 5.9 %convert_reduce_fusion = f32[8,2,36,16]{3,1,0,2:T(2,128)} fusion(f32[8,2,36,16]{3,1,0,2:T(2,128)S(1)} %copy.105, f32[36,8,2,16,128]{4,3,2,1,0:T(8,128)} %get-tuple-element.31, pred[8,2,16,128]{3,2,1,0:T(8,128)(4,1)} %copy-done.4), kind=kLoop, calls=%fused_computation.7 | loop fusion | flops 8248320 | bytes 4825088 | tf_op jit(solution)/shard_map/reduce_sum | solution.py:120
  69.7 1.1 copy.108
  70.8 4.4 %convolution_bitcast_fusion = f32[8,2,16,36,64]{4,2,1,0,3:T(8,128)S(1)} fusion(bf16[128,36,64,1,1]{2,1,0,4,3:T(8,128)(2,1)S(1)} %bitcast.130, f32[36,8,2,16,128]{4,3,2,1,0:T(8,128)} %get-tuple-element.31, f32[8,2,36,16]{3,1,0,2:T(2,128)S(1)} %copy.105, pred[8,2,16,128]{3,2,1,0:T(8,128)(4,1)} %copy-done.4), kind=kOutput, calls=%fused_computation.17 | convolution fusion | flops 156893184 | bytes 7737344 | tf_op jit(solution)/shard_map/ejhtk,khd->ejthd/dot_general | solution.py:121
  75.2 5.0 %copy.107 = f32[8,2,16,36,64]{4,3,2,1,0:T(8,128)} copy(f32[8,2,16,36,64]{4,2,1,0,3:T(8,128)S(1)} %convolution_bitcast_fusion) | data formatting | bytes 4718592 | tf_op jit(solution)/shard_map/ejhtk,khd->ejthd/transpose | solution.py:121
  80.2 5.0 %reshape.244 = f32[8,2,16,2304]{3,2,1,0:T(8,128)} reshape(f32[8,2,16,36,64]{4,3,2,1,0:T(8,128)} %copy.107) | data formatting | bytes 4718592 | tf_op jit(solution)/shard_map/reshape | solution.py:123
  85.2 1.3 dynamic-slice_convert_fusion
  86.8 2.5 %collective-permute-start.1 = (bf16[8,2,16,1224]{3,2,1,0:T(8,128)(2,1)S(1)}, bf16[8,2,16,1224]{3,2,1,0:T(8,128)(2,1)S(1)}, u32[]{:S(2)}, u32[]{:S(2)}) collective-permute-start(bf16[8,2,16,1224]{3,2,1,0:T(8,128)(2,1)S(1)} %concatenate.26), channel_id=1, source_target_pairs={{0,1},{1,0},{2,3},{3,2},{4,5},{5,4},{6,7},{7,6},{8,9},{9,8},{10,11... | collective-permute-start | bytes 1880072 | tf_op jit(solution)/shard_map/ppermute | solution.py:150
  89.3 1.7 collective-permute-done.1
  91.1 0.7 fusion.28
  91.8 2.1 add_convert_fusion
  94.1 1.1 reshape.245
  95.2 14.3 %all-to-all-start.1 = ((bf16[128,2,1224]{2,1,0:T(2,128)(2,1)}), bf16[128,2,1224]{2,1,0:T(2,128)(2,1)S(1)}, u32[]{:S(2)}, u32[]{:S(2)}) async-start(bf16[128,2,1224]{2,1,0:T(2,128)(2,1)} %reshape.245), calls=%async_computation.1 | async-start | bytes 1310720 | tf_op jit(solution)/shard_map/all_to_all | solution.py:174
  109.8 23.0 %all-to-all-done.1 = bf16[128,2,1224]{2,1,0:T(2,128)(2,1)S(1)} async-done(((bf16[128,2,1224]{2,1,0:T(2,128)(2,1)}), bf16[128,2,1224]{2,1,0:T(2,128)(2,1)S(1)}, u32[]{:S(2)}, u32[]{:S(2)}) %all-to-all-start.1) | async-done | bytes 626720 | tf_op jit(solution)/shard_map/all_to_all | solution.py:174
  132.8 1.2 fusion.73
  134.6 1.4 fusion.11
  136.0 1.4 fusion.10
  137.9 0.7 broadcast_in_dim.141
  138.6 3.8 %all-to-all-start.2 = ((bf16[16,2,2304]{2,1,0:T(2,128)(2,1)}), bf16[16,2,2304]{2,1,0:T(2,128)(2,1)S(1)}, u32[]{:S(2)}, u32[]{:S(2)}) async-start(bf16[16,2,2304]{2,1,0:T(2,128)(2,1)} %broadcast_in_dim.141), calls=%async_computation.2 | async-start | bytes 294912 | tf_op jit(solution)/shard_map/all_to_all | solution.py:28
  142.9 8.9 %all-to-all-done.2 = bf16[16,2,2304]{2,1,0:T(2,128)(2,1)S(1)} async-done(((bf16[16,2,2304]{2,1,0:T(2,128)(2,1)}), bf16[16,2,2304]{2,1,0:T(2,128)(2,1)S(1)}, u32[]{:S(2)}, u32[]{:S(2)}) %all-to-all-start.2) | async-done | bytes 147488 | tf_op jit(solution)/shard_map/all_to_all | solution.py:28
  152.1 0.8 broadcast_in_dim.142
  152.9 3.4 %all-to-all-start.3 = ((bf16[16,2,16,144]{3,2,1,0:T(8,128)(2,1)}), bf16[16,2,16,144]{3,2,1,0:T(8,128)(2,1)S(1)}, u32[]{:S(2)}, u32[]{:S(2)}) async-start(bf16[16,2,16,144]{3,2,1,0:T(8,128)(2,1)} %broadcast_in_dim.142), calls=%async_computation.3 | async-start | bytes 524288 | tf_op jit(solution)/shard_map/all_to_all | solution.py:28
  156.4 11.4 %all-to-all-done.3 = bf16[16,2,16,144]{3,2,1,0:T(8,128)(2,1)S(1)} async-done(((bf16[16,2,16,144]{3,2,1,0:T(8,128)(2,1)}), bf16[16,2,16,144]{3,2,1,0:T(8,128)(2,1)S(1)}, u32[]{:S(2)}, u32[]{:S(2)}) %all-to-all-start.3) | async-done | bytes 147488 | tf_op jit(solution)/shard_map/all_to_all | solution.py:28
  169.2 18.7 %all_to_all.35 = bf16[8,2,6,2304]{3,1,2,0:T(2,128)(2,1)S(1)} all-to-all(bf16[8,2,6,2304]{3,1,2,0:T(2,128)(2,1)S(1)} %copy.117), channel_id=1, replica_groups=mesh['req'=4,'exp'=8,'shard'=16] {'exp'}, dimensions={0} | all-to-all | bytes 884736 | tf_op jit(solution)/shard_map/all_to_all | solution.py:223
  188.1 0.6 fusion.8
  188.9 1.4 convolution_convert_fusion.1
  190.3 1.4 reshape.249
  191.7 1.7 copy.122
  193.4 5.8 %all-to-all-start.5 = ((bf16[128,2,6,144]{3,1,2,0:T(2,128)(2,1)}), bf16[128,2,6,144]{3,1,2,0:T(2,128)(2,1)S(1)}, u32[]{:S(2)}, u32[]{:S(2)}) async-start(bf16[128,2,6,144]{3,1,2,0:T(2,128)(2,1)} %bitcast.32), calls=%async_computation.5 | async-start | bytes 1572864 | tf_op jit(solution)/shard_map/all_to_all | solution.py:234
  199.3 25.9 %all-to-all-done.5 = bf16[128,2,6,144]{3,1,2,0:T(2,128)(2,1)S(1)} async-done(((bf16[128,2,6,144]{3,1,2,0:T(2,128)(2,1)}), bf16[128,2,6,144]{3,1,2,0:T(2,128)(2,1)S(1)}, u32[]{:S(2)}, u32[]{:S(2)}) %all-to-all-start.5) | async-done | bytes 442400 | tf_op jit(solution)/shard_map/all_to_all | solution.py:234
  225.3 0.8 bitcast_reduce_fusion.1
  226.2 15.4 %all_to_all.36 = bf16[16,2,16,144]{3,2,1,0:T(8,128)(2,1)S(1)} all-to-all(bf16[16,2,16,144]{3,2,1,0:T(8,128)(2,1)S(1)} %broadcast_in_dim.143), channel_id=1, replica_groups=mesh['req'=4,'exp'=8,'shard'=16] {'shard'}, dimensions={0} | all-to-all | bytes 294912 | tf_op jit(solution)/shard_map/all_to_all | solution.py:28
  241.8 1.0 reshape.252
  (94 shorter events, 7.9 us)
Async XLA Ops:
  0.0 188.1 %copy-start = (bf16[1,2,180,2304]{3,1,2,0:T(2,128)(2,1)S(1)}, bf16[1,2,180,2304]{3,1,2,0:T(2,128)(2,1)}, u32[]{:S(2)}) copy-start(bf16[1,2,180,2304]{3,1,2,0:T(2,128)(2,1)} %param.24) | copy-start | bytes 4976644
  0.0 26.3 %copy-start.9 = (bf16[2,16,2]{1,2,0:T(2,128)(2,1)S(1)}, bf16[2,16,2]{1,2,0:T(2,128)(2,1)}, u32[]{:S(2)}) copy-start(bf16[2,16,2]{1,2,0:T(2,128)(2,1)} %param.16) | copy-start | bytes 388
  0.0 26.4 %copy-start.8 = (s32[2,16,2]{1,2,0:T(2,128)S(1)}, s32[2,16,2]{1,2,0:T(2,128)}, u32[]{:S(2)}) copy-start(s32[2,16,2]{1,2,0:T(2,128)} %param.15) | copy-start | bytes 772
  0.0 26.6 %copy-start.11 = (s32[1,2]{1,0:T(1,128)S(1)}, s32[1,2]{1,0:T(1,128)}, u32[]{:S(2)}) copy-start(s32[1,2]{1,0:T(1,128)} %param.18) | copy-start | bytes 28
  0.0 26.7 %copy-start.10 = (s32[1,256]{1,0:T(1,128)S(1)}, s32[1,256]{1,0:T(1,128)}, u32[]{:S(2)}) copy-start(s32[1,256]{1,0:T(1,128)} %param.19) | copy-start | bytes 3076
  0.0 27.4 %copy-start.6 = (bf16[2,16,2304]{2,1,0:T(8,128)(2,1)S(1)}, bf16[2,16,2304]{2,1,0:T(8,128)(2,1)}, u32[]{:S(2)}) copy-start(bf16[2,16,2304]{2,1,0:T(8,128)(2,1)} %param.14) | copy-start | bytes 442372
  15.0 29.6 %all-to-all-start = ((bf16[8,1,16,2304]{3,2,1,0:T(8,128)(2,1)}), bf16[8,1,16,2304]{3,2,1,0:T(8,128)(2,1)S(1)}, u32[]{:S(2)}, u32[]{:S(2)}) async-start(bf16[8,1,16,2304]{3,2,1,0:T(8,128)(2,1)} %broadcast_in_dim.128), calls=%async_computation | async-start | bytes 1179648 | tf_op jit(solution)/shard_map/all_to_all | solution.py:28
  44.6 12.2 %copy-start.4 = (pred[8,2,16,128]{3,2,1,0:T(8,128)(4,1)}, pred[8,2,16,128]{3,2,1,0:T(8,128)(4,1)S(1)}, u32[]{:S(2)}) copy-start(pred[8,2,16,128]{3,2,1,0:T(8,128)(4,1)S(1)} %compare_and_fusion) | copy-start | bytes 98308
  44.6 9.1 %collective-permute-start = (bf16[8,1,16,2304]{3,2,1,0:T(8,128)(2,1)S(1)}, bf16[8,1,16,2304]{3,2,1,0:T(8,128)(2,1)S(1)}, u32[]{:S(2)}, u32[]{:S(2)}) collective-permute-start(bf16[8,1,16,2304]{3,2,1,0:T(8,128)(2,1)S(1)} %all-to-all-done), channel_id=1, source_target_pairs={{0,1},{1,0},{2,3},{3,2},{4,5},{5,4},{6,7},{7,6},{8,9},{9,8},{10,11... | collective-permute-start | bytes 1769480 | tf_op jit(solution)/shard_map/ppermute | solution.py:66
  63.8 7.0 %copy-start.1 = (bf16[128,36,64]{2,1,0:T(8,128)(2,1)S(1)}, bf16[128,36,64]{2,1,0:T(8,128)(2,1)}, u32[]{:S(2)}) copy-start(bf16[128,36,64]{2,1,0:T(8,128)(2,1)} %reshape.286) | copy-start | bytes 1769476
  80.2 6.3 %copy-start.5 = (bf16[8,2,16,36]{3,2,1,0:T(8,128)(2,1)S(1)}, bf16[8,2,16,36]{3,2,1,0:T(8,128)(2,1)}, u32[]{:S(2)}) copy-start(bf16[8,2,16,36]{3,2,1,0:T(8,128)(2,1)} %get-tuple-element.24) | copy-start | bytes 55300
  86.8 4.2 %collective-permute-start.1 = (bf16[8,2,16,1224]{3,2,1,0:T(8,128)(2,1)S(1)}, bf16[8,2,16,1224]{3,2,1,0:T(8,128)(2,1)S(1)}, u32[]{:S(2)}, u32[]{:S(2)}) collective-permute-start(bf16[8,2,16,1224]{3,2,1,0:T(8,128)(2,1)S(1)} %concatenate.26), channel_id=1, source_target_pairs={{0,1},{1,0},{2,3},{3,2},{4,5},{5,4},{6,7},{7,6},{8,9},{9,8},{10,11... | collective-permute-start | bytes 1880072 | tf_op jit(solution)/shard_map/ppermute | solution.py:150
  93.8 15.7 %copy-start.3 = (bf16[2,16,2308]{2,1,0:T(8,128)(2,1)S(1)}, bf16[2,16,2308]{2,1,0:T(8,128)(2,1)}, u32[]{:S(2)}) copy-start(bf16[2,16,2308]{2,1,0:T(8,128)(2,1)} %broadcast_select_fusion) | copy-start | bytes 443140
  95.2 56.6 %copy-start.2 = (bf16[144,2304]{1,0:T(8,128)(2,1)S(1)}, bf16[144,2304]{1,0:T(8,128)(2,1)}, u32[]{:S(2)}) copy-start(bf16[144,2304]{1,0:T(8,128)(2,1)} %param.23) | copy-start | bytes 1990660
  95.2 37.6 %all-to-all-start.1 = ((bf16[128,2,1224]{2,1,0:T(2,128)(2,1)}), bf16[128,2,1224]{2,1,0:T(2,128)(2,1)S(1)}, u32[]{:S(2)}, u32[]{:S(2)}) async-start(bf16[128,2,1224]{2,1,0:T(2,128)(2,1)} %reshape.245), calls=%async_computation.1 | async-start | bytes 1310720 | tf_op jit(solution)/shard_map/all_to_all | solution.py:174
  138.6 13.1 %all-to-all-start.2 = ((bf16[16,2,2304]{2,1,0:T(2,128)(2,1)}), bf16[16,2,2304]{2,1,0:T(2,128)(2,1)S(1)}, u32[]{:S(2)}, u32[]{:S(2)}) async-start(bf16[16,2,2304]{2,1,0:T(2,128)(2,1)} %broadcast_in_dim.141), calls=%async_computation.2 | async-start | bytes 294912 | tf_op jit(solution)/shard_map/all_to_all | solution.py:28
  151.8 16.7 %copy-start.7 = (f32[2304]{0:T(1024)S(1)}, f32[2304]{0:T(1024)}, u32[]{:S(2)}) copy-start(f32[2304]{0:T(1024)} %param.22) | copy-start | bytes 27652
  152.9 14.9 %all-to-all-start.3 = ((bf16[16,2,16,144]{3,2,1,0:T(8,128)(2,1)}), bf16[16,2,16,144]{3,2,1,0:T(8,128)(2,1)S(1)}, u32[]{:S(2)}, u32[]{:S(2)}) async-start(bf16[16,2,16,144]{3,2,1,0:T(8,128)(2,1)} %broadcast_in_dim.142), calls=%async_computation.3 | async-start | bytes 524288 | tf_op jit(solution)/shard_map/all_to_all | solution.py:28
  193.4 31.9 %all-to-all-start.5 = ((bf16[128,2,6,144]{3,1,2,0:T(2,128)(2,1)}), bf16[128,2,6,144]{3,1,2,0:T(2,128)(2,1)S(1)}, u32[]{:S(2)}, u32[]{:S(2)}) async-start(bf16[128,2,6,144]{3,1,2,0:T(2,128)(2,1)} %bitcast.32), calls=%async_computation.5 | async-start | bytes 1572864 | tf_op jit(solution)/shard_map/all_to_all | solution.py:234

commit v11 on v10

--- a/solution.py
+++ b/solution.py
@@ -3,7 +3,10 @@
 import jax
 import jax.numpy as jnp
 from jax import lax
+from jax.experimental import pallas as pl
+from jax.experimental.pallas import tpu as pltpu
 from jax.sharding import PartitionSpec as P
+import functools
 
 H = 36
 
@@ -21,6 +24,37 @@
     active = (jax.nn.silu(both[:, 0]) * both[:, 1]).astype(jnp.bfloat16)
     partial_out = jnp.dot(active, down_proj[0], preferred_element_type=jnp.float32)
     return partial_out.reshape(received.shape)
+
+
+def attend_kernel(heads, head_size, q_ref, k_ref, v_ref, mask_ref, ctx_ref, peak_ref, tot_ref):
+    vis = mask_ref[...] != 0
+    for h in range(heads):
+        cols = slice(h * head_size, (h + 1) * head_size)
+        q_h = q_ref[:, cols]
+        k_h = k_ref[:, cols]
+        s = lax.dot_general(q_h, k_h, (((1,), (1,)), ((), ())), preferred_element_type=jnp.float32)
+        s = jnp.where(vis, s * (1.0 / math.sqrt(head_size)), NEG_FILL)
+        m = jnp.max(s, axis=1, keepdims=True).astype(jnp.bfloat16).astype(jnp.float32)
+        w = jnp.where(vis, jnp.exp(s - m), 0.0).astype(jnp.bfloat16)
+        t = jnp.sum(w.astype(jnp.float32), axis=1, keepdims=True)
+        c = jnp.dot(w, v_ref[:, cols], preferred_element_type=jnp.float32)
+        ctx_ref[:, cols] = c
+        peak_ref[:, h : h + 1] = m
+        tot_ref[:, h : h + 1] = t
+
+def attend(q, k, v, mask, heads):
+    rows, width = q.shape
+    head_size = width // heads
+    return pl.pallas_call(
+        functools.partial(attend_kernel, heads, head_size),
+        out_shape=(
+            jax.ShapeDtypeStruct((rows, width), jnp.float32),
+            jax.ShapeDtypeStruct((rows, heads), jnp.float32),
+            jax.ShapeDtypeStruct((rows, heads), jnp.float32),
+        ),
+        in_specs=[pl.BlockSpec(memory_space=pltpu.VMEM)] * 4,
+        out_specs=[pl.BlockSpec(memory_space=pltpu.VMEM)] * 3,
+    )(q, k, v, mask)
 
 
 def gather_blocks(block, axis_name, count):
@@ -106,25 +140,21 @@
     visible = (key_owner[None, None, None, :] == jnp.arange(members, dtype=jnp.int32)[None, :, None, None]) & (
         key_place[None, None, None, :] <= query_place[..., None]
     )
-    query_rows = group_query.reshape(experts_count, members, tokens_here, H, head_size)
-    key_rows = key_pool[0].reshape(keys_here, H, head_size)
-    value_rows = value_pool[0].reshape(keys_here, H, head_size)
-    scores = jnp.einsum(
-        "ejthd,khd->ejhtk", query_rows, key_rows, preferred_element_type=jnp.float32
-    ) * (1.0 / math.sqrt(head_size))
-    scores = jnp.where(visible[:, :, None], scores, NEG_FILL)
-    local_peak = lax.reduce_precision(jnp.max(scores, axis=4), 8, 7)
-    weights_bf = jnp.where(
-        visible[:, :, None], jnp.exp(scores - local_peak[..., None]), 0.0
-    ).astype(jnp.bfloat16)
-    totals = jnp.sum(weights_bf, axis=4, dtype=jnp.float32)
-    context = jnp.einsum(
-        "ejhtk,khd->ejthd", weights_bf, value_rows, preferred_element_type=jnp.float32
-    ).reshape(experts_count, members, tokens_here, width)
+    attend_rows = experts_count * members * tokens_here
+    context, peak_rows, total_rows = attend(
+        group_query.reshape(attend_rows, width),
+        key_pool[0].reshape(keys_here, width),
+        value_pool[0].reshape(keys_here, width),
+        visible.reshape(attend_rows, keys_here).astype(jnp.int32),
+        H,
+    )
+    context = context.reshape(experts_count, members, tokens_here, width)
     half_width = width // 2
     half_heads = H // 2
-    own_peak = jnp.transpose(local_peak, (0, 1, 3, 2))
-    own_totals = lax.reduce_precision(jnp.transpose(totals, (0, 1, 3, 2)), 8, 7)
+    own_peak = peak_rows.reshape(experts_count, members, tokens_here, H)
+    own_totals = lax.reduce_precision(
+        total_rows.reshape(experts_count, members, tokens_here, H), 8, 7
+    )
     head_of_column = jnp.arange(half_width, dtype=jnp.int32) // head_size
     widen_table = (
         jnp.arange(half_heads, dtype=jnp.int32)[:, None] == head_of_column[None, :]

time: 244 us -> 222 us (0.910)
  local copies, waits for them, and re-layouts: 35.4 us -> 14.4 us
  Pallas kernels: 0 us -> 14.9 us
  matrix products: 18.9 us -> 6.94 us
  starting transfers between devices: 48.6 us -> 44.7 us
  waiting for transfers between devices: 71.7 us -> 75.6 us
  other arithmetic: 11.7 us -> 8.16 us
    pallas_call x0 -> x1, Pallas kernels: none -> 14.9 us  [attend(): pl.pallas_call(functools.partial(attend_kernel, heads, head_size), out_sh...]
    dot_general x2 -> x0, matrix products: 10.1 us -> none  [the longest x1 5.73 us: on_device(): jnp.einsum('ejthd,khd->ejhtk', query_rows, key_rows, preferred_element_ty...]
    reshape x2 -> x0, local copies, waits for them, and re-layouts: 8 us -> none  [the longest x1 4.96 us: on_device(): context = jnp.einsum('ejhtk,khd->ejthd', weights_bf, value_rows, preferre...]
    reduce_sum x1 -> x0, other arithmetic: 5.88 us -> none  [on_device(): totals = jnp.sum(weights_bf, axis=4, dtype=jnp.float32)]
    another operation x2 -> x0, local copies, waits for them, and re-layouts: 5.64 us -> none  [the longest x1 2.85 us: on_device(): value_rows = value_pool[0].reshape(keys_here, H, head_size)]
    transpose x1 -> x0, local copies, waits for them, and re-layouts: 5 us -> none  [on_device(): jnp.einsum('ejhtk,khd->ejthd', weights_bf, value_rows, preferred_element_...]
    all_to_all x3, waiting for transfers between devices: 20.3 us -> 23.6 us  [gather_blocks(): return lax.all_to_all(spread, axis_name, 0, 0, tiled=False)]
  transfers between devices with their start and end apart: 7 -> 7, of which waited for: 6 -> 7; matrix products, arithmetic and copies ran while one was open for 4% -> 2% of each run, Pallas kernels for 0% -> 0%
where the time goes in v11:
time: 222 us; the launch traced here: 221 us
  waiting for transfers between devices  75.6 us (34%)
  blocking collectives  55.9 us (25%)
  starting transfers between devices  44.7 us (20%)
  Pallas kernels  14.9 us (7%)
  local copies, waits for them, and re-layouts  14.4 us (6%)
  other arithmetic  8.16 us (4%)
  matrix products  6.94 us (3%)
    all_to_all x1, waiting for transfers between devices, on_device(): lax.all_to_all(partial_out, ('exp', 'shard'), 0, 0, tiled=True)  25.9 us
    all_to_all x3, waiting for transfers between devices, gather_blocks(): return lax.all_to_all(spread, axis_name, 0, 0, tiled=False)  23.6 us
    all_to_all x1, waiting for transfers between devices, on_device(): arrived = lax.all_to_all(packed, ('exp', 'shard'), 0, 0, tiled=True)  23 us
    all_to_all x1, blocking collectives, on_device(): lax.all_to_all(sent_rows, 'exp', split_axis=0, concat_axis=0, tiled=True)  18.7 us
    all_to_all x3, starting transfers between devices, gather_blocks(): return lax.all_to_all(spread, axis_name, 0, 0, tiled=False)  18.5 us
    all_to_all x1, blocking collectives, gather_blocks(): return lax.all_to_all(spread, axis_name, 0, 0, tiled=False)  15.4 us
    pallas_call x1, Pallas kernels, attend(): pl.pallas_call(functools.partial(attend_kernel, heads, head_size), out_sh...  14.9 us
    all_to_all x1, starting transfers between devices, on_device(): arrived = lax.all_to_all(packed, ('exp', 'shard'), 0, 0, tiled=True)  13.2 us
  transfers between devices with their start and end apart: 7, of which 7 were waited for; matrix products, arithmetic and copies ran while one was open for 2% of the time, Pallas kernels for 0%

profile of v11, /device:TPU:1, one launch (start us, length us, event | category | flops | bytes accessed | tf_op | source)
XLA Modules:
  0.0 221.1 jit_solution(11456623018087375934)
XLA Ops:
  0.0 0.9 compare_and_fusion
  0.9 11.4 %all_gather.6 = bf16[8,16,2304]{2,1,0:T(8,128)(2,1)S(1)} all-gather(bf16[2,16,2304]{2,1,0:T(8,128)(2,1)} %param.13), channel_id=1, replica_groups=mesh['req'=4,'exp'=8,'shard'=16] {'req'}, dimensions={0}, use_global_device_ids=true | all-gather | bytes 737280 | tf_op jit(solution)/shard_map/all_gather | solution.py:92
  12.3 0.6 dynamic-slice
  12.9 0.6 gather_fusion
  13.5 0.7 fusion.32
  14.1 0.8 broadcast_in_dim.64
  15.0 11.3 %all-to-all-start = ((bf16[8,1,16,2304]{3,2,1,0:T(8,128)(2,1)}), bf16[8,1,16,2304]{3,2,1,0:T(8,128)(2,1)S(1)}, u32[]{:S(2)}, u32[]{:S(2)}) async-start(bf16[8,1,16,2304]{3,2,1,0:T(8,128)(2,1)} %broadcast_in_dim.64), calls=%async_computation | async-start | bytes 1179648 | tf_op jit(solution)/shard_map/all_to_all | solution.py:62
  27.4 10.4 %all_gather.7 = bf16[8,16,2308]{2,1,0:T(8,128)(2,1)S(1)} all-gather(bf16[2,16,2308]{2,1,0:T(8,128)(2,1)S(1)} %concatenate.25), channel_id=1, replica_groups=mesh['req'=4,'exp'=8,'shard'=16] {'req'}, dimensions={0}, use_global_device_ids=true | all-gather | bytes 738560 | tf_op jit(solution)/shard_map/all_gather | solution.py:93
  37.8 0.6 gather_fusion.1
  38.9 0.8 fusion.24.mask_ref
  39.7 3.3 %all-to-all-done = bf16[8,1,16,2304]{3,2,1,0:T(8,128)(2,1)S(1)} async-done(((bf16[8,1,16,2304]{3,2,1,0:T(8,128)(2,1)}), bf16[8,1,16,2304]{3,2,1,0:T(8,128)(2,1)S(1)}, u32[]{:S(2)}, u32[]{:S(2)}) %all-to-all-start) | async-done | bytes 589856 | tf_op jit(solution)/shard_map/all_to_all | solution.py:62
  43.0 5.1 %collective-permute-start = (bf16[8,1,16,2304]{3,2,1,0:T(8,128)(2,1)S(1)}, bf16[8,1,16,2304]{3,2,1,0:T(8,128)(2,1)S(1)}, u32[]{:S(2)}, u32[]{:S(2)}) collective-permute-start(bf16[8,1,16,2304]{3,2,1,0:T(8,128)(2,1)S(1)} %all-to-all-done), channel_id=1, source_target_pairs={{0,1},{1,0},{2,3},{3,2},{4,5},{5,4},{6,7},{7,6},{8,9},{9,8},{10,11... | collective-permute-start | bytes 1769480 | tf_op jit(solution)/shard_map/ppermute | solution.py:100
  48.2 1.5 collective-permute-done
  49.7 1.1 maximum_select_fusion
  50.8 14.9 %shard_map.127 = (f32[256,2304]{1,0:T(8,128)}, f32[256,36]{1,0:T(8,128)}, f32[256,36]{1,0:T(8,128)}) custom-call(bf16[256,2304]{1,0:T(8,128)(2,1)} %bitcast.101, bf16[128,2304]{1,0:T(8,128)(2,1)} %bitcast.113, bf16[128,2304]{1,0:T(8,128)(2,1)} %bitcast.114, s32[256,128]{1,0:T(8,128)} %fusion.24.mask_ref), custom_call_target="tpu_custom_call" | custom-call | tf_op jit(solution)/shard_map/pallas_call | solution.py:48
  65.7 0.9 reduce_precision.6
  66.7 0.9 convert_element_type.137
  67.6 1.4 dynamic-slice_convert_fusion
  69.3 2.3 %collective-permute-start.1 = (bf16[8,2,16,1224]{3,2,1,0:T(8,128)(2,1)S(1)}, bf16[8,2,16,1224]{3,2,1,0:T(8,128)(2,1)S(1)}, u32[]{:S(2)}, u32[]{:S(2)}) collective-permute-start(bf16[8,2,16,1224]{3,2,1,0:T(8,128)(2,1)S(1)} %concatenate.26), channel_id=1, source_target_pairs={{0,1},{1,0},{2,3},{3,2},{4,5},{5,4},{6,7},{7,6},{8,9},{9,8},{10,11... | collective-permute-start | bytes 1880072 | tf_op jit(solution)/shard_map/ppermute | solution.py:180
  71.6 1.7 collective-permute-done.1
  73.4 0.7 fusion.19
  74.1 2.1 add_convert_fusion
  76.4 1.1 reshape.252
  77.5 13.2 %all-to-all-start.1 = ((bf16[128,2,1224]{2,1,0:T(2,128)(2,1)}), bf16[128,2,1224]{2,1,0:T(2,128)(2,1)S(1)}, u32[]{:S(2)}, u32[]{:S(2)}) async-start(bf16[128,2,1224]{2,1,0:T(2,128)(2,1)} %reshape.252), calls=%async_computation.1 | async-start | bytes 1310720 | tf_op jit(solution)/shard_map/all_to_all | solution.py:204
  91.1 23.0 %all-to-all-done.1 = bf16[128,2,1224]{2,1,0:T(2,128)(2,1)S(1)} async-done(((bf16[128,2,1224]{2,1,0:T(2,128)(2,1)}), bf16[128,2,1224]{2,1,0:T(2,128)(2,1)S(1)}, u32[]{:S(2)}, u32[]{:S(2)}) %all-to-all-start.1) | async-done | bytes 626720 | tf_op jit(solution)/shard_map/all_to_all | solution.py:204
  114.2 0.4 fusion.64
  115.0 0.5 fusion.5
  115.5 0.5 fusion.6
  116.4 0.7 broadcast_in_dim.114
  117.2 3.8 %all-to-all-start.2 = ((bf16[16,2,2304]{2,1,0:T(2,128)(2,1)}), bf16[16,2,2304]{2,1,0:T(2,128)(2,1)S(1)}, u32[]{:S(2)}, u32[]{:S(2)}) async-start(bf16[16,2,2304]{2,1,0:T(2,128)(2,1)} %broadcast_in_dim.114), calls=%async_computation.2 | async-start | bytes 294912 | tf_op jit(solution)/shard_map/all_to_all | solution.py:62
  121.4 8.9 %all-to-all-done.2 = bf16[16,2,2304]{2,1,0:T(2,128)(2,1)S(1)} async-done(((bf16[16,2,2304]{2,1,0:T(2,128)(2,1)}), bf16[16,2,2304]{2,1,0:T(2,128)(2,1)S(1)}, u32[]{:S(2)}, u32[]{:S(2)}) %all-to-all-start.2) | async-done | bytes 147488 | tf_op jit(solution)/shard_map/all_to_all | solution.py:62
  130.3 0.3 convolution_convert_fusion.2
  130.7 0.8 broadcast_in_dim.115
  131.4 3.4 %all-to-all-start.3 = ((bf16[16,2,16,144]{3,2,1,0:T(8,128)(2,1)}), bf16[16,2,16,144]{3,2,1,0:T(8,128)(2,1)S(1)}, u32[]{:S(2)}, u32[]{:S(2)}) async-start(bf16[16,2,16,144]{3,2,1,0:T(8,128)(2,1)} %broadcast_in_dim.115), calls=%async_computation.3 | async-start | bytes 524288 | tf_op jit(solution)/shard_map/all_to_all | solution.py:62
  134.9 11.4 %all-to-all-done.3 = bf16[16,2,16,144]{3,2,1,0:T(8,128)(2,1)S(1)} async-done(((bf16[16,2,16,144]{3,2,1,0:T(8,128)(2,1)}), bf16[16,2,16,144]{3,2,1,0:T(8,128)(2,1)S(1)}, u32[]{:S(2)}, u32[]{:S(2)}) %all-to-all-start.3) | async-done | bytes 147488 | tf_op jit(solution)/shard_map/all_to_all | solution.py:62
  146.3 0.3 copy.77
  147.1 0.3 fusion
  147.4 0.3 copy.81
  147.8 18.7 %all_to_all.35 = bf16[8,2,6,2304]{3,1,2,0:T(2,128)(2,1)S(1)} all-to-all(bf16[8,2,6,2304]{3,1,2,0:T(2,128)(2,1)S(1)} %copy.81), channel_id=1, replica_groups=mesh['req'=4,'exp'=8,'shard'=16] {'exp'}, dimensions={0} | all-to-all | bytes 884736 | tf_op jit(solution)/shard_map/all_to_all | solution.py:253
  166.7 0.6 fusion.3
  167.4 1.4 convolution_convert_fusion.1
  168.9 1.4 reshape.256
  170.2 1.7 copy.86
  171.9 5.6 %all-to-all-start.5 = ((bf16[128,2,6,144]{3,1,2,0:T(2,128)(2,1)}), bf16[128,2,6,144]{3,1,2,0:T(2,128)(2,1)S(1)}, u32[]{:S(2)}, u32[]{:S(2)}) async-start(bf16[128,2,6,144]{3,1,2,0:T(2,128)(2,1)} %bitcast.33), calls=%async_computation.5 | async-start | bytes 1572864 | tf_op jit(solution)/shard_map/all_to_all | solution.py:264
  177.7 25.9 %all-to-all-done.5 = bf16[128,2,6,144]{3,1,2,0:T(2,128)(2,1)S(1)} async-done(((bf16[128,2,6,144]{3,1,2,0:T(2,128)(2,1)}), bf16[128,2,6,144]{3,1,2,0:T(2,128)(2,1)S(1)}, u32[]{:S(2)}, u32[]{:S(2)}) %all-to-all-start.5) | async-done | bytes 442400 | tf_op jit(solution)/shard_map/all_to_all | solution.py:264
  203.6 0.8 bitcast_reduce_fusion
  204.6 15.4 %all_to_all.36 = bf16[16,2,16,144]{3,2,1,0:T(8,128)(2,1)S(1)} all-to-all(bf16[16,2,16,144]{3,2,1,0:T(8,128)(2,1)S(1)} %broadcast_in_dim.116), channel_id=1, replica_groups=mesh['req'=4,'exp'=8,'shard'=16] {'shard'}, dimensions={0} | all-to-all | bytes 294912 | tf_op jit(solution)/shard_map/all_to_all | solution.py:62
  220.1 1.0 reshape.259
  (81 shorter events, 5.5 us)
Async XLA Ops:
  0.0 166.6 %copy-start = (bf16[1,2,180,2304]{3,1,2,0:T(2,128)(2,1)S(1)}, bf16[1,2,180,2304]{3,1,2,0:T(2,128)(2,1)}, u32[]{:S(2)}) copy-start(bf16[1,2,180,2304]{3,1,2,0:T(2,128)(2,1)} %param.24) | copy-start | bytes 4976644
  12.3 14.0 %copy-start.5 = (s32[2,16,2]{1,2,0:T(2,128)S(1)}, s32[2,16,2]{1,2,0:T(2,128)}, u32[]{:S(2)}) copy-start(s32[2,16,2]{1,2,0:T(2,128)} %param.15) | copy-start | bytes 772
  12.3 14.1 %copy-start.6 = (bf16[2,16,2]{1,2,0:T(2,128)(2,1)S(1)}, bf16[2,16,2]{1,2,0:T(2,128)(2,1)}, u32[]{:S(2)}) copy-start(bf16[2,16,2]{1,2,0:T(2,128)(2,1)} %param.16) | copy-start | bytes 388
  12.3 14.3 %copy-start.8 = (s32[1,2]{1,0:T(1,128)S(1)}, s32[1,2]{1,0:T(1,128)}, u32[]{:S(2)}) copy-start(s32[1,2]{1,0:T(1,128)} %param.18) | copy-start | bytes 28
  12.3 14.4 %copy-start.7 = (s32[1,256]{1,0:T(1,128)S(1)}, s32[1,256]{1,0:T(1,128)}, u32[]{:S(2)}) copy-start(s32[1,256]{1,0:T(1,128)} %param.19) | copy-start | bytes 3076
  12.3 15.0 %copy-start.3 = (bf16[2,16,2304]{2,1,0:T(8,128)(2,1)S(1)}, bf16[2,16,2304]{2,1,0:T(8,128)(2,1)}, u32[]{:S(2)}) copy-start(bf16[2,16,2304]{2,1,0:T(8,128)(2,1)} %param.14) | copy-start | bytes 442372
  15.0 28.0 %all-to-all-start = ((bf16[8,1,16,2304]{3,2,1,0:T(8,128)(2,1)}), bf16[8,1,16,2304]{3,2,1,0:T(8,128)(2,1)S(1)}, u32[]{:S(2)}, u32[]{:S(2)}) async-start(bf16[8,1,16,2304]{3,2,1,0:T(8,128)(2,1)} %broadcast_in_dim.64), calls=%async_computation | async-start | bytes 1179648 | tf_op jit(solution)/shard_map/all_to_all | solution.py:62
  43.0 6.7 %collective-permute-start = (bf16[8,1,16,2304]{3,2,1,0:T(8,128)(2,1)S(1)}, bf16[8,1,16,2304]{3,2,1,0:T(8,128)(2,1)S(1)}, u32[]{:S(2)}, u32[]{:S(2)}) collective-permute-start(bf16[8,1,16,2304]{3,2,1,0:T(8,128)(2,1)S(1)} %all-to-all-done), channel_id=1, source_target_pairs={{0,1},{1,0},{2,3},{3,2},{4,5},{5,4},{6,7},{7,6},{8,9},{9,8},{10,11... | collective-permute-start | bytes 1769480 | tf_op jit(solution)/shard_map/ppermute | solution.py:100
  67.6 5.7 %copy-start.1 = (f32[256,36]{1,0:T(8,128)S(1)}, f32[256,36]{1,0:T(8,128)}, u32[]{:S(2)}) copy-start(f32[256,36]{1,0:T(8,128)} %get-tuple-element.12) | copy-start | bytes 110596
  69.3 4.0 %collective-permute-start.1 = (bf16[8,2,16,1224]{3,2,1,0:T(8,128)(2,1)S(1)}, bf16[8,2,16,1224]{3,2,1,0:T(8,128)(2,1)S(1)}, u32[]{:S(2)}, u32[]{:S(2)}) collective-permute-start(bf16[8,2,16,1224]{3,2,1,0:T(8,128)(2,1)S(1)} %concatenate.26), channel_id=1, source_target_pairs={{0,1},{1,0},{2,3},{3,2},{4,5},{5,4},{6,7},{7,6},{8,9},{9,8},{10,11... | collective-permute-start | bytes 1880072 | tf_op jit(solution)/shard_map/ppermute | solution.py:180
  77.5 36.5 %all-to-all-start.1 = ((bf16[128,2,1224]{2,1,0:T(2,128)(2,1)}), bf16[128,2,1224]{2,1,0:T(2,128)(2,1)S(1)}, u32[]{:S(2)}, u32[]{:S(2)}) async-start(bf16[128,2,1224]{2,1,0:T(2,128)(2,1)} %reshape.252), calls=%async_computation.1 | async-start | bytes 1310720 | tf_op jit(solution)/shard_map/all_to_all | solution.py:204
  114.6 15.8 %copy-start.2 = (bf16[144,2304]{1,0:T(8,128)(2,1)S(1)}, bf16[144,2304]{1,0:T(8,128)(2,1)}, u32[]{:S(2)}) copy-start(bf16[144,2304]{1,0:T(8,128)(2,1)} %param.23) | copy-start | bytes 1990660
  117.2 13.1 %all-to-all-start.2 = ((bf16[16,2,2304]{2,1,0:T(2,128)(2,1)}), bf16[16,2,2304]{2,1,0:T(2,128)(2,1)S(1)}, u32[]{:S(2)}, u32[]{:S(2)}) async-start(bf16[16,2,2304]{2,1,0:T(2,128)(2,1)} %broadcast_in_dim.114), calls=%async_computation.2 | async-start | bytes 294912 | tf_op jit(solution)/shard_map/all_to_all | solution.py:62
  131.4 14.9 %all-to-all-start.3 = ((bf16[16,2,16,144]{3,2,1,0:T(8,128)(2,1)}), bf16[16,2,16,144]{3,2,1,0:T(8,128)(2,1)S(1)}, u32[]{:S(2)}, u32[]{:S(2)}) async-start(bf16[16,2,16,144]{3,2,1,0:T(8,128)(2,1)} %broadcast_in_dim.115), calls=%async_computation.3 | async-start | bytes 524288 | tf_op jit(solution)/shard_map/all_to_all | solution.py:62
  146.3 0.7 copy-start.4
  171.9 31.6 %all-to-all-start.5 = ((bf16[128,2,6,144]{3,1,2,0:T(2,128)(2,1)}), bf16[128,2,6,144]{3,1,2,0:T(2,128)(2,1)S(1)}, u32[]{:S(2)}, u32[]{:S(2)}) async-start(bf16[128,2,6,144]{3,1,2,0:T(2,128)(2,1)} %bitcast.33), calls=%async_computation.5 | async-start | bytes 1572864 | tf_op jit(solution)/shard_map/all_to_all | solution.py:264

commit v12 on v11

--- a/solution.py
+++ b/solution.py
@@ -253,19 +253,24 @@
         lax.all_to_all(sent_rows, "exp", split_axis=0, concat_axis=0, tiled=True),
         gate_up,
         down_proj,
-    ).astype(jnp.bfloat16)
+    )
     feature_block = width // shard_count
-    partial_out = partial_out.reshape(
-        experts_count, members, capacity, shard_count, feature_block
-    )
-    partial_out = jnp.transpose(partial_out, (0, 3, 1, 2, 4)).reshape(
-        experts_count * shard_count, members, capacity, feature_block
-    )
-    gathered_parts = lax.all_to_all(partial_out, ("exp", "shard"), 0, 0, tiled=True)
+    keep_rows = lax.dynamic_slice_in_dim(partial_out, core_index, 1, 1)
+    give_rows = lax.dynamic_slice_in_dim(partial_out, 1 - core_index, 1, 1)
+    pair_rows = keep_rows + lax.ppermute(
+        give_rows, "shard", [(i, i ^ 1) for i in range(shard_count)]
+    )
+    pair_rows = pair_rows.astype(jnp.bfloat16).reshape(
+        experts_count, 1, capacity, shard_count, feature_block
+    )
+    pair_rows = jnp.transpose(pair_rows, (0, 3, 1, 2, 4)).reshape(
+        experts_count * shard_count, 1, capacity, feature_block
+    )
+    gathered_parts = lax.all_to_all(pair_rows, ("exp", "shard"), 0, 0, tiled=True)
     expert_out = (
         jnp.sum(
             gathered_parts.reshape(
-                experts_count, shard_count, members, capacity, feature_block
+                experts_count, shard_count // 2, 2, capacity, feature_block
             ).astype(jnp.float32),
             axis=1,
         )

time: 222 us -> 216 us (0.973)
  blocking collectives: 55.9 us -> 36.8 us
  waiting for transfers between devices: 75.6 us -> 82.6 us
  starting transfers between devices: 44.7 us -> 50.5 us
    all_to_all x1 -> x0, blocking collectives: 18.7 us -> none  [on_device(): lax.all_to_all(sent_rows, 'exp', split_axis=0, concat_axis=0, tiled=True)]
    all_to_all x1 -> x2, waiting for transfers between devices: 25.9 us -> 31.5 us  [the longest x1 16.2 us: on_device(): lax.all_to_all(sent_rows, 'exp', split_axis=0, concat_axis=0, tiled=True)]
    all_to_all x1 -> x2, starting transfers between devices: 5.6 us -> 9.01 us  [the longest x1 5.54 us: on_device(): lax.all_to_all(pair_rows, ('exp', 'shard'), 0, 0, tiled=True)]
    ppermute x0 -> x1, starting transfers between devices: none -> 2.33 us  [on_device(): lax.ppermute(give_rows, 'shard', [(i, i ^ 1) for i in range(shard_count)])]
  transfers between devices with their start and end apart: 7 -> 9, of which waited for: 7 -> 9; matrix products, arithmetic and copies ran while one was open for 2% -> 2% of each run, Pallas kernels for 0% -> 0%
where the time goes in v12:
time: 216 us; the launch traced here: 215 us
  waiting for transfers between devices  82.6 us (38%)
  starting transfers between devices  50.5 us (23%)
  blocking collectives  36.8 us (17%)
  local copies, waits for them, and re-layouts  15.5 us (7%)
  Pallas kernels  14.9 us (7%)
  other arithmetic  7.6 us (4%)
  matrix products  6.88 us (3%)
    all_to_all x3, waiting for transfers between devices, gather_blocks(): return lax.all_to_all(spread, axis_name, 0, 0, tiled=False)  23.6 us
    all_to_all x1, waiting for transfers between devices, on_device(): arrived = lax.all_to_all(packed, ('exp', 'shard'), 0, 0, tiled=True)  23 us
    all_to_all x3, starting transfers between devices, gather_blocks(): return lax.all_to_all(spread, axis_name, 0, 0, tiled=False)  18.6 us
    all_to_all x1, waiting for transfers between devices, on_device(): lax.all_to_all(sent_rows, 'exp', split_axis=0, concat_axis=0, tiled=True)  16.2 us
    all_to_all x1, waiting for transfers between devices, on_device(): lax.all_to_all(pair_rows, ('exp', 'shard'), 0, 0, tiled=True)  15.2 us
    all_to_all x1, blocking collectives, gather_blocks(): return lax.all_to_all(spread, axis_name, 0, 0, tiled=False)  15 us
    pallas_call x1, Pallas kernels, attend(): pl.pallas_call(functools.partial(attend_kernel, heads, head_size), out_sh...  14.9 us
    all_to_all x1, starting transfers between devices, on_device(): arrived = lax.all_to_all(packed, ('exp', 'shard'), 0, 0, tiled=True)  13.2 us
  transfers between devices with their start and end apart: 9, of which 9 were waited for; matrix products, arithmetic and copies ran while one was open for 2% of the time, Pallas kernels for 0%

profile of v12, /device:TPU:1, one launch (start us, length us, event | category | flops | bytes accessed | tf_op | source)
XLA Modules:
  0.0 215.2 jit_solution(3678371447969742773)
XLA Ops:
  0.0 0.9 compare_and_fusion
  0.9 11.4 %all_gather.6 = bf16[8,16,2304]{2,1,0:T(8,128)(2,1)S(1)} all-gather(bf16[2,16,2304]{2,1,0:T(8,128)(2,1)} %param.13), channel_id=1, replica_groups=mesh['req'=4,'exp'=8,'shard'=16] {'req'}, dimensions={0}, use_global_device_ids=true | all-gather | bytes 737280 | tf_op jit(solution)/shard_map/all_gather | solution.py:92
  12.3 0.6 dynamic-slice
  12.9 0.6 gather_fusion
  13.5 0.7 fusion.33
  14.1 0.8 broadcast_in_dim.64
  15.0 11.3 %all-to-all-start = ((bf16[8,1,16,2304]{3,2,1,0:T(8,128)(2,1)}), bf16[8,1,16,2304]{3,2,1,0:T(8,128)(2,1)S(1)}, u32[]{:S(2)}, u32[]{:S(2)}) async-start(bf16[8,1,16,2304]{3,2,1,0:T(8,128)(2,1)} %broadcast_in_dim.64), calls=%async_computation | async-start | bytes 1179648 | tf_op jit(solution)/shard_map/all_to_all | solution.py:62
  27.4 10.4 %all_gather.7 = bf16[8,16,2308]{2,1,0:T(8,128)(2,1)S(1)} all-gather(bf16[2,16,2308]{2,1,0:T(8,128)(2,1)S(1)} %concatenate.25), channel_id=1, replica_groups=mesh['req'=4,'exp'=8,'shard'=16] {'req'}, dimensions={0}, use_global_device_ids=true | all-gather | bytes 738560 | tf_op jit(solution)/shard_map/all_gather | solution.py:93
  37.8 0.6 gather_fusion.1
  38.9 0.8 fusion.25.mask_ref
  39.7 3.3 %all-to-all-done = bf16[8,1,16,2304]{3,2,1,0:T(8,128)(2,1)S(1)} async-done(((bf16[8,1,16,2304]{3,2,1,0:T(8,128)(2,1)}), bf16[8,1,16,2304]{3,2,1,0:T(8,128)(2,1)S(1)}, u32[]{:S(2)}, u32[]{:S(2)}) %all-to-all-start) | async-done | bytes 589856 | tf_op jit(solution)/shard_map/all_to_all | solution.py:62
  43.0 5.1 %collective-permute-start = (bf16[8,1,16,2304]{3,2,1,0:T(8,128)(2,1)S(1)}, bf16[8,1,16,2304]{3,2,1,0:T(8,128)(2,1)S(1)}, u32[]{:S(2)}, u32[]{:S(2)}) collective-permute-start(bf16[8,1,16,2304]{3,2,1,0:T(8,128)(2,1)S(1)} %all-to-all-done), channel_id=1, source_target_pairs={{0,1},{1,0},{2,3},{3,2},{4,5},{5,4},{6,7},{7,6},{8,9},{9,8},{10,11... | collective-permute-start | bytes 1769480 | tf_op jit(solution)/shard_map/ppermute | solution.py:100
  48.2 1.5 collective-permute-done
  49.7 1.1 maximum_select_fusion
  50.8 14.9 %shard_map.127 = (f32[256,2304]{1,0:T(8,128)}, f32[256,36]{1,0:T(8,128)}, f32[256,36]{1,0:T(8,128)}) custom-call(bf16[256,2304]{1,0:T(8,128)(2,1)} %bitcast.100, bf16[128,2304]{1,0:T(8,128)(2,1)} %bitcast.114, bf16[128,2304]{1,0:T(8,128)(2,1)} %bitcast.115, s32[256,128]{1,0:T(8,128)} %fusion.25.mask_ref), custom_call_target="tpu_custom_call" | custom-call | tf_op jit(solution)/shard_map/pallas_call | solution.py:48
  65.8 0.9 reduce_precision.6
  66.7 0.9 convert_element_type.137
  67.6 1.4 dynamic-slice_convert_fusion
  69.3 2.3 %collective-permute-start.1 = (bf16[8,2,16,1224]{3,2,1,0:T(8,128)(2,1)S(1)}, bf16[8,2,16,1224]{3,2,1,0:T(8,128)(2,1)S(1)}, u32[]{:S(2)}, u32[]{:S(2)}) collective-permute-start(bf16[8,2,16,1224]{3,2,1,0:T(8,128)(2,1)S(1)} %concatenate.26), channel_id=1, source_target_pairs={{0,1},{1,0},{2,3},{3,2},{4,5},{5,4},{6,7},{7,6},{8,9},{9,8},{10,11... | collective-permute-start | bytes 1880072 | tf_op jit(solution)/shard_map/ppermute | solution.py:180
  71.6 1.7 collective-permute-done.1
  73.4 0.7 fusion.20
  74.1 2.1 add_convert_fusion
  76.5 1.1 reshape.252
  77.6 13.2 %all-to-all-start.1 = ((bf16[128,2,1224]{2,1,0:T(2,128)(2,1)}), bf16[128,2,1224]{2,1,0:T(2,128)(2,1)S(1)}, u32[]{:S(2)}, u32[]{:S(2)}) async-start(bf16[128,2,1224]{2,1,0:T(2,128)(2,1)} %reshape.252), calls=%async_computation.1 | async-start | bytes 1310720 | tf_op jit(solution)/shard_map/all_to_all | solution.py:204
  91.1 23.0 %all-to-all-done.1 = bf16[128,2,1224]{2,1,0:T(2,128)(2,1)S(1)} async-done(((bf16[128,2,1224]{2,1,0:T(2,128)(2,1)}), bf16[128,2,1224]{2,1,0:T(2,128)(2,1)S(1)}, u32[]{:S(2)}, u32[]{:S(2)}) %all-to-all-start.1) | async-done | bytes 626720 | tf_op jit(solution)/shard_map/all_to_all | solution.py:204
  114.2 0.4 fusion.65
  115.0 0.5 fusion.5
  115.5 0.5 fusion.6
  116.4 0.7 broadcast_in_dim.114
  117.2 3.8 %all-to-all-start.2 = ((bf16[16,2,2304]{2,1,0:T(2,128)(2,1)}), bf16[16,2,2304]{2,1,0:T(2,128)(2,1)S(1)}, u32[]{:S(2)}, u32[]{:S(2)}) async-start(bf16[16,2,2304]{2,1,0:T(2,128)(2,1)} %broadcast_in_dim.114), calls=%async_computation.2 | async-start | bytes 294912 | tf_op jit(solution)/shard_map/all_to_all | solution.py:62
  121.4 8.9 %all-to-all-done.2 = bf16[16,2,2304]{2,1,0:T(2,128)(2,1)S(1)} async-done(((bf16[16,2,2304]{2,1,0:T(2,128)(2,1)}), bf16[16,2,2304]{2,1,0:T(2,128)(2,1)S(1)}, u32[]{:S(2)}, u32[]{:S(2)}) %all-to-all-start.2) | async-done | bytes 147488 | tf_op jit(solution)/shard_map/all_to_all | solution.py:62
  130.7 0.8 broadcast_in_dim.115
  131.4 3.4 %all-to-all-start.3 = ((bf16[16,2,16,144]{3,2,1,0:T(8,128)(2,1)}), bf16[16,2,16,144]{3,2,1,0:T(8,128)(2,1)S(1)}, u32[]{:S(2)}, u32[]{:S(2)}) async-start(bf16[16,2,16,144]{3,2,1,0:T(8,128)(2,1)} %broadcast_in_dim.115), calls=%async_computation.3 | async-start | bytes 524288 | tf_op jit(solution)/shard_map/all_to_all | solution.py:62
  134.9 11.4 %all-to-all-done.3 = bf16[16,2,16,144]{3,2,1,0:T(8,128)(2,1)S(1)} async-done(((bf16[16,2,16,144]{3,2,1,0:T(8,128)(2,1)}), bf16[16,2,16,144]{3,2,1,0:T(8,128)(2,1)S(1)}, u32[]{:S(2)}, u32[]{:S(2)}) %all-to-all-start.3) | async-done | bytes 147488 | tf_op jit(solution)/shard_map/all_to_all | solution.py:62
  147.4 1.1 copy.85
  148.5 3.5 %all-to-all-start.4 = ((bf16[8,2,6,2304]{3,1,2,0:T(2,128)(2,1)}), bf16[8,2,6,2304]{3,1,2,0:T(2,128)(2,1)S(1)}, u32[]{:S(2)}, u32[]{:S(2)}) async-start(bf16[8,2,6,2304]{3,1,2,0:T(2,128)(2,1)} %copy.85), calls=%async_computation.4 | async-start | bytes 884736 | tf_op jit(solution)/shard_map/all_to_all | solution.py:253
  152.0 16.2 %all-to-all-done.4 = bf16[8,2,6,2304]{3,1,2,0:T(2,128)(2,1)S(1)} async-done(((bf16[8,2,6,2304]{3,1,2,0:T(2,128)(2,1)}), bf16[8,2,6,2304]{3,1,2,0:T(2,128)(2,1)S(1)}, u32[]{:S(2)}, u32[]{:S(2)}) %all-to-all-start.4) | async-done | bytes 442400 | tf_op jit(solution)/shard_map/all_to_all | solution.py:253
  168.3 0.9 reshape.287
  169.2 1.7 fusion.3
  171.4 2.3 %collective-permute-start.2 = (f32[8,1,6,2304]{3,0,2,1:T(8,128)S(1)}, f32[8,1,6,2304]{3,0,2,1:T(8,128)S(1)}, u32[]{:S(2)}, u32[]{:S(2)}) collective-permute-start(f32[8,1,6,2304]{3,0,2,1:T(8,128)S(1)} %constant_dynamic-slice_fusion), channel_id=1, source_target_pairs={{0,1},{1,0},{2,3},{3,2},{4,5},{5,4},{6,7},{7,6},{8,9},{9,8},{10,11... | collective-permute-start | bytes 1327112 | tf_op jit(solution)/shard_map/ppermute | solution.py:260
  173.8 1.4 collective-permute-done.2
  175.2 0.6 reshape.256
  176.1 1.2 reshape.291
  177.3 5.5 %all-to-all-start.5 = ((bf16[128,2,432]{2,1,0:T(2,128)(2,1)}), bf16[128,2,432]{2,1,0:T(2,128)(2,1)S(1)}, u32[]{:S(2)}, u32[]{:S(2)}) async-start(bf16[128,2,432]{2,1,0:T(2,128)(2,1)} %reshape.291), calls=%async_computation.5 | async-start | bytes 524288 | tf_op jit(solution)/shard_map/all_to_all | solution.py:269
  183.0 15.2 %all-to-all-done.5 = bf16[128,2,432]{2,1,0:T(2,128)(2,1)S(1)} async-done(((bf16[128,2,432]{2,1,0:T(2,128)(2,1)}), bf16[128,2,432]{2,1,0:T(2,128)(2,1)S(1)}, u32[]{:S(2)}, u32[]{:S(2)}) %all-to-all-start.5) | async-done | bytes 221216 | tf_op jit(solution)/shard_map/all_to_all | solution.py:269
  198.3 0.5 reshape.292
  199.1 15.0 %all_to_all.35 = bf16[16,2,16,144]{3,2,1,0:T(8,128)(2,1)S(1)} all-to-all(bf16[16,2,16,144]{3,2,1,0:T(8,128)(2,1)S(1)} %broadcast_in_dim.116), channel_id=1, replica_groups=mesh['req'=4,'exp'=8,'shard'=16] {'shard'}, dimensions={0} | all-to-all | bytes 294912 | tf_op jit(solution)/shard_map/all_to_all | solution.py:62
  214.3 1.0 reshape.259
  (90 shorter events, 7.0 us)
Async XLA Ops:
  0.0 169.2 %copy-start = (bf16[1,2,180,2304]{3,1,2,0:T(2,128)(2,1)S(1)}, bf16[1,2,180,2304]{3,1,2,0:T(2,128)(2,1)}, u32[]{:S(2)}) copy-start(bf16[1,2,180,2304]{3,1,2,0:T(2,128)(2,1)} %param.24) | copy-start | bytes 4976644
  12.3 14.0 %copy-start.6 = (s32[2,16,2]{1,2,0:T(2,128)S(1)}, s32[2,16,2]{1,2,0:T(2,128)}, u32[]{:S(2)}) copy-start(s32[2,16,2]{1,2,0:T(2,128)} %param.15) | copy-start | bytes 772
  12.3 14.1 %copy-start.7 = (bf16[2,16,2]{1,2,0:T(2,128)(2,1)S(1)}, bf16[2,16,2]{1,2,0:T(2,128)(2,1)}, u32[]{:S(2)}) copy-start(bf16[2,16,2]{1,2,0:T(2,128)(2,1)} %param.16) | copy-start | bytes 388
  12.3 14.3 %copy-start.9 = (s32[1,2]{1,0:T(1,128)S(1)}, s32[1,2]{1,0:T(1,128)}, u32[]{:S(2)}) copy-start(s32[1,2]{1,0:T(1,128)} %param.18) | copy-start | bytes 28
  12.3 14.4 %copy-start.8 = (s32[1,256]{1,0:T(1,128)S(1)}, s32[1,256]{1,0:T(1,128)}, u32[]{:S(2)}) copy-start(s32[1,256]{1,0:T(1,128)} %param.19) | copy-start | bytes 3076
  12.3 15.0 %copy-start.4 = (bf16[2,16,2304]{2,1,0:T(8,128)(2,1)S(1)}, bf16[2,16,2304]{2,1,0:T(8,128)(2,1)}, u32[]{:S(2)}) copy-start(bf16[2,16,2304]{2,1,0:T(8,128)(2,1)} %param.14) | copy-start | bytes 442372
  15.0 28.0 %all-to-all-start = ((bf16[8,1,16,2304]{3,2,1,0:T(8,128)(2,1)}), bf16[8,1,16,2304]{3,2,1,0:T(8,128)(2,1)S(1)}, u32[]{:S(2)}, u32[]{:S(2)}) async-start(bf16[8,1,16,2304]{3,2,1,0:T(8,128)(2,1)} %broadcast_in_dim.64), calls=%async_computation | async-start | bytes 1179648 | tf_op jit(solution)/shard_map/all_to_all | solution.py:62
  43.0 6.7 %collective-permute-start = (bf16[8,1,16,2304]{3,2,1,0:T(8,128)(2,1)S(1)}, bf16[8,1,16,2304]{3,2,1,0:T(8,128)(2,1)S(1)}, u32[]{:S(2)}, u32[]{:S(2)}) collective-permute-start(bf16[8,1,16,2304]{3,2,1,0:T(8,128)(2,1)S(1)} %all-to-all-done), channel_id=1, source_target_pairs={{0,1},{1,0},{2,3},{3,2},{4,5},{5,4},{6,7},{7,6},{8,9},{9,8},{10,11... | collective-permute-start | bytes 1769480 | tf_op jit(solution)/shard_map/ppermute | solution.py:100
  67.6 5.7 %copy-start.1 = (f32[256,36]{1,0:T(8,128)S(1)}, f32[256,36]{1,0:T(8,128)}, u32[]{:S(2)}) copy-start(f32[256,36]{1,0:T(8,128)} %get-tuple-element.12) | copy-start | bytes 110596
  69.3 4.0 %collective-permute-start.1 = (bf16[8,2,16,1224]{3,2,1,0:T(8,128)(2,1)S(1)}, bf16[8,2,16,1224]{3,2,1,0:T(8,128)(2,1)S(1)}, u32[]{:S(2)}, u32[]{:S(2)}) collective-permute-start(bf16[8,2,16,1224]{3,2,1,0:T(8,128)(2,1)S(1)} %concatenate.26), channel_id=1, source_target_pairs={{0,1},{1,0},{2,3},{3,2},{4,5},{5,4},{6,7},{7,6},{8,9},{9,8},{10,11... | collective-permute-start | bytes 1880072 | tf_op jit(solution)/shard_map/ppermute | solution.py:180
  77.6 36.5 %all-to-all-start.1 = ((bf16[128,2,1224]{2,1,0:T(2,128)(2,1)}), bf16[128,2,1224]{2,1,0:T(2,128)(2,1)S(1)}, u32[]{:S(2)}, u32[]{:S(2)}) async-start(bf16[128,2,1224]{2,1,0:T(2,128)(2,1)} %reshape.252), calls=%async_computation.1 | async-start | bytes 1310720 | tf_op jit(solution)/shard_map/all_to_all | solution.py:204
  114.6 15.8 %copy-start.3 = (bf16[144,2304]{1,0:T(8,128)(2,1)S(1)}, bf16[144,2304]{1,0:T(8,128)(2,1)}, u32[]{:S(2)}) copy-start(bf16[144,2304]{1,0:T(8,128)(2,1)} %param.23) | copy-start | bytes 1990660
  117.2 13.1 %all-to-all-start.2 = ((bf16[16,2,2304]{2,1,0:T(2,128)(2,1)}), bf16[16,2,2304]{2,1,0:T(2,128)(2,1)S(1)}, u32[]{:S(2)}, u32[]{:S(2)}) async-start(bf16[16,2,2304]{2,1,0:T(2,128)(2,1)} %broadcast_in_dim.114), calls=%async_computation.2 | async-start | bytes 294912 | tf_op jit(solution)/shard_map/all_to_all | solution.py:62
  131.4 14.9 %all-to-all-start.3 = ((bf16[16,2,16,144]{3,2,1,0:T(8,128)(2,1)}), bf16[16,2,16,144]{3,2,1,0:T(8,128)(2,1)S(1)}, u32[]{:S(2)}, u32[]{:S(2)}) async-start(bf16[16,2,16,144]{3,2,1,0:T(8,128)(2,1)} %broadcast_in_dim.115), calls=%async_computation.3 | async-start | bytes 524288 | tf_op jit(solution)/shard_map/all_to_all | solution.py:62
  146.4 0.7 copy-start.5
  148.5 19.7 %all-to-all-start.4 = ((bf16[8,2,6,2304]{3,1,2,0:T(2,128)(2,1)}), bf16[8,2,6,2304]{3,1,2,0:T(2,128)(2,1)S(1)}, u32[]{:S(2)}, u32[]{:S(2)}) async-start(bf16[8,2,6,2304]{3,1,2,0:T(2,128)(2,1)} %copy.85), calls=%async_computation.4 | async-start | bytes 884736 | tf_op jit(solution)/shard_map/all_to_all | solution.py:253
  169.2 1.9 copy-start.2
  171.4 3.7 %collective-permute-start.2 = (f32[8,1,6,2304]{3,0,2,1:T(8,128)S(1)}, f32[8,1,6,2304]{3,0,2,1:T(8,128)S(1)}, u32[]{:S(2)}, u32[]{:S(2)}) collective-permute-start(f32[8,1,6,2304]{3,0,2,1:T(8,128)S(1)} %constant_dynamic-slice_fusion), channel_id=1, source_target_pairs={{0,1},{1,0},{2,3},{3,2},{4,5},{5,4},{6,7},{7,6},{8,9},{9,8},{10,11... | collective-permute-start | bytes 1327112 | tf_op jit(solution)/shard_map/ppermute | solution.py:260
  177.3 20.9 %all-to-all-start.5 = ((bf16[128,2,432]{2,1,0:T(2,128)(2,1)}), bf16[128,2,432]{2,1,0:T(2,128)(2,1)S(1)}, u32[]{:S(2)}, u32[]{:S(2)}) async-start(bf16[128,2,432]{2,1,0:T(2,128)(2,1)} %reshape.291), calls=%async_computation.5 | async-start | bytes 524288 | tf_op jit(solution)/shard_map/all_to_all | solution.py:269

commit v13 on v12

--- a/solution.py
+++ b/solution.py
@@ -249,11 +249,20 @@
     share_table = jnp.sum(
         place_table.astype(jnp.bfloat16) * served_probs[:, :, :, None, None], axis=2
     )
-    partial_out = expert_rows(
-        lax.all_to_all(sent_rows, "exp", split_axis=0, concat_axis=0, tiled=True),
-        gate_up,
-        down_proj,
-    )
+    own_rows = lax.all_to_all(
+        lax.dynamic_slice_in_dim(sent_rows, core_index, 1, 1),
+        "exp",
+        split_axis=0,
+        concat_axis=0,
+        tiled=True,
+    )
+    partner_rows = lax.ppermute(own_rows, "shard", [(i, i ^ 1) for i in range(shard_count)])
+    received_rows = jnp.where(
+        core_index == 0,
+        jnp.concatenate([own_rows, partner_rows], axis=1),
+        jnp.concatenate([partner_rows, own_rows], axis=1),
+    )
+    partial_out = expert_rows(received_rows, gate_up, down_proj)
     feature_block = width // shard_count
     keep_rows = lax.dynamic_slice_in_dim(partial_out, core_index, 1, 1)
     give_rows = lax.dynamic_slice_in_dim(partial_out, 1 - core_index, 1, 1)

time: 216 us -> 213 us (0.986)
  blocking collectives: 36.8 us -> 52.3 us
  waiting for transfers between devices: 82.6 us -> 67.6 us
    all_to_all x1 -> x0, waiting for transfers between devices: 16.2 us -> none  [on_device(): lax.all_to_all(sent_rows, 'exp', split_axis=0, concat_axis=0, tiled=True)]
    all_to_all x0 -> x1, blocking collectives: none -> 15.5 us  [on_device(): lax.all_to_all(lax.dynamic_slice_in_dim(sent_rows, core_index, 1, 1), 'ex...]
    all_to_all x1 -> x0, starting transfers between devices: 3.47 us -> none  [on_device(): lax.all_to_all(sent_rows, 'exp', split_axis=0, concat_axis=0, tiled=True)]
    ppermute x0 -> x1, starting transfers between devices: none -> 2.32 us  [on_device(): lax.ppermute(own_rows, 'shard', [(i, i ^ 1) for i in range(shard_count)])]
where the time goes in v13:
time: 213 us; the launch traced here: 212 us
  waiting for transfers between devices  67.6 us (32%)
  blocking collectives  52.3 us (25%)
  starting transfers between devices  49.3 us (23%)
  Pallas kernels  14.9 us (7%)
  local copies, waits for them, and re-layouts  14 us (7%)
  other arithmetic  7.77 us (4%)
  matrix products  5.79 us (3%)
    all_to_all x3, waiting for transfers between devices, gather_blocks(): return lax.all_to_all(spread, axis_name, 0, 0, tiled=False)  23.6 us
    all_to_all x1, waiting for transfers between devices, on_device(): arrived = lax.all_to_all(packed, ('exp', 'shard'), 0, 0, tiled=True)  23 us
    all_to_all x3, starting transfers between devices, gather_blocks(): return lax.all_to_all(spread, axis_name, 0, 0, tiled=False)  18.6 us
    all_to_all x1, blocking collectives, on_device(): lax.all_to_all(lax.dynamic_slice_in_dim(sent_rows, core_index, 1, 1), 'ex...  15.5 us
    all_to_all x1, waiting for transfers between devices, on_device(): lax.all_to_all(pair_rows, ('exp', 'shard'), 0, 0, tiled=True)  15.2 us
    all_to_all x1, blocking collectives, gather_blocks(): return lax.all_to_all(spread, axis_name, 0, 0, tiled=False)  15 us
    pallas_call x1, Pallas kernels, attend(): pl.pallas_call(functools.partial(attend_kernel, heads, head_size), out_sh...  14.9 us
    all_to_all x1, starting transfers between devices, on_device(): arrived = lax.all_to_all(packed, ('exp', 'shard'), 0, 0, tiled=True)  13.2 us
  transfers between devices with their start and end apart: 9, of which 9 were waited for; matrix products, arithmetic and copies ran while one was open for 2% of the time, Pallas kernels for 0%

profile of v13, /device:TPU:1, one launch (start us, length us, event | category | flops | bytes accessed | tf_op | source)
XLA Modules:
  0.0 212.1 jit_solution(14543393327291727087)
XLA Ops:
  0.0 0.9 compare_and_fusion
  0.9 11.4 %all_gather.6 = bf16[8,16,2304]{2,1,0:T(8,128)(2,1)S(1)} all-gather(bf16[2,16,2304]{2,1,0:T(8,128)(2,1)} %param.13), channel_id=1, replica_groups=mesh['req'=4,'exp'=8,'shard'=16] {'req'}, dimensions={0}, use_global_device_ids=true | all-gather | bytes 737280 | tf_op jit(solution)/shard_map/all_gather | solution.py:92
  12.3 0.6 dynamic-slice.4
  12.9 0.6 gather_fusion
  13.5 0.7 fusion.34
  14.1 0.8 broadcast_in_dim.64
  15.0 11.3 %all-to-all-start = ((bf16[8,1,16,2304]{3,2,1,0:T(8,128)(2,1)}), bf16[8,1,16,2304]{3,2,1,0:T(8,128)(2,1)S(1)}, u32[]{:S(2)}, u32[]{:S(2)}) async-start(bf16[8,1,16,2304]{3,2,1,0:T(8,128)(2,1)} %broadcast_in_dim.64), calls=%async_computation | async-start | bytes 1179648 | tf_op jit(solution)/shard_map/all_to_all | solution.py:62
  27.4 10.4 %all_gather.7 = bf16[8,16,2308]{2,1,0:T(8,128)(2,1)S(1)} all-gather(bf16[2,16,2308]{2,1,0:T(8,128)(2,1)S(1)} %concatenate.31), channel_id=1, replica_groups=mesh['req'=4,'exp'=8,'shard'=16] {'req'}, dimensions={0}, use_global_device_ids=true | all-gather | bytes 738560 | tf_op jit(solution)/shard_map/all_gather | solution.py:93
  37.8 0.6 gather_fusion.1
  38.9 0.8 fusion.26.mask_ref
  39.7 3.3 %all-to-all-done = bf16[8,1,16,2304]{3,2,1,0:T(8,128)(2,1)S(1)} async-done(((bf16[8,1,16,2304]{3,2,1,0:T(8,128)(2,1)}), bf16[8,1,16,2304]{3,2,1,0:T(8,128)(2,1)S(1)}, u32[]{:S(2)}, u32[]{:S(2)}) %all-to-all-start) | async-done | bytes 589856 | tf_op jit(solution)/shard_map/all_to_all | solution.py:62
  43.0 5.1 %collective-permute-start = (bf16[8,1,16,2304]{3,2,1,0:T(8,128)(2,1)S(1)}, bf16[8,1,16,2304]{3,2,1,0:T(8,128)(2,1)S(1)}, u32[]{:S(2)}, u32[]{:S(2)}) collective-permute-start(bf16[8,1,16,2304]{3,2,1,0:T(8,128)(2,1)S(1)} %all-to-all-done), channel_id=1, source_target_pairs={{0,1},{1,0},{2,3},{3,2},{4,5},{5,4},{6,7},{7,6},{8,9},{9,8},{10,11... | collective-permute-start | bytes 1769480 | tf_op jit(solution)/shard_map/ppermute | solution.py:100
  48.2 1.5 collective-permute-done
  49.7 1.1 maximum_select_fusion
  50.8 14.9 %shard_map.127 = (f32[256,2304]{1,0:T(8,128)}, f32[256,36]{1,0:T(8,128)}, f32[256,36]{1,0:T(8,128)}) custom-call(bf16[256,2304]{1,0:T(8,128)(2,1)} %bitcast.100, bf16[128,2304]{1,0:T(8,128)(2,1)} %bitcast.114, bf16[128,2304]{1,0:T(8,128)(2,1)} %bitcast.115, s32[256,128]{1,0:T(8,128)} %fusion.26.mask_ref), custom_call_target="tpu_custom_call" | custom-call | tf_op jit(solution)/shard_map/pallas_call | solution.py:48
  65.7 0.9 reduce_precision.6
  66.7 0.9 convert_element_type.135
  67.6 1.4 dynamic-slice_convert_fusion
  69.3 2.3 %collective-permute-start.1 = (bf16[8,2,16,1224]{3,2,1,0:T(8,128)(2,1)S(1)}, bf16[8,2,16,1224]{3,2,1,0:T(8,128)(2,1)S(1)}, u32[]{:S(2)}, u32[]{:S(2)}) collective-permute-start(bf16[8,2,16,1224]{3,2,1,0:T(8,128)(2,1)S(1)} %concatenate.32), channel_id=1, source_target_pairs={{0,1},{1,0},{2,3},{3,2},{4,5},{5,4},{6,7},{7,6},{8,9},{9,8},{10,11... | collective-permute-start | bytes 1880072 | tf_op jit(solution)/shard_map/ppermute | solution.py:180
  71.6 1.7 collective-permute-done.1
  73.4 0.7 fusion.21
  74.1 2.1 add_convert_fusion
  76.4 1.1 reshape.262
  77.5 13.2 %all-to-all-start.1 = ((bf16[128,2,1224]{2,1,0:T(2,128)(2,1)}), bf16[128,2,1224]{2,1,0:T(2,128)(2,1)S(1)}, u32[]{:S(2)}, u32[]{:S(2)}) async-start(bf16[128,2,1224]{2,1,0:T(2,128)(2,1)} %reshape.262), calls=%async_computation.1 | async-start | bytes 1310720 | tf_op jit(solution)/shard_map/all_to_all | solution.py:204
  91.1 23.0 %all-to-all-done.1 = bf16[128,2,1224]{2,1,0:T(2,128)(2,1)S(1)} async-done(((bf16[128,2,1224]{2,1,0:T(2,128)(2,1)}), bf16[128,2,1224]{2,1,0:T(2,128)(2,1)S(1)}, u32[]{:S(2)}, u32[]{:S(2)}) %all-to-all-start.1) | async-done | bytes 626720 | tf_op jit(solution)/shard_map/all_to_all | solution.py:204
  114.2 0.4 fusion.66
  115.0 0.5 fusion.4
  115.5 0.5 fusion.5
  116.4 0.7 broadcast_in_dim.114
  117.2 3.8 %all-to-all-start.2 = ((bf16[16,2,2304]{2,1,0:T(2,128)(2,1)}), bf16[16,2,2304]{2,1,0:T(2,128)(2,1)S(1)}, u32[]{:S(2)}, u32[]{:S(2)}) async-start(bf16[16,2,2304]{2,1,0:T(2,128)(2,1)} %broadcast_in_dim.114), calls=%async_computation.2 | async-start | bytes 294912 | tf_op jit(solution)/shard_map/all_to_all | solution.py:62
  121.4 8.9 %all-to-all-done.2 = bf16[16,2,2304]{2,1,0:T(2,128)(2,1)S(1)} async-done(((bf16[16,2,2304]{2,1,0:T(2,128)(2,1)}), bf16[16,2,2304]{2,1,0:T(2,128)(2,1)S(1)}, u32[]{:S(2)}, u32[]{:S(2)}) %all-to-all-start.2) | async-done | bytes 147488 | tf_op jit(solution)/shard_map/all_to_all | solution.py:62
  130.7 0.8 broadcast_in_dim.115
  131.4 3.4 %all-to-all-start.3 = ((bf16[16,2,16,144]{3,2,1,0:T(8,128)(2,1)}), bf16[16,2,16,144]{3,2,1,0:T(8,128)(2,1)S(1)}, u32[]{:S(2)}, u32[]{:S(2)}) async-start(bf16[16,2,16,144]{3,2,1,0:T(8,128)(2,1)} %broadcast_in_dim.115), calls=%async_computation.3 | async-start | bytes 524288 | tf_op jit(solution)/shard_map/all_to_all | solution.py:62
  134.9 11.4 %all-to-all-done.3 = bf16[16,2,16,144]{3,2,1,0:T(8,128)(2,1)S(1)} async-done(((bf16[16,2,16,144]{3,2,1,0:T(8,128)(2,1)}), bf16[16,2,16,144]{3,2,1,0:T(8,128)(2,1)S(1)}, u32[]{:S(2)}, u32[]{:S(2)}) %all-to-all-start.3) | async-done | bytes 147488 | tf_op jit(solution)/shard_map/all_to_all | solution.py:62
  147.5 15.5 %all_to_all.35 = bf16[8,1,6,2304]{3,2,1,0:T(8,128)(2,1)S(1)} all-to-all(bf16[8,1,6,2304]{3,2,1,0:T(8,128)(2,1)S(1)} %copy.69), channel_id=1, replica_groups=mesh['req'=4,'exp'=8,'shard'=16] {'exp'}, dimensions={0} | all-to-all | bytes 442368 | tf_op jit(solution)/shard_map/all_to_all | solution.py:252
  163.0 2.3 %collective-permute-start.2 = (bf16[8,1,6,2304]{3,2,1,0:T(8,128)(2,1)S(1)}, bf16[8,1,6,2304]{3,2,1,0:T(8,128)(2,1)S(1)}, u32[]{:S(2)}, u32[]{:S(2)}) collective-permute-start(bf16[8,1,6,2304]{3,2,1,0:T(8,128)(2,1)S(1)} %all_to_all.35), channel_id=1, source_target_pairs={{0,1},{1,0},{2,3},{3,2},{4,5},{5,4},{6,7},{7,6},{8,9},{9,8},{10,11... | collective-permute-start | bytes 663560 | tf_op jit(solution)/shard_map/ppermute | solution.py:259
  165.3 1.2 collective-permute-done.2
  166.9 0.6 fusion.2
  167.7 0.4 copy-done.2
  168.3 2.3 %collective-permute-start.3 = (f32[8,1,6,2304]{3,0,2,1:T(8,128)S(1)}, f32[8,1,6,2304]{3,0,2,1:T(8,128)S(1)}, u32[]{:S(2)}, u32[]{:S(2)}) collective-permute-start(f32[8,1,6,2304]{3,0,2,1:T(8,128)S(1)} %constant_dynamic-slice_fusion), channel_id=1, source_target_pairs={{0,1},{1,0},{2,3},{3,2},{4,5},{5,4},{6,7},{7,6},{8,9},{9,8},{10,11... | collective-permute-start | bytes 1327112 | tf_op jit(solution)/shard_map/ppermute | solution.py:269
  170.6 1.4 collective-permute-done.3
  172.1 0.6 reshape.265
  173.0 1.2 reshape.300
  174.2 5.5 %all-to-all-start.5 = ((bf16[128,2,432]{2,1,0:T(2,128)(2,1)}), bf16[128,2,432]{2,1,0:T(2,128)(2,1)S(1)}, u32[]{:S(2)}, u32[]{:S(2)}) async-start(bf16[128,2,432]{2,1,0:T(2,128)(2,1)} %reshape.300), calls=%async_computation.5 | async-start | bytes 524288 | tf_op jit(solution)/shard_map/all_to_all | solution.py:278
  179.9 15.2 %all-to-all-done.5 = bf16[128,2,432]{2,1,0:T(2,128)(2,1)S(1)} async-done(((bf16[128,2,432]{2,1,0:T(2,128)(2,1)}), bf16[128,2,432]{2,1,0:T(2,128)(2,1)S(1)}, u32[]{:S(2)}, u32[]{:S(2)}) %all-to-all-start.5) | async-done | bytes 221216 | tf_op jit(solution)/shard_map/all_to_all | solution.py:278
  195.1 0.5 reshape.301
  196.0 15.0 %all_to_all.36 = bf16[16,2,16,144]{3,2,1,0:T(8,128)(2,1)S(1)} all-to-all(bf16[16,2,16,144]{3,2,1,0:T(8,128)(2,1)S(1)} %broadcast_in_dim.116), channel_id=1, replica_groups=mesh['req'=4,'exp'=8,'shard'=16] {'shard'}, dimensions={0} | all-to-all | bytes 294912 | tf_op jit(solution)/shard_map/all_to_all | solution.py:62
  211.1 1.0 reshape.268
  (92 shorter events, 7.3 us)
Async XLA Ops:
  0.0 166.8 %copy-start = (bf16[1,2,180,2304]{3,1,2,0:T(2,128)(2,1)S(1)}, bf16[1,2,180,2304]{3,1,2,0:T(2,128)(2,1)}, u32[]{:S(2)}) copy-start(bf16[1,2,180,2304]{3,1,2,0:T(2,128)(2,1)} %param.24) | copy-start | bytes 4976644
  12.3 14.0 %copy-start.6 = (s32[2,16,2]{1,2,0:T(2,128)S(1)}, s32[2,16,2]{1,2,0:T(2,128)}, u32[]{:S(2)}) copy-start(s32[2,16,2]{1,2,0:T(2,128)} %param.15) | copy-start | bytes 772
  12.3 14.1 %copy-start.7 = (bf16[2,16,2]{1,2,0:T(2,128)(2,1)S(1)}, bf16[2,16,2]{1,2,0:T(2,128)(2,1)}, u32[]{:S(2)}) copy-start(bf16[2,16,2]{1,2,0:T(2,128)(2,1)} %param.16) | copy-start | bytes 388
  12.3 14.3 %copy-start.9 = (s32[1,2]{1,0:T(1,128)S(1)}, s32[1,2]{1,0:T(1,128)}, u32[]{:S(2)}) copy-start(s32[1,2]{1,0:T(1,128)} %param.18) | copy-start | bytes 28
  12.3 14.4 %copy-start.8 = (s32[1,256]{1,0:T(1,128)S(1)}, s32[1,256]{1,0:T(1,128)}, u32[]{:S(2)}) copy-start(s32[1,256]{1,0:T(1,128)} %param.19) | copy-start | bytes 3076
  12.3 15.0 %copy-start.4 = (bf16[2,16,2304]{2,1,0:T(8,128)(2,1)S(1)}, bf16[2,16,2304]{2,1,0:T(8,128)(2,1)}, u32[]{:S(2)}) copy-start(bf16[2,16,2304]{2,1,0:T(8,128)(2,1)} %param.14) | copy-start | bytes 442372
  15.0 28.0 %all-to-all-start = ((bf16[8,1,16,2304]{3,2,1,0:T(8,128)(2,1)}), bf16[8,1,16,2304]{3,2,1,0:T(8,128)(2,1)S(1)}, u32[]{:S(2)}, u32[]{:S(2)}) async-start(bf16[8,1,16,2304]{3,2,1,0:T(8,128)(2,1)} %broadcast_in_dim.64), calls=%async_computation | async-start | bytes 1179648 | tf_op jit(solution)/shard_map/all_to_all | solution.py:62
  43.0 6.7 %collective-permute-start = (bf16[8,1,16,2304]{3,2,1,0:T(8,128)(2,1)S(1)}, bf16[8,1,16,2304]{3,2,1,0:T(8,128)(2,1)S(1)}, u32[]{:S(2)}, u32[]{:S(2)}) collective-permute-start(bf16[8,1,16,2304]{3,2,1,0:T(8,128)(2,1)S(1)} %all-to-all-done), channel_id=1, source_target_pairs={{0,1},{1,0},{2,3},{3,2},{4,5},{5,4},{6,7},{7,6},{8,9},{9,8},{10,11... | collective-permute-start | bytes 1769480 | tf_op jit(solution)/shard_map/ppermute | solution.py:100
  67.6 5.7 %copy-start.1 = (f32[256,36]{1,0:T(8,128)S(1)}, f32[256,36]{1,0:T(8,128)}, u32[]{:S(2)}) copy-start(f32[256,36]{1,0:T(8,128)} %get-tuple-element.12) | copy-start | bytes 110596
  69.3 4.0 %collective-permute-start.1 = (bf16[8,2,16,1224]{3,2,1,0:T(8,128)(2,1)S(1)}, bf16[8,2,16,1224]{3,2,1,0:T(8,128)(2,1)S(1)}, u32[]{:S(2)}, u32[]{:S(2)}) collective-permute-start(bf16[8,2,16,1224]{3,2,1,0:T(8,128)(2,1)S(1)} %concatenate.32), channel_id=1, source_target_pairs={{0,1},{1,0},{2,3},{3,2},{4,5},{5,4},{6,7},{7,6},{8,9},{9,8},{10,11... | collective-permute-start | bytes 1880072 | tf_op jit(solution)/shard_map/ppermute | solution.py:180
  77.5 36.5 %all-to-all-start.1 = ((bf16[128,2,1224]{2,1,0:T(2,128)(2,1)}), bf16[128,2,1224]{2,1,0:T(2,128)(2,1)S(1)}, u32[]{:S(2)}, u32[]{:S(2)}) async-start(bf16[128,2,1224]{2,1,0:T(2,128)(2,1)} %reshape.262), calls=%async_computation.1 | async-start | bytes 1310720 | tf_op jit(solution)/shard_map/all_to_all | solution.py:204
  114.6 15.8 %copy-start.3 = (bf16[144,2304]{1,0:T(8,128)(2,1)S(1)}, bf16[144,2304]{1,0:T(8,128)(2,1)}, u32[]{:S(2)}) copy-start(bf16[144,2304]{1,0:T(8,128)(2,1)} %param.23) | copy-start | bytes 1990660
  117.2 13.1 %all-to-all-start.2 = ((bf16[16,2,2304]{2,1,0:T(2,128)(2,1)}), bf16[16,2,2304]{2,1,0:T(2,128)(2,1)S(1)}, u32[]{:S(2)}, u32[]{:S(2)}) async-start(bf16[16,2,2304]{2,1,0:T(2,128)(2,1)} %broadcast_in_dim.114), calls=%async_computation.2 | async-start | bytes 294912 | tf_op jit(solution)/shard_map/all_to_all | solution.py:62
  131.4 14.9 %all-to-all-start.3 = ((bf16[16,2,16,144]{3,2,1,0:T(8,128)(2,1)}), bf16[16,2,16,144]{3,2,1,0:T(8,128)(2,1)S(1)}, u32[]{:S(2)}, u32[]{:S(2)}) async-start(bf16[16,2,16,144]{3,2,1,0:T(8,128)(2,1)} %broadcast_in_dim.115), calls=%async_computation.3 | async-start | bytes 524288 | tf_op jit(solution)/shard_map/all_to_all | solution.py:62
  146.3 0.7 copy-start.5
  163.0 3.5 %collective-permute-start.2 = (bf16[8,1,6,2304]{3,2,1,0:T(8,128)(2,1)S(1)}, bf16[8,1,6,2304]{3,2,1,0:T(8,128)(2,1)S(1)}, u32[]{:S(2)}, u32[]{:S(2)}) collective-permute-start(bf16[8,1,6,2304]{3,2,1,0:T(8,128)(2,1)S(1)} %all_to_all.35), channel_id=1, source_target_pairs={{0,1},{1,0},{2,3},{3,2},{4,5},{5,4},{6,7},{7,6},{8,9},{9,8},{10,11... | collective-permute-start | bytes 663560 | tf_op jit(solution)/shard_map/ppermute | solution.py:259
  166.9 1.2 copy-start.2
  168.3 3.7 %collective-permute-start.3 = (f32[8,1,6,2304]{3,0,2,1:T(8,128)S(1)}, f32[8,1,6,2304]{3,0,2,1:T(8,128)S(1)}, u32[]{:S(2)}, u32[]{:S(2)}) collective-permute-start(f32[8,1,6,2304]{3,0,2,1:T(8,128)S(1)} %constant_dynamic-slice_fusion), channel_id=1, source_target_pairs={{0,1},{1,0},{2,3},{3,2},{4,5},{5,4},{6,7},{7,6},{8,9},{9,8},{10,11... | collective-permute-start | bytes 1327112 | tf_op jit(solution)/shard_map/ppermute | solution.py:269
  174.2 20.9 %all-to-all-start.5 = ((bf16[128,2,432]{2,1,0:T(2,128)(2,1)}), bf16[128,2,432]{2,1,0:T(2,128)(2,1)S(1)}, u32[]{:S(2)}, u32[]{:S(2)}) async-start(bf16[128,2,432]{2,1,0:T(2,128)(2,1)} %reshape.300), calls=%async_computation.5 | async-start | bytes 524288 | tf_op jit(solution)/shard_map/all_to_all | solution.py:278

commit v14 on v13

--- a/solution.py
+++ b/solution.py
@@ -89,8 +89,11 @@
     extras = jnp.concatenate(
         [resid_stretch, route_probs, route_ids.astype(jnp.bfloat16)], axis=2
     )
-    all_query = lax.all_gather(query_stretch, "req", axis=0, tiled=True)
-    all_extras = lax.all_gather(extras, "req", axis=0, tiled=True)
+    group_count = lax.axis_size("req")
+    all_query = gather_blocks(query_stretch, "req", group_count).reshape(
+        (-1,) + query_stretch.shape[1:]
+    )
+    all_extras = gather_blocks(extras, "req", group_count).reshape((-1,) + extras.shape[1:])
     served = lax.dynamic_slice_in_dim(request_order, group_index * members, members)
     served_query = jnp.take(all_query, served, axis=0)
     served_extras = jnp.take(all_extras, served, axis=0)

time: 213 us -> 222 us (1.042)
  waiting for transfers between devices: 67.6 us -> 90.2 us
  blocking collectives: 52.3 us -> 30.5 us
  starting transfers between devices: 49.3 us -> 55.3 us
  local copies, waits for them, and re-layouts: 14 us -> 16.7 us
    all_to_all x3 -> x5, waiting for transfers between devices: 23.6 us -> 46.2 us  [gather_blocks(): return lax.all_to_all(spread, axis_name, 0, 0, tiled=False)]
    all_gather x2 -> x0, blocking collectives: 21.8 us -> none  [the longest x1 11.4 us: on_device(): all_query = lax.all_gather(query_stretch, 'req', axis=0, tiled=True)]
    all_to_all x3 -> x5, starting transfers between devices: 18.6 us -> 28.5 us  [gather_blocks(): return lax.all_to_all(spread, axis_name, 0, 0, tiled=False)]
    all_to_all x1, starting transfers between devices: 13.2 us -> 8.82 us  [on_device(): arrived = lax.all_to_all(packed, ('exp', 'shard'), 0, 0, tiled=True)]
    broadcast_in_dim x4 -> x6, local copies, waits for them, and re-layouts: 2.4 us -> 5.14 us  [gather_blocks(): spread = jnp.broadcast_to(block[None], (count,) + block.shape)]
  transfers between devices with their start and end apart: 9 -> 11, of which waited for: 9 -> 11; matrix products, arithmetic and copies ran while one was open for 2% -> 3% of each run, Pallas kernels for 0% -> 0%
where the time goes in v14:
time: 222 us; the launch traced here: 221 us
  waiting for transfers between devices  90.2 us (41%)
  starting transfers between devices  55.3 us (25%)
  blocking collectives  30.5 us (14%)
  local copies, waits for them, and re-layouts  16.7 us (8%)
  Pallas kernels  14.9 us (7%)
  other arithmetic  6.98 us (3%)
  matrix products  5.79 us (3%)
    all_to_all x5, waiting for transfers between devices, gather_blocks(): return lax.all_to_all(spread, axis_name, 0, 0, tiled=False)  46.2 us
    all_to_all x5, starting transfers between devices, gather_blocks(): return lax.all_to_all(spread, axis_name, 0, 0, tiled=False)  28.5 us
    all_to_all x1, waiting for transfers between devices, on_device(): arrived = lax.all_to_all(packed, ('exp', 'shard'), 0, 0, tiled=True)  23 us
    all_to_all x1, blocking collectives, on_device(): lax.all_to_all(lax.dynamic_slice_in_dim(sent_rows, core_index, 1, 1), 'ex...  15.5 us
    all_to_all x1, waiting for transfers between devices, on_device(): lax.all_to_all(pair_rows, ('exp', 'shard'), 0, 0, tiled=True)  15.2 us
    all_to_all x1, blocking collectives, gather_blocks(): return lax.all_to_all(spread, axis_name, 0, 0, tiled=False)  15 us
    pallas_call x1, Pallas kernels, attend(): pl.pallas_call(functools.partial(attend_kernel, heads, head_size), out_sh...  14.9 us
    all_to_all x1, starting transfers between devices, on_device(): arrived = lax.all_to_all(packed, ('exp', 'shard'), 0, 0, tiled=True)  8.82 us
  transfers between devices with their start and end apart: 11, of which 11 were waited for; matrix products, arithmetic and copies ran while one was open for 3% of the time, Pallas kernels for 0%

profile of v14, /device:TPU:1, one launch (start us, length us, event | category | flops | bytes accessed | tf_op | source)
XLA Modules:
  0.0 221.0 jit_solution(7928078421812172516)
XLA Ops:
  0.1 1.9 broadcast_in_dim.65
  1.9 4.8 %all-to-all-start = ((bf16[4,2,16,2304]{3,2,1,0:T(8,128)(2,1)}), bf16[4,2,16,2304]{3,2,1,0:T(8,128)(2,1)S(1)}, u32[]{:S(2)}, u32[]{:S(2)}) async-start(bf16[4,2,16,2304]{3,2,1,0:T(8,128)(2,1)} %broadcast_in_dim.65), calls=%async_computation | async-start | bytes 1179648 | tf_op jit(solution)/shard_map/all_to_all | solution.py:62
  7.3 0.6 dynamic-slice.4
  8.5 5.5 %all-to-all-done = bf16[4,2,16,2304]{3,2,1,0:T(8,128)(2,1)S(1)} async-done(((bf16[4,2,16,2304]{3,2,1,0:T(8,128)(2,1)}), bf16[4,2,16,2304]{3,2,1,0:T(8,128)(2,1)S(1)}, u32[]{:S(2)}, u32[]{:S(2)}) %all-to-all-start) | async-done | bytes 589856 | tf_op jit(solution)/shard_map/all_to_all | solution.py:62
  14.1 0.9 broadcast_in_dim.71
  14.9 3.5 %all-to-all-start.2 = ((bf16[4,2,16,2308]{3,2,1,0:T(8,128)(2,1)}), bf16[4,2,16,2308]{3,2,1,0:T(8,128)(2,1)S(1)}, u32[]{:S(2)}, u32[]{:S(2)}) async-start(bf16[4,2,16,2308]{3,2,1,0:T(8,128)(2,1)} %broadcast_in_dim.71), calls=%async_computation.2 | async-start | bytes 1245184 | tf_op jit(solution)/shard_map/all_to_all | solution.py:62
  18.4 0.6 gather_fusion
  19.0 0.7 fusion.34
  19.7 6.2 %all-to-all-done.2 = bf16[4,2,16,2308]{3,2,1,0:T(8,128)(2,1)S(1)} async-done(((bf16[4,2,16,2308]{3,2,1,0:T(8,128)(2,1)}), bf16[4,2,16,2308]{3,2,1,0:T(8,128)(2,1)S(1)}, u32[]{:S(2)}, u32[]{:S(2)}) %all-to-all-start.2) | async-done | bytes 590880 | tf_op jit(solution)/shard_map/all_to_all | solution.py:62
  25.8 0.8 broadcast_in_dim.69
  26.7 13.0 %all-to-all-start.1 = ((bf16[8,1,16,2304]{3,2,1,0:T(8,128)(2,1)}), bf16[8,1,16,2304]{3,2,1,0:T(8,128)(2,1)S(1)}, u32[]{:S(2)}, u32[]{:S(2)}) async-start(bf16[8,1,16,2304]{3,2,1,0:T(8,128)(2,1)} %broadcast_in_dim.69), calls=%async_computation.1 | async-start | bytes 1179648 | tf_op jit(solution)/shard_map/all_to_all | solution.py:62
  40.2 0.8 fusion.26.mask_ref
  41.0 0.6 gather_fusion.1
  41.6 14.2 %all-to-all-done.1 = bf16[8,1,16,2304]{3,2,1,0:T(8,128)(2,1)S(1)} async-done(((bf16[8,1,16,2304]{3,2,1,0:T(8,128)(2,1)}), bf16[8,1,16,2304]{3,2,1,0:T(8,128)(2,1)S(1)}, u32[]{:S(2)}, u32[]{:S(2)}) %all-to-all-start.1) | async-done | bytes 589856 | tf_op jit(solution)/shard_map/all_to_all | solution.py:62
  55.8 5.6 %collective-permute-start = (bf16[8,1,16,2304]{3,2,1,0:T(8,128)(2,1)S(1)}, bf16[8,1,16,2304]{3,2,1,0:T(8,128)(2,1)S(1)}, u32[]{:S(2)}, u32[]{:S(2)}) collective-permute-start(bf16[8,1,16,2304]{3,2,1,0:T(8,128)(2,1)S(1)} %all-to-all-done.1), channel_id=1, source_target_pairs={{0,1},{1,0},{2,3},{3,2},{4,5},{5,4},{6,7},{7,6},{8,9},{9,8},{10,11... | collective-permute-start | bytes 1769480 | tf_op jit(solution)/shard_map/ppermute | solution.py:103
  61.5 1.5 collective-permute-done
  63.0 1.1 maximum_select_fusion
  64.1 14.9 %shard_map.127 = (f32[256,2304]{1,0:T(8,128)}, f32[256,36]{1,0:T(8,128)}, f32[256,36]{1,0:T(8,128)}) custom-call(bf16[256,2304]{1,0:T(8,128)(2,1)} %bitcast.102, bf16[128,2304]{1,0:T(8,128)(2,1)} %bitcast.118, bf16[128,2304]{1,0:T(8,128)(2,1)} %bitcast.119, s32[256,128]{1,0:T(8,128)} %fusion.26.mask_ref), custom_call_target="tpu_custom_call" | custom-call | tf_op jit(solution)/shard_map/pallas_call | solution.py:48
  79.1 0.9 reduce_precision.6
  80.0 0.9 convert_element_type.135
  80.9 1.4 dynamic-slice_convert_fusion
  82.6 2.3 %collective-permute-start.1 = (bf16[8,2,16,1224]{3,2,1,0:T(8,128)(2,1)S(1)}, bf16[8,2,16,1224]{3,2,1,0:T(8,128)(2,1)S(1)}, u32[]{:S(2)}, u32[]{:S(2)}) collective-permute-start(bf16[8,2,16,1224]{3,2,1,0:T(8,128)(2,1)S(1)} %concatenate.32), channel_id=1, source_target_pairs={{0,1},{1,0},{2,3},{3,2},{4,5},{5,4},{6,7},{7,6},{8,9},{9,8},{10,11... | collective-permute-start | bytes 1880072 | tf_op jit(solution)/shard_map/ppermute | solution.py:183
  84.9 1.7 collective-permute-done.1
  86.7 0.7 fusion.21
  87.4 2.1 add_convert_fusion
  89.8 1.1 reshape.272
  90.9 8.8 %all-to-all-start.3 = ((bf16[128,2,1224]{2,1,0:T(2,128)(2,1)}), bf16[128,2,1224]{2,1,0:T(2,128)(2,1)S(1)}, u32[]{:S(2)}, u32[]{:S(2)}) async-start(bf16[128,2,1224]{2,1,0:T(2,128)(2,1)} %reshape.272), calls=%async_computation.3 | async-start | bytes 1310720 | tf_op jit(solution)/shard_map/all_to_all | solution.py:207
  100.0 23.0 %all-to-all-done.3 = bf16[128,2,1224]{2,1,0:T(2,128)(2,1)S(1)} async-done(((bf16[128,2,1224]{2,1,0:T(2,128)(2,1)}), bf16[128,2,1224]{2,1,0:T(2,128)(2,1)S(1)}, u32[]{:S(2)}, u32[]{:S(2)}) %all-to-all-start.3) | async-done | bytes 626720 | tf_op jit(solution)/shard_map/all_to_all | solution.py:207
  123.9 0.5 fusion.4
  124.4 0.5 fusion.5
  125.3 0.7 broadcast_in_dim.128
  126.1 3.8 %all-to-all-start.4 = ((bf16[16,2,2304]{2,1,0:T(2,128)(2,1)}), bf16[16,2,2304]{2,1,0:T(2,128)(2,1)S(1)}, u32[]{:S(2)}, u32[]{:S(2)}) async-start(bf16[16,2,2304]{2,1,0:T(2,128)(2,1)} %broadcast_in_dim.128), calls=%async_computation.4 | async-start | bytes 294912 | tf_op jit(solution)/shard_map/all_to_all | solution.py:62
  130.3 8.9 %all-to-all-done.4 = bf16[16,2,2304]{2,1,0:T(2,128)(2,1)S(1)} async-done(((bf16[16,2,2304]{2,1,0:T(2,128)(2,1)}), bf16[16,2,2304]{2,1,0:T(2,128)(2,1)S(1)}, u32[]{:S(2)}, u32[]{:S(2)}) %all-to-all-start.4) | async-done | bytes 147488 | tf_op jit(solution)/shard_map/all_to_all | solution.py:62
  139.6 0.8 broadcast_in_dim.129
  140.3 3.4 %all-to-all-start.5 = ((bf16[16,2,16,144]{3,2,1,0:T(8,128)(2,1)}), bf16[16,2,16,144]{3,2,1,0:T(8,128)(2,1)S(1)}, u32[]{:S(2)}, u32[]{:S(2)}) async-start(bf16[16,2,16,144]{3,2,1,0:T(8,128)(2,1)} %broadcast_in_dim.129), calls=%async_computation.5 | async-start | bytes 524288 | tf_op jit(solution)/shard_map/all_to_all | solution.py:62
  143.8 11.4 %all-to-all-done.5 = bf16[16,2,16,144]{3,2,1,0:T(8,128)(2,1)S(1)} async-done(((bf16[16,2,16,144]{3,2,1,0:T(8,128)(2,1)}), bf16[16,2,16,144]{3,2,1,0:T(8,128)(2,1)S(1)}, u32[]{:S(2)}, u32[]{:S(2)}) %all-to-all-start.5) | async-done | bytes 147488 | tf_op jit(solution)/shard_map/all_to_all | solution.py:62
  156.4 15.5 %all_to_all.45 = bf16[8,1,6,2304]{3,2,1,0:T(8,128)(2,1)S(1)} all-to-all(bf16[8,1,6,2304]{3,2,1,0:T(8,128)(2,1)S(1)} %copy.69), channel_id=1, replica_groups=mesh['req'=4,'exp'=8,'shard'=16] {'exp'}, dimensions={0} | all-to-all | bytes 442368 | tf_op jit(solution)/shard_map/all_to_all | solution.py:255
  171.9 2.3 %collective-permute-start.2 = (bf16[8,1,6,2304]{3,2,1,0:T(8,128)(2,1)S(1)}, bf16[8,1,6,2304]{3,2,1,0:T(8,128)(2,1)S(1)}, u32[]{:S(2)}, u32[]{:S(2)}) collective-permute-start(bf16[8,1,6,2304]{3,2,1,0:T(8,128)(2,1)S(1)} %all_to_all.45), channel_id=1, source_target_pairs={{0,1},{1,0},{2,3},{3,2},{4,5},{5,4},{6,7},{7,6},{8,9},{9,8},{10,11... | collective-permute-start | bytes 663560 | tf_op jit(solution)/shard_map/ppermute | solution.py:262
  174.2 1.2 collective-permute-done.2
  175.8 0.6 fusion.2
  177.3 2.3 %collective-permute-start.3 = (f32[8,1,6,2304]{3,0,2,1:T(8,128)S(1)}, f32[8,1,6,2304]{3,0,2,1:T(8,128)S(1)}, u32[]{:S(2)}, u32[]{:S(2)}) collective-permute-start(f32[8,1,6,2304]{3,0,2,1:T(8,128)S(1)} %constant_dynamic-slice_fusion), channel_id=1, source_target_pairs={{0,1},{1,0},{2,3},{3,2},{4,5},{5,4},{6,7},{7,6},{8,9},{9,8},{10,11... | collective-permute-start | bytes 1327112 | tf_op jit(solution)/shard_map/ppermute | solution.py:272
  179.6 1.4 collective-permute-done.3
  181.0 0.6 reshape.275
  181.9 1.2 reshape.310
  183.1 5.5 %all-to-all-start.7 = ((bf16[128,2,432]{2,1,0:T(2,128)(2,1)}), bf16[128,2,432]{2,1,0:T(2,128)(2,1)S(1)}, u32[]{:S(2)}, u32[]{:S(2)}) async-start(bf16[128,2,432]{2,1,0:T(2,128)(2,1)} %reshape.310), calls=%async_computation.7 | async-start | bytes 524288 | tf_op jit(solution)/shard_map/all_to_all | solution.py:281
  188.8 15.2 %all-to-all-done.7 = bf16[128,2,432]{2,1,0:T(2,128)(2,1)S(1)} async-done(((bf16[128,2,432]{2,1,0:T(2,128)(2,1)}), bf16[128,2,432]{2,1,0:T(2,128)(2,1)S(1)}, u32[]{:S(2)}, u32[]{:S(2)}) %all-to-all-start.7) | async-done | bytes 221216 | tf_op jit(solution)/shard_map/all_to_all | solution.py:281
  204.9 15.0 %all_to_all.46 = bf16[16,2,16,144]{3,2,1,0:T(8,128)(2,1)S(1)} all-to-all(bf16[16,2,16,144]{3,2,1,0:T(8,128)(2,1)S(1)} %broadcast_in_dim.130), channel_id=1, replica_groups=mesh['req'=4,'exp'=8,'shard'=16] {'shard'}, dimensions={0} | all-to-all | bytes 294912 | tf_op jit(solution)/shard_map/all_to_all | solution.py:62
  220.0 1.0 reshape.278
  (98 shorter events, 8.6 us)
Async XLA Ops:
  0.0 175.8 %copy-start = (bf16[1,2,180,2304]{3,1,2,0:T(2,128)(2,1)S(1)}, bf16[1,2,180,2304]{3,1,2,0:T(2,128)(2,1)}, u32[]{:S(2)}) copy-start(bf16[1,2,180,2304]{3,1,2,0:T(2,128)(2,1)} %param.24) | copy-start | bytes 4976644
  0.0 6.8 %copy-start.6 = (s32[2,16,2]{1,2,0:T(2,128)S(1)}, s32[2,16,2]{1,2,0:T(2,128)}, u32[]{:S(2)}) copy-start(s32[2,16,2]{1,2,0:T(2,128)} %param.15) | copy-start | bytes 772
  0.0 6.9 %copy-start.7 = (bf16[2,16,2]{1,2,0:T(2,128)(2,1)S(1)}, bf16[2,16,2]{1,2,0:T(2,128)(2,1)}, u32[]{:S(2)}) copy-start(bf16[2,16,2]{1,2,0:T(2,128)(2,1)} %param.16) | copy-start | bytes 388
  0.0 7.0 %copy-start.10 = (s32[1,2]{1,0:T(1,128)S(1)}, s32[1,2]{1,0:T(1,128)}, u32[]{:S(2)}) copy-start(s32[1,2]{1,0:T(1,128)} %param.18) | copy-start | bytes 28
  0.0 7.2 %copy-start.9 = (s32[8]{0:T(128)S(1)}, s32[8]{0:T(128)}, u32[]{:S(2)}) copy-start(s32[8]{0:T(128)} %param.17) | copy-start | bytes 100
  0.0 7.8 %copy-start.8 = (s32[1,256]{1,0:T(1,128)S(1)}, s32[1,256]{1,0:T(1,128)}, u32[]{:S(2)}) copy-start(s32[1,256]{1,0:T(1,128)} %param.19) | copy-start | bytes 3076
  0.0 8.0 %copy-start.4 = (bf16[2,16,2304]{2,1,0:T(8,128)(2,1)S(1)}, bf16[2,16,2304]{2,1,0:T(8,128)(2,1)}, u32[]{:S(2)}) copy-start(bf16[2,16,2304]{2,1,0:T(8,128)(2,1)} %param.14) | copy-start | bytes 442372
  1.9 12.1 %all-to-all-start = ((bf16[4,2,16,2304]{3,2,1,0:T(8,128)(2,1)}), bf16[4,2,16,2304]{3,2,1,0:T(8,128)(2,1)S(1)}, u32[]{:S(2)}, u32[]{:S(2)}) async-start(bf16[4,2,16,2304]{3,2,1,0:T(8,128)(2,1)} %broadcast_in_dim.65), calls=%async_computation | async-start | bytes 1179648 | tf_op jit(solution)/shard_map/all_to_all | solution.py:62
  14.9 10.9 %all-to-all-start.2 = ((bf16[4,2,16,2308]{3,2,1,0:T(8,128)(2,1)}), bf16[4,2,16,2308]{3,2,1,0:T(8,128)(2,1)S(1)}, u32[]{:S(2)}, u32[]{:S(2)}) async-start(bf16[4,2,16,2308]{3,2,1,0:T(8,128)(2,1)} %broadcast_in_dim.71), calls=%async_computation.2 | async-start | bytes 1245184 | tf_op jit(solution)/shard_map/all_to_all | solution.py:62
  26.7 29.1 %all-to-all-start.1 = ((bf16[8,1,16,2304]{3,2,1,0:T(8,128)(2,1)}), bf16[8,1,16,2304]{3,2,1,0:T(8,128)(2,1)S(1)}, u32[]{:S(2)}, u32[]{:S(2)}) async-start(bf16[8,1,16,2304]{3,2,1,0:T(8,128)(2,1)} %broadcast_in_dim.69), calls=%async_computation.1 | async-start | bytes 1179648 | tf_op jit(solution)/shard_map/all_to_all | solution.py:62
  55.8 7.2 %collective-permute-start = (bf16[8,1,16,2304]{3,2,1,0:T(8,128)(2,1)S(1)}, bf16[8,1,16,2304]{3,2,1,0:T(8,128)(2,1)S(1)}, u32[]{:S(2)}, u32[]{:S(2)}) collective-permute-start(bf16[8,1,16,2304]{3,2,1,0:T(8,128)(2,1)S(1)} %all-to-all-done.1), channel_id=1, source_target_pairs={{0,1},{1,0},{2,3},{3,2},{4,5},{5,4},{6,7},{7,6},{8,9},{9,8},{10,11... | collective-permute-start | bytes 1769480 | tf_op jit(solution)/shard_map/ppermute | solution.py:103
  80.9 5.7 %copy-start.1 = (f32[256,36]{1,0:T(8,128)S(1)}, f32[256,36]{1,0:T(8,128)}, u32[]{:S(2)}) copy-start(f32[256,36]{1,0:T(8,128)} %get-tuple-element.12) | copy-start | bytes 110596
  82.6 4.0 %collective-permute-start.1 = (bf16[8,2,16,1224]{3,2,1,0:T(8,128)(2,1)S(1)}, bf16[8,2,16,1224]{3,2,1,0:T(8,128)(2,1)S(1)}, u32[]{:S(2)}, u32[]{:S(2)}) collective-permute-start(bf16[8,2,16,1224]{3,2,1,0:T(8,128)(2,1)S(1)} %concatenate.32), channel_id=1, source_target_pairs={{0,1},{1,0},{2,3},{3,2},{4,5},{5,4},{6,7},{7,6},{8,9},{9,8},{10,11... | collective-permute-start | bytes 1880072 | tf_op jit(solution)/shard_map/ppermute | solution.py:183
  90.9 32.1 %all-to-all-start.3 = ((bf16[128,2,1224]{2,1,0:T(2,128)(2,1)}), bf16[128,2,1224]{2,1,0:T(2,128)(2,1)S(1)}, u32[]{:S(2)}, u32[]{:S(2)}) async-start(bf16[128,2,1224]{2,1,0:T(2,128)(2,1)} %reshape.272), calls=%async_computation.3 | async-start | bytes 1310720 | tf_op jit(solution)/shard_map/all_to_all | solution.py:207
  123.5 15.8 %copy-start.3 = (bf16[144,2304]{1,0:T(8,128)(2,1)S(1)}, bf16[144,2304]{1,0:T(8,128)(2,1)}, u32[]{:S(2)}) copy-start(bf16[144,2304]{1,0:T(8,128)(2,1)} %param.23) | copy-start | bytes 1990660
  126.1 13.1 %all-to-all-start.4 = ((bf16[16,2,2304]{2,1,0:T(2,128)(2,1)}), bf16[16,2,2304]{2,1,0:T(2,128)(2,1)S(1)}, u32[]{:S(2)}, u32[]{:S(2)}) async-start(bf16[16,2,2304]{2,1,0:T(2,128)(2,1)} %broadcast_in_dim.128), calls=%async_computation.4 | async-start | bytes 294912 | tf_op jit(solution)/shard_map/all_to_all | solution.py:62
  140.3 14.9 %all-to-all-start.5 = ((bf16[16,2,16,144]{3,2,1,0:T(8,128)(2,1)}), bf16[16,2,16,144]{3,2,1,0:T(8,128)(2,1)S(1)}, u32[]{:S(2)}, u32[]{:S(2)}) async-start(bf16[16,2,16,144]{3,2,1,0:T(8,128)(2,1)} %broadcast_in_dim.129), calls=%async_computation.5 | async-start | bytes 524288 | tf_op jit(solution)/shard_map/all_to_all | solution.py:62
  155.3 0.7 copy-start.5
  171.9 3.5 %collective-permute-start.2 = (bf16[8,1,6,2304]{3,2,1,0:T(8,128)(2,1)S(1)}, bf16[8,1,6,2304]{3,2,1,0:T(8,128)(2,1)S(1)}, u32[]{:S(2)}, u32[]{:S(2)}) collective-permute-start(bf16[8,1,6,2304]{3,2,1,0:T(8,128)(2,1)S(1)} %all_to_all.45), channel_id=1, source_target_pairs={{0,1},{1,0},{2,3},{3,2},{4,5},{5,4},{6,7},{7,6},{8,9},{9,8},{10,11... | collective-permute-start | bytes 663560 | tf_op jit(solution)/shard_map/ppermute | solution.py:262
  175.8 1.2 copy-start.2
  177.3 3.7 %collective-permute-start.3 = (f32[8,1,6,2304]{3,0,2,1:T(8,128)S(1)}, f32[8,1,6,2304]{3,0,2,1:T(8,128)S(1)}, u32[]{:S(2)}, u32[]{:S(2)}) collective-permute-start(f32[8,1,6,2304]{3,0,2,1:T(8,128)S(1)} %constant_dynamic-slice_fusion), channel_id=1, source_target_pairs={{0,1},{1,0},{2,3},{3,2},{4,5},{5,4},{6,7},{7,6},{8,9},{9,8},{10,11... | collective-permute-start | bytes 1327112 | tf_op jit(solution)/shard_map/ppermute | solution.py:272
  183.1 20.9 %all-to-all-start.7 = ((bf16[128,2,432]{2,1,0:T(2,128)(2,1)}), bf16[128,2,432]{2,1,0:T(2,128)(2,1)S(1)}, u32[]{:S(2)}, u32[]{:S(2)}) async-start(bf16[128,2,432]{2,1,0:T(2,128)(2,1)} %reshape.310), calls=%async_computation.7 | async-start | bytes 524288 | tf_op jit(solution)/shard_map/all_to_all | solution.py:281

commit v15 on v13

--- a/solution.py
+++ b/solution.py
@@ -31,8 +31,7 @@
     for h in range(heads):
         cols = slice(h * head_size, (h + 1) * head_size)
         q_h = q_ref[:, cols]
-        k_h = k_ref[:, cols]
-        s = lax.dot_general(q_h, k_h, (((1,), (1,)), ((), ())), preferred_element_type=jnp.float32)
+        s = jnp.dot(q_h, k_ref[cols, :], preferred_element_type=jnp.float32)
         s = jnp.where(vis, s * (1.0 / math.sqrt(head_size)), NEG_FILL)
         m = jnp.max(s, axis=1, keepdims=True).astype(jnp.bfloat16).astype(jnp.float32)
         w = jnp.where(vis, jnp.exp(s - m), 0.0).astype(jnp.bfloat16)
@@ -143,7 +142,7 @@
     attend_rows = experts_count * members * tokens_here
     context, peak_rows, total_rows = attend(
         group_query.reshape(attend_rows, width),
-        key_pool[0].reshape(keys_here, width),
+        jnp.transpose(key_pool[0].reshape(keys_here, width)),
         value_pool[0].reshape(keys_here, width),
         visible.reshape(attend_rows, keys_here).astype(jnp.int32),
         H,

time: 213 us -> 215 us (level)
  waiting for transfers between devices: 67.6 us -> 65.4 us
  transfers between devices with their start and end apart: 9 -> 9, of which waited for: 9 -> 9; matrix products, arithmetic and copies ran while one was open for 2% -> 3% of each run, Pallas kernels for 0% -> 0%
where the time goes in v15:
time: 215 us; the launch traced here: 214 us
  waiting for transfers between devices  65.4 us (30%)
  blocking collectives  52.3 us (24%)
  starting transfers between devices  51.4 us (24%)
  local copies, waits for them, and re-layouts  16.1 us (7%)
  Pallas kernels  14.6 us (7%)
  other arithmetic  7.79 us (4%)
  matrix products  5.79 us (3%)
    all_to_all x1, waiting for transfers between devices, on_device(): arrived = lax.all_to_all(packed, ('exp', 'shard'), 0, 0, tiled=True)  23 us
    all_to_all x3, waiting for transfers between devices, gather_blocks(): return lax.all_to_all(spread, axis_name, 0, 0, tiled=False)  21.4 us
    all_to_all x3, starting transfers between devices, gather_blocks(): return lax.all_to_all(spread, axis_name, 0, 0, tiled=False)  18.5 us
    all_to_all x1, blocking collectives, on_device(): lax.all_to_all(lax.dynamic_slice_in_dim(sent_rows, core_index, 1, 1), 'ex...  15.5 us
    all_to_all x1, waiting for transfers between devices, on_device(): lax.all_to_all(pair_rows, ('exp', 'shard'), 0, 0, tiled=True)  15.2 us
    all_to_all x1, blocking collectives, gather_blocks(): return lax.all_to_all(spread, axis_name, 0, 0, tiled=False)  15 us
    pallas_call x1, Pallas kernels, attend(): pl.pallas_call(functools.partial(attend_kernel, heads, head_size), out_sh...  14.6 us
    all_to_all x1, starting transfers between devices, on_device(): arrived = lax.all_to_all(packed, ('exp', 'shard'), 0, 0, tiled=True)  14.2 us
  transfers between devices with their start and end apart: 9, of which 9 were waited for; matrix products, arithmetic and copies ran while one was open for 3% of the time, Pallas kernels for 0%

profile of v15, /device:TPU:1, one launch (start us, length us, event | category | flops | bytes accessed | tf_op | source)
XLA Modules:
  0.0 213.9 jit_solution(9232538536327564397)
XLA Ops:
  0.0 0.9 compare_and_fusion
  0.9 11.4 %all_gather.6 = bf16[8,16,2304]{2,1,0:T(8,128)(2,1)S(1)} all-gather(bf16[2,16,2304]{2,1,0:T(8,128)(2,1)} %param.13), channel_id=1, replica_groups=mesh['req'=4,'exp'=8,'shard'=16] {'req'}, dimensions={0}, use_global_device_ids=true | all-gather | bytes 737280 | tf_op jit(solution)/shard_map/all_gather | solution.py:91
  12.3 0.6 dynamic-slice.4
  12.9 0.6 gather_fusion
  13.5 0.7 fusion.34
  14.1 0.8 broadcast_in_dim.64
  15.0 11.3 %all-to-all-start = ((bf16[8,1,16,2304]{3,2,1,0:T(8,128)(2,1)}), bf16[8,1,16,2304]{3,2,1,0:T(8,128)(2,1)S(1)}, u32[]{:S(2)}, u32[]{:S(2)}) async-start(bf16[8,1,16,2304]{3,2,1,0:T(8,128)(2,1)} %broadcast_in_dim.64), calls=%async_computation | async-start | bytes 1179648 | tf_op jit(solution)/shard_map/all_to_all | solution.py:61
  27.4 10.4 %all_gather.7 = bf16[8,16,2308]{2,1,0:T(8,128)(2,1)S(1)} all-gather(bf16[2,16,2308]{2,1,0:T(8,128)(2,1)S(1)} %concatenate.31), channel_id=1, replica_groups=mesh['req'=4,'exp'=8,'shard'=16] {'req'}, dimensions={0}, use_global_device_ids=true | all-gather | bytes 738560 | tf_op jit(solution)/shard_map/all_gather | solution.py:92
  37.8 0.6 gather_fusion.1
  38.9 2.1 copy.65
  41.0 0.8 fusion.26.mask_ref
  41.8 1.2 all-to-all-done
  43.0 6.3 %collective-permute-start = (bf16[8,1,16,2304]{3,2,1,0:T(8,128)(2,1)S(1)}, bf16[8,1,16,2304]{3,2,1,0:T(8,128)(2,1)S(1)}, u32[]{:S(2)}, u32[]{:S(2)}) collective-permute-start(bf16[8,1,16,2304]{3,2,1,0:T(8,128)(2,1)S(1)} %all-to-all-done), channel_id=1, source_target_pairs={{0,1},{1,0},{2,3},{3,2},{4,5},{5,4},{6,7},{7,6},{8,9},{9,8},{10,11... | collective-permute-start | bytes 1769480 | tf_op jit(solution)/shard_map/ppermute | solution.py:99
  49.3 1.5 collective-permute-done
  50.9 1.1 maximum_select_fusion
  52.0 14.6 %shard_map.127 = (f32[256,2304]{1,0:T(8,128)}, f32[256,36]{1,0:T(8,128)}, f32[256,36]{1,0:T(8,128)}) custom-call(bf16[256,2304]{1,0:T(8,128)(2,1)} %bitcast.101, bf16[2304,128]{1,0:T(8,128)(2,1)} %bitcast.104, bf16[128,2304]{1,0:T(8,128)(2,1)} %bitcast.116, s32[256,128]{1,0:T(8,128)} %fusion.26.mask_ref), custom_call_target="tpu_custom_call" | custom-call | tf_op jit(solution)/shard_map/pallas_call | solution.py:47
  66.6 0.9 reduce_precision.6
  67.5 0.9 convert_element_type.135
  68.5 1.4 dynamic-slice_convert_fusion
  70.1 2.3 %collective-permute-start.1 = (bf16[8,2,16,1224]{3,2,1,0:T(8,128)(2,1)S(1)}, bf16[8,2,16,1224]{3,2,1,0:T(8,128)(2,1)S(1)}, u32[]{:S(2)}, u32[]{:S(2)}) collective-permute-start(bf16[8,2,16,1224]{3,2,1,0:T(8,128)(2,1)S(1)} %concatenate.32), channel_id=1, source_target_pairs={{0,1},{1,0},{2,3},{3,2},{4,5},{5,4},{6,7},{7,6},{8,9},{9,8},{10,11... | collective-permute-start | bytes 1880072 | tf_op jit(solution)/shard_map/ppermute | solution.py:179
  72.4 1.7 collective-permute-done.1
  74.2 0.7 fusion.21
  74.9 2.1 add_convert_fusion
  77.3 1.1 reshape.262
  78.4 14.2 %all-to-all-start.1 = ((bf16[128,2,1224]{2,1,0:T(2,128)(2,1)}), bf16[128,2,1224]{2,1,0:T(2,128)(2,1)S(1)}, u32[]{:S(2)}, u32[]{:S(2)}) async-start(bf16[128,2,1224]{2,1,0:T(2,128)(2,1)} %reshape.262), calls=%async_computation.1 | async-start | bytes 1310720 | tf_op jit(solution)/shard_map/all_to_all | solution.py:203
  92.9 23.0 %all-to-all-done.1 = bf16[128,2,1224]{2,1,0:T(2,128)(2,1)S(1)} async-done(((bf16[128,2,1224]{2,1,0:T(2,128)(2,1)}), bf16[128,2,1224]{2,1,0:T(2,128)(2,1)S(1)}, u32[]{:S(2)}, u32[]{:S(2)}) %all-to-all-start.1) | async-done | bytes 626720 | tf_op jit(solution)/shard_map/all_to_all | solution.py:203
  116.0 0.4 fusion.66
  116.8 0.5 fusion.4
  117.3 0.5 fusion.5
  118.2 0.7 broadcast_in_dim.114
  118.9 3.8 %all-to-all-start.2 = ((bf16[16,2,2304]{2,1,0:T(2,128)(2,1)}), bf16[16,2,2304]{2,1,0:T(2,128)(2,1)S(1)}, u32[]{:S(2)}, u32[]{:S(2)}) async-start(bf16[16,2,2304]{2,1,0:T(2,128)(2,1)} %broadcast_in_dim.114), calls=%async_computation.2 | async-start | bytes 294912 | tf_op jit(solution)/shard_map/all_to_all | solution.py:61
  123.2 8.9 %all-to-all-done.2 = bf16[16,2,2304]{2,1,0:T(2,128)(2,1)S(1)} async-done(((bf16[16,2,2304]{2,1,0:T(2,128)(2,1)}), bf16[16,2,2304]{2,1,0:T(2,128)(2,1)S(1)}, u32[]{:S(2)}, u32[]{:S(2)}) %all-to-all-start.2) | async-done | bytes 147488 | tf_op jit(solution)/shard_map/all_to_all | solution.py:61
  132.4 0.8 broadcast_in_dim.115
  133.2 3.4 %all-to-all-start.3 = ((bf16[16,2,16,144]{3,2,1,0:T(8,128)(2,1)}), bf16[16,2,16,144]{3,2,1,0:T(8,128)(2,1)S(1)}, u32[]{:S(2)}, u32[]{:S(2)}) async-start(bf16[16,2,16,144]{3,2,1,0:T(8,128)(2,1)} %broadcast_in_dim.115), calls=%async_computation.3 | async-start | bytes 524288 | tf_op jit(solution)/shard_map/all_to_all | solution.py:61
  136.7 11.4 %all-to-all-done.3 = bf16[16,2,16,144]{3,2,1,0:T(8,128)(2,1)S(1)} async-done(((bf16[16,2,16,144]{3,2,1,0:T(8,128)(2,1)}), bf16[16,2,16,144]{3,2,1,0:T(8,128)(2,1)S(1)}, u32[]{:S(2)}, u32[]{:S(2)}) %all-to-all-start.3) | async-done | bytes 147488 | tf_op jit(solution)/shard_map/all_to_all | solution.py:61
  149.3 15.5 %all_to_all.35 = bf16[8,1,6,2304]{3,2,1,0:T(8,128)(2,1)S(1)} all-to-all(bf16[8,1,6,2304]{3,2,1,0:T(8,128)(2,1)S(1)} %copy.74), channel_id=1, replica_groups=mesh['req'=4,'exp'=8,'shard'=16] {'exp'}, dimensions={0} | all-to-all | bytes 442368 | tf_op jit(solution)/shard_map/all_to_all | solution.py:251
  164.8 2.3 %collective-permute-start.2 = (bf16[8,1,6,2304]{3,2,1,0:T(8,128)(2,1)S(1)}, bf16[8,1,6,2304]{3,2,1,0:T(8,128)(2,1)S(1)}, u32[]{:S(2)}, u32[]{:S(2)}) collective-permute-start(bf16[8,1,6,2304]{3,2,1,0:T(8,128)(2,1)S(1)} %all_to_all.35), channel_id=1, source_target_pairs={{0,1},{1,0},{2,3},{3,2},{4,5},{5,4},{6,7},{7,6},{8,9},{9,8},{10,11... | collective-permute-start | bytes 663560 | tf_op jit(solution)/shard_map/ppermute | solution.py:258
  167.1 1.2 collective-permute-done.2
  168.7 0.6 fusion.2
  170.1 2.3 %collective-permute-start.3 = (f32[8,1,6,2304]{3,0,2,1:T(8,128)S(1)}, f32[8,1,6,2304]{3,0,2,1:T(8,128)S(1)}, u32[]{:S(2)}, u32[]{:S(2)}) collective-permute-start(f32[8,1,6,2304]{3,0,2,1:T(8,128)S(1)} %constant_dynamic-slice_fusion), channel_id=1, source_target_pairs={{0,1},{1,0},{2,3},{3,2},{4,5},{5,4},{6,7},{7,6},{8,9},{9,8},{10,11... | collective-permute-start | bytes 1327112 | tf_op jit(solution)/shard_map/ppermute | solution.py:268
  172.4 1.4 collective-permute-done.3
  173.9 0.6 reshape.265
  174.7 1.2 reshape.300
  176.0 5.5 %all-to-all-start.5 = ((bf16[128,2,432]{2,1,0:T(2,128)(2,1)}), bf16[128,2,432]{2,1,0:T(2,128)(2,1)S(1)}, u32[]{:S(2)}, u32[]{:S(2)}) async-start(bf16[128,2,432]{2,1,0:T(2,128)(2,1)} %reshape.300), calls=%async_computation.5 | async-start | bytes 524288 | tf_op jit(solution)/shard_map/all_to_all | solution.py:277
  181.7 15.2 %all-to-all-done.5 = bf16[128,2,432]{2,1,0:T(2,128)(2,1)S(1)} async-done(((bf16[128,2,432]{2,1,0:T(2,128)(2,1)}), bf16[128,2,432]{2,1,0:T(2,128)(2,1)S(1)}, u32[]{:S(2)}, u32[]{:S(2)}) %all-to-all-start.5) | async-done | bytes 221216 | tf_op jit(solution)/shard_map/all_to_all | solution.py:277
  196.9 0.5 reshape.301
  197.7 15.0 %all_to_all.36 = bf16[16,2,16,144]{3,2,1,0:T(8,128)(2,1)S(1)} all-to-all(bf16[16,2,16,144]{3,2,1,0:T(8,128)(2,1)S(1)} %broadcast_in_dim.116), channel_id=1, replica_groups=mesh['req'=4,'exp'=8,'shard'=16] {'shard'}, dimensions={0} | all-to-all | bytes 294912 | tf_op jit(solution)/shard_map/all_to_all | solution.py:61
  212.9 1.0 reshape.268
  (93 shorter events, 7.7 us)
Async XLA Ops:
  0.0 168.6 %copy-start = (bf16[1,2,180,2304]{3,1,2,0:T(2,128)(2,1)S(1)}, bf16[1,2,180,2304]{3,1,2,0:T(2,128)(2,1)}, u32[]{:S(2)}) copy-start(bf16[1,2,180,2304]{3,1,2,0:T(2,128)(2,1)} %param.24) | copy-start | bytes 4976644
  12.3 14.0 %copy-start.6 = (s32[2,16,2]{1,2,0:T(2,128)S(1)}, s32[2,16,2]{1,2,0:T(2,128)}, u32[]{:S(2)}) copy-start(s32[2,16,2]{1,2,0:T(2,128)} %param.15) | copy-start | bytes 772
  12.3 14.1 %copy-start.7 = (bf16[2,16,2]{1,2,0:T(2,128)(2,1)S(1)}, bf16[2,16,2]{1,2,0:T(2,128)(2,1)}, u32[]{:S(2)}) copy-start(bf16[2,16,2]{1,2,0:T(2,128)(2,1)} %param.16) | copy-start | bytes 388
  12.3 14.3 %copy-start.9 = (s32[1,2]{1,0:T(1,128)S(1)}, s32[1,2]{1,0:T(1,128)}, u32[]{:S(2)}) copy-start(s32[1,2]{1,0:T(1,128)} %param.18) | copy-start | bytes 28
  12.3 14.4 %copy-start.8 = (s32[1,256]{1,0:T(1,128)S(1)}, s32[1,256]{1,0:T(1,128)}, u32[]{:S(2)}) copy-start(s32[1,256]{1,0:T(1,128)} %param.19) | copy-start | bytes 3076
  12.3 15.0 %copy-start.4 = (bf16[2,16,2304]{2,1,0:T(8,128)(2,1)S(1)}, bf16[2,16,2304]{2,1,0:T(8,128)(2,1)}, u32[]{:S(2)}) copy-start(bf16[2,16,2304]{2,1,0:T(8,128)(2,1)} %param.14) | copy-start | bytes 442372
  15.0 28.0 %all-to-all-start = ((bf16[8,1,16,2304]{3,2,1,0:T(8,128)(2,1)}), bf16[8,1,16,2304]{3,2,1,0:T(8,128)(2,1)S(1)}, u32[]{:S(2)}, u32[]{:S(2)}) async-start(bf16[8,1,16,2304]{3,2,1,0:T(8,128)(2,1)} %broadcast_in_dim.64), calls=%async_computation | async-start | bytes 1179648 | tf_op jit(solution)/shard_map/all_to_all | solution.py:61
  43.0 7.9 %collective-permute-start = (bf16[8,1,16,2304]{3,2,1,0:T(8,128)(2,1)S(1)}, bf16[8,1,16,2304]{3,2,1,0:T(8,128)(2,1)S(1)}, u32[]{:S(2)}, u32[]{:S(2)}) collective-permute-start(bf16[8,1,16,2304]{3,2,1,0:T(8,128)(2,1)S(1)} %all-to-all-done), channel_id=1, source_target_pairs={{0,1},{1,0},{2,3},{3,2},{4,5},{5,4},{6,7},{7,6},{8,9},{9,8},{10,11... | collective-permute-start | bytes 1769480 | tf_op jit(solution)/shard_map/ppermute | solution.py:99
  68.4 5.7 %copy-start.1 = (f32[256,36]{1,0:T(8,128)S(1)}, f32[256,36]{1,0:T(8,128)}, u32[]{:S(2)}) copy-start(f32[256,36]{1,0:T(8,128)} %get-tuple-element.12) | copy-start | bytes 110596
  70.1 4.0 %collective-permute-start.1 = (bf16[8,2,16,1224]{3,2,1,0:T(8,128)(2,1)S(1)}, bf16[8,2,16,1224]{3,2,1,0:T(8,128)(2,1)S(1)}, u32[]{:S(2)}, u32[]{:S(2)}) collective-permute-start(bf16[8,2,16,1224]{3,2,1,0:T(8,128)(2,1)S(1)} %concatenate.32), channel_id=1, source_target_pairs={{0,1},{1,0},{2,3},{3,2},{4,5},{5,4},{6,7},{7,6},{8,9},{9,8},{10,11... | collective-permute-start | bytes 1880072 | tf_op jit(solution)/shard_map/ppermute | solution.py:179
  78.4 37.5 %all-to-all-start.1 = ((bf16[128,2,1224]{2,1,0:T(2,128)(2,1)}), bf16[128,2,1224]{2,1,0:T(2,128)(2,1)S(1)}, u32[]{:S(2)}, u32[]{:S(2)}) async-start(bf16[128,2,1224]{2,1,0:T(2,128)(2,1)} %reshape.262), calls=%async_computation.1 | async-start | bytes 1310720 | tf_op jit(solution)/shard_map/all_to_all | solution.py:203
  116.4 15.8 %copy-start.3 = (bf16[144,2304]{1,0:T(8,128)(2,1)S(1)}, bf16[144,2304]{1,0:T(8,128)(2,1)}, u32[]{:S(2)}) copy-start(bf16[144,2304]{1,0:T(8,128)(2,1)} %param.23) | copy-start | bytes 1990660
  118.9 13.1 %all-to-all-start.2 = ((bf16[16,2,2304]{2,1,0:T(2,128)(2,1)}), bf16[16,2,2304]{2,1,0:T(2,128)(2,1)S(1)}, u32[]{:S(2)}, u32[]{:S(2)}) async-start(bf16[16,2,2304]{2,1,0:T(2,128)(2,1)} %broadcast_in_dim.114), calls=%async_computation.2 | async-start | bytes 294912 | tf_op jit(solution)/shard_map/all_to_all | solution.py:61
  133.2 14.9 %all-to-all-start.3 = ((bf16[16,2,16,144]{3,2,1,0:T(8,128)(2,1)}), bf16[16,2,16,144]{3,2,1,0:T(8,128)(2,1)S(1)}, u32[]{:S(2)}, u32[]{:S(2)}) async-start(bf16[16,2,16,144]{3,2,1,0:T(8,128)(2,1)} %broadcast_in_dim.115), calls=%async_computation.3 | async-start | bytes 524288 | tf_op jit(solution)/shard_map/all_to_all | solution.py:61
  148.1 0.7 copy-start.5
  164.8 3.5 %collective-permute-start.2 = (bf16[8,1,6,2304]{3,2,1,0:T(8,128)(2,1)S(1)}, bf16[8,1,6,2304]{3,2,1,0:T(8,128)(2,1)S(1)}, u32[]{:S(2)}, u32[]{:S(2)}) collective-permute-start(bf16[8,1,6,2304]{3,2,1,0:T(8,128)(2,1)S(1)} %all_to_all.35), channel_id=1, source_target_pairs={{0,1},{1,0},{2,3},{3,2},{4,5},{5,4},{6,7},{7,6},{8,9},{9,8},{10,11... | collective-permute-start | bytes 663560 | tf_op jit(solution)/shard_map/ppermute | solution.py:258
  168.6 1.2 copy-start.2
  170.1 3.7 %collective-permute-start.3 = (f32[8,1,6,2304]{3,0,2,1:T(8,128)S(1)}, f32[8,1,6,2304]{3,0,2,1:T(8,128)S(1)}, u32[]{:S(2)}, u32[]{:S(2)}) collective-permute-start(f32[8,1,6,2304]{3,0,2,1:T(8,128)S(1)} %constant_dynamic-slice_fusion), channel_id=1, source_target_pairs={{0,1},{1,0},{2,3},{3,2},{4,5},{5,4},{6,7},{7,6},{8,9},{9,8},{10,11... | collective-permute-start | bytes 1327112 | tf_op jit(solution)/shard_map/ppermute | solution.py:268
  176.0 20.9 %all-to-all-start.5 = ((bf16[128,2,432]{2,1,0:T(2,128)(2,1)}), bf16[128,2,432]{2,1,0:T(2,128)(2,1)S(1)}, u32[]{:S(2)}, u32[]{:S(2)}) async-start(bf16[128,2,432]{2,1,0:T(2,128)(2,1)} %reshape.300), calls=%async_computation.5 | async-start | bytes 524288 | tf_op jit(solution)/shard_map/all_to_all | solution.py:277

commit v16 on v13

--- a/solution.py
+++ b/solution.py
@@ -105,7 +105,6 @@
         jnp.concatenate([own_query, partner_query], axis=1),
         jnp.concatenate([partner_query, own_query], axis=1),
     )
-    group_query, served_extras = lax.optimization_barrier((group_query, served_extras))
     top_count = route_ids.shape[2]
     served_resid = served_extras[:, :, :width]
     served_probs = served_extras[:, :, width : width + top_count]

time: 213 us -> 209 us (0.981)
  starting transfers between devices: 49.3 us -> 45 us
    all_to_all x3, waiting for transfers between devices: 23.6 us -> 35.8 us  [gather_blocks(): return lax.all_to_all(spread, axis_name, 0, 0, tiled=False)]
    all_to_all x1, waiting for transfers between devices: 23 us -> 11.1 us  [on_device(): arrived = lax.all_to_all(packed, ('exp', 'shard'), 0, 0, tiled=True)]
    all_to_all x1, starting transfers between devices: 13.2 us -> 8.94 us  [on_device(): arrived = lax.all_to_all(packed, ('exp', 'shard'), 0, 0, tiled=True)]
where the time goes in v16:
time: 209 us; the launch traced here: 208 us
  waiting for transfers between devices  66.8 us (32%)
  blocking collectives  53.1 us (25%)
  starting transfers between devices  45 us (22%)
  Pallas kernels  14.9 us (7%)
  local copies, waits for them, and re-layouts  14 us (7%)
  other arithmetic  7.76 us (4%)
  matrix products  5.79 us (3%)
    all_to_all x3, waiting for transfers between devices, gather_blocks(): return lax.all_to_all(spread, axis_name, 0, 0, tiled=False)  35.8 us
    all_to_all x3, starting transfers between devices, gather_blocks(): return lax.all_to_all(spread, axis_name, 0, 0, tiled=False)  18.5 us
    all_to_all x1, blocking collectives, on_device(): lax.all_to_all(lax.dynamic_slice_in_dim(sent_rows, core_index, 1, 1), 'ex...  15.5 us
    all_to_all x1, waiting for transfers between devices, on_device(): lax.all_to_all(pair_rows, ('exp', 'shard'), 0, 0, tiled=True)  15.2 us
    all_to_all x1, blocking collectives, gather_blocks(): return lax.all_to_all(spread, axis_name, 0, 0, tiled=False)  15 us
    pallas_call x1, Pallas kernels, attend(): pl.pallas_call(functools.partial(attend_kernel, heads, head_size), out_sh...  14.9 us
    all_gather x1, blocking collectives, on_device(): all_query = lax.all_gather(query_stretch, 'req', axis=0, tiled=True)  11.4 us
    all_gather x1, blocking collectives, on_device(): all_extras = lax.all_gather(extras, 'req', axis=0, tiled=True)  11.2 us
  transfers between devices with their start and end apart: 9, of which 9 were waited for; matrix products, arithmetic and copies ran while one was open for 2% of the time, Pallas kernels for 0%

profile of v16, /device:TPU:1, one launch (start us, length us, event | category | flops | bytes accessed | tf_op | source)
XLA Modules:
  0.0 207.8 jit_solution(9976469653204110442)
XLA Ops:
  0.0 0.9 compare_and_fusion
  0.9 11.4 %all_gather.7 = bf16[8,16,2304]{2,1,0:T(8,128)(2,1)S(1)} all-gather(bf16[2,16,2304]{2,1,0:T(8,128)(2,1)} %param.13), channel_id=1, replica_groups=mesh['req'=4,'exp'=8,'shard'=16] {'req'}, dimensions={0}, use_global_device_ids=true | all-gather | bytes 737280 | tf_op jit(solution)/shard_map/all_gather | solution.py:92
  12.3 0.6 dynamic-slice.4
  12.9 0.6 gather_fusion.1
  13.5 0.7 fusion.34
  14.1 0.8 broadcast_in_dim.66
  15.0 11.3 %all-to-all-start = ((bf16[8,1,16,2304]{3,2,1,0:T(8,128)(2,1)}), bf16[8,1,16,2304]{3,2,1,0:T(8,128)(2,1)S(1)}, u32[]{:S(2)}, u32[]{:S(2)}) async-start(bf16[8,1,16,2304]{3,2,1,0:T(8,128)(2,1)} %broadcast_in_dim.66), calls=%async_computation | async-start | bytes 1179648 | tf_op jit(solution)/shard_map/all_to_all | solution.py:62
  27.4 15.6 %all-to-all-done = bf16[8,1,16,2304]{3,2,1,0:T(8,128)(2,1)S(1)} async-done(((bf16[8,1,16,2304]{3,2,1,0:T(8,128)(2,1)}), bf16[8,1,16,2304]{3,2,1,0:T(8,128)(2,1)S(1)}, u32[]{:S(2)}, u32[]{:S(2)}) %all-to-all-start) | async-done | bytes 589856 | tf_op jit(solution)/shard_map/all_to_all | solution.py:62
  43.0 5.1 %collective-permute-start = (bf16[8,1,16,2304]{3,2,1,0:T(8,128)(2,1)S(1)}, bf16[8,1,16,2304]{3,2,1,0:T(8,128)(2,1)S(1)}, u32[]{:S(2)}, u32[]{:S(2)}) collective-permute-start(bf16[8,1,16,2304]{3,2,1,0:T(8,128)(2,1)S(1)} %all-to-all-done), channel_id=1, source_target_pairs={{0,1},{1,0},{2,3},{3,2},{4,5},{5,4},{6,7},{7,6},{8,9},{9,8},{10,11... | collective-permute-start | bytes 1769480 | tf_op jit(solution)/shard_map/ppermute | solution.py:100
  48.3 0.8 fusion.26.mask_ref
  49.1 0.6 collective-permute-done
  49.7 1.1 maximum_select_fusion
  50.8 14.9 %shard_map.127 = (f32[256,2304]{1,0:T(8,128)}, f32[256,36]{1,0:T(8,128)}, f32[256,36]{1,0:T(8,128)}) custom-call(bf16[256,2304]{1,0:T(8,128)(2,1)} %bitcast.100, bf16[128,2304]{1,0:T(8,128)(2,1)} %bitcast.114, bf16[128,2304]{1,0:T(8,128)(2,1)} %bitcast.115, s32[256,128]{1,0:T(8,128)} %fusion.26.mask_ref), custom_call_target="tpu_custom_call" | custom-call | tf_op jit(solution)/shard_map/pallas_call | solution.py:48
  65.7 0.9 reduce_precision.6
  66.6 0.9 convert_element_type.135
  67.6 1.4 dynamic-slice_convert_fusion
  69.3 2.3 %collective-permute-start.1 = (bf16[8,2,16,1224]{3,2,1,0:T(8,128)(2,1)S(1)}, bf16[8,2,16,1224]{3,2,1,0:T(8,128)(2,1)S(1)}, u32[]{:S(2)}, u32[]{:S(2)}) collective-permute-start(bf16[8,2,16,1224]{3,2,1,0:T(8,128)(2,1)S(1)} %concatenate.32), channel_id=1, source_target_pairs={{0,1},{1,0},{2,3},{3,2},{4,5},{5,4},{6,7},{7,6},{8,9},{9,8},{10,11... | collective-permute-start | bytes 1880072 | tf_op jit(solution)/shard_map/ppermute | solution.py:179
  71.9 1.4 collective-permute-done.1
  73.4 0.7 fusion.21
  74.1 2.1 %add_convert_fusion = bf16[8,2,16,1152]{3,2,1,0:T(8,128)(2,1)S(1)} fusion(f32[8,2,16,1152]{3,2,1,0:T(8,128)S(1)} %fusion.21, bf16[8,2,16,1224]{3,2,1,0:T(8,128)(2,1)S(1)} %collective-permute-done.1, f32[8,2,16,2304]{3,2,1,0:T(8,128)} %bitcast.107, s32[]{:T(128)S(6)} %select_n.117, f32[8,2,16,36]{3,2,1,0:T(8,128)S(1)} %get-tuple-element.14, ...), kind=kOutput, calls=%fused_computation.14 | convolution fusion | flops 65196288 | bytes 3580424 | tf_op jit(solution)/shard_map/...h,hc->...c/dot_general | solution.py:163
  76.5 1.1 reshape.263
  77.6 8.9 %all-to-all-start.1 = ((bf16[128,2,1224]{2,1,0:T(2,128)(2,1)}), bf16[128,2,1224]{2,1,0:T(2,128)(2,1)S(1)}, u32[]{:S(2)}, u32[]{:S(2)}) async-start(bf16[128,2,1224]{2,1,0:T(2,128)(2,1)} %reshape.263), calls=%async_computation.1 | async-start | bytes 1310720 | tf_op jit(solution)/shard_map/all_to_all | solution.py:203
  86.5 11.2 %all_gather.6 = bf16[8,16,2308]{2,1,0:T(8,128)(2,1)S(1)} all-gather(bf16[2,16,2308]{2,1,0:T(8,128)(2,1)S(1)} %concatenate.29), channel_id=1, replica_groups=mesh['req'=4,'exp'=8,'shard'=16] {'req'}, dimensions={0}, use_global_device_ids=true | all-gather | bytes 738560 | tf_op jit(solution)/shard_map/all_gather | solution.py:93
  97.7 0.6 gather_fusion
  98.6 11.1 %all-to-all-done.1 = bf16[128,2,1224]{2,1,0:T(2,128)(2,1)S(1)} async-done(((bf16[128,2,1224]{2,1,0:T(2,128)(2,1)}), bf16[128,2,1224]{2,1,0:T(2,128)(2,1)S(1)}, u32[]{:S(2)}, u32[]{:S(2)}) %all-to-all-start.1) | async-done | bytes 626720 | tf_op jit(solution)/shard_map/all_to_all | solution.py:203
  109.9 0.4 fusion.66
  110.7 0.5 fusion.4
  111.2 0.5 fusion.5
  112.1 0.7 broadcast_in_dim.114
  112.9 3.8 %all-to-all-start.2 = ((bf16[16,2,2304]{2,1,0:T(2,128)(2,1)}), bf16[16,2,2304]{2,1,0:T(2,128)(2,1)S(1)}, u32[]{:S(2)}, u32[]{:S(2)}) async-start(bf16[16,2,2304]{2,1,0:T(2,128)(2,1)} %broadcast_in_dim.114), calls=%async_computation.2 | async-start | bytes 294912 | tf_op jit(solution)/shard_map/all_to_all | solution.py:62
  117.1 8.9 %all-to-all-done.2 = bf16[16,2,2304]{2,1,0:T(2,128)(2,1)S(1)} async-done(((bf16[16,2,2304]{2,1,0:T(2,128)(2,1)}), bf16[16,2,2304]{2,1,0:T(2,128)(2,1)S(1)}, u32[]{:S(2)}, u32[]{:S(2)}) %all-to-all-start.2) | async-done | bytes 147488 | tf_op jit(solution)/shard_map/all_to_all | solution.py:62
  126.4 0.8 broadcast_in_dim.115
  127.2 3.4 %all-to-all-start.3 = ((bf16[16,2,16,144]{3,2,1,0:T(8,128)(2,1)}), bf16[16,2,16,144]{3,2,1,0:T(8,128)(2,1)S(1)}, u32[]{:S(2)}, u32[]{:S(2)}) async-start(bf16[16,2,16,144]{3,2,1,0:T(8,128)(2,1)} %broadcast_in_dim.115), calls=%async_computation.3 | async-start | bytes 524288 | tf_op jit(solution)/shard_map/all_to_all | solution.py:62
  130.6 11.4 %all-to-all-done.3 = bf16[16,2,16,144]{3,2,1,0:T(8,128)(2,1)S(1)} async-done(((bf16[16,2,16,144]{3,2,1,0:T(8,128)(2,1)}), bf16[16,2,16,144]{3,2,1,0:T(8,128)(2,1)S(1)}, u32[]{:S(2)}, u32[]{:S(2)}) %all-to-all-start.3) | async-done | bytes 147488 | tf_op jit(solution)/shard_map/all_to_all | solution.py:62
  143.2 15.5 %all_to_all.35 = bf16[8,1,6,2304]{3,2,1,0:T(8,128)(2,1)S(1)} all-to-all(bf16[8,1,6,2304]{3,2,1,0:T(8,128)(2,1)S(1)} %copy.69), channel_id=1, replica_groups=mesh['req'=4,'exp'=8,'shard'=16] {'exp'}, dimensions={0} | all-to-all | bytes 442368 | tf_op jit(solution)/shard_map/all_to_all | solution.py:251
  158.7 2.3 %collective-permute-start.2 = (bf16[8,1,6,2304]{3,2,1,0:T(8,128)(2,1)S(1)}, bf16[8,1,6,2304]{3,2,1,0:T(8,128)(2,1)S(1)}, u32[]{:S(2)}, u32[]{:S(2)}) collective-permute-start(bf16[8,1,6,2304]{3,2,1,0:T(8,128)(2,1)S(1)} %all_to_all.35), channel_id=1, source_target_pairs={{0,1},{1,0},{2,3},{3,2},{4,5},{5,4},{6,7},{7,6},{8,9},{9,8},{10,11... | collective-permute-start | bytes 663560 | tf_op jit(solution)/shard_map/ppermute | solution.py:258
  161.0 1.2 collective-permute-done.2
  162.6 0.6 fusion.2
  163.4 0.4 copy-done.2
  164.1 2.3 %collective-permute-start.3 = (f32[8,1,6,2304]{3,0,2,1:T(8,128)S(1)}, f32[8,1,6,2304]{3,0,2,1:T(8,128)S(1)}, u32[]{:S(2)}, u32[]{:S(2)}) collective-permute-start(f32[8,1,6,2304]{3,0,2,1:T(8,128)S(1)} %constant_dynamic-slice_fusion), channel_id=1, source_target_pairs={{0,1},{1,0},{2,3},{3,2},{4,5},{5,4},{6,7},{7,6},{8,9},{9,8},{10,11... | collective-permute-start | bytes 1327112 | tf_op jit(solution)/shard_map/ppermute | solution.py:268
  166.4 1.4 collective-permute-done.3
  167.8 0.6 reshape.266
  168.7 1.2 reshape.301
  169.9 5.5 %all-to-all-start.5 = ((bf16[128,2,432]{2,1,0:T(2,128)(2,1)}), bf16[128,2,432]{2,1,0:T(2,128)(2,1)S(1)}, u32[]{:S(2)}, u32[]{:S(2)}) async-start(bf16[128,2,432]{2,1,0:T(2,128)(2,1)} %reshape.301), calls=%async_computation.5 | async-start | bytes 524288 | tf_op jit(solution)/shard_map/all_to_all | solution.py:277
  175.6 15.2 %all-to-all-done.5 = bf16[128,2,432]{2,1,0:T(2,128)(2,1)S(1)} async-done(((bf16[128,2,432]{2,1,0:T(2,128)(2,1)}), bf16[128,2,432]{2,1,0:T(2,128)(2,1)S(1)}, u32[]{:S(2)}, u32[]{:S(2)}) %all-to-all-start.5) | async-done | bytes 221216 | tf_op jit(solution)/shard_map/all_to_all | solution.py:277
  190.8 0.5 reshape.302
  191.7 15.0 %all_to_all.36 = bf16[16,2,16,144]{3,2,1,0:T(8,128)(2,1)S(1)} all-to-all(bf16[16,2,16,144]{3,2,1,0:T(8,128)(2,1)S(1)} %broadcast_in_dim.116), channel_id=1, replica_groups=mesh['req'=4,'exp'=8,'shard'=16] {'shard'}, dimensions={0} | all-to-all | bytes 294912 | tf_op jit(solution)/shard_map/all_to_all | solution.py:62
  206.8 1.0 reshape.269
  (96 shorter events, 7.3 us)
Async XLA Ops:
  0.0 162.6 %copy-start = (bf16[1,2,180,2304]{3,1,2,0:T(2,128)(2,1)S(1)}, bf16[1,2,180,2304]{3,1,2,0:T(2,128)(2,1)}, u32[]{:S(2)}) copy-start(bf16[1,2,180,2304]{3,1,2,0:T(2,128)(2,1)} %param.24) | copy-start | bytes 4976644
  0.9 11.4 %copy-start.6 = (pred[2]{0:T(512)(128)(4,1)}, pred[2]{0:T(512)(128)(4,1)S(1)}, u32[]{:S(2)}) copy-start(pred[2]{0:T(512)(128)(4,1)S(1)} %get-tuple-element.16) | copy-start | bytes 10
  12.3 14.0 %copy-start.11 = (s32[1,2]{1,0:T(1,128)S(1)}, s32[1,2]{1,0:T(1,128)}, u32[]{:S(2)}) copy-start(s32[1,2]{1,0:T(1,128)} %param.18) | copy-start | bytes 28
  12.3 14.0 %copy-start.10 = (s32[1,256]{1,0:T(1,128)S(1)}, s32[1,256]{1,0:T(1,128)}, u32[]{:S(2)}) copy-start(s32[1,256]{1,0:T(1,128)} %param.19) | copy-start | bytes 3076
  15.0 28.0 %all-to-all-start = ((bf16[8,1,16,2304]{3,2,1,0:T(8,128)(2,1)}), bf16[8,1,16,2304]{3,2,1,0:T(8,128)(2,1)S(1)}, u32[]{:S(2)}, u32[]{:S(2)}) async-start(bf16[8,1,16,2304]{3,2,1,0:T(8,128)(2,1)} %broadcast_in_dim.66), calls=%async_computation | async-start | bytes 1179648 | tf_op jit(solution)/shard_map/all_to_all | solution.py:62
  43.0 6.7 %collective-permute-start = (bf16[8,1,16,2304]{3,2,1,0:T(8,128)(2,1)S(1)}, bf16[8,1,16,2304]{3,2,1,0:T(8,128)(2,1)S(1)}, u32[]{:S(2)}, u32[]{:S(2)}) collective-permute-start(bf16[8,1,16,2304]{3,2,1,0:T(8,128)(2,1)S(1)} %all-to-all-done), channel_id=1, source_target_pairs={{0,1},{1,0},{2,3},{3,2},{4,5},{5,4},{6,7},{7,6},{8,9},{9,8},{10,11... | collective-permute-start | bytes 1769480 | tf_op jit(solution)/shard_map/ppermute | solution.py:100
  67.6 4.0 %copy-start.8 = (s32[2,16,2]{1,2,0:T(2,128)S(1)}, s32[2,16,2]{1,2,0:T(2,128)}, u32[]{:S(2)}) copy-start(s32[2,16,2]{1,2,0:T(2,128)} %param.15) | copy-start | bytes 772
  67.6 4.1 %copy-start.9 = (bf16[2,16,2]{1,2,0:T(2,128)(2,1)S(1)}, bf16[2,16,2]{1,2,0:T(2,128)(2,1)}, u32[]{:S(2)}) copy-start(bf16[2,16,2]{1,2,0:T(2,128)(2,1)} %param.16) | copy-start | bytes 388
  67.6 4.2 %copy-start.4 = (bf16[2,16,2304]{2,1,0:T(8,128)(2,1)S(1)}, bf16[2,16,2304]{2,1,0:T(8,128)(2,1)}, u32[]{:S(2)}) copy-start(bf16[2,16,2304]{2,1,0:T(8,128)(2,1)} %param.14) | copy-start | bytes 442372
  67.6 5.7 %copy-start.1 = (f32[256,36]{1,0:T(8,128)S(1)}, f32[256,36]{1,0:T(8,128)}, u32[]{:S(2)}) copy-start(f32[256,36]{1,0:T(8,128)} %get-tuple-element.8) | copy-start | bytes 110596
  69.3 4.0 %collective-permute-start.1 = (bf16[8,2,16,1224]{3,2,1,0:T(8,128)(2,1)S(1)}, bf16[8,2,16,1224]{3,2,1,0:T(8,128)(2,1)S(1)}, u32[]{:S(2)}, u32[]{:S(2)}) collective-permute-start(bf16[8,2,16,1224]{3,2,1,0:T(8,128)(2,1)S(1)} %concatenate.32), channel_id=1, source_target_pairs={{0,1},{1,0},{2,3},{3,2},{4,5},{5,4},{6,7},{7,6},{8,9},{9,8},{10,11... | collective-permute-start | bytes 1880072 | tf_op jit(solution)/shard_map/ppermute | solution.py:179
  77.6 20.7 %copy-start.7 = (pred[2]{0:T(512)(128)(4,1)S(1)}, pred[2]{0:T(512)(128)(4,1)}, u32[]{:S(2)}) copy-start(pred[2]{0:T(512)(128)(4,1)} %copy-done.6) | copy-start | bytes 10
  77.6 32.2 %all-to-all-start.1 = ((bf16[128,2,1224]{2,1,0:T(2,128)(2,1)}), bf16[128,2,1224]{2,1,0:T(2,128)(2,1)S(1)}, u32[]{:S(2)}, u32[]{:S(2)}) async-start(bf16[128,2,1224]{2,1,0:T(2,128)(2,1)} %reshape.263), calls=%async_computation.1 | async-start | bytes 1310720 | tf_op jit(solution)/shard_map/all_to_all | solution.py:203
  110.3 15.8 %copy-start.3 = (bf16[144,2304]{1,0:T(8,128)(2,1)S(1)}, bf16[144,2304]{1,0:T(8,128)(2,1)}, u32[]{:S(2)}) copy-start(bf16[144,2304]{1,0:T(8,128)(2,1)} %param.23) | copy-start | bytes 1990660
  112.9 13.1 %all-to-all-start.2 = ((bf16[16,2,2304]{2,1,0:T(2,128)(2,1)}), bf16[16,2,2304]{2,1,0:T(2,128)(2,1)S(1)}, u32[]{:S(2)}, u32[]{:S(2)}) async-start(bf16[16,2,2304]{2,1,0:T(2,128)(2,1)} %broadcast_in_dim.114), calls=%async_computation.2 | async-start | bytes 294912 | tf_op jit(solution)/shard_map/all_to_all | solution.py:62
  127.2 14.9 %all-to-all-start.3 = ((bf16[16,2,16,144]{3,2,1,0:T(8,128)(2,1)}), bf16[16,2,16,144]{3,2,1,0:T(8,128)(2,1)S(1)}, u32[]{:S(2)}, u32[]{:S(2)}) async-start(bf16[16,2,16,144]{3,2,1,0:T(8,128)(2,1)} %broadcast_in_dim.115), calls=%async_computation.3 | async-start | bytes 524288 | tf_op jit(solution)/shard_map/all_to_all | solution.py:62
  142.1 0.7 copy-start.5
  158.7 3.5 %collective-permute-start.2 = (bf16[8,1,6,2304]{3,2,1,0:T(8,128)(2,1)S(1)}, bf16[8,1,6,2304]{3,2,1,0:T(8,128)(2,1)S(1)}, u32[]{:S(2)}, u32[]{:S(2)}) collective-permute-start(bf16[8,1,6,2304]{3,2,1,0:T(8,128)(2,1)S(1)} %all_to_all.35), channel_id=1, source_target_pairs={{0,1},{1,0},{2,3},{3,2},{4,5},{5,4},{6,7},{7,6},{8,9},{9,8},{10,11... | collective-permute-start | bytes 663560 | tf_op jit(solution)/shard_map/ppermute | solution.py:258
  162.6 1.2 copy-start.2
  164.1 3.7 %collective-permute-start.3 = (f32[8,1,6,2304]{3,0,2,1:T(8,128)S(1)}, f32[8,1,6,2304]{3,0,2,1:T(8,128)S(1)}, u32[]{:S(2)}, u32[]{:S(2)}) collective-permute-start(f32[8,1,6,2304]{3,0,2,1:T(8,128)S(1)} %constant_dynamic-slice_fusion), channel_id=1, source_target_pairs={{0,1},{1,0},{2,3},{3,2},{4,5},{5,4},{6,7},{7,6},{8,9},{9,8},{10,11... | collective-permute-start | bytes 1327112 | tf_op jit(solution)/shard_map/ppermute | solution.py:268
  169.9 20.9 %all-to-all-start.5 = ((bf16[128,2,432]{2,1,0:T(2,128)(2,1)}), bf16[128,2,432]{2,1,0:T(2,128)(2,1)S(1)}, u32[]{:S(2)}, u32[]{:S(2)}) async-start(bf16[128,2,432]{2,1,0:T(2,128)(2,1)} %reshape.301), calls=%async_computation.5 | async-start | bytes 524288 | tf_op jit(solution)/shard_map/all_to_all | solution.py:277
